TPU v7x, 32 devices: a whole 2x2x4 slice. The times are simulated.
32 devices in a mesh: dp: 4 (over y, x), ctx: 8 (over z, core).
Axes of the slice: x: 2, y: 2, z: 4, core: 2. Of those that a mesh axis runs over, the one named last changes fastest.
Arguments:
- clip_tokens: bfloat16 [4, 2048, 3072], P('dp', 'ctx'), may hold values from -6 to 6
- qkv_weight: bfloat16 [3, 3072, 1536], P(None, None, 'dp'), may hold values from -0.15625 to 0.15625
- out_weight: bfloat16 [1536, 3072], P('dp'), may hold values from -0.5 to 0.5
- neighbours: int32 [32, 10], P('ctx'), may hold values from 0 to 31, as said below
- counts: int32 [32], P('ctx'), may hold values from 2 to 10, as said below
- bias_index: int32 [32, 10], P('ctx'), may hold values from 0 to 342
- rel_bias: float32 [12, 343], P('dp'), may hold values from -4 to 262
Outputs:
- layer_out: bfloat16 [4, 2048, 3072], P('dp', 'ctx')
Inputs may be any that keep to these rules, and one draw needn't show every extreme that they name: `neighbours`: tile g lies on ctx index g / 4. Row g starts with g itself; its first counts[g] entries are distinct tiles on ctx indices at most 6 away from that of g; the entries from counts[g] on equal g. Of the tiles of one ctx index, those named in the live entries of the rows of another index are at most 2, and exactly 2 for some pairs of indices. `counts`: some tile has 10 live slots.
All inputs are finite; a program needn't handle non-finite values.
Results may differ from a plain program's by a relative error of at most 0.012.
Values may be sent and summed in bfloat16 or wider, within the bound.
No kernel may reach another device: no remote copies, remote signals or barrier semaphores. Data moves between devices by JAX's collectives and lax.ppermute only.
A program may use at most 128 MiB of HBM per device.

v0:
```python
import math

import jax
import jax.numpy as jnp
from jax import lax
from jax.sharding import PartitionSpec as P

TILE = 64
REACH = 6
KMAX = 10


def shifted(value, axis, steps):
    count = lax.axis_size(axis)
    first, last = (max(0, -steps), min(count, count - steps))
    return lax.ppermute(value, axis, [(source, source + steps) for source in range(first, last)])


def local(clip_tokens, qkv_weight, out_weight, neighbours, counts, bias_index, rel_bias):
    heads_here = rel_bias.shape[0]
    width_here = out_weight.shape[0]
    head_size = width_here // heads_here
    tile_count = clip_tokens.shape[1] // TILE
    projected = jnp.einsum(
        "ctd,sdh->scth",
        lax.all_gather(clip_tokens, "dp", axis=0, tiled=True),
        qkv_weight,
        preferred_element_type=jnp.float32,
    ).astype(jnp.bfloat16)
    clip_count = projected.shape[1]
    queries = projected[0].reshape(clip_count, tile_count, TILE, heads_here, head_size)
    key_values = projected[1:3].reshape(2, clip_count, tile_count, TILE, width_here)
    own_index = lax.axis_index("ctx")
    offsets = list(range(1, REACH + 1)) + [-amount for amount in range(1, REACH + 1)]
    live_slots = jnp.arange(KMAX)[None, :] < counts[:, None]
    collected = [key_values]
    for offset in offsets:
        collected.append(shifted(key_values, "ctx", offset))
    buffer_tiles = jnp.concatenate(collected, axis=2)
    distance = own_index - neighbours // tile_count
    which_block = jnp.where(distance > 0, distance, jnp.where(distance < 0, REACH - distance, 0))
    position = which_block * tile_count + neighbours % tile_count
    gathered = jnp.take(buffer_tiles, position.reshape(-1), axis=2)
    gathered = gathered.reshape(2, clip_count, tile_count, KMAX, TILE, heads_here, head_size)
    scores = jnp.einsum(
        "ctihd,ctmjhd->cthimj", queries, gathered[0], preferred_element_type=jnp.float32
    ) * (1.0 / math.sqrt(head_size))
    one_hot = (bias_index[:, :, None] == jnp.arange(rel_bias.shape[1])[None, None, :]).astype(
        jnp.float32
    )
    looked_up = jnp.einsum("tmr,hr->thm", one_hot, rel_bias, precision=lax.Precision.HIGHEST)
    scores = scores + looked_up[None, :, :, None, :, None]
    scores = jnp.where(live_slots[None, :, None, None, :, None], scores, -1e30)
    row_max = jnp.max(scores, axis=(4, 5), keepdims=True)
    weights = jnp.exp(scores - row_max)
    weight_sum = jnp.sum(weights, axis=(4, 5))
    blended = jnp.einsum(
        "cthimj,ctmjhd->ctihd",
        weights.astype(jnp.bfloat16),
        gathered[1],
        preferred_element_type=jnp.float32,
    )
    attended = (blended / jnp.transpose(weight_sum, (0, 1, 3, 2))[..., None]).astype(jnp.bfloat16)
    attended = attended.reshape(clip_count, tile_count * TILE, width_here)
    partial_out = jnp.einsum(
        "cth,hd->ctd", attended, out_weight, preferred_element_type=jnp.float32
    ).astype(jnp.bfloat16)
    return lax.psum_scatter(
        lax.optimization_barrier(partial_out).astype(jnp.float32).astype(jnp.bfloat16),
        "dp",
        scatter_dimension=0,
        tiled=True,
    )


def solution(mesh):
    placed = (
        P("dp", "ctx", None),
        P(None, None, "dp"),
        P("dp", None),
        P("ctx", None),
        P("ctx"),
        P("ctx", None),
        P("dp", None),
    )
    return jax.shard_map(
        local, mesh=mesh, in_specs=placed, out_specs=P("dp", "ctx", None), check_vma=False
    )
```

profile of v0, /device:TPU:0, one launch (start us, length us, event | category | flops | bytes accessed | tf_op | source)
XLA Modules:
  0.0 739.2 jit_solution(10897213490841283450)
XLA Ops:
  7.3 74.8 %all-gather.2.cloned.1.call-done = bf16[4,256,3072]{2,1,0:T(8,128)(2,1)} async-done(((bf16[1,256,3072]{2,1,0:T(8,128)(2,1)}), bf16[4,256,3072]{2,1,0:T(8,128)(2,1)}) %all-gather.2.cloned.1.call-update) | async-done | bytes 6291472 | tf_op jit(solution)/shard_map/all_gather | solution.py:26
  82.1 12.5 %convert_bitcast_fusion = bf16[3,4,256,384]{3,2,1,0:T(8,128)(2,1)S(1)} fusion(bf16[4,256,3072]{2,1,0:T(8,128)(2,1)} %all-gather.2.cloned.1.call-done, bf16[3,3072,384]{2,1,0:T(8,128)(2,1)} %param.8), kind=kOutput, calls=%fused_computation.19 | convolution fusion | flops 7248936960 | bytes 15728640 | tf_op jit(solution)/shard_map/ctd,sdh->scth/dot_general | solution.py:24
  100.2 3.6 collective-permute-start.1
  103.8 4.3 collective-permute-start.2
  113.0 27.0 %collective-permute-start.5 = (bf16[2,4,4,64,384]{4,3,2,1,0:T(8,128)(2,1)}, bf16[2,4,4,64,384]{4,3,2,1,0:T(8,128)(2,1)}, u32[]{:S(2)}, u32[]{:S(2)}) collective-permute-start(bf16[2,4,4,64,384]{4,3,2,1,0:T(8,128)(2,1)} %bitcast.4), channel_id=1, source_target_pairs={{0,6},{1,7},{8,14},{9,15},{16,22},{17,23},{24,30},{25,31}} | collective-permute-start | bytes 4718600 | tf_op jit(solution)/shard_map/ppermute | solution.py:16
  141.9 29.6 %collective-permute-done.2 = bf16[2,4,4,64,384]{4,3,2,1,0:T(8,128)(2,1)} collective-permute-done((bf16[2,4,4,64,384]{4,3,2,1,0:T(8,128)(2,1)}, bf16[2,4,4,64,384]{4,3,2,1,0:T(8,128)(2,1)}, u32[]{:S(2)}, u32[]{:S(2)}) %collective-permute-start.2) | collective-permute-done | bytes 1572896 | tf_op jit(solution)/shard_map/ppermute | solution.py:16
  172.8 32.5 %collective-permute-done.3 = bf16[2,4,4,64,384]{4,3,2,1,0:T(8,128)(2,1)} collective-permute-done((bf16[2,4,4,64,384]{4,3,2,1,0:T(8,128)(2,1)}, bf16[2,4,4,64,384]{4,3,2,1,0:T(8,128)(2,1)}, u32[]{:S(2)}, u32[]{:S(2)}) %collective-permute-start.3) | collective-permute-done | bytes 1572896 | tf_op jit(solution)/shard_map/ppermute | solution.py:16
  206.6 32.3 %collective-permute-done.4 = bf16[2,4,4,64,384]{4,3,2,1,0:T(8,128)(2,1)} collective-permute-done((bf16[2,4,4,64,384]{4,3,2,1,0:T(8,128)(2,1)}, bf16[2,4,4,64,384]{4,3,2,1,0:T(8,128)(2,1)}, u32[]{:S(2)}, u32[]{:S(2)}) %collective-permute-start.4) | collective-permute-done | bytes 1572896 | tf_op jit(solution)/shard_map/ppermute | solution.py:16
  240.2 32.4 %collective-permute-done.5 = bf16[2,4,4,64,384]{4,3,2,1,0:T(8,128)(2,1)} collective-permute-done((bf16[2,4,4,64,384]{4,3,2,1,0:T(8,128)(2,1)}, bf16[2,4,4,64,384]{4,3,2,1,0:T(8,128)(2,1)}, u32[]{:S(2)}, u32[]{:S(2)}) %collective-permute-start.5) | collective-permute-done | bytes 1572896 | tf_op jit(solution)/shard_map/ppermute | solution.py:16
  302.0 9.5 %collective-permute-done.7 = bf16[2,4,4,64,384]{4,3,2,1,0:T(8,128)(2,1)} collective-permute-done((bf16[2,4,4,64,384]{4,3,2,1,0:T(8,128)(2,1)}, bf16[2,4,4,64,384]{4,3,2,1,0:T(8,128)(2,1)}, u32[]{:S(2)}, u32[]{:S(2)}) %collective-permute-start.7) | collective-permute-done | bytes 1572896 | tf_op jit(solution)/shard_map/ppermute | solution.py:16
  314.3 66.1 %collective-permute-done.8 = bf16[2,4,4,64,384]{4,3,2,1,0:T(8,128)(2,1)} collective-permute-done((bf16[2,4,4,64,384]{4,3,2,1,0:T(8,128)(2,1)}, bf16[2,4,4,64,384]{4,3,2,1,0:T(8,128)(2,1)}, u32[]{:S(2)}, u32[]{:S(2)}) %collective-permute-start.8) | collective-permute-done | bytes 1572896 | tf_op jit(solution)/shard_map/ppermute | solution.py:16
  385.9 146.2 %collective-permute-done.10 = bf16[2,4,4,64,384]{4,3,2,1,0:T(8,128)(2,1)} collective-permute-done((bf16[2,4,4,64,384]{4,3,2,1,0:T(8,128)(2,1)}, bf16[2,4,4,64,384]{4,3,2,1,0:T(8,128)(2,1)}, u32[]{:S(2)}, u32[]{:S(2)}) %collective-permute-start.10) | collective-permute-done | bytes 1572896 | tf_op jit(solution)/shard_map/ppermute | solution.py:16
  536.2 15.1 %gather_fusion = bf16[40,2,4,64,384]{4,3,2,1,0:T(8,128)(2,1)} fusion(bf16[2,4,52,64,384]{4,3,2,1,0:T(8,128)(2,1)} %constant_dynamic-update-slice_fusion, s32[1024]{0:T(1024)S(1)} %pad_clamp_fusion), kind=kCustom, calls=%fused_computation | custom fusion | bytes 31457440 | tf_op jit(solution)/shard_map/jit(_take)/gather | solution.py:43
  551.3 8.4 %select_bitcast_fusion = bf16[2,4,40,64,384]{4,3,1,0,2:T(8,128)(2,1)S(1)} fusion(bf16[40,2,4,64,384]{4,3,2,1,0:T(8,128)(2,1)} %gather_fusion, pred[40]{0:T(512)(128)(4,1)S(1)} %compare_and_fusion), kind=kLoop, calls=%fused_computation.1 | loop fusion | flops 7864320 | bytes 31457320 | tf_op jit(solution)/shard_map/jit(_take)/select_n | solution.py:43
  559.7 6.3 fusion.35
  566.0 20.6 %reshape.95 = bf16[4,4,10,64,3,128]{5,4,3,0,2,1:T(4,128)(2,1)} reshape(bf16[1,4,40,64,384]{4,3,1,0,2:T(8,128)(2,1)} %get-tuple-element.6) | data formatting | bytes 15728640 | tf_op jit(solution)/shard_map/squeeze | solution.py:46
  586.6 9.4 %copy.25 = bf16[4,4,10,64,3,128]{5,3,2,4,1,0:T(8,128)(2,1)} copy(bf16[4,4,10,64,3,128]{5,4,3,0,2,1:T(4,128)(2,1)} %reshape.95) | data formatting | bytes 15728640 | tf_op jit(solution)/shard_map/squeeze | solution.py:46
  596.0 10.9 %fusion.24 = f32[4,4,3,64,640]{3,4,2,1,0} fusion(bf16[4,4,3,128,640]{3,4,2,1,0:T(8,128)(2,1)} %bitcast.55, bf16[4,4,64,3,128]{4,3,2,1,0:T(4,128)(2,1)S(1)} %reshape_squeeze.3), kind=kOutput, calls=%fused_computation.23 | convolution fusion | flops 503316480 | bytes 16515072
  606.9 8.9 %fusion.2 = f32[4,4,3,64]{3,2,1,0:T(4,128)S(1)} fusion(f32[4,4,3,64,10,64]{3,5,4,2,1,0:T(8,128)} %bitcast.52, f32[4,3,10]{2,1,0:T(4,128)S(1)} %convolution_bitcast_fusion, pred[4,10]{1,0:T(4,128)(4,1)S(1)} %iota_compare_fusion.2), kind=kLoop, calls=%fused_computation.6 | loop fusion | flops 7861248 | bytes 7877128 | tf_op jit(solution)/shard_map/reduce_max | solution.py:54
  615.8 8.0 %fusion = f32[4,4,3,64]{3,2,1,0:T(4,128)S(1)} fusion(f32[4,4,3,64,10,64]{3,5,4,2,1,0:T(8,128)} %bitcast.53, f32[4,4,3,64]{3,2,1,0:T(4,128)S(1)} %fusion.2, f32[4,3,10]{2,1,0:T(4,128)S(1)} %convolution_bitcast_fusion, pred[4,10]{1,0:T(4,128)(4,1)S(1)} %iota_compare_fusion.2), kind=kLoop, calls=%fused_computation.4 | loop fusion | flops 9827328 | bytes 7889416 | tf_op jit(solution)/shard_map/reduce_sum | solution.py:56
  623.8 20.7 %reshape.94 = bf16[4,4,10,64,3,128]{5,4,3,0,2,1:T(4,128)(2,1)} reshape(bf16[1,4,40,64,384]{4,3,1,0,2:T(8,128)(2,1)} %get-tuple-element.5) | data formatting | bytes 15728640 | tf_op jit(solution)/shard_map/squeeze | solution.py:60
  644.5 11.6 %fusion.19 = bf16[4,4,64,3,128]{4,2,3,1,0:T(8,128)(2,1)S(1)} fusion(f32[4,4,3,64,10,64]{3,5,4,2,1,0:T(8,128)} %bitcast.54, f32[4,4,3,64]{3,2,1,0:T(4,128)S(1)} %fusion.2, f32[4,3,10]{2,1,0:T(4,128)S(1)} %convolution_bitcast_fusion, pred[4,10]{1,0:T(4,128)(4,1)S(1)} %iota_compare_fusion.2, bf16[4,4,10,64,3,128]{5,4,3,0,2,1:T(4,128)(2,1)} %reshape.94, ...), kind=kOutput, calls=%fused_computation.21 | convolution fusion | flops 513933312 | bytes 16540168 | tf_op jit(solution)/shard_map/cthimj,ctmjhd->ctihd/dot_general | solution.py:57
  658.2 6.5 convolution_convert_fusion
  664.7 67.6 %reduce-scatter.4.cloned.1.call-done = bf16[1,256,3072]{2,1,0:T(8,128)(2,1)} async-done(((bf16[4,256,3072]{2,1,0:T(8,128)(2,1)}), bf16[1,256,3072]{2,1,0:T(8,128)(2,1)}) %reduce-scatter.4.cloned.1.call-update) | async-done | bytes 1572880
  (56 shorter events, 60.9 us)
Async XLA Ops:
  6.5 651.7 %copy-start = (bf16[384,3072]{1,0:T(8,128)(2,1)S(1)}, bf16[384,3072]{1,0:T(8,128)(2,1)}, u32[]{:S(2)}) copy-start(bf16[384,3072]{1,0:T(8,128)(2,1)} %param.9) | copy-start | bytes 7077892
  6.5 75.6 %all-gather.2.cloned.1.call-start = ((), (), s32[]{:S(2)}) async-start(), calls=%async_computation.1 | async-start | bytes 7864320 | tf_op jit(solution)/shard_map/all_gather | solution.py:26
  7.3 134.0 %copy-start.2 = (s32[4,10]{1,0:T(4,128)S(1)}, s32[4,10]{1,0:T(4,128)}, u32[]{:S(2)}) copy-start(s32[4,10]{1,0:T(4,128)} %param.10) | copy-start | bytes 484
  7.3 134.2 %copy-start.3 = (f32[3,343]{1,0:T(4,128)S(1)}, f32[3,343]{1,0:T(4,128)}, u32[]{:S(2)}) copy-start(f32[3,343]{1,0:T(4,128)} %param.13) | copy-start | bytes 12352
  7.3 134.2 %copy-start.4 = (s32[4,10]{1,0:T(4,128)S(1)}, s32[4,10]{1,0:T(4,128)}, u32[]{:S(2)}) copy-start(s32[4,10]{1,0:T(4,128)} %param.12) | copy-start | bytes 484
  7.3 199.2 %copy-start.5 = (s32[4]{0:T(128)S(1)}, s32[4]{0:T(128)}, u32[]{:S(2)}) copy-start(s32[4]{0:T(128)} %param.11) | copy-start | bytes 52
  7.3 725.0 %reduce-scatter.4.cloned.1.call-start = ((), (), s32[]{:S(2)}) async-start(), calls=%async_computation.2 | async-start | bytes 7864320
  94.6 1.4 copy-start.1
  97.3 15.7 %collective-permute-start = (bf16[2,4,4,64,384]{4,3,2,1,0:T(8,128)(2,1)}, bf16[2,4,4,64,384]{4,3,2,1,0:T(8,128)(2,1)}, u32[]{:S(2)}, u32[]{:S(2)}) collective-permute-start(bf16[2,4,4,64,384]{4,3,2,1,0:T(8,128)(2,1)} %bitcast.4), channel_id=1, source_target_pairs={{0,1},{1,2},{2,3},{3,4},{4,5},{5,6},{6,7},{8,9},{9,10},{10,11},{11... | collective-permute-start | bytes 4718600 | tf_op jit(solution)/shard_map/ppermute | solution.py:16
  100.2 39.8 %collective-permute-start.1 = (bf16[2,4,4,64,384]{4,3,2,1,0:T(8,128)(2,1)}, bf16[2,4,4,64,384]{4,3,2,1,0:T(8,128)(2,1)}, u32[]{:S(2)}, u32[]{:S(2)}) collective-permute-start(bf16[2,4,4,64,384]{4,3,2,1,0:T(8,128)(2,1)} %bitcast.4), channel_id=1, source_target_pairs={{0,2},{1,3},{2,4},{3,5},{4,6},{5,7},{8,10},{9,11},{10,12},{11,13},... | collective-permute-start | bytes 4718600 | tf_op jit(solution)/shard_map/ppermute | solution.py:16
  103.8 67.7 %collective-permute-start.2 = (bf16[2,4,4,64,384]{4,3,2,1,0:T(8,128)(2,1)}, bf16[2,4,4,64,384]{4,3,2,1,0:T(8,128)(2,1)}, u32[]{:S(2)}, u32[]{:S(2)}) collective-permute-start(bf16[2,4,4,64,384]{4,3,2,1,0:T(8,128)(2,1)} %bitcast.4), channel_id=1, source_target_pairs={{0,3},{1,4},{2,5},{3,6},{4,7},{8,11},{9,12},{10,13},{11,14},{12,15... | collective-permute-start | bytes 4718600 | tf_op jit(solution)/shard_map/ppermute | solution.py:16
  108.1 97.2 %collective-permute-start.3 = (bf16[2,4,4,64,384]{4,3,2,1,0:T(8,128)(2,1)}, bf16[2,4,4,64,384]{4,3,2,1,0:T(8,128)(2,1)}, u32[]{:S(2)}, u32[]{:S(2)}) collective-permute-start(bf16[2,4,4,64,384]{4,3,2,1,0:T(8,128)(2,1)} %bitcast.4), channel_id=1, source_target_pairs={{0,4},{1,5},{2,6},{3,7},{8,12},{9,13},{10,14},{11,15},{16,20},{17,... | collective-permute-start | bytes 4718600 | tf_op jit(solution)/shard_map/ppermute | solution.py:16
  110.5 128.4 %collective-permute-start.4 = (bf16[2,4,4,64,384]{4,3,2,1,0:T(8,128)(2,1)}, bf16[2,4,4,64,384]{4,3,2,1,0:T(8,128)(2,1)}, u32[]{:S(2)}, u32[]{:S(2)}) collective-permute-start(bf16[2,4,4,64,384]{4,3,2,1,0:T(8,128)(2,1)} %bitcast.4), channel_id=1, source_target_pairs={{0,5},{1,6},{2,7},{8,13},{9,14},{10,15},{16,21},{17,22},{18,23},{2... | collective-permute-start | bytes 4718600 | tf_op jit(solution)/shard_map/ppermute | solution.py:16
  113.0 159.7 %collective-permute-start.5 = (bf16[2,4,4,64,384]{4,3,2,1,0:T(8,128)(2,1)}, bf16[2,4,4,64,384]{4,3,2,1,0:T(8,128)(2,1)}, u32[]{:S(2)}, u32[]{:S(2)}) collective-permute-start(bf16[2,4,4,64,384]{4,3,2,1,0:T(8,128)(2,1)} %bitcast.4), channel_id=1, source_target_pairs={{0,6},{1,7},{8,14},{9,15},{16,22},{17,23},{24,30},{25,31}} | collective-permute-start | bytes 4718600 | tf_op jit(solution)/shard_map/ppermute | solution.py:16
  140.0 141.2 %collective-permute-start.6 = (bf16[2,4,4,64,384]{4,3,2,1,0:T(8,128)(2,1)}, bf16[2,4,4,64,384]{4,3,2,1,0:T(8,128)(2,1)}, u32[]{:S(2)}, u32[]{:S(2)}) collective-permute-start(bf16[2,4,4,64,384]{4,3,2,1,0:T(8,128)(2,1)} %bitcast.4), channel_id=1, source_target_pairs={{1,0},{2,1},{3,2},{4,3},{5,4},{6,5},{7,6},{9,8},{10,9},{11,10},{12... | collective-permute-start | bytes 4718600 | tf_op jit(solution)/shard_map/ppermute | solution.py:16
  171.5 140.1 %collective-permute-start.7 = (bf16[2,4,4,64,384]{4,3,2,1,0:T(8,128)(2,1)}, bf16[2,4,4,64,384]{4,3,2,1,0:T(8,128)(2,1)}, u32[]{:S(2)}, u32[]{:S(2)}) collective-permute-start(bf16[2,4,4,64,384]{4,3,2,1,0:T(8,128)(2,1)} %bitcast.4), channel_id=1, source_target_pairs={{2,0},{3,1},{4,2},{5,3},{6,4},{7,5},{10,8},{11,9},{12,10},{13,11},... | collective-permute-start | bytes 4718600 | tf_op jit(solution)/shard_map/ppermute | solution.py:16
  205.2 175.2 %collective-permute-start.8 = (bf16[2,4,4,64,384]{4,3,2,1,0:T(8,128)(2,1)}, bf16[2,4,4,64,384]{4,3,2,1,0:T(8,128)(2,1)}, u32[]{:S(2)}, u32[]{:S(2)}) collective-permute-start(bf16[2,4,4,64,384]{4,3,2,1,0:T(8,128)(2,1)} %bitcast.4), channel_id=1, source_target_pairs={{3,0},{4,1},{5,2},{6,3},{7,4},{11,8},{12,9},{13,10},{14,11},{15,12... | collective-permute-start | bytes 4718600 | tf_op jit(solution)/shard_map/ppermute | solution.py:16
  238.9 144.2 %collective-permute-start.9 = (bf16[2,4,4,64,384]{4,3,2,1,0:T(8,128)(2,1)}, bf16[2,4,4,64,384]{4,3,2,1,0:T(8,128)(2,1)}, u32[]{:S(2)}, u32[]{:S(2)}) collective-permute-start(bf16[2,4,4,64,384]{4,3,2,1,0:T(8,128)(2,1)} %bitcast.4), channel_id=1, source_target_pairs={{4,0},{5,1},{6,2},{7,3},{12,8},{13,9},{14,10},{15,11},{20,16},{21,... | collective-permute-start | bytes 4718600 | tf_op jit(solution)/shard_map/ppermute | solution.py:16
  272.6 259.4 %collective-permute-start.10 = (bf16[2,4,4,64,384]{4,3,2,1,0:T(8,128)(2,1)}, bf16[2,4,4,64,384]{4,3,2,1,0:T(8,128)(2,1)}, u32[]{:S(2)}, u32[]{:S(2)}) collective-permute-start(bf16[2,4,4,64,384]{4,3,2,1,0:T(8,128)(2,1)} %bitcast.4), channel_id=1, source_target_pairs={{5,0},{6,1},{7,2},{13,8},{14,9},{15,10},{21,16},{22,17},{23,18},{2... | collective-permute-start | bytes 4718600 | tf_op jit(solution)/shard_map/ppermute | solution.py:16
  281.2 253.6 %collective-permute-start.11 = (bf16[2,4,4,64,384]{4,3,2,1,0:T(8,128)(2,1)}, bf16[2,4,4,64,384]{4,3,2,1,0:T(8,128)(2,1)S(1)}, u32[]{:S(2)}, u32[]{:S(2)}) collective-permute-start(bf16[2,4,4,64,384]{4,3,2,1,0:T(8,128)(2,1)} %bitcast.4), channel_id=1, source_target_pairs={{6,0},{7,1},{14,8},{15,9},{22,16},{23,17},{30,24},{31,25}} | collective-permute-start | bytes 4718600 | tf_op jit(solution)/shard_map/ppermute | solution.py:16
Sparse Core Ops, SparseCore 0:
  9.2 72.8 all-gather.1
  664.9 67.4 reduce-scatter.3
where the time goes:
time: 741 us; the launch traced here: 739 us
  waiting for transfers between devices  492 us (66%)
  local copies, waits for them, and re-layouts  116 us (16%)
  starting transfers between devices  50.4 us (7%)
  matrix products  41.9 us (6%)
  other arithmetic  25.4 us (3%)
  between operations  13.6 us (2%)
    ppermute x12, waiting for transfers between devices, shifted(): lax.ppermute(value, axis, [(source, source + steps) for source in range(f...  349 us
    all_gather x1, waiting for transfers between devices, local(): lax.all_gather(clip_tokens, 'dp', axis=0, tiled=True)  74.8 us
    unnamed x3, waiting for transfers between devices  68.3 us
    ppermute x12, starting transfers between devices, shifted(): lax.ppermute(value, axis, [(source, source + steps) for source in range(f...  50.4 us
    unnamed x24, local copies, waits for them, and re-layouts  34.7 us
    squeeze x2, local copies, waits for them, and re-layouts, local(): gathered[0]  30 us
    squeeze x1, local copies, waits for them, and re-layouts, local(): gathered[1]  20.7 us
    gather x1, local copies, waits for them, and re-layouts, local(): gathered = jnp.take(buffer_tiles, position.reshape(-1), axis=2)  15.1 us
  transfers between devices with their start and end apart: 14, of which 9 were waited for; matrix products, arithmetic and copies ran while one was open for 5% of the time, Pallas kernels for 0%

commit v1 on v0

v1 whole, which is shorter than its diff:
```python
import functools
import math

import jax
import jax.numpy as jnp
from jax import lax
from jax.experimental import pallas as pl
from jax.experimental.pallas import tpu as pltpu
from jax.sharding import PartitionSpec as P

TILE = 64
REACH = 6
KMAX = 10
CAP = 2


def shifted(value, axis, steps):
    count = lax.axis_size(axis)
    first, last = (max(0, -steps), min(count, count - steps))
    return lax.ppermute(value, axis, [(source, source + steps) for source in range(first, last)])


def chosen_tiles(rows, rows_live, source, tiles_per_device):
    local = jnp.arange(tiles_per_device, dtype=jnp.int32)
    wanted = source * tiles_per_device + local
    named = jnp.any(
        (rows[:, :, None] == wanted[None, None, :]) & rows_live[:, :, None], axis=(0, 1)
    )
    rank = jnp.cumsum(named.astype(jnp.int32)) - 1
    picks = [
        jnp.sum(jnp.where(named & (rank == slot), local, 0)) for slot in range(CAP)
    ]
    return jnp.stack(picks).astype(jnp.int32)


def attention_kernel(pos_ref, count_ref, bias_ref, q_ref, *refs, heads, head_size, scale):
    kv_refs = refs[:KMAX]
    out_ref = refs[KMAX]
    tile = pl.program_id(0)
    live_count = count_ref[tile]
    queries = q_ref[...]
    clip_count = queries.shape[0]
    for head in range(heads):
        cols = slice(head * head_size, (head + 1) * head_size)
        q_head = queries[:, :, cols]
        scores = []
        for slot in range(KMAX):
            k_head = kv_refs[slot][0, :, :, cols]
            s = lax.dot_general(
                q_head, k_head, (((2,), (2,)), ((0,), (0,))), preferred_element_type=jnp.float32
            )
            s = s * scale + bias_ref[tile, head, slot]
            s = jnp.where(slot < live_count, s, -1e30)
            scores.append(s)
        row_max = scores[0].max(axis=2, keepdims=True)
        for s in scores[1:]:
            row_max = jnp.maximum(row_max, s.max(axis=2, keepdims=True))
        total = jnp.zeros((clip_count, TILE, head_size), jnp.float32)
        weight_sum = jnp.zeros((clip_count, TILE, 1), jnp.float32)
        for slot in range(KMAX):
            w = jnp.exp(scores[slot] - row_max)
            weight_sum = weight_sum + w.sum(axis=2, keepdims=True)
            v_head = kv_refs[slot][1, :, :, cols]
            total = total + lax.dot_general(
                w.astype(jnp.bfloat16), v_head, (((2,), (1,)), ((0,), (0,))),
                preferred_element_type=jnp.float32,
            )
        out_ref[:, :, cols] = (total / weight_sum).astype(out_ref.dtype)


def attend(positions, live_counts, bias, queries, key_values, heads, head_size):
    clip_count, token_count, width = queries.shape
    tile_count = token_count // TILE

    def kv_spec(slot):
        return pl.BlockSpec(
            (None, 2, clip_count, TILE, width),
            lambda t, pos, cnt, slot=slot: (pos[t, slot], 0, 0, 0, 0),
        )

    kernel = functools.partial(
        attention_kernel, heads=heads, head_size=head_size, scale=1.0 / math.sqrt(head_size)
    )
    return pl.pallas_call(
        kernel,
        out_shape=jax.ShapeDtypeStruct(queries.shape, jnp.bfloat16),
        grid_spec=pltpu.PrefetchScalarGridSpec(
            num_scalar_prefetch=2,
            grid=(tile_count,),
            in_specs=[pl.BlockSpec(memory_space=pltpu.SMEM),
                      pl.BlockSpec((clip_count, TILE, width), lambda t, pos, cnt: (0, t, 0))]
            + [kv_spec(slot) for slot in range(KMAX)],
            out_specs=pl.BlockSpec((clip_count, TILE, width), lambda t, pos, cnt: (0, t, 0)),
        ),
    )(positions, live_counts, bias, queries, *([key_values] * KMAX))


def local(clip_tokens, qkv_weight, out_weight, neighbours, counts, bias_index, rel_bias):
    heads_here = rel_bias.shape[0]
    width_here = out_weight.shape[0]
    head_size = width_here // heads_here
    tile_count = clip_tokens.shape[1] // TILE
    n_ctx = lax.axis_size("ctx")
    tokens = lax.all_gather(clip_tokens, "dp", axis=0, tiled=True)
    clip_count = tokens.shape[0]
    projected = jnp.einsum(
        "ctd,sdh->scth", tokens, qkv_weight, preferred_element_type=jnp.float32
    ).astype(jnp.bfloat16)
    queries = projected[0]
    by_tile = projected[1:3].reshape(2, clip_count, tile_count, TILE, width_here)
    by_tile = jnp.transpose(by_tile, (2, 0, 1, 3, 4))
    own_index = lax.axis_index("ctx").astype(jnp.int32)

    all_rows = lax.all_gather(neighbours, "ctx", axis=0, tiled=True)
    all_counts = lax.all_gather(counts, "ctx", axis=0, tiled=True)
    all_live = jnp.arange(KMAX)[None, :] < all_counts[:, None]
    live = jnp.arange(KMAX)[None, :] < counts[:, None]

    offsets = [step for amount in range(1, REACH + 1) for step in (amount, -amount) if amount < n_ctx]
    pieces = [by_tile]
    received_picks = []
    for step in offsets:
        target = own_index + step
        target_rows = lax.dynamic_slice_in_dim(
            all_rows, jnp.clip(target, 0, n_ctx - 1) * tile_count, tile_count, axis=0
        )
        target_live = lax.dynamic_slice_in_dim(
            all_live, jnp.clip(target, 0, n_ctx - 1) * tile_count, tile_count, axis=0
        )
        send_picks = chosen_tiles(target_rows, target_live, own_index, tile_count)
        outgoing = jnp.take(by_tile, send_picks, axis=0)
        pieces.append(shifted(outgoing, "ctx", step))
        received_picks.append(chosen_tiles(neighbours, live, own_index - step, tile_count))
    key_values = jnp.concatenate(pieces, axis=0)

    source = neighbours // tile_count
    within = neighbours % tile_count
    distance = own_index - source
    positions = jnp.where(distance == 0, within, 0)
    for index, step in enumerate(offsets):
        first = received_picks[index][0]
        slot = tile_count + CAP * index + jnp.where(within == first, 0, 1)
        positions = jnp.where(distance == step, slot, positions)
    positions = positions.astype(jnp.int32)

    bias = jnp.transpose(jnp.take(rel_bias, bias_index, axis=1), (1, 0, 2))
    attended = attend(positions, counts.astype(jnp.int32), bias, queries, key_values, heads_here, head_size)
    partial_out = jnp.einsum(
        "cth,hd->ctd", attended, out_weight, preferred_element_type=jnp.float32
    ).astype(jnp.bfloat16)
    return lax.psum_scatter(partial_out, "dp", scatter_dimension=0, tiled=True)


def solution(mesh):
    placed = (
        P("dp", "ctx", None),
        P(None, None, "dp"),
        P("dp", None),
        P("ctx", None),
        P("ctx"),
        P("ctx", None),
        P("dp", None),
    )
    return jax.shard_map(
        local, mesh=mesh, in_specs=placed, out_specs=P("dp", "ctx", None), check_vma=False
    )
```

time: 741 us -> 369 us (0.50)
  waiting for transfers between devices: 492 us -> 135 us
  local copies, waits for them, and re-layouts: 116 us -> 56.5 us
  other arithmetic: 25.4 us -> 62.6 us
  blocking collectives: 0 us -> 23.4 us
  matrix products: 41.9 us -> 19 us
  Pallas kernels: 0 us -> 16 us
  starting transfers between devices: 50.4 us -> 39.8 us
    ppermute x12, waiting for transfers between devices: 349 us -> 65.2 us  [shifted(): lax.ppermute(value, axis, [(source, source + steps) for source in range(f...]
    all_gather x1, waiting for transfers between devices: 74.8 us -> 1.35 us  [local(): tokens = lax.all_gather(clip_tokens, 'dp', axis=0, tiled=True)]
    squeeze x3 -> x1, local copies, waits for them, and re-layouts: 50.7 us -> 2.09 us  [local(): queries = projected[0]]
    select_n x2 -> x15, other arithmetic: 8.38 us -> 27.4 us  [the longest x12 17.5 us: local(): outgoing = jnp.take(by_tile, send_picks, axis=0)]
    and x1 -> x7, other arithmetic: 0.01 us -> 16.1 us  [the longest x6 15.4 us: local(): outgoing = jnp.take(by_tile, send_picks, axis=0)]
    pallas_call x0 -> x1, Pallas kernels: none -> 16 us  [attend(): pl.pallas_call(kernel, out_shape=jax.ShapeDtypeStruct(queries.shape, jnp....]
    gather x1 -> x15, local copies, waits for them, and re-layouts: 15.1 us -> 30.5 us  [the longest x12 29.7 us: local(): outgoing = jnp.take(by_tile, send_picks, axis=0)]
    unnamed x24 -> x20, local copies, waits for them, and re-layouts: 34.7 us -> 21.2 us
  transfers between devices with their start and end apart: 14 -> 14, of which waited for: 9 -> 4; matrix products, arithmetic and copies ran while one was open for 5% -> 30% of each run, Pallas kernels for 0% -> 0%
where the time goes in v1:
time: 369 us; the launch traced here: 367 us
  waiting for transfers between devices  135 us (37%)
  other arithmetic  62.6 us (17%)
  local copies, waits for them, and re-layouts  56.5 us (15%)
  starting transfers between devices  39.8 us (11%)
  blocking collectives  23.4 us (6%)
  matrix products  19 us (5%)
  Pallas kernels  16 us (4%)
  between operations  14.7 us (4%)
    unnamed x3, waiting for transfers between devices  68.3 us
    ppermute x12, waiting for transfers between devices, shifted(): lax.ppermute(value, axis, [(source, source + steps) for source in range(f...  65.2 us
    ppermute x12, starting transfers between devices, shifted(): lax.ppermute(value, axis, [(source, source + steps) for source in range(f...  39.8 us
    gather x12, local copies, waits for them, and re-layouts, local(): outgoing = jnp.take(by_tile, send_picks, axis=0)  29.7 us
    unnamed x20, local copies, waits for them, and re-layouts  21.2 us
    select_n x12, other arithmetic, local(): outgoing = jnp.take(by_tile, send_picks, axis=0)  17.5 us
    pallas_call x1, Pallas kernels, attend(): pl.pallas_call(kernel, out_shape=jax.ShapeDtypeStruct(queries.shape, jnp....  16 us
    and x6, other arithmetic, local(): outgoing = jnp.take(by_tile, send_picks, axis=0)  15.4 us
  transfers between devices with their start and end apart: 14, of which 4 were waited for; matrix products, arithmetic and copies ran while one was open for 30% of the time, Pallas kernels for 0%

profile of v1, /device:TPU:0, one launch (start us, length us, event | category | flops | bytes accessed | tf_op | source)
XLA Modules:
  0.0 366.7 jit_solution(9471251712451403474)
XLA Ops:
  16.7 10.6 %all-reduce = s32[32]{0:T(128)S(1)} all-reduce(s32[32]{0:T(128)S(1)} %dynamic-update-slice), channel_id=1, replica_groups=mesh['dp'=4,'ctx'=8] {'ctx'}, use_global_device_ids=true, to_apply=%add | all-reduce | flops 32 | bytes 256
  27.3 12.8 %all-gather = s32[8,4,10]{2,1,0:T(4,128)S(1)} all-gather(s32[1,4,10]{2,1,0:T(4,128)} %bitcast.337), channel_id=1, replica_groups=mesh['dp'=4,'ctx'=8] {'ctx'}, dimensions={0}, use_global_device_ids=true | all-gather | bytes 1440 | tf_op jit(solution)/shard_map/all_gather | solution.py:114
  44.4 2.6 compare_and_fusion.10
  48.4 2.6 compare_and_fusion.8
  56.2 2.6 compare_and_fusion.4
  60.1 2.6 compare_and_fusion.2
  71.5 8.7 %select_select_fusion.pos_ref = s32[4,10]{1,0:T(4,128)} fusion(s32[4,10]{1,0:T(4,128)} %param.12, s32[]{:T(128)} %get-tuple-element.125, s32[]{:T(128)} %get-tuple-element.124, s32[]{:T(128)} %get-tuple-element.123, s32[]{:T(128)} %get-tuple-element.122, s32[]{:T(128)} %get-tuple-element.121, s32[]{:T(128)} %get-tuple-element.120, s32[]{:T(128)} %get-tuple-element.119, ...), kind=kLoop, calls=%fused_computation.129 | loop fusion | flops 3280 | bytes 372 | tf_op jit(solution)/shard_map/jit(_where)/select_n | solution.py:143
  82.1 12.5 %convert_bitcast_fusion = bf16[3,4,256,384]{3,2,1,0:T(8,128)(2,1)S(1)} fusion(bf16[4,256,3072]{2,1,0:T(8,128)(2,1)} %all-gather.3.cloned.1.call-done, bf16[3,3072,384]{2,1,0:T(8,128)(2,1)} %param.10), kind=kOutput, calls=%fused_computation.18 | convolution fusion | flops 7248936960 | bytes 15728640 | tf_op jit(solution)/shard_map/ctd,sdh->scth/dot_general | solution.py:106
  101.0 2.7 collective-permute-start
  111.3 5.9 %collective-permute-start.2 = (bf16[2,2,4,64,384]{4,3,2,1,0:T(8,128)(2,1)}, bf16[2,2,4,64,384]{4,3,2,1,0:T(8,128)(2,1)}, u32[]{:S(2)}, u32[]{:S(2)}) collective-permute-start(bf16[2,2,4,64,384]{4,3,2,1,0:T(8,128)(2,1)} %broadcast_select_fusion.9), channel_id=1, source_target_pairs={{0,2},{1,3},{2,4},{3,5},{4,6},{5,7},{8,10},{9,11},{10,12},{11,13},... | collective-permute-start | bytes 2359304 | tf_op jit(solution)/shard_map/ppermute | solution.py:20
  124.9 4.3 %collective-permute-start.4 = (bf16[2,2,4,64,384]{4,3,2,1,0:T(8,128)(2,1)}, bf16[2,2,4,64,384]{4,3,2,1,0:T(8,128)(2,1)}, u32[]{:S(2)}, u32[]{:S(2)}) collective-permute-start(bf16[2,2,4,64,384]{4,3,2,1,0:T(8,128)(2,1)} %broadcast_select_fusion.7), channel_id=1, source_target_pairs={{0,3},{1,4},{2,5},{3,6},{4,7},{8,11},{9,12},{10,13},{11,14},{12,15... | collective-permute-start | bytes 2359304 | tf_op jit(solution)/shard_map/ppermute | solution.py:20
  129.2 3.0 gather_fusion.6
  132.2 2.9 gather_fusion.7
  135.2 3.0 gather_fusion.8
  138.1 3.0 gather_fusion.9
  141.1 3.0 gather_fusion.10
  161.8 6.3 %collective-permute-start.6 = (bf16[2,2,4,64,384]{4,3,2,1,0:T(8,128)(2,1)}, bf16[2,2,4,64,384]{4,3,2,1,0:T(8,128)(2,1)S(1)}, u32[]{:S(2)}, u32[]{:S(2)}) collective-permute-start(bf16[2,2,4,64,384]{4,3,2,1,0:T(8,128)(2,1)} %broadcast_select_fusion.5), channel_id=1, source_target_pairs={{0,4},{1,5},{2,6},{3,7},{8,12},{9,13},{10,14},{11,15},{16,20},{17,... | collective-permute-start | bytes 2359304 | tf_op jit(solution)/shard_map/ppermute | solution.py:20
  175.8 3.0 collective-permute-start.8
  184.3 9.8 %collective-permute-start.10 = (bf16[2,2,4,64,384]{4,3,2,1,0:T(8,128)(2,1)}, bf16[2,2,4,64,384]{4,3,2,1,0:T(8,128)(2,1)S(1)}, u32[]{:S(2)}, u32[]{:S(2)}) collective-permute-start(bf16[2,2,4,64,384]{4,3,2,1,0:T(8,128)(2,1)} %broadcast_select_fusion.1), channel_id=1, source_target_pairs={{0,6},{1,7},{8,14},{9,15},{16,22},{17,23},{24,30},{25,31}} | collective-permute-start | bytes 2359304 | tf_op jit(solution)/shard_map/ppermute | solution.py:20
  199.6 61.1 %collective-permute-done.7 = bf16[2,2,4,64,384]{4,3,2,1,0:T(8,128)(2,1)S(1)} collective-permute-done((bf16[2,2,4,64,384]{4,3,2,1,0:T(8,128)(2,1)}, bf16[2,2,4,64,384]{4,3,2,1,0:T(8,128)(2,1)S(1)}, u32[]{:S(2)}, u32[]{:S(2)}) %collective-permute-start.7) | collective-permute-done | bytes 786464 | tf_op jit(solution)/shard_map/ppermute | solution.py:20
  262.7 4.1 %collective-permute-done.9 = bf16[2,2,4,64,384]{4,3,2,1,0:T(8,128)(2,1)S(1)} collective-permute-done((bf16[2,2,4,64,384]{4,3,2,1,0:T(8,128)(2,1)}, bf16[2,2,4,64,384]{4,3,2,1,0:T(8,128)(2,1)S(1)}, u32[]{:S(2)}, u32[]{:S(2)}) %collective-permute-start.9) | collective-permute-done | bytes 786464 | tf_op jit(solution)/shard_map/ppermute | solution.py:20
  269.8 16.0 %shard_map.73 = bf16[4,256,384]{2,1,0:T(8,128)(2,1)} custom-call(s32[4,10]{1,0:T(4,128)} %select_select_fusion.pos_ref, s32[4]{0:T(128)} %count_ref.1, f32[4,3,10]{2,1,0:T(4,128)} %fusion.8.bias_ref, bf16[4,256,384]{2,1,0:T(8,128)(2,1)} %slice_bitcast_fusion.q_ref, ...), custom_call_target="tpu_custom_call" | custom-call | tf_op jit(solution)/shard_map/pallas_call | solution.py:84
  285.8 6.5 %convolution_convert_fusion = bf16[4,256,3072]{2,1,0:T(8,128)(2,1)} fusion(bf16[4,256,384]{2,1,0:T(8,128)(2,1)} %shard_map.73, bf16[384,3072]{1,0:T(8,128)(2,1)S(1)} %copy-done), kind=kOutput, calls=%fused_computation.16 | convolution fusion | flops 2419064832 | bytes 9437184 | tf_op jit(solution)/shard_map/cth,hd->ctd/dot_general | solution.py:148
  292.3 67.6 %reduce-scatter.4.cloned.1.call-done = bf16[1,256,3072]{2,1,0:T(8,128)(2,1)} async-done(((bf16[4,256,3072]{2,1,0:T(8,128)(2,1)}), bf16[1,256,3072]{2,1,0:T(8,128)(2,1)}) %reduce-scatter.4.cloned.1.call-update) | async-done | bytes 1572880
  (172 shorter events, 95.1 us)
Async XLA Ops:
  6.5 279.3 %copy-start = (bf16[384,3072]{1,0:T(8,128)(2,1)S(1)}, bf16[384,3072]{1,0:T(8,128)(2,1)}, u32[]{:S(2)}) copy-start(bf16[384,3072]{1,0:T(8,128)(2,1)} %param.11) | copy-start | bytes 7077892
  6.5 75.6 %all-gather.3.cloned.1.call-start = ((), (), s32[]{:S(2)}) async-start(), calls=%async_computation.1 | async-start | bytes 7864320 | tf_op jit(solution)/shard_map/all_gather | solution.py:104
  7.3 352.6 %reduce-scatter.4.cloned.1.call-start = ((), (), s32[]{:S(2)}) async-start(), calls=%async_computation.2 | async-start | bytes 7864320
  94.6 3.2 copy-start.1
  101.0 59.6 %collective-permute-start = (bf16[2,2,4,64,384]{4,3,2,1,0:T(8,128)(2,1)}, bf16[2,2,4,64,384]{4,3,2,1,0:T(8,128)(2,1)}, u32[]{:S(2)}, u32[]{:S(2)}) collective-permute-start(bf16[2,2,4,64,384]{4,3,2,1,0:T(8,128)(2,1)} %broadcast_select_fusion.11), channel_id=1, source_target_pairs={{0,1},{1,2},{2,3},{3,4},{4,5},{5,6},{6,7},{8,9},{9,10},{10,11},{11... | collective-permute-start | bytes 2359304 | tf_op jit(solution)/shard_map/ppermute | solution.py:20
  106.8 55.0 %collective-permute-start.1 = (bf16[2,2,4,64,384]{4,3,2,1,0:T(8,128)(2,1)}, bf16[2,2,4,64,384]{4,3,2,1,0:T(8,128)(2,1)}, u32[]{:S(2)}, u32[]{:S(2)}) collective-permute-start(bf16[2,2,4,64,384]{4,3,2,1,0:T(8,128)(2,1)} %broadcast_select_fusion.10), channel_id=1, source_target_pairs={{1,0},{2,1},{3,2},{4,3},{5,4},{6,5},{7,6},{9,8},{10,9},{11,10},{12... | collective-permute-start | bytes 2359304 | tf_op jit(solution)/shard_map/ppermute | solution.py:20
  111.3 61.1 %collective-permute-start.2 = (bf16[2,2,4,64,384]{4,3,2,1,0:T(8,128)(2,1)}, bf16[2,2,4,64,384]{4,3,2,1,0:T(8,128)(2,1)}, u32[]{:S(2)}, u32[]{:S(2)}) collective-permute-start(bf16[2,2,4,64,384]{4,3,2,1,0:T(8,128)(2,1)} %broadcast_select_fusion.9), channel_id=1, source_target_pairs={{0,2},{1,3},{2,4},{3,5},{4,6},{5,7},{8,10},{9,11},{10,12},{11,13},... | collective-permute-start | bytes 2359304 | tf_op jit(solution)/shard_map/ppermute | solution.py:20
  120.4 55.4 %collective-permute-start.3 = (bf16[2,2,4,64,384]{4,3,2,1,0:T(8,128)(2,1)}, bf16[2,2,4,64,384]{4,3,2,1,0:T(8,128)(2,1)}, u32[]{:S(2)}, u32[]{:S(2)}) collective-permute-start(bf16[2,2,4,64,384]{4,3,2,1,0:T(8,128)(2,1)} %broadcast_select_fusion.8), channel_id=1, source_target_pairs={{2,0},{3,1},{4,2},{5,3},{6,4},{7,5},{10,8},{11,9},{12,10},{13,11},... | collective-permute-start | bytes 2359304 | tf_op jit(solution)/shard_map/ppermute | solution.py:20
  124.9 56.1 %collective-permute-start.4 = (bf16[2,2,4,64,384]{4,3,2,1,0:T(8,128)(2,1)}, bf16[2,2,4,64,384]{4,3,2,1,0:T(8,128)(2,1)}, u32[]{:S(2)}, u32[]{:S(2)}) collective-permute-start(bf16[2,2,4,64,384]{4,3,2,1,0:T(8,128)(2,1)} %broadcast_select_fusion.7), channel_id=1, source_target_pairs={{0,3},{1,4},{2,5},{3,6},{4,7},{8,11},{9,12},{10,13},{11,14},{12,15... | collective-permute-start | bytes 2359304 | tf_op jit(solution)/shard_map/ppermute | solution.py:20
  160.5 23.8 %collective-permute-start.5 = (bf16[2,2,4,64,384]{4,3,2,1,0:T(8,128)(2,1)}, bf16[2,2,4,64,384]{4,3,2,1,0:T(8,128)(2,1)S(1)}, u32[]{:S(2)}, u32[]{:S(2)}) collective-permute-start(bf16[2,2,4,64,384]{4,3,2,1,0:T(8,128)(2,1)} %broadcast_select_fusion.6), channel_id=1, source_target_pairs={{3,0},{4,1},{5,2},{6,3},{7,4},{11,8},{12,9},{13,10},{14,11},{15,12... | collective-permute-start | bytes 2359304 | tf_op jit(solution)/shard_map/ppermute | solution.py:20
  161.8 34.4 %collective-permute-start.6 = (bf16[2,2,4,64,384]{4,3,2,1,0:T(8,128)(2,1)}, bf16[2,2,4,64,384]{4,3,2,1,0:T(8,128)(2,1)S(1)}, u32[]{:S(2)}, u32[]{:S(2)}) collective-permute-start(bf16[2,2,4,64,384]{4,3,2,1,0:T(8,128)(2,1)} %broadcast_select_fusion.5), channel_id=1, source_target_pairs={{0,4},{1,5},{2,6},{3,7},{8,12},{9,13},{10,14},{11,15},{16,20},{17,... | collective-permute-start | bytes 2359304 | tf_op jit(solution)/shard_map/ppermute | solution.py:20
  172.4 88.3 %collective-permute-start.7 = (bf16[2,2,4,64,384]{4,3,2,1,0:T(8,128)(2,1)}, bf16[2,2,4,64,384]{4,3,2,1,0:T(8,128)(2,1)S(1)}, u32[]{:S(2)}, u32[]{:S(2)}) collective-permute-start(bf16[2,2,4,64,384]{4,3,2,1,0:T(8,128)(2,1)} %broadcast_select_fusion.4), channel_id=1, source_target_pairs={{4,0},{5,1},{6,2},{7,3},{12,8},{13,9},{14,10},{15,11},{20,16},{21,... | collective-permute-start | bytes 2359304 | tf_op jit(solution)/shard_map/ppermute | solution.py:20
  175.8 85.9 %collective-permute-start.8 = (bf16[2,2,4,64,384]{4,3,2,1,0:T(8,128)(2,1)}, bf16[2,2,4,64,384]{4,3,2,1,0:T(8,128)(2,1)S(1)}, u32[]{:S(2)}, u32[]{:S(2)}) collective-permute-start(bf16[2,2,4,64,384]{4,3,2,1,0:T(8,128)(2,1)} %broadcast_select_fusion.3), channel_id=1, source_target_pairs={{0,5},{1,6},{2,7},{8,13},{9,14},{10,15},{16,21},{17,22},{18,23},{2... | collective-permute-start | bytes 2359304 | tf_op jit(solution)/shard_map/ppermute | solution.py:20
  180.9 85.8 %collective-permute-start.9 = (bf16[2,2,4,64,384]{4,3,2,1,0:T(8,128)(2,1)}, bf16[2,2,4,64,384]{4,3,2,1,0:T(8,128)(2,1)S(1)}, u32[]{:S(2)}, u32[]{:S(2)}) collective-permute-start(bf16[2,2,4,64,384]{4,3,2,1,0:T(8,128)(2,1)} %broadcast_select_fusion.2), channel_id=1, source_target_pairs={{5,0},{6,1},{7,2},{13,8},{14,9},{15,10},{21,16},{22,17},{23,18},{2... | collective-permute-start | bytes 2359304 | tf_op jit(solution)/shard_map/ppermute | solution.py:20
  184.3 83.5 %collective-permute-start.10 = (bf16[2,2,4,64,384]{4,3,2,1,0:T(8,128)(2,1)}, bf16[2,2,4,64,384]{4,3,2,1,0:T(8,128)(2,1)S(1)}, u32[]{:S(2)}, u32[]{:S(2)}) collective-permute-start(bf16[2,2,4,64,384]{4,3,2,1,0:T(8,128)(2,1)} %broadcast_select_fusion.1), channel_id=1, source_target_pairs={{0,6},{1,7},{8,14},{9,15},{16,22},{17,23},{24,30},{25,31}} | collective-permute-start | bytes 2359304 | tf_op jit(solution)/shard_map/ppermute | solution.py:20
  196.3 72.5 %collective-permute-start.11 = (bf16[2,2,4,64,384]{4,3,2,1,0:T(8,128)(2,1)S(1)}, bf16[2,2,4,64,384]{4,3,2,1,0:T(8,128)(2,1)S(1)}, u32[]{:S(2)}, u32[]{:S(2)}) collective-permute-start(bf16[2,2,4,64,384]{4,3,2,1,0:T(8,128)(2,1)S(1)} %broadcast_select_fusion), channel_id=1, source_target_pairs={{6,0},{7,1},{14,8},{15,9},{22,16},{23,17},{30,24},{31,25}} | collective-permute-start | bytes 2359304 | tf_op jit(solution)/shard_map/ppermute | solution.py:20
Sparse Core Ops, SparseCore 0:
  9.2 72.8 all-gather.2
  292.4 67.4 reduce-scatter.3

commit v2 on v1

--- a/solution.py
+++ b/solution.py
@@ -95,43 +95,35 @@
     )(positions, live_counts, bias, queries, *([key_values] * KMAX))
 
 
+def partner_pairs(count, step):
+    return [(source, source ^ step) for source in range(count)]
+
+
 def local(clip_tokens, qkv_weight, out_weight, neighbours, counts, bias_index, rel_bias):
     heads_here = rel_bias.shape[0]
     width_here = out_weight.shape[0]
     head_size = width_here // heads_here
-    tile_count = clip_tokens.shape[1] // TILE
+    token_count = clip_tokens.shape[1]
+    tile_count = token_count // TILE
     n_ctx = lax.axis_size("ctx")
-    tokens = lax.all_gather(clip_tokens, "dp", axis=0, tiled=True)
-    clip_count = tokens.shape[0]
-    projected = jnp.einsum(
-        "ctd,sdh->scth", tokens, qkv_weight, preferred_element_type=jnp.float32
-    ).astype(jnp.bfloat16)
-    queries = projected[0]
-    by_tile = projected[1:3].reshape(2, clip_count, tile_count, TILE, width_here)
-    by_tile = jnp.transpose(by_tile, (2, 0, 1, 3, 4))
+    n_dp = lax.axis_size("dp")
     own_index = lax.axis_index("ctx").astype(jnp.int32)
 
-    all_rows = lax.all_gather(neighbours, "ctx", axis=0, tiled=True)
-    all_counts = lax.all_gather(counts, "ctx", axis=0, tiled=True)
-    all_live = jnp.arange(KMAX)[None, :] < all_counts[:, None]
+    table = jnp.concatenate([neighbours, counts[:, None]], axis=1)
+    all_table = lax.all_gather(table, "ctx", axis=0, tiled=True)
+    all_rows = all_table[:, :KMAX]
+    all_live = jnp.arange(KMAX)[None, :] < all_table[:, KMAX:]
     live = jnp.arange(KMAX)[None, :] < counts[:, None]
 
     offsets = [step for amount in range(1, REACH + 1) for step in (amount, -amount) if amount < n_ctx]
-    pieces = [by_tile]
+    send_picks = []
     received_picks = []
     for step in offsets:
-        target = own_index + step
-        target_rows = lax.dynamic_slice_in_dim(
-            all_rows, jnp.clip(target, 0, n_ctx - 1) * tile_count, tile_count, axis=0
-        )
-        target_live = lax.dynamic_slice_in_dim(
-            all_live, jnp.clip(target, 0, n_ctx - 1) * tile_count, tile_count, axis=0
-        )
-        send_picks = chosen_tiles(target_rows, target_live, own_index, tile_count)
-        outgoing = jnp.take(by_tile, send_picks, axis=0)
-        pieces.append(shifted(outgoing, "ctx", step))
+        target = jnp.clip(own_index + step, 0, n_ctx - 1) * tile_count
+        target_rows = lax.dynamic_slice_in_dim(all_rows, target, tile_count, axis=0)
+        target_live = lax.dynamic_slice_in_dim(all_live, target, tile_count, axis=0)
+        send_picks.append(chosen_tiles(target_rows, target_live, own_index, tile_count))
         received_picks.append(chosen_tiles(neighbours, live, own_index - step, tile_count))
-    key_values = jnp.concatenate(pieces, axis=0)
 
     source = neighbours // tile_count
     within = neighbours % tile_count
@@ -142,13 +134,36 @@
         slot = tile_count + CAP * index + jnp.where(within == first, 0, 1)
         positions = jnp.where(distance == step, slot, positions)
     positions = positions.astype(jnp.int32)
+    bias = jnp.transpose(jnp.take(rel_bias, bias_index, axis=1), (1, 0, 2))
+    live_counts = counts.astype(jnp.int32)
 
-    bias = jnp.transpose(jnp.take(rel_bias, bias_index, axis=1), (1, 0, 2))
-    attended = attend(positions, counts.astype(jnp.int32), bias, queries, key_values, heads_here, head_size)
-    partial_out = jnp.einsum(
-        "cth,hd->ctd", attended, out_weight, preferred_element_type=jnp.float32
-    ).astype(jnp.bfloat16)
-    return lax.psum_scatter(partial_out, "dp", scatter_dimension=0, tiled=True)
+    own_tokens = clip_tokens[0]
+    clip_inputs = [own_tokens] + [
+        lax.ppermute(own_tokens, "dp", partner_pairs(n_dp, step)) for step in range(1, n_dp)
+    ]
+    total = None
+    for step in range(n_dp):
+        projected = jnp.einsum(
+            "td,sdh->sth", clip_inputs[step], qkv_weight, preferred_element_type=jnp.float32
+        ).astype(jnp.bfloat16)
+        queries = projected[0][None]
+        by_tile = jnp.transpose(
+            projected[1:3].reshape(2, tile_count, TILE, width_here), (1, 0, 2, 3)
+        )[:, :, None]
+        pieces = [by_tile]
+        for index, offset in enumerate(offsets):
+            outgoing = jnp.take(by_tile, send_picks[index], axis=0)
+            pieces.append(shifted(outgoing, "ctx", offset))
+        key_values = jnp.concatenate(pieces, axis=0)
+        attended = attend(positions, live_counts, bias, queries, key_values, heads_here, head_size)
+        partial_out = jnp.dot(
+            attended[0], out_weight, preferred_element_type=jnp.float32
+        ).astype(jnp.bfloat16)
+        if step > 0:
+            partial_out = lax.ppermute(partial_out, "dp", partner_pairs(n_dp, step))
+        contribution = partial_out.astype(jnp.float32)
+        total = contribution if total is None else total + contribution
+    return total.astype(jnp.bfloat16)[None]
 
 
 def solution(mesh):

time: 369 us -> 455 us (1.23)
  starting transfers between devices: 39.8 us -> 135 us
  waiting for transfers between devices: 135 us -> 56.8 us
  local copies, waits for them, and re-layouts: 56.5 us -> 112 us
  Pallas kernels: 16 us -> 34.4 us
  matrix products: 19 us -> 37.2 us
  between operations: 14.7 us -> 1.6 us
  blocking collectives: 23.4 us -> 13.4 us
    ppermute x12 -> x48, starting transfers between devices: 39.8 us -> 126 us  [shifted(): lax.ppermute(value, axis, [(source, source + steps) for source in range(f...]
    unnamed x3 -> x0, waiting for transfers between devices: 68.3 us -> none
    gather x12 -> x48, local copies, waits for them, and re-layouts: 29.7 us -> 63.2 us  [local(): outgoing = jnp.take(by_tile, send_picks[index], axis=0)]
    unnamed x20 -> x246, local copies, waits for them, and re-layouts: 21.2 us -> 39.8 us
    pallas_call x1 -> x4, Pallas kernels: 16 us -> 34.4 us  [attend(): pl.pallas_call(kernel, out_shape=jax.ShapeDtypeStruct(queries.shape, jnp....]
    dot_general x2 -> x8, matrix products: 19 us -> 37.2 us  [the longest x4 22.8 us: local(): jnp.einsum('td,sdh->sth', clip_inputs[step], qkv_weight, preferred_elemen...]
    unnamed x1 -> x0, blocking collectives: 10.6 us -> none
    ppermute x0 -> x6, starting transfers between devices: none -> 9.07 us  [the longest x3 4.57 us: local(): partial_out = lax.ppermute(partial_out, 'dp', partner_pairs(n_dp, step))]
  transfers between devices with their start and end apart: 14 -> 54, of which waited for: 4 -> 25; matrix products, arithmetic and copies ran while one was open for 30% -> 39% of each run, Pallas kernels for 0% -> 8%
where the time goes in v2:
time: 455 us; the launch traced here: 452 us
  starting transfers between devices  135 us (30%)
  local copies, waits for them, and re-layouts  112 us (25%)
  other arithmetic  61.8 us (14%)
  waiting for transfers between devices  56.8 us (12%)
  matrix products  37.2 us (8%)
  Pallas kernels  34.4 us (8%)
  blocking collectives  13.4 us (3%)
    ppermute x48, starting transfers between devices, shifted(): lax.ppermute(value, axis, [(source, source + steps) for source in range(f...  126 us
    gather x48, local copies, waits for them, and re-layouts, local(): outgoing = jnp.take(by_tile, send_picks[index], axis=0)  63.2 us
    ppermute x48, waiting for transfers between devices, shifted(): lax.ppermute(value, axis, [(source, source + steps) for source in range(f...  56.8 us
    unnamed x246, local copies, waits for them, and re-layouts  39.8 us
    pallas_call x4, Pallas kernels, attend(): pl.pallas_call(kernel, out_shape=jax.ShapeDtypeStruct(queries.shape, jnp....  34.4 us
    dot_general x4, matrix products, local(): jnp.einsum('td,sdh->sth', clip_inputs[step], qkv_weight, preferred_elemen...  22.8 us
    and x6, other arithmetic, local(): outgoing = jnp.take(by_tile, send_picks[index], axis=0)  18.9 us
    dot_general x4, matrix products, local(): jnp.dot(attended[0], out_weight, preferred_element_type=jnp.float32)  14.4 us
  transfers between devices with their start and end apart: 54, of which 25 were waited for; matrix products, arithmetic and copies ran while one was open for 39% of the time, Pallas kernels for 8%

profile of v2, /device:TPU:0, one launch (start us, length us, event | category | flops | bytes accessed | tf_op | source)
XLA Modules:
  0.0 452.2 jit_solution(5184760981328678435)
XLA Ops:
  10.6 13.4 %all-gather = s32[8,4,11]{2,1,0:T(4,128)S(1)} all-gather(s32[1,4,11]{2,1,0:T(4,128)S(1)} %add_bitcast_fusion), channel_id=1, replica_groups=mesh['dp'=4,'ctx'=8] {'ctx'}, dimensions={0}, use_global_device_ids=true | all-gather | bytes 1584 | tf_op jit(solution)/shard_map/all_gather | solution.py:113
  59.3 8.7 %select_select_fusion.pos_ref = s32[4,10]{1,0:T(4,128)} fusion(s32[4,10]{1,0:T(4,128)} %param.12, s32[]{:T(128)} %get-tuple-element.173, s32[]{:T(128)} %get-tuple-element.172, s32[]{:T(128)} %get-tuple-element.171, s32[]{:T(128)} %get-tuple-element.170, s32[]{:T(128)} %get-tuple-element.169, s32[]{:T(128)} %get-tuple-element.168, s32[]{:T(128)} %get-tuple-element.167, ...), kind=kLoop, calls=%fused_computation.267 | loop fusion | flops 3280 | bytes 372 | tf_op jit(solution)/shard_map/jit(_where)/select_n | solution.py:135
  68.0 5.7 %fusion.35 = bf16[3,256,384]{2,1,0:T(8,128)(2,1)S(1)} fusion(bf16[3,3072,384]{2,1,0:T(8,128)(2,1)} %param.10, bf16[1,256,3072]{2,1,0:T(8,128)(2,1)} %param.9), kind=kOutput, calls=%fused_computation.74 | convolution fusion | flops 1812234240 | bytes 9240576 | tf_op jit(solution)/shard_map/td,sdh->sth/dot_general | solution.py:146
  90.4 5.7 %fusion.29 = bf16[3,256,384]{2,1,0:T(8,128)(2,1)S(1)} fusion(bf16[3,3072,384]{2,1,0:T(8,128)(2,1)} %param.10, bf16[256,3072]{1,0:T(8,128)(2,1)} %collective-permute-done.26), kind=kOutput, calls=%fused_computation.72 | convolution fusion | flops 1812234240 | bytes 9240576 | tf_op jit(solution)/shard_map/td,sdh->sth/dot_general | solution.py:146
  113.0 5.7 %fusion.32 = bf16[3,256,384]{2,1,0:T(8,128)(2,1)S(1)} fusion(bf16[3,3072,384]{2,1,0:T(8,128)(2,1)} %param.10, bf16[256,3072]{1,0:T(8,128)(2,1)} %collective-permute-done.12), kind=kOutput, calls=%fused_computation.73 | convolution fusion | flops 1812234240 | bytes 9240576 | tf_op jit(solution)/shard_map/td,sdh->sth/dot_general | solution.py:146
  136.1 5.7 %fusion.26 = bf16[3,256,384]{2,1,0:T(8,128)(2,1)S(1)} fusion(bf16[3,3072,384]{2,1,0:T(8,128)(2,1)} %param.10, bf16[256,3072]{1,0:T(8,128)(2,1)} %collective-permute-done.40), kind=kOutput, calls=%fused_computation.71 | convolution fusion | flops 1812234240 | bytes 9240576 | tf_op jit(solution)/shard_map/td,sdh->sth/dot_general | solution.py:146
  205.5 5.7 %collective-permute-start.47 = (bf16[2,2,1,64,384]{4,3,2,1,0:T(8,128)(2,1)S(1)}, bf16[2,2,1,64,384]{4,3,2,1,0:T(8,128)(2,1)S(1)}, u32[]{:S(2)}, u32[]{:S(2)}) collective-permute-start(bf16[2,2,1,64,384]{4,3,2,1,0:T(8,128)(2,1)S(1)} %get-tuple-element.125), channel_id=1, source_target_pairs={{0,4},{1,5},{2,6},{3,7},{8,12},{9,13},{10,14},{11,15},{16,20},{17,... | collective-permute-start | bytes 589832 | tf_op jit(solution)/shard_map/ppermute | solution.py:20
  226.4 6.9 %collective-permute-start.51 = (bf16[2,2,1,64,384]{4,3,2,1,0:T(8,128)(2,1)S(1)}, bf16[2,2,1,64,384]{4,3,2,1,0:T(8,128)(2,1)S(1)}, u32[]{:S(2)}, u32[]{:S(2)}) collective-permute-start(bf16[2,2,1,64,384]{4,3,2,1,0:T(8,128)(2,1)S(1)} %get-tuple-element.109), channel_id=1, source_target_pairs={{0,6},{1,7},{8,14},{9,15},{16,22},{17,23},{24,30},{25,31}} | collective-permute-start | bytes 589832 | tf_op jit(solution)/shard_map/ppermute | solution.py:20
  239.0 5.9 %collective-permute-done.52 = bf16[2,2,1,64,384]{4,3,2,1,0:T(8,128)(2,1)S(1)} collective-permute-done((bf16[2,2,1,64,384]{4,3,2,1,0:T(8,128)(2,1)S(1)}, bf16[2,2,1,64,384]{4,3,2,1,0:T(8,128)(2,1)S(1)}, u32[]{:S(2)}, u32[]{:S(2)}) %collective-permute-start.52) | collective-permute-done | bytes 196640 | tf_op jit(solution)/shard_map/ppermute | solution.py:20
  246.9 8.6 %shard_map.76 = bf16[1,256,384]{2,1,0:T(8,128)(2,1)} custom-call(s32[4,10]{1,0:T(4,128)} %select_select_fusion.pos_ref, s32[4]{0:T(128)} %count_ref.7, f32[4,3,10]{2,1,0:T(4,128)} %fusion.42.bias_ref, bf16[1,256,384]{2,1,0:T(8,128)(2,1)} %slice.146.q_ref, ...), custom_call_target="tpu_custom_call" | custom-call | tf_op jit(solution)/shard_map/pallas_call | solution.py:84
  273.5 5.6 %collective-permute-start.19 = (bf16[2,2,1,64,384]{4,3,2,1,0:T(8,128)(2,1)S(1)}, bf16[2,2,1,64,384]{4,3,2,1,0:T(8,128)(2,1)S(1)}, u32[]{:S(2)}, u32[]{:S(2)}) collective-permute-start(bf16[2,2,1,64,384]{4,3,2,1,0:T(8,128)(2,1)S(1)} %copy-done.72), channel_id=1, source_target_pairs={{0,4},{1,5},{2,6},{3,7},{8,12},{9,13},{10,14},{11,15},{16,20},{17,... | collective-permute-start | bytes 589832 | tf_op jit(solution)/shard_map/ppermute | solution.py:20
  284.3 5.0 %collective-permute-start.21 = (bf16[2,2,1,64,384]{4,3,2,1,0:T(8,128)(2,1)S(1)}, bf16[2,2,1,64,384]{4,3,2,1,0:T(8,128)(2,1)S(1)}, u32[]{:S(2)}, u32[]{:S(2)}) collective-permute-start(bf16[2,2,1,64,384]{4,3,2,1,0:T(8,128)(2,1)S(1)} %copy-done.70), channel_id=1, source_target_pairs={{0,5},{1,6},{2,7},{8,13},{9,14},{10,15},{16,21},{17,22},{18,23},{2... | collective-permute-start | bytes 589832 | tf_op jit(solution)/shard_map/ppermute | solution.py:20
  295.4 6.1 %collective-permute-start.23 = (bf16[2,2,1,64,384]{4,3,2,1,0:T(8,128)(2,1)S(1)}, bf16[2,2,1,64,384]{4,3,2,1,0:T(8,128)(2,1)S(1)}, u32[]{:S(2)}, u32[]{:S(2)}) collective-permute-start(bf16[2,2,1,64,384]{4,3,2,1,0:T(8,128)(2,1)S(1)} %copy-done.67), channel_id=1, source_target_pairs={{0,6},{1,7},{8,14},{9,15},{16,22},{17,23},{24,30},{25,31}} | collective-permute-start | bytes 589832 | tf_op jit(solution)/shard_map/ppermute | solution.py:20
  308.1 5.5 %collective-permute-done.24 = bf16[2,2,1,64,384]{4,3,2,1,0:T(8,128)(2,1)S(1)} collective-permute-done((bf16[2,2,1,64,384]{4,3,2,1,0:T(8,128)(2,1)S(1)}, bf16[2,2,1,64,384]{4,3,2,1,0:T(8,128)(2,1)S(1)}, u32[]{:S(2)}, u32[]{:S(2)}) %collective-permute-start.24) | collective-permute-done | bytes 196640 | tf_op jit(solution)/shard_map/ppermute | solution.py:20
  316.2 8.7 %shard_map.74 = bf16[1,256,384]{2,1,0:T(8,128)(2,1)} custom-call(s32[4,10]{1,0:T(4,128)} %select_select_fusion.pos_ref, s32[4]{0:T(128)} %count_ref.7, f32[4,3,10]{2,1,0:T(4,128)} %fusion.42.bias_ref, bf16[1,256,384]{2,1,0:T(8,128)(2,1)} %slice.142.q_ref, ...), custom_call_target="tpu_custom_call" | custom-call | tf_op jit(solution)/shard_map/pallas_call | solution.py:84
  335.8 5.6 %collective-permute-start.33 = (bf16[2,2,1,64,384]{4,3,2,1,0:T(8,128)(2,1)S(1)}, bf16[2,2,1,64,384]{4,3,2,1,0:T(8,128)(2,1)S(1)}, u32[]{:S(2)}, u32[]{:S(2)}) collective-permute-start(bf16[2,2,1,64,384]{4,3,2,1,0:T(8,128)(2,1)S(1)} %copy-done.63), channel_id=1, source_target_pairs={{0,4},{1,5},{2,6},{3,7},{8,12},{9,13},{10,14},{11,15},{16,20},{17,... | collective-permute-start | bytes 589832 | tf_op jit(solution)/shard_map/ppermute | solution.py:20
  344.1 5.0 %collective-permute-start.35 = (bf16[2,2,1,64,384]{4,3,2,1,0:T(8,128)(2,1)S(1)}, bf16[2,2,1,64,384]{4,3,2,1,0:T(8,128)(2,1)S(1)}, u32[]{:S(2)}, u32[]{:S(2)}) collective-permute-start(bf16[2,2,1,64,384]{4,3,2,1,0:T(8,128)(2,1)S(1)} %copy-done.61), channel_id=1, source_target_pairs={{0,5},{1,6},{2,7},{8,13},{9,14},{10,15},{16,21},{17,22},{18,23},{2... | collective-permute-start | bytes 589832 | tf_op jit(solution)/shard_map/ppermute | solution.py:20
  370.5 8.6 %shard_map.75 = bf16[1,256,384]{2,1,0:T(8,128)(2,1)} custom-call(s32[4,10]{1,0:T(4,128)} %select_select_fusion.pos_ref, s32[4]{0:T(128)} %count_ref.7, f32[4,3,10]{2,1,0:T(4,128)} %fusion.42.bias_ref, bf16[1,256,384]{2,1,0:T(8,128)(2,1)} %slice.144.q_ref, ...), custom_call_target="tpu_custom_call" | custom-call | tf_op jit(solution)/shard_map/pallas_call | solution.py:84
  397.9 4.9 %collective-permute-start.6 = (bf16[2,2,1,64,384]{4,3,2,1,0:T(8,128)(2,1)S(1)}, bf16[2,2,1,64,384]{4,3,2,1,0:T(8,128)(2,1)S(1)}, u32[]{:S(2)}, u32[]{:S(2)}) collective-permute-start(bf16[2,2,1,64,384]{4,3,2,1,0:T(8,128)(2,1)S(1)} %copy-done.53), channel_id=1, source_target_pairs={{0,4},{1,5},{2,6},{3,7},{8,12},{9,13},{10,14},{11,15},{16,20},{17,... | collective-permute-start | bytes 589832 | tf_op jit(solution)/shard_map/ppermute | solution.py:20
  407.1 6.1 %collective-permute-start.8 = (bf16[2,2,1,64,384]{4,3,2,1,0:T(8,128)(2,1)S(1)}, bf16[2,2,1,64,384]{4,3,2,1,0:T(8,128)(2,1)S(1)}, u32[]{:S(2)}, u32[]{:S(2)}) collective-permute-start(bf16[2,2,1,64,384]{4,3,2,1,0:T(8,128)(2,1)S(1)} %copy-done.51), channel_id=1, source_target_pairs={{0,5},{1,6},{2,7},{8,13},{9,14},{10,15},{16,21},{17,22},{18,23},{2... | collective-permute-start | bytes 589832 | tf_op jit(solution)/shard_map/ppermute | solution.py:20
  419.8 6.8 %collective-permute-start.10 = (bf16[2,2,1,64,384]{4,3,2,1,0:T(8,128)(2,1)S(1)}, bf16[2,2,1,64,384]{4,3,2,1,0:T(8,128)(2,1)S(1)}, u32[]{:S(2)}, u32[]{:S(2)}) collective-permute-start(bf16[2,2,1,64,384]{4,3,2,1,0:T(8,128)(2,1)S(1)} %copy-done.49), channel_id=1, source_target_pairs={{0,6},{1,7},{8,14},{9,15},{16,22},{17,23},{24,30},{25,31}} | collective-permute-start | bytes 589832 | tf_op jit(solution)/shard_map/ppermute | solution.py:20
  431.6 6.4 %collective-permute-done.11 = bf16[2,2,1,64,384]{4,3,2,1,0:T(8,128)(2,1)S(1)} collective-permute-done((bf16[2,2,1,64,384]{4,3,2,1,0:T(8,128)(2,1)S(1)}, bf16[2,2,1,64,384]{4,3,2,1,0:T(8,128)(2,1)S(1)}, u32[]{:S(2)}, u32[]{:S(2)}) %collective-permute-start.11) | collective-permute-done | bytes 196640 | tf_op jit(solution)/shard_map/ppermute | solution.py:20
  438.7 8.5 %shard_map.73 = bf16[1,256,384]{2,1,0:T(8,128)(2,1)} custom-call(s32[4,10]{1,0:T(4,128)} %select_select_fusion.pos_ref, s32[4]{0:T(128)} %count_ref.7, f32[4,3,10]{2,1,0:T(4,128)} %fusion.42.bias_ref, bf16[1,256,384]{2,1,0:T(8,128)(2,1)} %slice.138.q_ref, ...), custom_call_target="tpu_custom_call" | custom-call | tf_op jit(solution)/shard_map/pallas_call | solution.py:84
  447.2 4.9 %fusion.5 = bf16[1,256,3072]{2,1,0:T(8,128)(2,1)} fusion(bf16[384,3072]{1,0:T(8,128)(2,1)S(1)} %copy-done, bf16[256,3072]{1,0:T(8,128)(2,1)} %collective-permute-done.53, bf16[256,3072]{1,0:T(8,128)(2,1)} %collective-permute-done.39, bf16[256,3072]{1,0:T(8,128)(2,1)} %collective-permute-done.25, bf16[1,256,384]{2,1,0:T(8,128)(2,1)} %shard_map.73), kind=kOutput, calls=%fused_computation.58 | convolution fusion | flops 611057664 | bytes 8847360 | tf_op jit(solution)/shard_map/dot_general | solution.py:159
  (535 shorter events, 291.1 us)
Async XLA Ops:
  0.0 90.4 %collective-permute-start.26 = (bf16[256,3072]{1,0:T(8,128)(2,1)}, bf16[256,3072]{1,0:T(8,128)(2,1)}, u32[]{:S(2)}, u32[]{:S(2)}) collective-permute-start(bf16[256,3072]{1,0:T(8,128)(2,1)} %bitcast.593), channel_id=1, source_target_pairs={{0,16},{8,24},{16,0},{24,8},{1,17},{9,25},{17,1},{25,9},{2,18},{10... | collective-permute-start | bytes 4718600 | tf_op jit(solution)/shard_map/ppermute | solution.py:142
  3.0 110.0 %collective-permute-start.12 = (bf16[256,3072]{1,0:T(8,128)(2,1)}, bf16[256,3072]{1,0:T(8,128)(2,1)}, u32[]{:S(2)}, u32[]{:S(2)}) collective-permute-start(bf16[256,3072]{1,0:T(8,128)(2,1)} %bitcast.594), channel_id=1, source_target_pairs={{0,8},{8,0},{16,24},{24,16},{1,9},{9,1},{17,25},{25,17},{2,10},{10... | collective-permute-start | bytes 4718600 | tf_op jit(solution)/shard_map/ppermute | solution.py:142
  4.5 131.7 %collective-permute-start.40 = (bf16[256,3072]{1,0:T(8,128)(2,1)}, bf16[256,3072]{1,0:T(8,128)(2,1)}, u32[]{:S(2)}, u32[]{:S(2)}) collective-permute-start(bf16[256,3072]{1,0:T(8,128)(2,1)} %bitcast.595), channel_id=1, source_target_pairs={{0,24},{8,16},{16,8},{24,0},{1,25},{9,17},{17,9},{25,1},{2,26},{10... | collective-permute-start | bytes 4718600 | tf_op jit(solution)/shard_map/ppermute | solution.py:142
  166.3 220.0 %collective-permute-start = (bf16[2,2,1,64,384]{4,3,2,1,0:T(8,128)(2,1)}, bf16[2,2,1,64,384]{4,3,2,1,0:T(8,128)(2,1)S(1)}, u32[]{:S(2)}, u32[]{:S(2)}) collective-permute-start(bf16[2,2,1,64,384]{4,3,2,1,0:T(8,128)(2,1)} %get-tuple-element.146), channel_id=1, source_target_pairs={{0,1},{1,2},{2,3},{3,4},{4,5},{5,6},{6,7},{8,9},{9,10},{10,11},{11... | collective-permute-start | bytes 589832 | tf_op jit(solution)/shard_map/ppermute | solution.py:20
  168.7 90.0 %collective-permute-start.13 = (bf16[2,2,1,64,384]{4,3,2,1,0:T(8,128)(2,1)}, bf16[2,2,1,64,384]{4,3,2,1,0:T(8,128)(2,1)S(1)}, u32[]{:S(2)}, u32[]{:S(2)}) collective-permute-start(bf16[2,2,1,64,384]{4,3,2,1,0:T(8,128)(2,1)} %get-tuple-element.147), channel_id=1, source_target_pairs={{0,1},{1,2},{2,3},{3,4},{4,5},{5,6},{6,7},{8,9},{9,10},{10,11},{11... | collective-permute-start | bytes 589832 | tf_op jit(solution)/shard_map/ppermute | solution.py:20
  172.0 156.2 %collective-permute-start.27 = (bf16[2,2,1,64,384]{4,3,2,1,0:T(8,128)(2,1)}, bf16[2,2,1,64,384]{4,3,2,1,0:T(8,128)(2,1)S(1)}, u32[]{:S(2)}, u32[]{:S(2)}) collective-permute-start(bf16[2,2,1,64,384]{4,3,2,1,0:T(8,128)(2,1)} %get-tuple-element.148), channel_id=1, source_target_pairs={{0,1},{1,2},{2,3},{3,4},{4,5},{5,6},{6,7},{8,9},{9,10},{10,11},{11... | collective-permute-start | bytes 589832 | tf_op jit(solution)/shard_map/ppermute | solution.py:20
  174.2 14.4 %collective-permute-start.41 = (bf16[2,2,1,64,384]{4,3,2,1,0:T(8,128)(2,1)S(1)}, bf16[2,2,1,64,384]{4,3,2,1,0:T(8,128)(2,1)S(1)}, u32[]{:S(2)}, u32[]{:S(2)}) collective-permute-start(bf16[2,2,1,64,384]{4,3,2,1,0:T(8,128)(2,1)S(1)} %get-tuple-element.149), channel_id=1, source_target_pairs={{0,1},{1,2},{2,3},{3,4},{4,5},{5,6},{6,7},{8,9},{9,10},{10,11},{11... | collective-permute-start | bytes 589832 | tf_op jit(solution)/shard_map/ppermute | solution.py:20
  177.3 16.2 %collective-permute-start.42 = (bf16[2,2,1,64,384]{4,3,2,1,0:T(8,128)(2,1)S(1)}, bf16[2,2,1,64,384]{4,3,2,1,0:T(8,128)(2,1)S(1)}, u32[]{:S(2)}, u32[]{:S(2)}) collective-permute-start(bf16[2,2,1,64,384]{4,3,2,1,0:T(8,128)(2,1)S(1)} %get-tuple-element.145), channel_id=1, source_target_pairs={{1,0},{2,1},{3,2},{4,3},{5,4},{6,5},{7,6},{9,8},{10,9},{11,10},{12... | collective-permute-start | bytes 589832 | tf_op jit(solution)/shard_map/ppermute | solution.py:20
  211.9 12.5 %collective-permute-start.48 = (bf16[2,2,1,64,384]{4,3,2,1,0:T(8,128)(2,1)S(1)}, bf16[2,2,1,64,384]{4,3,2,1,0:T(8,128)(2,1)S(1)}, u32[]{:S(2)}, u32[]{:S(2)}) collective-permute-start(bf16[2,2,1,64,384]{4,3,2,1,0:T(8,128)(2,1)S(1)} %get-tuple-element.121), channel_id=1, source_target_pairs={{4,0},{5,1},{6,2},{7,3},{12,8},{13,9},{14,10},{15,11},{20,16},{21,... | collective-permute-start | bytes 589832 | tf_op jit(solution)/shard_map/ppermute | solution.py:20
  237.0 151.3 %collective-permute-start.1 = (bf16[2,2,1,64,384]{4,3,2,1,0:T(8,128)(2,1)}, bf16[2,2,1,64,384]{4,3,2,1,0:T(8,128)(2,1)S(1)}, u32[]{:S(2)}, u32[]{:S(2)}) collective-permute-start(bf16[2,2,1,64,384]{4,3,2,1,0:T(8,128)(2,1)} %get-tuple-element.142), channel_id=1, source_target_pairs={{1,0},{2,1},{3,2},{4,3},{5,4},{6,5},{7,6},{9,8},{10,9},{11,10},{12... | collective-permute-start | bytes 589832 | tf_op jit(solution)/shard_map/ppermute | solution.py:20
  244.9 17.5 %collective-permute-start.14 = (bf16[2,2,1,64,384]{4,3,2,1,0:T(8,128)(2,1)}, bf16[2,2,1,64,384]{4,3,2,1,0:T(8,128)(2,1)}, u32[]{:S(2)}, u32[]{:S(2)}) collective-permute-start(bf16[2,2,1,64,384]{4,3,2,1,0:T(8,128)(2,1)} %get-tuple-element.143), channel_id=1, source_target_pairs={{1,0},{2,1},{3,2},{4,3},{5,4},{6,5},{7,6},{9,8},{10,9},{11,10},{12... | collective-permute-start | bytes 589832 | tf_op jit(solution)/shard_map/ppermute | solution.py:20
  279.8 13.6 %collective-permute-start.20 = (bf16[2,2,1,64,384]{4,3,2,1,0:T(8,128)(2,1)S(1)}, bf16[2,2,1,64,384]{4,3,2,1,0:T(8,128)(2,1)S(1)}, u32[]{:S(2)}, u32[]{:S(2)}) collective-permute-start(bf16[2,2,1,64,384]{4,3,2,1,0:T(8,128)(2,1)S(1)} %copy-done.71), channel_id=1, source_target_pairs={{4,0},{5,1},{6,2},{7,3},{12,8},{13,9},{14,10},{15,11},{20,16},{21,... | collective-permute-start | bytes 589832 | tf_op jit(solution)/shard_map/ppermute | solution.py:20
  306.1 24.1 %collective-permute-start.28 = (bf16[2,2,1,64,384]{4,3,2,1,0:T(8,128)(2,1)}, bf16[2,2,1,64,384]{4,3,2,1,0:T(8,128)(2,1)S(1)}, u32[]{:S(2)}, u32[]{:S(2)}) collective-permute-start(bf16[2,2,1,64,384]{4,3,2,1,0:T(8,128)(2,1)} %get-tuple-element.144), channel_id=1, source_target_pairs={{1,0},{2,1},{3,2},{4,3},{5,4},{6,5},{7,6},{9,8},{10,9},{11,10},{12... | collective-permute-start | bytes 589832 | tf_op jit(solution)/shard_map/ppermute | solution.py:20
  313.6 18.6 %collective-permute-start.29 = (bf16[2,2,1,64,384]{4,3,2,1,0:T(8,128)(2,1)}, bf16[2,2,1,64,384]{4,3,2,1,0:T(8,128)(2,1)}, u32[]{:S(2)}, u32[]{:S(2)}) collective-permute-start(bf16[2,2,1,64,384]{4,3,2,1,0:T(8,128)(2,1)} %get-tuple-element.140), channel_id=1, source_target_pairs={{0,2},{1,3},{2,4},{3,5},{4,6},{5,7},{8,10},{9,11},{10,12},{11,13},... | collective-permute-start | bytes 589832 | tf_op jit(solution)/shard_map/ppermute | solution.py:20
  330.2 11.9 %collective-permute-start.31 = (bf16[2,2,1,64,384]{4,3,2,1,0:T(8,128)(2,1)S(1)}, bf16[2,2,1,64,384]{4,3,2,1,0:T(8,128)(2,1)S(1)}, u32[]{:S(2)}, u32[]{:S(2)}) collective-permute-start(bf16[2,2,1,64,384]{4,3,2,1,0:T(8,128)(2,1)S(1)} %copy-done.66), channel_id=1, source_target_pairs={{0,3},{1,4},{2,5},{3,6},{4,7},{8,11},{9,12},{10,13},{11,14},{12,15... | collective-permute-start | bytes 589832 | tf_op jit(solution)/shard_map/ppermute | solution.py:20
  335.8 14.0 %collective-permute-start.33 = (bf16[2,2,1,64,384]{4,3,2,1,0:T(8,128)(2,1)S(1)}, bf16[2,2,1,64,384]{4,3,2,1,0:T(8,128)(2,1)S(1)}, u32[]{:S(2)}, u32[]{:S(2)}) collective-permute-start(bf16[2,2,1,64,384]{4,3,2,1,0:T(8,128)(2,1)S(1)} %copy-done.63), channel_id=1, source_target_pairs={{0,4},{1,5},{2,6},{3,7},{8,12},{9,13},{10,14},{11,15},{16,20},{17,... | collective-permute-start | bytes 589832 | tf_op jit(solution)/shard_map/ppermute | solution.py:20
  342.1 13.9 %collective-permute-start.34 = (bf16[2,2,1,64,384]{4,3,2,1,0:T(8,128)(2,1)S(1)}, bf16[2,2,1,64,384]{4,3,2,1,0:T(8,128)(2,1)S(1)}, u32[]{:S(2)}, u32[]{:S(2)}) collective-permute-start(bf16[2,2,1,64,384]{4,3,2,1,0:T(8,128)(2,1)S(1)} %copy-done.62), channel_id=1, source_target_pairs={{4,0},{5,1},{6,2},{7,3},{12,8},{13,9},{14,10},{15,11},{20,16},{21,... | collective-permute-start | bytes 589832 | tf_op jit(solution)/shard_map/ppermute | solution.py:20
  344.1 16.4 %collective-permute-start.35 = (bf16[2,2,1,64,384]{4,3,2,1,0:T(8,128)(2,1)S(1)}, bf16[2,2,1,64,384]{4,3,2,1,0:T(8,128)(2,1)S(1)}, u32[]{:S(2)}, u32[]{:S(2)}) collective-permute-start(bf16[2,2,1,64,384]{4,3,2,1,0:T(8,128)(2,1)S(1)} %copy-done.61), channel_id=1, source_target_pairs={{0,5},{1,6},{2,7},{8,13},{9,14},{10,15},{16,21},{17,22},{18,23},{2... | collective-permute-start | bytes 589832 | tf_op jit(solution)/shard_map/ppermute | solution.py:20
  349.8 12.9 %collective-permute-start.36 = (bf16[2,2,1,64,384]{4,3,2,1,0:T(8,128)(2,1)S(1)}, bf16[2,2,1,64,384]{4,3,2,1,0:T(8,128)(2,1)S(1)}, u32[]{:S(2)}, u32[]{:S(2)}) collective-permute-start(bf16[2,2,1,64,384]{4,3,2,1,0:T(8,128)(2,1)S(1)} %copy-done.59), channel_id=1, source_target_pairs={{5,0},{6,1},{7,2},{13,8},{14,9},{15,10},{21,16},{22,17},{23,18},{2... | collective-permute-start | bytes 589832 | tf_op jit(solution)/shard_map/ppermute | solution.py:20
  362.7 84.5 %collective-permute-start.53 = (bf16[256,3072]{1,0:T(8,128)(2,1)}, bf16[256,3072]{1,0:T(8,128)(2,1)}, u32[]{:S(2)}, u32[]{:S(2)}) collective-permute-start(bf16[256,3072]{1,0:T(8,128)(2,1)} %convolution_convert_fusion), channel_id=1, source_target_pairs={{0,24},{8,16},{16,8},{24,0},{1,25},{9,17},{17,9},{25,1},{2,26},{10... | collective-permute-start | bytes 4718600 | tf_op jit(solution)/shard_map/ppermute | solution.py:163
  365.8 81.4 %collective-permute-start.25 = (bf16[256,3072]{1,0:T(8,128)(2,1)}, bf16[256,3072]{1,0:T(8,128)(2,1)}, u32[]{:S(2)}, u32[]{:S(2)}) collective-permute-start(bf16[256,3072]{1,0:T(8,128)(2,1)} %convolution_convert_fusion.2), channel_id=1, source_target_pairs={{0,8},{8,0},{16,24},{24,16},{1,9},{9,1},{17,25},{25,17},{2,10},{10... | collective-permute-start | bytes 4718600 | tf_op jit(solution)/shard_map/ppermute | solution.py:163
  382.3 64.9 %collective-permute-start.39 = (bf16[256,3072]{1,0:T(8,128)(2,1)}, bf16[256,3072]{1,0:T(8,128)(2,1)}, u32[]{:S(2)}, u32[]{:S(2)}) collective-permute-start(bf16[256,3072]{1,0:T(8,128)(2,1)} %convolution_convert_fusion.1), channel_id=1, source_target_pairs={{0,16},{8,24},{16,0},{24,8},{1,17},{9,25},{17,1},{25,9},{2,18},{10... | collective-permute-start | bytes 4718600 | tf_op jit(solution)/shard_map/ppermute | solution.py:163
  404.0 13.8 %collective-permute-start.7 = (bf16[2,2,1,64,384]{4,3,2,1,0:T(8,128)(2,1)S(1)}, bf16[2,2,1,64,384]{4,3,2,1,0:T(8,128)(2,1)S(1)}, u32[]{:S(2)}, u32[]{:S(2)}) collective-permute-start(bf16[2,2,1,64,384]{4,3,2,1,0:T(8,128)(2,1)S(1)} %copy-done.52), channel_id=1, source_target_pairs={{4,0},{5,1},{6,2},{7,3},{12,8},{13,9},{14,10},{15,11},{20,16},{21,... | collective-permute-start | bytes 589832 | tf_op jit(solution)/shard_map/ppermute | solution.py:20
  407.1 12.7 %collective-permute-start.8 = (bf16[2,2,1,64,384]{4,3,2,1,0:T(8,128)(2,1)S(1)}, bf16[2,2,1,64,384]{4,3,2,1,0:T(8,128)(2,1)S(1)}, u32[]{:S(2)}, u32[]{:S(2)}) collective-permute-start(bf16[2,2,1,64,384]{4,3,2,1,0:T(8,128)(2,1)S(1)} %copy-done.51), channel_id=1, source_target_pairs={{0,5},{1,6},{2,7},{8,13},{9,14},{10,15},{16,21},{17,22},{18,23},{2... | collective-permute-start | bytes 589832 | tf_op jit(solution)/shard_map/ppermute | solution.py:20
  (128 other events, 1856.4 us)

commit v3 on v2

--- a/solution.py
+++ b/solution.py
@@ -14,23 +14,18 @@
 CAP = 2
 
 
-def shifted(value, axis, steps):
-    count = lax.axis_size(axis)
-    first, last = (max(0, -steps), min(count, count - steps))
-    return lax.ppermute(value, axis, [(source, source + steps) for source in range(first, last)])
-
-
-def chosen_tiles(rows, rows_live, source, tiles_per_device):
+def first_two(rows, rows_live, sources, tiles_per_device):
     local = jnp.arange(tiles_per_device, dtype=jnp.int32)
-    wanted = source * tiles_per_device + local
+    wanted = sources[:, None] * tiles_per_device + local[None, :]
     named = jnp.any(
-        (rows[:, :, None] == wanted[None, None, :]) & rows_live[:, :, None], axis=(0, 1)
+        (rows[:, :, :, None] == wanted[:, None, None, :]) & rows_live[:, :, :, None], axis=(1, 2)
     )
-    rank = jnp.cumsum(named.astype(jnp.int32)) - 1
-    picks = [
-        jnp.sum(jnp.where(named & (rank == slot), local, 0)) for slot in range(CAP)
-    ]
-    return jnp.stack(picks).astype(jnp.int32)
+    order = jnp.where(named, local[None, :], tiles_per_device)
+    first = jnp.min(order, axis=1)
+    second = jnp.min(jnp.where(order > first[:, None], order, tiles_per_device), axis=1)
+    first = jnp.where(first == tiles_per_device, 0, first)
+    second = jnp.where(second == tiles_per_device, 0, second)
+    return first.astype(jnp.int32), second.astype(jnp.int32)
 
 
 def attention_kernel(pos_ref, count_ref, bias_ref, q_ref, *refs, heads, head_size, scale):
@@ -108,32 +103,28 @@
     n_ctx = lax.axis_size("ctx")
     n_dp = lax.axis_size("dp")
     own_index = lax.axis_index("ctx").astype(jnp.int32)
+    devices = jnp.arange(n_ctx, dtype=jnp.int32)
 
-    table = jnp.concatenate([neighbours, counts[:, None]], axis=1)
-    all_table = lax.all_gather(table, "ctx", axis=0, tiled=True)
-    all_rows = all_table[:, :KMAX]
-    all_live = jnp.arange(KMAX)[None, :] < all_table[:, KMAX:]
+    table = jnp.concatenate([neighbours, counts[:, None]], axis=1).astype(jnp.float32)
+    all_table = lax.all_gather(table, "ctx", axis=0, tiled=True).astype(jnp.int32)
+    all_table = all_table.reshape(n_ctx, tile_count, KMAX + 1)
+    all_live = jnp.arange(KMAX)[None, None, :] < all_table[:, :, KMAX:]
+    send_first, send_second = first_two(
+        all_table[:, :, :KMAX], all_live, jnp.full((n_ctx,), own_index), tile_count
+    )
+    send_picks = jnp.stack([send_first, send_second], axis=1).reshape(-1)
+
     live = jnp.arange(KMAX)[None, :] < counts[:, None]
-
-    offsets = [step for amount in range(1, REACH + 1) for step in (amount, -amount) if amount < n_ctx]
-    send_picks = []
-    received_picks = []
-    for step in offsets:
-        target = jnp.clip(own_index + step, 0, n_ctx - 1) * tile_count
-        target_rows = lax.dynamic_slice_in_dim(all_rows, target, tile_count, axis=0)
-        target_live = lax.dynamic_slice_in_dim(all_live, target, tile_count, axis=0)
-        send_picks.append(chosen_tiles(target_rows, target_live, own_index, tile_count))
-        received_picks.append(chosen_tiles(neighbours, live, own_index - step, tile_count))
-
+    recv_first, _ = first_two(
+        jnp.broadcast_to(neighbours[None], (n_ctx,) + neighbours.shape),
+        jnp.broadcast_to(live[None], (n_ctx,) + live.shape),
+        devices,
+        tile_count,
+    )
     source = neighbours // tile_count
     within = neighbours % tile_count
-    distance = own_index - source
-    positions = jnp.where(distance == 0, within, 0)
-    for index, step in enumerate(offsets):
-        first = received_picks[index][0]
-        slot = tile_count + CAP * index + jnp.where(within == first, 0, 1)
-        positions = jnp.where(distance == step, slot, positions)
-    positions = positions.astype(jnp.int32)
+    remote_slot = tile_count + CAP * source + jnp.where(within == recv_first[source], 0, 1)
+    positions = jnp.where(source == own_index, within, remote_slot).astype(jnp.int32)
     bias = jnp.transpose(jnp.take(rel_bias, bias_index, axis=1), (1, 0, 2))
     live_counts = counts.astype(jnp.int32)
 
@@ -150,11 +141,9 @@
         by_tile = jnp.transpose(
             projected[1:3].reshape(2, tile_count, TILE, width_here), (1, 0, 2, 3)
         )[:, :, None]
-        pieces = [by_tile]
-        for index, offset in enumerate(offsets):
-            outgoing = jnp.take(by_tile, send_picks[index], axis=0)
-            pieces.append(shifted(outgoing, "ctx", offset))
-        key_values = jnp.concatenate(pieces, axis=0)
+        outgoing = jnp.take(by_tile, send_picks, axis=0)
+        incoming = lax.all_to_all(outgoing, "ctx", 0, 0, tiled=True)
+        key_values = jnp.concatenate([by_tile, incoming], axis=0)
         attended = attend(positions, live_counts, bias, queries, key_values, heads_here, head_size)
         partial_out = jnp.dot(
             attended[0], out_weight, preferred_element_type=jnp.float32

time: 455 us -> 338 us (0.74)
  starting transfers between devices: 135 us -> 16.9 us
  local copies, waits for them, and re-layouts: 112 us -> 25.9 us
  blocking collectives: 13.4 us -> 97.1 us
  waiting for transfers between devices: 56.8 us -> 103 us
  other arithmetic: 61.8 us -> 22.6 us
    ppermute x48 -> x0, starting transfers between devices: 126 us -> none  [shifted(): lax.ppermute(value, axis, [(source, source + steps) for source in range(f...]
    all_to_all x0 -> x2, blocking collectives: none -> 83.7 us  [local(): incoming = lax.all_to_all(outgoing, 'ctx', 0, 0, tiled=True)]
    ppermute x48 -> x0, waiting for transfers between devices: 56.8 us -> none  [shifted(): lax.ppermute(value, axis, [(source, source + steps) for source in range(f...]
    ppermute x3, waiting for transfers between devices: 0.01 us -> 54.1 us  [local(): partial_out = lax.ppermute(partial_out, 'dp', partner_pairs(n_dp, step))]
    gather x48 -> x6, local copies, waits for them, and re-layouts: 63.2 us -> 9.12 us  [the longest x4 7.66 us: local(): outgoing = jnp.take(by_tile, send_picks, axis=0)]
    unnamed x246 -> x23, local copies, waits for them, and re-layouts: 39.8 us -> 4.51 us
    ppermute x3, waiting for transfers between devices: 0.01 us -> 27.1 us  [local(): lax.ppermute(own_tokens, 'dp', partner_pairs(n_dp, step))]
    all_to_all x0 -> x2, waiting for transfers between devices: none -> 21.4 us  [local(): incoming = lax.all_to_all(outgoing, 'ctx', 0, 0, tiled=True)]
  transfers between devices with their start and end apart: 54 -> 8, of which waited for: 25 -> 5; matrix products, arithmetic and copies ran while one was open for 39% -> 19% of each run, Pallas kernels for 8% -> 11%
where the time goes in v3:
time: 338 us; the launch traced here: 336 us
  waiting for transfers between devices  103 us (30%)
  blocking collectives  97.1 us (29%)
  Pallas kernels  35.8 us (11%)
  matrix products  35.2 us (10%)
  local copies, waits for them, and re-layouts  25.9 us (8%)
  other arithmetic  22.6 us (7%)
  starting transfers between devices  16.9 us (5%)
    all_to_all x2, blocking collectives, local(): incoming = lax.all_to_all(outgoing, 'ctx', 0, 0, tiled=True)  83.7 us
    ppermute x3, waiting for transfers between devices, local(): partial_out = lax.ppermute(partial_out, 'dp', partner_pairs(n_dp, step))  54.1 us
    pallas_call x4, Pallas kernels, attend(): pl.pallas_call(kernel, out_shape=jax.ShapeDtypeStruct(queries.shape, jnp....  35.8 us
    ppermute x3, waiting for transfers between devices, local(): lax.ppermute(own_tokens, 'dp', partner_pairs(n_dp, step))  27.1 us
    dot_general x4, matrix products, local(): jnp.einsum('td,sdh->sth', clip_inputs[step], qkv_weight, preferred_elemen...  22.8 us
    all_to_all x2, waiting for transfers between devices, local(): incoming = lax.all_to_all(outgoing, 'ctx', 0, 0, tiled=True)  21.4 us
    all_gather x1, blocking collectives, local(): lax.all_gather(table, 'ctx', axis=0, tiled=True).astype(jnp.int32)  13.4 us
    dot_general x4, matrix products, local(): jnp.dot(attended[0], out_weight, preferred_element_type=jnp.float32)  12.4 us
  transfers between devices with their start and end apart: 8, of which 5 were waited for; matrix products, arithmetic and copies ran while one was open for 19% of the time, Pallas kernels for 11%

profile of v3, /device:TPU:0, one launch (start us, length us, event | category | flops | bytes accessed | tf_op | source)
XLA Modules:
  0.0 336.2 jit_solution(15511296425704498529)
XLA Ops:
  0.0 3.0 collective-permute-start.2
  6.0 13.4 %all-gather = f32[8,4,11]{2,1,0:T(4,128)S(1)} all-gather(f32[1,4,11]{2,1,0:T(4,128)S(1)} %fusion.42), channel_id=1, replica_groups=mesh['dp'=4,'ctx'=8] {'ctx'}, dimensions={0}, use_global_device_ids=true | all-gather | bytes 1584 | tf_op jit(solution)/shard_map/all_gather | solution.py:109
  20.1 5.7 %fusion.31 = bf16[3,256,384]{2,1,0:T(8,128)(2,1)S(1)} fusion(bf16[3,3072,384]{2,1,0:T(8,128)(2,1)} %param.10, bf16[1,256,3072]{2,1,0:T(8,128)(2,1)} %param.9), kind=kOutput, calls=%fused_computation.36 | convolution fusion | flops 1812234240 | bytes 9240576 | tf_op jit(solution)/shard_map/td,sdh->sth/dot_general | solution.py:137
  28.6 9.1 %collective-permute-done.2 = bf16[256,3072]{1,0:T(8,128)(2,1)} collective-permute-done((bf16[256,3072]{1,0:T(8,128)(2,1)}, bf16[256,3072]{1,0:T(8,128)(2,1)}, u32[]{:S(2)}, u32[]{:S(2)}) %collective-permute-start.2) | collective-permute-done | bytes 1572896 | tf_op jit(solution)/shard_map/ppermute | solution.py:133
  37.7 5.7 %fusion.25 = bf16[3,256,384]{2,1,0:T(8,128)(2,1)S(1)} fusion(bf16[3,3072,384]{2,1,0:T(8,128)(2,1)} %param.10, bf16[256,3072]{1,0:T(8,128)(2,1)} %collective-permute-done.2), kind=kOutput, calls=%fused_computation.34 | convolution fusion | flops 1812234240 | bytes 9240576 | tf_op jit(solution)/shard_map/td,sdh->sth/dot_general | solution.py:137
  46.2 5.7 %fusion.28 = bf16[3,256,384]{2,1,0:T(8,128)(2,1)S(1)} fusion(bf16[3,3072,384]{2,1,0:T(8,128)(2,1)} %param.10, bf16[256,3072]{1,0:T(8,128)(2,1)} %collective-permute-done), kind=kOutput, calls=%fused_computation.35 | convolution fusion | flops 1812234240 | bytes 9240576 | tf_op jit(solution)/shard_map/td,sdh->sth/dot_general | solution.py:137
  54.7 18.0 %collective-permute-done.4 = bf16[256,3072]{1,0:T(8,128)(2,1)} collective-permute-done((bf16[256,3072]{1,0:T(8,128)(2,1)}, bf16[256,3072]{1,0:T(8,128)(2,1)}, u32[]{:S(2)}, u32[]{:S(2)}) %collective-permute-start.4) | collective-permute-done | bytes 1572896 | tf_op jit(solution)/shard_map/ppermute | solution.py:133
  72.6 5.7 %fusion.22 = bf16[3,256,384]{2,1,0:T(8,128)(2,1)S(1)} fusion(bf16[3,3072,384]{2,1,0:T(8,128)(2,1)} %param.10, bf16[256,3072]{1,0:T(8,128)(2,1)} %collective-permute-done.4), kind=kOutput, calls=%fused_computation.33 | convolution fusion | flops 1812234240 | bytes 9240576 | tf_op jit(solution)/shard_map/td,sdh->sth/dot_general | solution.py:137
  81.1 5.4 %bitcast_select_fusion.3 = (bf16[16,2,1,64,384]{4,3,2,1,0:T(8,128)(2,1)}, bf16[16,2,1,64,384]{4,3,2,1,0:T(8,128)(2,1)S(1)}, bf16[16,2,1,64,384]{4,3,2,1,0:T(8,128)(2,1)S(1)}, bf16[16,2,1,64,384]{4,3,2,1,0:T(8,128)(2,1)}) fusion(bf16[16,2,64,384]{3,2,1,0:T(8,128)(2,1)} %gather_fusion.2, pred[16]{0:T(512)(128)(4,1)S(1)} %compare_and_fusion, ...), kind=kLoop, calls=%fused_computation.26 | loop fusion | flops 3145728 | bytes 12582928 | tf_op jit(solution)/shard_map/jit(_take)/select_n | solution.py:144
  86.5 42.8 %all_to_all.20 = bf16[16,2,1,64,384]{4,3,2,1,0:T(8,128)(2,1)} all-to-all(bf16[16,2,1,64,384]{4,3,2,1,0:T(8,128)(2,1)S(1)} %get-tuple-element.15), channel_id=1, replica_groups=mesh['dp'=4,'ctx'=8] {'ctx'}, dimensions={0} | all-to-all | bytes 3145728 | tf_op jit(solution)/shard_map/all_to_all | solution.py:145
  129.2 40.9 %all_to_all.21 = bf16[16,2,1,64,384]{4,3,2,1,0:T(8,128)(2,1)} all-to-all(bf16[16,2,1,64,384]{4,3,2,1,0:T(8,128)(2,1)S(1)} %get-tuple-element.16), channel_id=1, replica_groups=mesh['dp'=4,'ctx'=8] {'ctx'}, dimensions={0} | all-to-all | bytes 3145728 | tf_op jit(solution)/shard_map/all_to_all | solution.py:145
  170.2 4.5 %all-to-all-start.3 = ((bf16[16,2,1,64,384]{4,3,2,1,0:T(8,128)(2,1)}), bf16[16,2,1,64,384]{4,3,2,1,0:T(8,128)(2,1)}, u32[]{:S(2)}, u32[]{:S(2)}) async-start(bf16[16,2,1,64,384]{4,3,2,1,0:T(8,128)(2,1)} %get-tuple-element.17), calls=%async_computation.3 | async-start | bytes 3145728 | tf_op jit(solution)/shard_map/all_to_all | solution.py:145
  191.1 21.4 %all-to-all-done.3 = bf16[16,2,1,64,384]{4,3,2,1,0:T(8,128)(2,1)} async-done(((bf16[16,2,1,64,384]{4,3,2,1,0:T(8,128)(2,1)}), bf16[16,2,1,64,384]{4,3,2,1,0:T(8,128)(2,1)}, u32[]{:S(2)}, u32[]{:S(2)}) %all-to-all-start.3) | async-done | bytes 1572896 | tf_op jit(solution)/shard_map/all_to_all | solution.py:145
  212.5 4.5 %all-to-all-start = ((bf16[16,2,1,64,384]{4,3,2,1,0:T(8,128)(2,1)}), bf16[16,2,1,64,384]{4,3,2,1,0:T(8,128)(2,1)}, u32[]{:S(2)}, u32[]{:S(2)}) async-start(bf16[16,2,1,64,384]{4,3,2,1,0:T(8,128)(2,1)} %get-tuple-element.14), calls=%async_computation | async-start | bytes 3145728 | tf_op jit(solution)/shard_map/all_to_all | solution.py:145
  217.0 3.0 pad_maximum_fusion.1.refs_0_.refs_1_.refs_2_.refs_3_.refs_4_.refs_5_.refs_6_.refs_7_.refs_8_.refs_9_
  220.0 9.0 %shard_map.74 = bf16[1,256,384]{2,1,0:T(8,128)(2,1)} custom-call(s32[4,10]{1,0:T(4,128)} %add_select_fusion.2.pos_ref, s32[4]{0:T(128)} %count_ref.7, f32[4,3,10]{2,1,0:T(4,128)} %fusion.40.bias_ref, bf16[1,256,384]{2,1,0:T(8,128)(2,1)} %slice.56.q_ref, ...), custom_call_target="tpu_custom_call" | custom-call | tf_op jit(solution)/shard_map/pallas_call | solution.py:79
  231.9 8.9 %shard_map.75 = bf16[1,256,384]{2,1,0:T(8,128)(2,1)} custom-call(s32[4,10]{1,0:T(4,128)} %add_select_fusion.2.pos_ref, s32[4]{0:T(128)} %count_ref.7, f32[4,3,10]{2,1,0:T(4,128)} %fusion.40.bias_ref, bf16[1,256,384]{2,1,0:T(8,128)(2,1)} %slice.58.q_ref, ...), custom_call_target="tpu_custom_call" | custom-call | tf_op jit(solution)/shard_map/pallas_call | solution.py:79
  243.7 9.0 %shard_map.76 = bf16[1,256,384]{2,1,0:T(8,128)(2,1)} custom-call(s32[4,10]{1,0:T(4,128)} %add_select_fusion.2.pos_ref, s32[4]{0:T(128)} %count_ref.7, f32[4,3,10]{2,1,0:T(4,128)} %fusion.40.bias_ref, bf16[1,256,384]{2,1,0:T(8,128)(2,1)} %slice.60.q_ref, ...), custom_call_target="tpu_custom_call" | custom-call | tf_op jit(solution)/shard_map/pallas_call | solution.py:79
  252.7 3.1 convolution_convert_fusion
  265.3 2.9 pad_maximum_fusion.refs_0_.refs_1_.refs_2_.refs_3_.refs_4_.refs_5_.refs_6_.refs_7_.refs_8_.refs_9_
  268.3 8.9 %shard_map.73 = bf16[1,256,384]{2,1,0:T(8,128)(2,1)} custom-call(s32[4,10]{1,0:T(4,128)} %add_select_fusion.2.pos_ref, s32[4]{0:T(128)} %count_ref.7, f32[4,3,10]{2,1,0:T(4,128)} %fusion.40.bias_ref, bf16[1,256,384]{2,1,0:T(8,128)(2,1)} %slice.52.q_ref, ...), custom_call_target="tpu_custom_call" | custom-call | tf_op jit(solution)/shard_map/pallas_call | solution.py:79
  277.2 20.6 %collective-permute-done.1 = bf16[256,3072]{1,0:T(8,128)(2,1)} collective-permute-done((bf16[256,3072]{1,0:T(8,128)(2,1)}, bf16[256,3072]{1,0:T(8,128)(2,1)}, u32[]{:S(2)}, u32[]{:S(2)}) %collective-permute-start.1) | collective-permute-done | bytes 1572896 | tf_op jit(solution)/shard_map/ppermute | solution.py:152
  297.8 33.5 %collective-permute-done.3 = bf16[256,3072]{1,0:T(8,128)(2,1)} collective-permute-done((bf16[256,3072]{1,0:T(8,128)(2,1)}, bf16[256,3072]{1,0:T(8,128)(2,1)}, u32[]{:S(2)}, u32[]{:S(2)}) %collective-permute-start.3) | collective-permute-done | bytes 1572896 | tf_op jit(solution)/shard_map/ppermute | solution.py:152
  331.3 4.9 %fusion.1 = bf16[1,256,3072]{2,1,0:T(8,128)(2,1)} fusion(bf16[256,3072]{1,0:T(8,128)(2,1)} %collective-permute-done.5, bf16[256,3072]{1,0:T(8,128)(2,1)} %collective-permute-done.3, bf16[256,3072]{1,0:T(8,128)(2,1)} %collective-permute-done.1, bf16[384,3072]{1,0:T(8,128)(2,1)S(1)} %copy-done, bf16[1,256,384]{2,1,0:T(8,128)(2,1)} %shard_map.73), kind=kOutput, calls=%fused_computation.16 | convolution fusion | flops 611057664 | bytes 8847360 | tf_op jit(solution)/shard_map/dot_general | solution.py:148
  (89 shorter events, 46.6 us)
Async XLA Ops:
  0.0 252.7 %copy-start = (bf16[384,3072]{1,0:T(8,128)(2,1)S(1)}, bf16[384,3072]{1,0:T(8,128)(2,1)}, u32[]{:S(2)}) copy-start(bf16[384,3072]{1,0:T(8,128)(2,1)} %param.11) | copy-start | bytes 7077892
  0.0 37.7 %collective-permute-start.2 = (bf16[256,3072]{1,0:T(8,128)(2,1)}, bf16[256,3072]{1,0:T(8,128)(2,1)}, u32[]{:S(2)}, u32[]{:S(2)}) collective-permute-start(bf16[256,3072]{1,0:T(8,128)(2,1)} %bitcast.133), channel_id=1, source_target_pairs={{0,16},{8,24},{16,0},{24,8},{1,17},{9,25},{17,1},{25,9},{2,18},{10... | collective-permute-start | bytes 4718600 | tf_op jit(solution)/shard_map/ppermute | solution.py:133
  3.0 43.2 %collective-permute-start = (bf16[256,3072]{1,0:T(8,128)(2,1)}, bf16[256,3072]{1,0:T(8,128)(2,1)}, u32[]{:S(2)}, u32[]{:S(2)}) collective-permute-start(bf16[256,3072]{1,0:T(8,128)(2,1)} %bitcast.134), channel_id=1, source_target_pairs={{0,8},{8,0},{16,24},{24,16},{1,9},{9,1},{17,25},{25,17},{2,10},{10... | collective-permute-start | bytes 4718600 | tf_op jit(solution)/shard_map/ppermute | solution.py:133
  4.5 68.2 %collective-permute-start.4 = (bf16[256,3072]{1,0:T(8,128)(2,1)}, bf16[256,3072]{1,0:T(8,128)(2,1)}, u32[]{:S(2)}, u32[]{:S(2)}) collective-permute-start(bf16[256,3072]{1,0:T(8,128)(2,1)} %bitcast.135), channel_id=1, source_target_pairs={{0,24},{8,16},{16,8},{24,0},{1,25},{9,17},{17,9},{25,1},{2,26},{10... | collective-permute-start | bytes 4718600 | tf_op jit(solution)/shard_map/ppermute | solution.py:133
  25.8 0.9 copy-start.4
  43.4 0.9 copy-start.5
  51.9 0.9 copy-start.6
  52.7 1.9 copy-start.1
  78.3 0.8 copy-start.7
  170.2 4.5 %copy-start.10 = (s32[4,10]{1,0:T(4,128)S(1)}, s32[4,10]{1,0:T(4,128)}, u32[]{:S(2)}) copy-start(s32[4,10]{1,0:T(4,128)} %param.14) | copy-start | bytes 484
  170.2 5.1 %copy-start.8 = (s32[4,10]{1,0:T(4,128)S(1)}, s32[4,10]{1,0:T(4,128)}, u32[]{:S(2)}) copy-start(s32[4,10]{1,0:T(4,128)} %param.12) | copy-start | bytes 484
  170.2 6.5 %copy-start.9 = (s32[4]{0:T(128)S(1)}, s32[4]{0:T(128)}, u32[]{:S(2)}) copy-start(s32[4]{0:T(128)} %count_ref.7) | copy-start | bytes 52
  170.2 42.3 %all-to-all-start.3 = ((bf16[16,2,1,64,384]{4,3,2,1,0:T(8,128)(2,1)}), bf16[16,2,1,64,384]{4,3,2,1,0:T(8,128)(2,1)}, u32[]{:S(2)}, u32[]{:S(2)}) async-start(bf16[16,2,1,64,384]{4,3,2,1,0:T(8,128)(2,1)} %get-tuple-element.17), calls=%async_computation.3 | async-start | bytes 3145728 | tf_op jit(solution)/shard_map/all_to_all | solution.py:145
  212.5 52.9 %all-to-all-start = ((bf16[16,2,1,64,384]{4,3,2,1,0:T(8,128)(2,1)}), bf16[16,2,1,64,384]{4,3,2,1,0:T(8,128)(2,1)}, u32[]{:S(2)}, u32[]{:S(2)}) async-start(bf16[16,2,1,64,384]{4,3,2,1,0:T(8,128)(2,1)} %get-tuple-element.14), calls=%async_computation | async-start | bytes 3145728 | tf_op jit(solution)/shard_map/all_to_all | solution.py:145
  252.7 3.1 copy-start.3
  255.8 2.2 copy-start.2
  260.2 37.6 %collective-permute-start.1 = (bf16[256,3072]{1,0:T(8,128)(2,1)}, bf16[256,3072]{1,0:T(8,128)(2,1)}, u32[]{:S(2)}, u32[]{:S(2)}) collective-permute-start(bf16[256,3072]{1,0:T(8,128)(2,1)} %convolution_convert_fusion.2), channel_id=1, source_target_pairs={{0,8},{8,0},{16,24},{24,16},{1,9},{9,1},{17,25},{25,17},{2,10},{10... | collective-permute-start | bytes 4718600 | tf_op jit(solution)/shard_map/ppermute | solution.py:152
  261.7 69.6 %collective-permute-start.3 = (bf16[256,3072]{1,0:T(8,128)(2,1)}, bf16[256,3072]{1,0:T(8,128)(2,1)}, u32[]{:S(2)}, u32[]{:S(2)}) collective-permute-start(bf16[256,3072]{1,0:T(8,128)(2,1)} %convolution_convert_fusion.1), channel_id=1, source_target_pairs={{0,16},{8,24},{16,0},{24,8},{1,17},{9,25},{17,1},{25,9},{2,18},{10... | collective-permute-start | bytes 4718600 | tf_op jit(solution)/shard_map/ppermute | solution.py:152
  263.2 68.1 %collective-permute-start.5 = (bf16[256,3072]{1,0:T(8,128)(2,1)}, bf16[256,3072]{1,0:T(8,128)(2,1)}, u32[]{:S(2)}, u32[]{:S(2)}) collective-permute-start(bf16[256,3072]{1,0:T(8,128)(2,1)} %convolution_convert_fusion), channel_id=1, source_target_pairs={{0,24},{8,16},{16,8},{24,0},{1,25},{9,17},{17,9},{25,1},{2,26},{10... | collective-permute-start | bytes 4718600 | tf_op jit(solution)/shard_map/ppermute | solution.py:152

commit v4 on v3

--- a/solution.py
+++ b/solution.py
@@ -129,22 +129,29 @@
     live_counts = counts.astype(jnp.int32)
 
     own_tokens = clip_tokens[0]
-    clip_inputs = [own_tokens] + [
-        lax.ppermute(own_tokens, "dp", partner_pairs(n_dp, step)) for step in range(1, n_dp)
-    ]
-    total = None
-    for step in range(n_dp):
+    order = list(range(1, n_dp)) + [0]
+    clip_inputs = {0: own_tokens}
+    for step in range(1, n_dp):
+        clip_inputs[step] = lax.ppermute(own_tokens, "dp", partner_pairs(n_dp, step))
+    outgoing = {}
+    for step in order:
         projected = jnp.einsum(
             "td,sdh->sth", clip_inputs[step], qkv_weight, preferred_element_type=jnp.float32
         ).astype(jnp.bfloat16)
-        queries = projected[0][None]
         by_tile = jnp.transpose(
             projected[1:3].reshape(2, tile_count, TILE, width_here), (1, 0, 2, 3)
         )[:, :, None]
-        outgoing = jnp.take(by_tile, send_picks, axis=0)
-        incoming = lax.all_to_all(outgoing, "ctx", 0, 0, tiled=True)
+        outgoing[step] = (projected[0][None], by_tile, jnp.take(by_tile, send_picks, axis=0))
+    total = None
+    finished = []
+    for index, step in enumerate(order):
+        queries, by_tile, payload = outgoing[step]
+        if index >= 2:
+            payload, _ = lax.optimization_barrier((payload, finished[index - 2]))
+        incoming = lax.all_to_all(payload, "ctx", 0, 0, tiled=True)
         key_values = jnp.concatenate([by_tile, incoming], axis=0)
         attended = attend(positions, live_counts, bias, queries, key_values, heads_here, head_size)
+        finished.append(attended)
         partial_out = jnp.dot(
             attended[0], out_weight, preferred_element_type=jnp.float32
         ).astype(jnp.bfloat16)

time: 338 us -> 311 us (0.920)
  blocking collectives: 97.1 us -> 56.1 us
  waiting for transfers between devices: 103 us -> 113 us
  starting transfers between devices: 16.9 us -> 21.3 us
    all_to_all x2 -> x1, blocking collectives: 83.7 us -> 42.8 us  [local(): incoming = lax.all_to_all(payload, 'ctx', 0, 0, tiled=True)]
    all_to_all x2 -> x3, waiting for transfers between devices: 21.4 us -> 49.6 us  [local(): incoming = lax.all_to_all(payload, 'ctx', 0, 0, tiled=True)]
    ppermute x3, waiting for transfers between devices: 54.1 us -> 28.5 us  [local(): partial_out = lax.ppermute(partial_out, 'dp', partner_pairs(n_dp, step))]
    ppermute x3, waiting for transfers between devices: 27.1 us -> 35.2 us  [local(): lax.ppermute(own_tokens, 'dp', partner_pairs(n_dp, step))]
    all_to_all x2 -> x3, starting transfers between devices: 8.93 us -> 13.2 us  [local(): incoming = lax.all_to_all(payload, 'ctx', 0, 0, tiled=True)]
  transfers between devices with their start and end apart: 8 -> 9, of which waited for: 5 -> 6; matrix products, arithmetic and copies ran while one was open for 19% -> 20% of each run, Pallas kernels for 11% -> 11%
where the time goes in v4:
time: 311 us; the launch traced here: 310 us
  waiting for transfers between devices  113 us (36%)
  blocking collectives  56.1 us (18%)
  matrix products  34.8 us (11%)
  Pallas kernels  34.5 us (11%)
  local copies, waits for them, and re-layouts  26.9 us (9%)
  other arithmetic  22.5 us (7%)
  starting transfers between devices  21.3 us (7%)
    all_to_all x3, waiting for transfers between devices, local(): incoming = lax.all_to_all(payload, 'ctx', 0, 0, tiled=True)  49.6 us
    all_to_all x1, blocking collectives, local(): incoming = lax.all_to_all(payload, 'ctx', 0, 0, tiled=True)  42.8 us
    ppermute x3, waiting for transfers between devices, local(): lax.ppermute(own_tokens, 'dp', partner_pairs(n_dp, step))  35.2 us
    pallas_call x4, Pallas kernels, attend(): pl.pallas_call(kernel, out_shape=jax.ShapeDtypeStruct(queries.shape, jnp....  34.5 us
    ppermute x3, waiting for transfers between devices, local(): partial_out = lax.ppermute(partial_out, 'dp', partner_pairs(n_dp, step))  28.5 us
    dot_general x4, matrix products, local(): jnp.einsum('td,sdh->sth', clip_inputs[step], qkv_weight, preferred_elemen...  22.8 us
    all_gather x1, blocking collectives, local(): lax.all_gather(table, 'ctx', axis=0, tiled=True).astype(jnp.int32)  13.3 us
    all_to_all x3, starting transfers between devices, local(): incoming = lax.all_to_all(payload, 'ctx', 0, 0, tiled=True)  13.2 us
  transfers between devices with their start and end apart: 9, of which 6 were waited for; matrix products, arithmetic and copies ran while one was open for 20% of the time, Pallas kernels for 11%

profile of v4, /device:TPU:0, one launch (start us, length us, event | category | flops | bytes accessed | tf_op | source)
XLA Modules:
  0.0 309.7 jit_solution(8768203965295503962)
XLA Ops:
  0.0 3.9 %collective-permute-start.4 = (bf16[256,3072]{1,0:T(8,128)(2,1)}, bf16[256,3072]{1,0:T(8,128)(2,1)}, u32[]{:S(2)}, u32[]{:S(2)}) collective-permute-start(bf16[256,3072]{1,0:T(8,128)(2,1)} %bitcast.133), channel_id=1, source_target_pairs={{0,24},{8,16},{16,8},{24,0},{1,25},{9,17},{17,9},{25,1},{2,26},{10... | collective-permute-start | bytes 4718600 | tf_op jit(solution)/shard_map/ppermute | solution.py:135
  6.0 13.3 %all-gather = f32[8,4,11]{2,1,0:T(4,128)S(1)} all-gather(f32[1,4,11]{2,1,0:T(4,128)S(1)} %fusion.42), channel_id=1, replica_groups=mesh['dp'=4,'ctx'=8] {'ctx'}, dimensions={0}, use_global_device_ids=true | all-gather | bytes 1584 | tf_op jit(solution)/shard_map/all_gather | solution.py:109
  20.1 5.7 %fusion.22 = bf16[3,256,384]{2,1,0:T(8,128)(2,1)S(1)} fusion(bf16[3,3072,384]{2,1,0:T(8,128)(2,1)} %param.10, bf16[1,256,3072]{2,1,0:T(8,128)(2,1)} %param.9), kind=kOutput, calls=%fused_computation.33 | convolution fusion | flops 1812234240 | bytes 9240576 | tf_op jit(solution)/shard_map/td,sdh->sth/dot_general | solution.py:138
  28.6 10.9 %collective-permute-done.4 = bf16[256,3072]{1,0:T(8,128)(2,1)} collective-permute-done((bf16[256,3072]{1,0:T(8,128)(2,1)}, bf16[256,3072]{1,0:T(8,128)(2,1)}, u32[]{:S(2)}, u32[]{:S(2)}) %collective-permute-start.4) | collective-permute-done | bytes 1572896 | tf_op jit(solution)/shard_map/ppermute | solution.py:135
  39.5 5.7 %fusion.25 = bf16[3,256,384]{2,1,0:T(8,128)(2,1)S(1)} fusion(bf16[3,3072,384]{2,1,0:T(8,128)(2,1)} %param.10, bf16[256,3072]{1,0:T(8,128)(2,1)} %collective-permute-done.4), kind=kOutput, calls=%fused_computation.34 | convolution fusion | flops 1812234240 | bytes 9240576 | tf_op jit(solution)/shard_map/td,sdh->sth/dot_general | solution.py:138
  48.0 24.3 %collective-permute-done.2 = bf16[256,3072]{1,0:T(8,128)(2,1)} collective-permute-done((bf16[256,3072]{1,0:T(8,128)(2,1)}, bf16[256,3072]{1,0:T(8,128)(2,1)}, u32[]{:S(2)}, u32[]{:S(2)}) %collective-permute-start.2) | collective-permute-done | bytes 1572896 | tf_op jit(solution)/shard_map/ppermute | solution.py:135
  72.3 5.7 %fusion.28 = bf16[3,256,384]{2,1,0:T(8,128)(2,1)S(1)} fusion(bf16[3,3072,384]{2,1,0:T(8,128)(2,1)} %param.10, bf16[256,3072]{1,0:T(8,128)(2,1)} %collective-permute-done.2), kind=kOutput, calls=%fused_computation.35 | convolution fusion | flops 1812234240 | bytes 9240576 | tf_op jit(solution)/shard_map/td,sdh->sth/dot_general | solution.py:138
  80.8 5.7 %fusion.31 = bf16[3,256,384]{2,1,0:T(8,128)(2,1)S(1)} fusion(bf16[3,3072,384]{2,1,0:T(8,128)(2,1)} %param.10, bf16[256,3072]{1,0:T(8,128)(2,1)} %collective-permute-done), kind=kOutput, calls=%fused_computation.36 | convolution fusion | flops 1812234240 | bytes 9240576 | tf_op jit(solution)/shard_map/td,sdh->sth/dot_general | solution.py:138
  90.3 5.3 %bitcast_select_fusion = (bf16[16,2,1,64,384]{4,3,2,1,0:T(8,128)(2,1)}, bf16[16,2,1,64,384]{4,3,2,1,0:T(8,128)(2,1)}, bf16[16,2,1,64,384]{4,3,2,1,0:T(8,128)(2,1)}, bf16[16,2,1,64,384]{4,3,2,1,0:T(8,128)(2,1)S(1)}) fusion(bf16[16,2,64,384]{3,2,1,0:T(8,128)(2,1)} %gather_fusion.5, pred[16]{0:T(512)(128)(4,1)S(1)} %compare_and_fusion, ...), kind=kLoop, calls=%fused_computation.17 | loop fusion | flops 3145728 | bytes 12582928 | tf_op jit(solution)/shard_map/jit(_take)/select_n | solution.py:144
  95.7 42.8 %all_to_all.20 = bf16[16,2,1,64,384]{4,3,2,1,0:T(8,128)(2,1)} all-to-all(bf16[16,2,1,64,384]{4,3,2,1,0:T(8,128)(2,1)S(1)} %get-tuple-element.21), channel_id=1, replica_groups=mesh['dp'=4,'ctx'=8] {'ctx'}, dimensions={0} | all-to-all | bytes 3145728 | tf_op jit(solution)/shard_map/all_to_all | solution.py:151
  138.5 4.4 %all-to-all-start.1 = ((bf16[16,2,1,64,384]{4,3,2,1,0:T(8,128)(2,1)}), bf16[16,2,1,64,384]{4,3,2,1,0:T(8,128)(2,1)}, u32[]{:S(2)}, u32[]{:S(2)}) async-start(bf16[16,2,1,64,384]{4,3,2,1,0:T(8,128)(2,1)} %get-tuple-element.19), calls=%async_computation.1 | async-start | bytes 3145728 | tf_op jit(solution)/shard_map/all_to_all | solution.py:151
  156.1 3.0 pad_maximum_fusion.refs_0_.refs_1_.refs_2_.refs_3_.refs_4_.refs_5_.refs_6_.refs_7_.refs_8_.refs_9_
  159.1 8.6 %shard_map.73 = bf16[1,256,384]{2,1,0:T(8,128)(2,1)} custom-call(s32[4,10]{1,0:T(4,128)} %add_select_fusion.2.pos_ref, s32[4]{0:T(128)} %count_ref.7, f32[4,3,10]{2,1,0:T(4,128)} %fusion.40.bias_ref, bf16[1,256,384]{2,1,0:T(8,128)(2,1)} %slice.52.q_ref, ...), custom_call_target="tpu_custom_call" | custom-call | tf_op jit(solution)/shard_map/pallas_call | solution.py:79
  167.7 13.1 %all-to-all-done.1 = bf16[16,2,1,64,384]{4,3,2,1,0:T(8,128)(2,1)} async-done(((bf16[16,2,1,64,384]{4,3,2,1,0:T(8,128)(2,1)}), bf16[16,2,1,64,384]{4,3,2,1,0:T(8,128)(2,1)}, u32[]{:S(2)}, u32[]{:S(2)}) %all-to-all-start.1) | async-done | bytes 1572896 | tf_op jit(solution)/shard_map/all_to_all | solution.py:151
  180.8 4.5 %all-to-all-start.2 = ((bf16[16,2,1,64,384]{4,3,2,1,0:T(8,128)(2,1)}), bf16[16,2,1,64,384]{4,3,2,1,0:T(8,128)(2,1)}, u32[]{:S(2)}, u32[]{:S(2)}) async-start(bf16[16,2,1,64,384]{4,3,2,1,0:T(8,128)(2,1)} %get-tuple-element.8), calls=%async_computation.2 | async-start | bytes 3145728 | tf_op jit(solution)/shard_map/all_to_all | solution.py:151
  189.8 8.6 %shard_map.74 = bf16[1,256,384]{2,1,0:T(8,128)(2,1)} custom-call(s32[4,10]{1,0:T(4,128)} %add_select_fusion.2.pos_ref, s32[4]{0:T(128)} %count_ref.7, f32[4,3,10]{2,1,0:T(4,128)} %fusion.40.bias_ref, bf16[1,256,384]{2,1,0:T(8,128)(2,1)} %slice.56.q_ref, ...), custom_call_target="tpu_custom_call" | custom-call | tf_op jit(solution)/shard_map/pallas_call | solution.py:79
  198.4 24.5 %all-to-all-done.2 = bf16[16,2,1,64,384]{4,3,2,1,0:T(8,128)(2,1)} async-done(((bf16[16,2,1,64,384]{4,3,2,1,0:T(8,128)(2,1)}), bf16[16,2,1,64,384]{4,3,2,1,0:T(8,128)(2,1)}, u32[]{:S(2)}, u32[]{:S(2)}) %all-to-all-start.2) | async-done | bytes 1572896 | tf_op jit(solution)/shard_map/all_to_all | solution.py:151
  222.9 4.3 %all-to-all-start.3 = ((bf16[16,2,1,64,384]{4,3,2,1,0:T(8,128)(2,1)}), bf16[16,2,1,64,384]{4,3,2,1,0:T(8,128)(2,1)}, u32[]{:S(2)}, u32[]{:S(2)}) async-start(bf16[16,2,1,64,384]{4,3,2,1,0:T(8,128)(2,1)} %get-tuple-element.9), calls=%async_computation.3 | async-start | bytes 3145728 | tf_op jit(solution)/shard_map/all_to_all | solution.py:151
  238.5 8.6 %shard_map.75 = bf16[1,256,384]{2,1,0:T(8,128)(2,1)} custom-call(s32[4,10]{1,0:T(4,128)} %add_select_fusion.2.pos_ref, s32[4]{0:T(128)} %count_ref.7, f32[4,3,10]{2,1,0:T(4,128)} %fusion.40.bias_ref, bf16[1,256,384]{2,1,0:T(8,128)(2,1)} %slice.58.q_ref, ...), custom_call_target="tpu_custom_call" | custom-call | tf_op jit(solution)/shard_map/pallas_call | solution.py:79
  247.1 3.1 %convolution_convert_fusion.1 = bf16[256,3072]{1,0:T(8,128)(2,1)} fusion(bf16[384,3072]{1,0:T(8,128)(2,1)S(1)} %copy-done, bf16[1,256,384]{2,1,0:T(8,128)(2,1)} %shard_map.75), kind=kOutput, calls=%fused_computation.8 | convolution fusion | flops 604766208 | bytes 4128768 | tf_op jit(solution)/shard_map/dot_general | solution.py:155
  253.0 12.0 %all-to-all-done.3 = bf16[16,2,1,64,384]{4,3,2,1,0:T(8,128)(2,1)} async-done(((bf16[16,2,1,64,384]{4,3,2,1,0:T(8,128)(2,1)}), bf16[16,2,1,64,384]{4,3,2,1,0:T(8,128)(2,1)}, u32[]{:S(2)}, u32[]{:S(2)}) %all-to-all-start.3) | async-done | bytes 1572896 | tf_op jit(solution)/shard_map/all_to_all | solution.py:151
  268.0 8.6 %shard_map.76 = bf16[1,256,384]{2,1,0:T(8,128)(2,1)} custom-call(s32[4,10]{1,0:T(4,128)} %add_select_fusion.2.pos_ref, s32[4]{0:T(128)} %count_ref.7, f32[4,3,10]{2,1,0:T(4,128)} %fusion.40.bias_ref, bf16[1,256,384]{2,1,0:T(8,128)(2,1)} %slice.60.q_ref, ...), custom_call_target="tpu_custom_call" | custom-call | tf_op jit(solution)/shard_map/pallas_call | solution.py:79
  276.6 28.5 %collective-permute-done.5 = bf16[256,3072]{1,0:T(8,128)(2,1)} collective-permute-done((bf16[256,3072]{1,0:T(8,128)(2,1)}, bf16[256,3072]{1,0:T(8,128)(2,1)}, u32[]{:S(2)}, u32[]{:S(2)}) %collective-permute-start.5) | collective-permute-done | bytes 1572896 | tf_op jit(solution)/shard_map/ppermute | solution.py:159
  305.1 4.6 %fusion.1 = bf16[1,256,3072]{2,1,0:T(8,128)(2,1)} fusion(bf16[256,3072]{1,0:T(8,128)(2,1)} %collective-permute-done.5, bf16[256,3072]{1,0:T(8,128)(2,1)} %collective-permute-done.3, bf16[256,3072]{1,0:T(8,128)(2,1)} %collective-permute-done.1, bf16[384,3072]{1,0:T(8,128)(2,1)S(1)} %copy-done, bf16[1,256,384]{2,1,0:T(8,128)(2,1)} %shard_map.76), kind=kOutput, calls=%fused_computation.16 | convolution fusion | flops 611057664 | bytes 8847360 | tf_op jit(solution)/shard_map/dot_general | solution.py:155
  (88 shorter events, 49.7 us)
Async XLA Ops:
  0.0 228.8 %copy-start = (bf16[384,3072]{1,0:T(8,128)(2,1)S(1)}, bf16[384,3072]{1,0:T(8,128)(2,1)}, u32[]{:S(2)}) copy-start(bf16[384,3072]{1,0:T(8,128)(2,1)} %param.11) | copy-start | bytes 7077892
  0.0 39.5 %collective-permute-start.4 = (bf16[256,3072]{1,0:T(8,128)(2,1)}, bf16[256,3072]{1,0:T(8,128)(2,1)}, u32[]{:S(2)}, u32[]{:S(2)}) collective-permute-start(bf16[256,3072]{1,0:T(8,128)(2,1)} %bitcast.133), channel_id=1, source_target_pairs={{0,24},{8,16},{16,8},{24,0},{1,25},{9,17},{17,9},{25,1},{2,26},{10... | collective-permute-start | bytes 4718600 | tf_op jit(solution)/shard_map/ppermute | solution.py:135
  3.9 68.4 %collective-permute-start.2 = (bf16[256,3072]{1,0:T(8,128)(2,1)}, bf16[256,3072]{1,0:T(8,128)(2,1)}, u32[]{:S(2)}, u32[]{:S(2)}) collective-permute-start(bf16[256,3072]{1,0:T(8,128)(2,1)} %bitcast.134), channel_id=1, source_target_pairs={{0,16},{8,24},{16,0},{24,8},{1,17},{9,25},{17,1},{25,9},{2,18},{10... | collective-permute-start | bytes 4718600 | tf_op jit(solution)/shard_map/ppermute | solution.py:135
  4.4 76.4 %collective-permute-start = (bf16[256,3072]{1,0:T(8,128)(2,1)}, bf16[256,3072]{1,0:T(8,128)(2,1)}, u32[]{:S(2)}, u32[]{:S(2)}) collective-permute-start(bf16[256,3072]{1,0:T(8,128)(2,1)} %bitcast.135), channel_id=1, source_target_pairs={{0,8},{8,0},{16,24},{24,16},{1,9},{9,1},{17,25},{25,17},{2,10},{10... | collective-permute-start | bytes 4718600 | tf_op jit(solution)/shard_map/ppermute | solution.py:135
  25.8 0.8 copy-start.3
  45.2 0.9 copy-start.4
  78.0 0.9 copy-start.5
  86.5 0.9 copy-start.6
  138.5 4.5 %copy-start.9 = (s32[4,10]{1,0:T(4,128)S(1)}, s32[4,10]{1,0:T(4,128)}, u32[]{:S(2)}) copy-start(s32[4,10]{1,0:T(4,128)} %param.14) | copy-start | bytes 484
  138.5 5.1 %copy-start.7 = (s32[4,10]{1,0:T(4,128)S(1)}, s32[4,10]{1,0:T(4,128)}, u32[]{:S(2)}) copy-start(s32[4,10]{1,0:T(4,128)} %param.12) | copy-start | bytes 484
  138.5 6.5 %copy-start.8 = (s32[4]{0:T(128)S(1)}, s32[4]{0:T(128)}, u32[]{:S(2)}) copy-start(s32[4]{0:T(128)} %count_ref.7) | copy-start | bytes 52
  138.5 42.3 %all-to-all-start.1 = ((bf16[16,2,1,64,384]{4,3,2,1,0:T(8,128)(2,1)}), bf16[16,2,1,64,384]{4,3,2,1,0:T(8,128)(2,1)}, u32[]{:S(2)}, u32[]{:S(2)}) async-start(bf16[16,2,1,64,384]{4,3,2,1,0:T(8,128)(2,1)} %get-tuple-element.19), calls=%async_computation.1 | async-start | bytes 3145728 | tf_op jit(solution)/shard_map/all_to_all | solution.py:151
  180.8 42.1 %all-to-all-start.2 = ((bf16[16,2,1,64,384]{4,3,2,1,0:T(8,128)(2,1)}), bf16[16,2,1,64,384]{4,3,2,1,0:T(8,128)(2,1)}, u32[]{:S(2)}, u32[]{:S(2)}) async-start(bf16[16,2,1,64,384]{4,3,2,1,0:T(8,128)(2,1)} %get-tuple-element.8), calls=%async_computation.2 | async-start | bytes 3145728 | tf_op jit(solution)/shard_map/all_to_all | solution.py:151
  198.4 30.4 %copy-start.2 = (bf16[1,256,384]{2,1,0:T(8,128)(2,1)S(1)}, bf16[1,256,384]{2,1,0:T(8,128)(2,1)}, u32[]{:S(2)}) copy-start(bf16[1,256,384]{2,1,0:T(8,128)(2,1)} %shard_map.74) | copy-start | bytes 589828
  222.9 42.1 %all-to-all-start.3 = ((bf16[16,2,1,64,384]{4,3,2,1,0:T(8,128)(2,1)}), bf16[16,2,1,64,384]{4,3,2,1,0:T(8,128)(2,1)}, u32[]{:S(2)}, u32[]{:S(2)}) async-start(bf16[16,2,1,64,384]{4,3,2,1,0:T(8,128)(2,1)} %get-tuple-element.9), calls=%async_computation.3 | async-start | bytes 3145728 | tf_op jit(solution)/shard_map/all_to_all | solution.py:151
  228.8 3.7 %copy-start.1 = (bf16[1,256,384]{2,1,0:T(8,128)(2,1)S(1)}, bf16[1,256,384]{2,1,0:T(8,128)(2,1)}, u32[]{:S(2)}) copy-start(bf16[1,256,384]{2,1,0:T(8,128)(2,1)} %shard_map.73) | copy-start | bytes 589828
  231.0 45.6 %collective-permute-start.3 = (bf16[256,3072]{1,0:T(8,128)(2,1)}, bf16[256,3072]{1,0:T(8,128)(2,1)}, u32[]{:S(2)}, u32[]{:S(2)}) collective-permute-start(bf16[256,3072]{1,0:T(8,128)(2,1)} %convolution_convert_fusion.2), channel_id=1, source_target_pairs={{0,16},{8,24},{16,0},{24,8},{1,17},{9,25},{17,1},{25,9},{2,18},{10... | collective-permute-start | bytes 4718600 | tf_op jit(solution)/shard_map/ppermute | solution.py:159
  234.8 41.9 %collective-permute-start.1 = (bf16[256,3072]{1,0:T(8,128)(2,1)}, bf16[256,3072]{1,0:T(8,128)(2,1)}, u32[]{:S(2)}, u32[]{:S(2)}) collective-permute-start(bf16[256,3072]{1,0:T(8,128)(2,1)} %convolution_convert_fusion.3), channel_id=1, source_target_pairs={{0,8},{8,0},{16,24},{24,16},{1,9},{9,1},{17,25},{25,17},{2,10},{10... | collective-permute-start | bytes 4718600 | tf_op jit(solution)/shard_map/ppermute | solution.py:159
  250.2 54.9 %collective-permute-start.5 = (bf16[256,3072]{1,0:T(8,128)(2,1)}, bf16[256,3072]{1,0:T(8,128)(2,1)}, u32[]{:S(2)}, u32[]{:S(2)}) collective-permute-start(bf16[256,3072]{1,0:T(8,128)(2,1)} %convolution_convert_fusion.1), channel_id=1, source_target_pairs={{0,24},{8,16},{16,8},{24,0},{1,25},{9,17},{17,9},{25,1},{2,26},{10... | collective-permute-start | bytes 4718600 | tf_op jit(solution)/shard_map/ppermute | solution.py:159

commit v5 on v3

--- a/solution.py
+++ b/solution.py
@@ -129,25 +129,35 @@
     live_counts = counts.astype(jnp.int32)
 
     own_tokens = clip_tokens[0]
-    clip_inputs = [own_tokens] + [
-        lax.ppermute(own_tokens, "dp", partner_pairs(n_dp, step)) for step in range(1, n_dp)
-    ]
+    order = [1, 3, 2, 0] if n_dp == 4 else list(range(1, n_dp)) + [0]
+    arrived = {0: own_tokens}
+    for step in range(1, n_dp):
+        arrived[step] = lax.ppermute(own_tokens, "dp", partner_pairs(n_dp, step))
     total = None
-    for step in range(n_dp):
+    received = []
+    partials = []
+    for index, step in enumerate(order):
+        tokens = arrived[step]
+        if index >= 1:
+            tokens, _ = lax.optimization_barrier((tokens, received[max(index - 2, 0)]))
         projected = jnp.einsum(
-            "td,sdh->sth", clip_inputs[step], qkv_weight, preferred_element_type=jnp.float32
+            "td,sdh->sth", tokens, qkv_weight, preferred_element_type=jnp.float32
         ).astype(jnp.bfloat16)
         queries = projected[0][None]
         by_tile = jnp.transpose(
             projected[1:3].reshape(2, tile_count, TILE, width_here), (1, 0, 2, 3)
         )[:, :, None]
-        outgoing = jnp.take(by_tile, send_picks, axis=0)
-        incoming = lax.all_to_all(outgoing, "ctx", 0, 0, tiled=True)
+        payload = jnp.take(by_tile, send_picks, axis=0)
+        if index >= 2:
+            payload, _ = lax.optimization_barrier((payload, partials[index - 2]))
+        incoming = lax.all_to_all(payload, "ctx", 0, 0, tiled=True)
+        received.append(incoming)
         key_values = jnp.concatenate([by_tile, incoming], axis=0)
         attended = attend(positions, live_counts, bias, queries, key_values, heads_here, head_size)
         partial_out = jnp.dot(
             attended[0], out_weight, preferred_element_type=jnp.float32
         ).astype(jnp.bfloat16)
+        partials.append(partial_out)
         if step > 0:
             partial_out = lax.ppermute(partial_out, "dp", partner_pairs(n_dp, step))
         contribution = partial_out.astype(jnp.float32)

time: 338 us -> 304 us (0.90)
  blocking collectives: 97.1 us -> 12.9 us
  waiting for transfers between devices: 103 us -> 144 us
  starting transfers between devices: 16.9 us -> 28.6 us
  local copies, waits for them, and re-layouts: 25.9 us -> 20.5 us
    all_to_all x2 -> x0, blocking collectives: 83.7 us -> none  [local(): incoming = lax.all_to_all(outgoing, 'ctx', 0, 0, tiled=True)]
    ppermute x3, waiting for transfers between devices: 27.1 us -> 67.1 us  [local(): arrived[step] = lax.ppermute(own_tokens, 'dp', partner_pairs(n_dp, step))]
    all_to_all x2 -> x4, waiting for transfers between devices: 21.4 us -> 37.3 us  [local(): incoming = lax.all_to_all(payload, 'ctx', 0, 0, tiled=True)]
    ppermute x3, waiting for transfers between devices: 54.1 us -> 39.8 us  [local(): partial_out = lax.ppermute(partial_out, 'dp', partner_pairs(n_dp, step))]
    all_to_all x2 -> x4, starting transfers between devices: 8.93 us -> 19.2 us  [local(): incoming = lax.all_to_all(payload, 'ctx', 0, 0, tiled=True)]
    select_n x2 -> x4, other arithmetic: 5.4 us -> 9.62 us  [local(): payload = jnp.take(by_tile, send_picks, axis=0)]
  transfers between devices with their start and end apart: 8 -> 10, of which waited for: 5 -> 7; matrix products, arithmetic and copies ran while one was open for 19% -> 17% of each run, Pallas kernels for 11% -> 12%
where the time goes in v5:
time: 304 us; the launch traced here: 303 us
  waiting for transfers between devices  144 us (47%)
  matrix products  36.6 us (12%)
  Pallas kernels  35.7 us (12%)
  starting transfers between devices  28.6 us (9%)
  other arithmetic  24 us (8%)
  local copies, waits for them, and re-layouts  20.5 us (7%)
  blocking collectives  12.9 us (4%)
    ppermute x3, waiting for transfers between devices, local(): arrived[step] = lax.ppermute(own_tokens, 'dp', partner_pairs(n_dp, step))  67.1 us
    ppermute x3, waiting for transfers between devices, local(): partial_out = lax.ppermute(partial_out, 'dp', partner_pairs(n_dp, step))  39.8 us
    all_to_all x4, waiting for transfers between devices, local(): incoming = lax.all_to_all(payload, 'ctx', 0, 0, tiled=True)  37.3 us
    pallas_call x4, Pallas kernels, attend(): pl.pallas_call(kernel, out_shape=jax.ShapeDtypeStruct(queries.shape, jnp....  35.7 us
    dot_general x4, matrix products, local(): jnp.einsum('td,sdh->sth', tokens, qkv_weight, preferred_element_type=jnp....  22.8 us
    all_to_all x4, starting transfers between devices, local(): incoming = lax.all_to_all(payload, 'ctx', 0, 0, tiled=True)  19.2 us
    dot_general x4, matrix products, local(): jnp.dot(attended[0], out_weight, preferred_element_type=jnp.float32)  13.8 us
    all_gather x1, blocking collectives, local(): lax.all_gather(table, 'ctx', axis=0, tiled=True).astype(jnp.int32)  12.9 us
  transfers between devices with their start and end apart: 10, of which 7 were waited for; matrix products, arithmetic and copies ran while one was open for 17% of the time, Pallas kernels for 12%

profile of v5, /device:TPU:0, one launch (start us, length us, event | category | flops | bytes accessed | tf_op | source)
XLA Modules:
  0.0 302.8 jit_solution(9314143028059266472)
XLA Ops:
  4.4 12.9 %all-gather = f32[8,4,11]{2,1,0:T(4,128)S(1)} all-gather(f32[1,4,11]{2,1,0:T(4,128)S(1)} %fusion.42), channel_id=1, replica_groups=mesh['dp'=4,'ctx'=8] {'ctx'}, dimensions={0}, use_global_device_ids=true | all-gather | bytes 1584 | tf_op jit(solution)/shard_map/all_gather | solution.py:109
  18.1 19.5 %collective-permute-done = bf16[256,3072]{1,0:T(8,128)(2,1)} collective-permute-done((bf16[256,3072]{1,0:T(8,128)(2,1)}, bf16[256,3072]{1,0:T(8,128)(2,1)}, u32[]{:S(2)}, u32[]{:S(2)}) %collective-permute-start) | collective-permute-done | bytes 1572896 | tf_op jit(solution)/shard_map/ppermute | solution.py:135
  37.6 5.7 %fusion.31 = bf16[3,256,384]{2,1,0:T(8,128)(2,1)S(1)} fusion(bf16[3,3072,384]{2,1,0:T(8,128)(2,1)} %param.10, bf16[256,3072]{1,0:T(8,128)(2,1)} %collective-permute-done), kind=kOutput, calls=%fused_computation.36 | convolution fusion | flops 1812234240 | bytes 9240576 | tf_op jit(solution)/shard_map/td,sdh->sth/dot_general | solution.py:143
  48.9 5.3 %all-to-all-start = ((bf16[16,2,1,64,384]{4,3,2,1,0:T(8,128)(2,1)}), bf16[16,2,1,64,384]{4,3,2,1,0:T(8,128)(2,1)}, u32[]{:S(2)}, u32[]{:S(2)}) async-start(bf16[16,2,1,64,384]{4,3,2,1,0:T(8,128)(2,1)} %bitcast_select_fusion.3), calls=%async_computation | async-start | bytes 3145728 | tf_op jit(solution)/shard_map/all_to_all | solution.py:153
  57.2 35.1 %collective-permute-done.2 = bf16[256,3072]{1,0:T(8,128)(2,1)} collective-permute-done((bf16[256,3072]{1,0:T(8,128)(2,1)}, bf16[256,3072]{1,0:T(8,128)(2,1)}, u32[]{:S(2)}, u32[]{:S(2)}) %collective-permute-start.2) | collective-permute-done | bytes 1572896 | tf_op jit(solution)/shard_map/ppermute | solution.py:135
  92.3 5.7 %fusion.28 = bf16[3,256,384]{2,1,0:T(8,128)(2,1)S(1)} fusion(bf16[3,3072,384]{2,1,0:T(8,128)(2,1)} %param.10, bf16[256,3072]{1,0:T(8,128)(2,1)} %collective-permute-done.2), kind=kOutput, calls=%fused_computation.35 | convolution fusion | flops 1812234240 | bytes 9240576 | tf_op jit(solution)/shard_map/td,sdh->sth/dot_general | solution.py:143
  103.5 4.7 %all-to-all-start.1 = ((bf16[16,2,1,64,384]{4,3,2,1,0:T(8,128)(2,1)}), bf16[16,2,1,64,384]{4,3,2,1,0:T(8,128)(2,1)}, u32[]{:S(2)}, u32[]{:S(2)}) async-start(bf16[16,2,1,64,384]{4,3,2,1,0:T(8,128)(2,1)} %bitcast_select_fusion.2), calls=%async_computation.1 | async-start | bytes 3145728 | tf_op jit(solution)/shard_map/all_to_all | solution.py:153
  113.3 12.6 %collective-permute-done.4 = bf16[256,3072]{1,0:T(8,128)(2,1)} collective-permute-done((bf16[256,3072]{1,0:T(8,128)(2,1)}, bf16[256,3072]{1,0:T(8,128)(2,1)}, u32[]{:S(2)}, u32[]{:S(2)}) %collective-permute-start.4) | collective-permute-done | bytes 1572896 | tf_op jit(solution)/shard_map/ppermute | solution.py:135
  125.9 5.7 %fusion.25 = bf16[3,256,384]{2,1,0:T(8,128)(2,1)S(1)} fusion(bf16[3,3072,384]{2,1,0:T(8,128)(2,1)} %param.10, bf16[256,3072]{1,0:T(8,128)(2,1)} %collective-permute-done.4), kind=kOutput, calls=%fused_computation.34 | convolution fusion | flops 1812234240 | bytes 9240576 | tf_op jit(solution)/shard_map/td,sdh->sth/dot_general | solution.py:143
  137.3 8.9 %shard_map.73 = bf16[1,256,384]{2,1,0:T(8,128)(2,1)} custom-call(s32[4,10]{1,0:T(4,128)} %add_select_fusion.2.pos_ref, s32[4]{0:T(128)} %count_ref.7, f32[4,3,10]{2,1,0:T(4,128)} %fusion.40.bias_ref, bf16[1,256,384]{2,1,0:T(8,128)(2,1)} %slice.52.q_ref, ...), custom_call_target="tpu_custom_call" | custom-call | tf_op jit(solution)/shard_map/pallas_call | solution.py:79
  149.3 5.7 %fusion.22 = bf16[3,256,384]{2,1,0:T(8,128)(2,1)S(1)} fusion(bf16[3,3072,384]{2,1,0:T(8,128)(2,1)} %param.10, bf16[256,3072]{1,0:T(8,128)(2,1)} %bitcast.136), kind=kOutput, calls=%fused_computation.33 | convolution fusion | flops 1812234240 | bytes 9240576 | tf_op jit(solution)/shard_map/td,sdh->sth/dot_general | solution.py:143
  157.8 4.0 %bitcast_select_fusion = (bf16[16,2,1,64,384]{4,3,2,1,0:T(8,128)(2,1)}, bf16[16,2,1,64,384]{4,3,2,1,0:T(8,128)(2,1)}) fusion(bf16[16,2,64,384]{3,2,1,0:T(8,128)(2,1)} %gather_fusion.5, pred[16]{0:T(512)(128)(4,1)S(1)} %compare_and_fusion, bf16[16,2,64,384]{3,2,1,0:T(8,128)(2,1)} %gather_fusion.4), kind=kLoop, calls=%fused_computation.17 | loop fusion | flops 1572864 | bytes 6291472 | tf_op jit(solution)/shard_map/jit(_take)/select_n | solution.py:150
  161.8 4.7 %all-to-all-start.2 = ((bf16[16,2,1,64,384]{4,3,2,1,0:T(8,128)(2,1)}), bf16[16,2,1,64,384]{4,3,2,1,0:T(8,128)(2,1)}, u32[]{:S(2)}, u32[]{:S(2)}) async-start(bf16[16,2,1,64,384]{4,3,2,1,0:T(8,128)(2,1)} %get-tuple-element.13), calls=%async_computation.2 | async-start | bytes 3145728 | tf_op jit(solution)/shard_map/all_to_all | solution.py:153
  171.1 8.9 %shard_map.74 = bf16[1,256,384]{2,1,0:T(8,128)(2,1)} custom-call(s32[4,10]{1,0:T(4,128)} %add_select_fusion.2.pos_ref, s32[4]{0:T(128)} %count_ref.7, f32[4,3,10]{2,1,0:T(4,128)} %fusion.40.bias_ref, bf16[1,256,384]{2,1,0:T(8,128)(2,1)} %slice.56.q_ref, ...), custom_call_target="tpu_custom_call" | custom-call | tf_op jit(solution)/shard_map/pallas_call | solution.py:79
  180.0 3.1 %convolution_convert_fusion.2 = bf16[256,3072]{1,0:T(8,128)(2,1)} fusion(bf16[384,3072]{1,0:T(8,128)(2,1)S(1)} %copy-done, bf16[1,256,384]{2,1,0:T(8,128)(2,1)} %shard_map.74), kind=kOutput, calls=%fused_computation.9 | convolution fusion | flops 604766208 | bytes 4128768 | tf_op jit(solution)/shard_map/dot_general | solution.py:157
  183.1 21.4 %all-to-all-done.2 = bf16[16,2,1,64,384]{4,3,2,1,0:T(8,128)(2,1)} async-done(((bf16[16,2,1,64,384]{4,3,2,1,0:T(8,128)(2,1)}), bf16[16,2,1,64,384]{4,3,2,1,0:T(8,128)(2,1)}, u32[]{:S(2)}, u32[]{:S(2)}) %all-to-all-start.2) | async-done | bytes 1572896 | tf_op jit(solution)/shard_map/all_to_all | solution.py:153
  204.5 4.5 %all-to-all-start.3 = ((bf16[16,2,1,64,384]{4,3,2,1,0:T(8,128)(2,1)}), bf16[16,2,1,64,384]{4,3,2,1,0:T(8,128)(2,1)}, u32[]{:S(2)}, u32[]{:S(2)}) async-start(bf16[16,2,1,64,384]{4,3,2,1,0:T(8,128)(2,1)} %get-tuple-element.15), calls=%async_computation.3 | async-start | bytes 3145728 | tf_op jit(solution)/shard_map/all_to_all | solution.py:153
  216.5 8.9 %shard_map.75 = bf16[1,256,384]{2,1,0:T(8,128)(2,1)} custom-call(s32[4,10]{1,0:T(4,128)} %add_select_fusion.2.pos_ref, s32[4]{0:T(128)} %count_ref.7, f32[4,3,10]{2,1,0:T(4,128)} %fusion.40.bias_ref, bf16[1,256,384]{2,1,0:T(8,128)(2,1)} %slice.58.q_ref, ...), custom_call_target="tpu_custom_call" | custom-call | tf_op jit(solution)/shard_map/pallas_call | solution.py:79
  225.4 3.1 %convolution_convert_fusion.1 = bf16[256,3072]{1,0:T(8,128)(2,1)} fusion(bf16[384,3072]{1,0:T(8,128)(2,1)S(1)} %copy-done, bf16[1,256,384]{2,1,0:T(8,128)(2,1)} %shard_map.75), kind=kOutput, calls=%fused_computation.8 | convolution fusion | flops 604766208 | bytes 4128768 | tf_op jit(solution)/shard_map/dot_general | solution.py:157
  230.7 15.9 %all-to-all-done.3 = bf16[16,2,1,64,384]{4,3,2,1,0:T(8,128)(2,1)} async-done(((bf16[16,2,1,64,384]{4,3,2,1,0:T(8,128)(2,1)}), bf16[16,2,1,64,384]{4,3,2,1,0:T(8,128)(2,1)}, u32[]{:S(2)}, u32[]{:S(2)}) %all-to-all-start.3) | async-done | bytes 1572896 | tf_op jit(solution)/shard_map/all_to_all | solution.py:153
  249.5 8.9 %shard_map.76 = bf16[1,256,384]{2,1,0:T(8,128)(2,1)} custom-call(s32[4,10]{1,0:T(4,128)} %add_select_fusion.2.pos_ref, s32[4]{0:T(128)} %count_ref.7, f32[4,3,10]{2,1,0:T(4,128)} %fusion.40.bias_ref, bf16[1,256,384]{2,1,0:T(8,128)(2,1)} %slice.60.q_ref, ...), custom_call_target="tpu_custom_call" | custom-call | tf_op jit(solution)/shard_map/pallas_call | solution.py:79
  258.5 23.7 %collective-permute-done.3 = bf16[256,3072]{1,0:T(8,128)(2,1)} collective-permute-done((bf16[256,3072]{1,0:T(8,128)(2,1)}, bf16[256,3072]{1,0:T(8,128)(2,1)}, u32[]{:S(2)}, u32[]{:S(2)}) %collective-permute-start.3) | collective-permute-done | bytes 1572896 | tf_op jit(solution)/shard_map/ppermute | solution.py:162
  282.2 16.1 %collective-permute-done.5 = bf16[256,3072]{1,0:T(8,128)(2,1)} collective-permute-done((bf16[256,3072]{1,0:T(8,128)(2,1)}, bf16[256,3072]{1,0:T(8,128)(2,1)}, u32[]{:S(2)}, u32[]{:S(2)}) %collective-permute-start.5) | collective-permute-done | bytes 1572896 | tf_op jit(solution)/shard_map/ppermute | solution.py:162
  298.3 4.6 %fusion.1 = bf16[1,256,3072]{2,1,0:T(8,128)(2,1)} fusion(bf16[256,3072]{1,0:T(8,128)(2,1)} %collective-permute-done.5, bf16[256,3072]{1,0:T(8,128)(2,1)} %collective-permute-done.3, bf16[256,3072]{1,0:T(8,128)(2,1)} %collective-permute-done.1, bf16[384,3072]{1,0:T(8,128)(2,1)S(1)} %copy-done, bf16[1,256,384]{2,1,0:T(8,128)(2,1)} %shard_map.76), kind=kOutput, calls=%fused_computation.16 | convolution fusion | flops 611057664 | bytes 8847360 | tf_op jit(solution)/shard_map/dot_general | solution.py:157
  (89 shorter events, 52.9 us)
Async XLA Ops:
  0.0 146.3 %copy-start = (bf16[384,3072]{1,0:T(8,128)(2,1)S(1)}, bf16[384,3072]{1,0:T(8,128)(2,1)}, u32[]{:S(2)}) copy-start(bf16[384,3072]{1,0:T(8,128)(2,1)} %param.11) | copy-start | bytes 7077892
  0.0 37.6 %collective-permute-start = (bf16[256,3072]{1,0:T(8,128)(2,1)}, bf16[256,3072]{1,0:T(8,128)(2,1)}, u32[]{:S(2)}, u32[]{:S(2)}) collective-permute-start(bf16[256,3072]{1,0:T(8,128)(2,1)} %bitcast.133), channel_id=1, source_target_pairs={{0,8},{8,0},{16,24},{24,16},{1,9},{9,1},{17,25},{25,17},{2,10},{10... | collective-permute-start | bytes 4718600 | tf_op jit(solution)/shard_map/ppermute | solution.py:135
  43.3 0.8 copy-start.2
  48.9 8.2 %copy-start.6 = (s32[4]{0:T(128)S(1)}, s32[4]{0:T(128)}, u32[]{:S(2)}) copy-start(s32[4]{0:T(128)} %count_ref.7) | copy-start | bytes 52
  48.9 8.3 %copy-start.5 = (s32[4,10]{1,0:T(4,128)S(1)}, s32[4,10]{1,0:T(4,128)}, u32[]{:S(2)}) copy-start(s32[4,10]{1,0:T(4,128)} %param.12) | copy-start | bytes 484
  48.9 8.3 %copy-start.7 = (s32[4,10]{1,0:T(4,128)S(1)}, s32[4,10]{1,0:T(4,128)}, u32[]{:S(2)}) copy-start(s32[4,10]{1,0:T(4,128)} %param.14) | copy-start | bytes 484
  48.9 43.4 %all-to-all-start = ((bf16[16,2,1,64,384]{4,3,2,1,0:T(8,128)(2,1)}), bf16[16,2,1,64,384]{4,3,2,1,0:T(8,128)(2,1)}, u32[]{:S(2)}, u32[]{:S(2)}) async-start(bf16[16,2,1,64,384]{4,3,2,1,0:T(8,128)(2,1)} %bitcast_select_fusion.3), calls=%async_computation | async-start | bytes 3145728 | tf_op jit(solution)/shard_map/all_to_all | solution.py:153
  54.1 38.1 %collective-permute-start.2 = (bf16[256,3072]{1,0:T(8,128)(2,1)}, bf16[256,3072]{1,0:T(8,128)(2,1)}, u32[]{:S(2)}, u32[]{:S(2)}) collective-permute-start(bf16[256,3072]{1,0:T(8,128)(2,1)} %bitcast.134), channel_id=1, source_target_pairs={{0,24},{8,16},{16,8},{24,0},{1,25},{9,17},{17,9},{25,1},{2,26},{10... | collective-permute-start | bytes 4718600 | tf_op jit(solution)/shard_map/ppermute | solution.py:135
  56.6 69.3 %collective-permute-start.4 = (bf16[256,3072]{1,0:T(8,128)(2,1)}, bf16[256,3072]{1,0:T(8,128)(2,1)}, u32[]{:S(2)}, u32[]{:S(2)}) collective-permute-start(bf16[256,3072]{1,0:T(8,128)(2,1)} %bitcast.135), channel_id=1, source_target_pairs={{0,16},{8,24},{16,0},{24,8},{1,17},{9,25},{17,1},{25,9},{2,18},{10... | collective-permute-start | bytes 4718600 | tf_op jit(solution)/shard_map/ppermute | solution.py:135
  98.0 0.8 copy-start.1
  103.5 45.8 %all-to-all-start.1 = ((bf16[16,2,1,64,384]{4,3,2,1,0:T(8,128)(2,1)}), bf16[16,2,1,64,384]{4,3,2,1,0:T(8,128)(2,1)}, u32[]{:S(2)}, u32[]{:S(2)}) async-start(bf16[16,2,1,64,384]{4,3,2,1,0:T(8,128)(2,1)} %bitcast_select_fusion.2), calls=%async_computation.1 | async-start | bytes 3145728 | tf_op jit(solution)/shard_map/all_to_all | solution.py:153
  108.2 1.3 copy-start.8
  131.6 0.8 copy-start.4
  155.0 0.9 copy-start.3
  161.8 42.7 %all-to-all-start.2 = ((bf16[16,2,1,64,384]{4,3,2,1,0:T(8,128)(2,1)}), bf16[16,2,1,64,384]{4,3,2,1,0:T(8,128)(2,1)}, u32[]{:S(2)}, u32[]{:S(2)}) async-start(bf16[16,2,1,64,384]{4,3,2,1,0:T(8,128)(2,1)} %get-tuple-element.13), calls=%async_computation.2 | async-start | bytes 3145728 | tf_op jit(solution)/shard_map/all_to_all | solution.py:153
  204.5 42.1 %all-to-all-start.3 = ((bf16[16,2,1,64,384]{4,3,2,1,0:T(8,128)(2,1)}), bf16[16,2,1,64,384]{4,3,2,1,0:T(8,128)(2,1)}, u32[]{:S(2)}, u32[]{:S(2)}) async-start(bf16[16,2,1,64,384]{4,3,2,1,0:T(8,128)(2,1)} %get-tuple-element.15), calls=%async_computation.3 | async-start | bytes 3145728 | tf_op jit(solution)/shard_map/all_to_all | solution.py:153
  210.6 47.8 %collective-permute-start.1 = (bf16[256,3072]{1,0:T(8,128)(2,1)}, bf16[256,3072]{1,0:T(8,128)(2,1)}, u32[]{:S(2)}, u32[]{:S(2)}) collective-permute-start(bf16[256,3072]{1,0:T(8,128)(2,1)} %convolution_convert_fusion.3), channel_id=1, source_target_pairs={{0,8},{8,0},{16,24},{24,16},{1,9},{9,1},{17,25},{25,17},{2,10},{10... | collective-permute-start | bytes 4718600 | tf_op jit(solution)/shard_map/ppermute | solution.py:162
  212.1 70.1 %collective-permute-start.3 = (bf16[256,3072]{1,0:T(8,128)(2,1)}, bf16[256,3072]{1,0:T(8,128)(2,1)}, u32[]{:S(2)}, u32[]{:S(2)}) collective-permute-start(bf16[256,3072]{1,0:T(8,128)(2,1)} %convolution_convert_fusion.2), channel_id=1, source_target_pairs={{0,24},{8,16},{16,8},{24,0},{1,25},{9,17},{17,9},{25,1},{2,26},{10... | collective-permute-start | bytes 4718600 | tf_op jit(solution)/shard_map/ppermute | solution.py:162
  228.5 69.7 %collective-permute-start.5 = (bf16[256,3072]{1,0:T(8,128)(2,1)}, bf16[256,3072]{1,0:T(8,128)(2,1)}, u32[]{:S(2)}, u32[]{:S(2)}) collective-permute-start(bf16[256,3072]{1,0:T(8,128)(2,1)} %convolution_convert_fusion.1), channel_id=1, source_target_pairs={{0,16},{8,24},{16,0},{24,8},{1,17},{9,25},{17,1},{25,9},{2,18},{10... | collective-permute-start | bytes 4718600 | tf_op jit(solution)/shard_map/ppermute | solution.py:162

commit v6 on v5

--- a/solution.py
+++ b/solution.py
@@ -136,6 +136,7 @@
     total = None
     received = []
     partials = []
+    sent = []
     for index, step in enumerate(order):
         tokens = arrived[step]
         if index >= 1:
@@ -150,9 +151,13 @@
         payload = jnp.take(by_tile, send_picks, axis=0)
         if index >= 2:
             payload, _ = lax.optimization_barrier((payload, partials[index - 2]))
+        if index == len(order) - 1 and len(sent) >= 2:
+            payload, _ = lax.optimization_barrier((payload, sent[-3]))
         incoming = lax.all_to_all(payload, "ctx", 0, 0, tiled=True)
         received.append(incoming)
         key_values = jnp.concatenate([by_tile, incoming], axis=0)
+        if index == len(order) - 1 and len(sent) >= 2:
+            key_values, _ = lax.optimization_barrier((key_values, sent[-2]))
         attended = attend(positions, live_counts, bias, queries, key_values, heads_here, head_size)
         partial_out = jnp.dot(
             attended[0], out_weight, preferred_element_type=jnp.float32
@@ -160,6 +165,7 @@
         partials.append(partial_out)
         if step > 0:
             partial_out = lax.ppermute(partial_out, "dp", partner_pairs(n_dp, step))
+            sent.append(partial_out)
         contribution = partial_out.astype(jnp.float32)
         total = contribution if total is None else total + contribution
     return total.astype(jnp.bfloat16)[None]

time: 304 us -> 287 us (0.944)
  waiting for transfers between devices: 144 us -> 127 us
    all_to_all x4, waiting for transfers between devices: 37.3 us -> 17.4 us  [local(): incoming = lax.all_to_all(payload, 'ctx', 0, 0, tiled=True)]
  transfers between devices with their start and end apart: 10 -> 10, of which waited for: 7 -> 7; matrix products, arithmetic and copies ran while one was open for 17% -> 18% of each run, Pallas kernels for 12% -> 12%
where the time goes in v6:
time: 287 us; the launch traced here: 286 us
  waiting for transfers between devices  127 us (44%)
  matrix products  36.7 us (13%)
  Pallas kernels  35.2 us (12%)
  starting transfers between devices  29.5 us (10%)
  other arithmetic  23.9 us (8%)
  local copies, waits for them, and re-layouts  20.3 us (7%)
  blocking collectives  12.9 us (4%)
    ppermute x3, waiting for transfers between devices, local(): arrived[step] = lax.ppermute(own_tokens, 'dp', partner_pairs(n_dp, step))  67.2 us
    ppermute x3, waiting for transfers between devices, local(): partial_out = lax.ppermute(partial_out, 'dp', partner_pairs(n_dp, step))  42.8 us
    pallas_call x4, Pallas kernels, attend(): pl.pallas_call(kernel, out_shape=jax.ShapeDtypeStruct(queries.shape, jnp....  35.2 us
    dot_general x4, matrix products, local(): jnp.einsum('td,sdh->sth', tokens, qkv_weight, preferred_element_type=jnp....  22.8 us
    all_to_all x4, starting transfers between devices, local(): incoming = lax.all_to_all(payload, 'ctx', 0, 0, tiled=True)  19.1 us
    all_to_all x4, waiting for transfers between devices, local(): incoming = lax.all_to_all(payload, 'ctx', 0, 0, tiled=True)  17.4 us
    dot_general x4, matrix products, local(): jnp.dot(attended[0], out_weight, preferred_element_type=jnp.float32)  13.9 us
    all_gather x1, blocking collectives, local(): lax.all_gather(table, 'ctx', axis=0, tiled=True).astype(jnp.int32)  12.9 us
  transfers between devices with their start and end apart: 10, of which 7 were waited for; matrix products, arithmetic and copies ran while one was open for 18% of the time, Pallas kernels for 12%

profile of v6, /device:TPU:0, one launch (start us, length us, event | category | flops | bytes accessed | tf_op | source)
XLA Modules:
  0.0 286.2 jit_solution(18234055497590277679)
XLA Ops:
  4.4 12.9 %all-gather = f32[8,4,11]{2,1,0:T(4,128)S(1)} all-gather(f32[1,4,11]{2,1,0:T(4,128)S(1)} %fusion.42), channel_id=1, replica_groups=mesh['dp'=4,'ctx'=8] {'ctx'}, dimensions={0}, use_global_device_ids=true | all-gather | bytes 1584 | tf_op jit(solution)/shard_map/all_gather | solution.py:109
  18.1 19.5 %collective-permute-done = bf16[256,3072]{1,0:T(8,128)(2,1)} collective-permute-done((bf16[256,3072]{1,0:T(8,128)(2,1)}, bf16[256,3072]{1,0:T(8,128)(2,1)}, u32[]{:S(2)}, u32[]{:S(2)}) %collective-permute-start) | collective-permute-done | bytes 1572896 | tf_op jit(solution)/shard_map/ppermute | solution.py:135
  37.6 5.7 %fusion.31 = bf16[3,256,384]{2,1,0:T(8,128)(2,1)S(1)} fusion(bf16[3,3072,384]{2,1,0:T(8,128)(2,1)} %param.10, bf16[256,3072]{1,0:T(8,128)(2,1)} %collective-permute-done), kind=kOutput, calls=%fused_computation.36 | convolution fusion | flops 1812234240 | bytes 9240576 | tf_op jit(solution)/shard_map/td,sdh->sth/dot_general | solution.py:144
  48.9 5.3 %all-to-all-start = ((bf16[16,2,1,64,384]{4,3,2,1,0:T(8,128)(2,1)}), bf16[16,2,1,64,384]{4,3,2,1,0:T(8,128)(2,1)}, u32[]{:S(2)}, u32[]{:S(2)}) async-start(bf16[16,2,1,64,384]{4,3,2,1,0:T(8,128)(2,1)} %bitcast_select_fusion.3), calls=%async_computation | async-start | bytes 3145728 | tf_op jit(solution)/shard_map/all_to_all | solution.py:156
  57.2 35.1 %collective-permute-done.2 = bf16[256,3072]{1,0:T(8,128)(2,1)} collective-permute-done((bf16[256,3072]{1,0:T(8,128)(2,1)}, bf16[256,3072]{1,0:T(8,128)(2,1)}, u32[]{:S(2)}, u32[]{:S(2)}) %collective-permute-start.2) | collective-permute-done | bytes 1572896 | tf_op jit(solution)/shard_map/ppermute | solution.py:135
  92.3 5.7 %fusion.28 = bf16[3,256,384]{2,1,0:T(8,128)(2,1)S(1)} fusion(bf16[3,3072,384]{2,1,0:T(8,128)(2,1)} %param.10, bf16[256,3072]{1,0:T(8,128)(2,1)} %collective-permute-done.2), kind=kOutput, calls=%fused_computation.35 | convolution fusion | flops 1812234240 | bytes 9240576 | tf_op jit(solution)/shard_map/td,sdh->sth/dot_general | solution.py:144
  103.5 4.7 %all-to-all-start.1 = ((bf16[16,2,1,64,384]{4,3,2,1,0:T(8,128)(2,1)}), bf16[16,2,1,64,384]{4,3,2,1,0:T(8,128)(2,1)}, u32[]{:S(2)}, u32[]{:S(2)}) async-start(bf16[16,2,1,64,384]{4,3,2,1,0:T(8,128)(2,1)} %bitcast_select_fusion.2), calls=%async_computation.1 | async-start | bytes 3145728 | tf_op jit(solution)/shard_map/all_to_all | solution.py:156
  113.2 12.6 %collective-permute-done.4 = bf16[256,3072]{1,0:T(8,128)(2,1)} collective-permute-done((bf16[256,3072]{1,0:T(8,128)(2,1)}, bf16[256,3072]{1,0:T(8,128)(2,1)}, u32[]{:S(2)}, u32[]{:S(2)}) %collective-permute-start.4) | collective-permute-done | bytes 1572896 | tf_op jit(solution)/shard_map/ppermute | solution.py:135
  125.9 5.7 %fusion.25 = bf16[3,256,384]{2,1,0:T(8,128)(2,1)S(1)} fusion(bf16[3,3072,384]{2,1,0:T(8,128)(2,1)} %param.10, bf16[256,3072]{1,0:T(8,128)(2,1)} %collective-permute-done.4), kind=kOutput, calls=%fused_computation.34 | convolution fusion | flops 1812234240 | bytes 9240576 | tf_op jit(solution)/shard_map/td,sdh->sth/dot_general | solution.py:144
  137.2 8.8 %shard_map.73 = bf16[1,256,384]{2,1,0:T(8,128)(2,1)} custom-call(s32[4,10]{1,0:T(4,128)} %add_select_fusion.2.pos_ref, s32[4]{0:T(128)} %count_ref.7, f32[4,3,10]{2,1,0:T(4,128)} %fusion.40.bias_ref, bf16[1,256,384]{2,1,0:T(8,128)(2,1)} %slice.52.q_ref, ...), custom_call_target="tpu_custom_call" | custom-call | tf_op jit(solution)/shard_map/pallas_call | solution.py:79
  146.0 3.1 %convolution_convert_fusion.3 = bf16[256,3072]{1,0:T(8,128)(2,1)} fusion(bf16[384,3072]{1,0:T(8,128)(2,1)S(1)} %copy-done, bf16[1,256,384]{2,1,0:T(8,128)(2,1)} %shard_map.73), kind=kOutput, calls=%fused_computation.10 | convolution fusion | flops 604766208 | bytes 4128768 | tf_op jit(solution)/shard_map/dot_general | solution.py:162
  149.2 5.7 %fusion.22 = bf16[3,256,384]{2,1,0:T(8,128)(2,1)S(1)} fusion(bf16[3,3072,384]{2,1,0:T(8,128)(2,1)} %param.10, bf16[256,3072]{1,0:T(8,128)(2,1)} %bitcast.136), kind=kOutput, calls=%fused_computation.33 | convolution fusion | flops 1812234240 | bytes 9240576 | tf_op jit(solution)/shard_map/td,sdh->sth/dot_general | solution.py:144
  157.6 4.0 %bitcast_select_fusion = (bf16[16,2,1,64,384]{4,3,2,1,0:T(8,128)(2,1)}, bf16[16,2,1,64,384]{4,3,2,1,0:T(8,128)(2,1)}) fusion(bf16[16,2,64,384]{3,2,1,0:T(8,128)(2,1)} %gather_fusion.5, pred[16]{0:T(512)(128)(4,1)S(1)} %compare_and_fusion, bf16[16,2,64,384]{3,2,1,0:T(8,128)(2,1)} %gather_fusion.4), kind=kLoop, calls=%fused_computation.17 | loop fusion | flops 1572864 | bytes 6291472 | tf_op jit(solution)/shard_map/jit(_take)/select_n | solution.py:151
  161.5 4.6 %all-to-all-start.2 = ((bf16[16,2,1,64,384]{4,3,2,1,0:T(8,128)(2,1)}), bf16[16,2,1,64,384]{4,3,2,1,0:T(8,128)(2,1)}, u32[]{:S(2)}, u32[]{:S(2)}) async-start(bf16[16,2,1,64,384]{4,3,2,1,0:T(8,128)(2,1)} %get-tuple-element.15), calls=%async_computation.2 | async-start | bytes 3145728 | tf_op jit(solution)/shard_map/all_to_all | solution.py:156
  172.2 8.8 %shard_map.74 = bf16[1,256,384]{2,1,0:T(8,128)(2,1)} custom-call(s32[4,10]{1,0:T(4,128)} %add_select_fusion.2.pos_ref, s32[4]{0:T(128)} %count_ref.7, f32[4,3,10]{2,1,0:T(4,128)} %fusion.40.bias_ref, bf16[1,256,384]{2,1,0:T(8,128)(2,1)} %slice.56.q_ref, ...), custom_call_target="tpu_custom_call" | custom-call | tf_op jit(solution)/shard_map/pallas_call | solution.py:79
  181.0 3.1 %convolution_convert_fusion.2 = bf16[256,3072]{1,0:T(8,128)(2,1)} fusion(bf16[384,3072]{1,0:T(8,128)(2,1)S(1)} %copy-done, bf16[1,256,384]{2,1,0:T(8,128)(2,1)} %shard_map.74), kind=kOutput, calls=%fused_computation.9 | convolution fusion | flops 604766208 | bytes 4128768 | tf_op jit(solution)/shard_map/dot_general | solution.py:162
  184.1 19.1 %collective-permute-done.1 = bf16[256,3072]{1,0:T(8,128)(2,1)} collective-permute-done((bf16[256,3072]{1,0:T(8,128)(2,1)}, bf16[256,3072]{1,0:T(8,128)(2,1)}, u32[]{:S(2)}, u32[]{:S(2)}) %collective-permute-start.1) | collective-permute-done | bytes 1572896 | tf_op jit(solution)/shard_map/ppermute | solution.py:167
  204.1 4.5 %all-to-all-start.3 = ((bf16[16,2,1,64,384]{4,3,2,1,0:T(8,128)(2,1)}), bf16[16,2,1,64,384]{4,3,2,1,0:T(8,128)(2,1)}, u32[]{:S(2)}, u32[]{:S(2)}) async-start(bf16[16,2,1,64,384]{4,3,2,1,0:T(8,128)(2,1)} %get-tuple-element.18), calls=%async_computation.3 | async-start | bytes 3145728 | tf_op jit(solution)/shard_map/all_to_all | solution.py:156
  214.6 8.8 %shard_map.75 = bf16[1,256,384]{2,1,0:T(8,128)(2,1)} custom-call(s32[4,10]{1,0:T(4,128)} %add_select_fusion.2.pos_ref, s32[4]{0:T(128)} %count_ref.7, f32[4,3,10]{2,1,0:T(4,128)} %fusion.40.bias_ref, bf16[1,256,384]{2,1,0:T(8,128)(2,1)} %slice.58.q_ref, ...), custom_call_target="tpu_custom_call" | custom-call | tf_op jit(solution)/shard_map/pallas_call | solution.py:79
  223.3 3.1 %convolution_convert_fusion.1 = bf16[256,3072]{1,0:T(8,128)(2,1)} fusion(bf16[384,3072]{1,0:T(8,128)(2,1)S(1)} %copy-done, bf16[1,256,384]{2,1,0:T(8,128)(2,1)} %shard_map.75), kind=kOutput, calls=%fused_computation.8 | convolution fusion | flops 604766208 | bytes 4128768 | tf_op jit(solution)/shard_map/dot_general | solution.py:162
  229.6 16.6 %all-to-all-done.3 = bf16[16,2,1,64,384]{4,3,2,1,0:T(8,128)(2,1)} async-done(((bf16[16,2,1,64,384]{4,3,2,1,0:T(8,128)(2,1)}), bf16[16,2,1,64,384]{4,3,2,1,0:T(8,128)(2,1)}, u32[]{:S(2)}, u32[]{:S(2)}) %all-to-all-start.3) | async-done | bytes 1572896 | tf_op jit(solution)/shard_map/all_to_all | solution.py:156
  249.1 8.8 %shard_map.76 = bf16[1,256,384]{2,1,0:T(8,128)(2,1)} custom-call(s32[4,10]{1,0:T(4,128)} %add_select_fusion.2.pos_ref, s32[4]{0:T(128)} %count_ref.7, f32[4,3,10]{2,1,0:T(4,128)} %fusion.40.bias_ref, bf16[1,256,384]{2,1,0:T(8,128)(2,1)} %slice.60.q_ref, ...), custom_call_target="tpu_custom_call" | custom-call | tf_op jit(solution)/shard_map/pallas_call | solution.py:79
  257.9 23.7 %collective-permute-done.5 = bf16[256,3072]{1,0:T(8,128)(2,1)} collective-permute-done((bf16[256,3072]{1,0:T(8,128)(2,1)}, bf16[256,3072]{1,0:T(8,128)(2,1)}, u32[]{:S(2)}, u32[]{:S(2)}) %collective-permute-start.5) | collective-permute-done | bytes 1572896 | tf_op jit(solution)/shard_map/ppermute | solution.py:167
  281.6 4.6 %fusion.1 = bf16[1,256,3072]{2,1,0:T(8,128)(2,1)} fusion(bf16[256,3072]{1,0:T(8,128)(2,1)} %collective-permute-done.5, bf16[256,3072]{1,0:T(8,128)(2,1)} %collective-permute-done.3, bf16[256,3072]{1,0:T(8,128)(2,1)} %collective-permute-done.1, bf16[384,3072]{1,0:T(8,128)(2,1)S(1)} %copy-done, bf16[1,256,384]{2,1,0:T(8,128)(2,1)} %shard_map.76), kind=kOutput, calls=%fused_computation.16 | convolution fusion | flops 611057664 | bytes 8847360 | tf_op jit(solution)/shard_map/dot_general | solution.py:162
  (89 shorter events, 51.5 us)
Async XLA Ops:
  0.0 146.0 %copy-start = (bf16[384,3072]{1,0:T(8,128)(2,1)S(1)}, bf16[384,3072]{1,0:T(8,128)(2,1)}, u32[]{:S(2)}) copy-start(bf16[384,3072]{1,0:T(8,128)(2,1)} %param.11) | copy-start | bytes 7077892
  0.0 37.6 %collective-permute-start = (bf16[256,3072]{1,0:T(8,128)(2,1)}, bf16[256,3072]{1,0:T(8,128)(2,1)}, u32[]{:S(2)}, u32[]{:S(2)}) collective-permute-start(bf16[256,3072]{1,0:T(8,128)(2,1)} %bitcast.133), channel_id=1, source_target_pairs={{0,8},{8,0},{16,24},{24,16},{1,9},{9,1},{17,25},{25,17},{2,10},{10... | collective-permute-start | bytes 4718600 | tf_op jit(solution)/shard_map/ppermute | solution.py:135
  43.3 0.8 copy-start.2
  48.9 8.2 %copy-start.6 = (s32[4]{0:T(128)S(1)}, s32[4]{0:T(128)}, u32[]{:S(2)}) copy-start(s32[4]{0:T(128)} %count_ref.7) | copy-start | bytes 52
  48.9 8.3 %copy-start.5 = (s32[4,10]{1,0:T(4,128)S(1)}, s32[4,10]{1,0:T(4,128)}, u32[]{:S(2)}) copy-start(s32[4,10]{1,0:T(4,128)} %param.12) | copy-start | bytes 484
  48.9 8.3 %copy-start.7 = (s32[4,10]{1,0:T(4,128)S(1)}, s32[4,10]{1,0:T(4,128)}, u32[]{:S(2)}) copy-start(s32[4,10]{1,0:T(4,128)} %param.14) | copy-start | bytes 484
  48.9 43.4 %all-to-all-start = ((bf16[16,2,1,64,384]{4,3,2,1,0:T(8,128)(2,1)}), bf16[16,2,1,64,384]{4,3,2,1,0:T(8,128)(2,1)}, u32[]{:S(2)}, u32[]{:S(2)}) async-start(bf16[16,2,1,64,384]{4,3,2,1,0:T(8,128)(2,1)} %bitcast_select_fusion.3), calls=%async_computation | async-start | bytes 3145728 | tf_op jit(solution)/shard_map/all_to_all | solution.py:156
  54.1 38.1 %collective-permute-start.2 = (bf16[256,3072]{1,0:T(8,128)(2,1)}, bf16[256,3072]{1,0:T(8,128)(2,1)}, u32[]{:S(2)}, u32[]{:S(2)}) collective-permute-start(bf16[256,3072]{1,0:T(8,128)(2,1)} %bitcast.134), channel_id=1, source_target_pairs={{0,24},{8,16},{16,8},{24,0},{1,25},{9,17},{17,9},{25,1},{2,26},{10... | collective-permute-start | bytes 4718600 | tf_op jit(solution)/shard_map/ppermute | solution.py:135
  56.6 69.3 %collective-permute-start.4 = (bf16[256,3072]{1,0:T(8,128)(2,1)}, bf16[256,3072]{1,0:T(8,128)(2,1)}, u32[]{:S(2)}, u32[]{:S(2)}) collective-permute-start(bf16[256,3072]{1,0:T(8,128)(2,1)} %bitcast.135), channel_id=1, source_target_pairs={{0,16},{8,24},{16,0},{24,8},{1,17},{9,25},{17,1},{25,9},{2,18},{10... | collective-permute-start | bytes 4718600 | tf_op jit(solution)/shard_map/ppermute | solution.py:135
  98.0 0.8 copy-start.1
  103.5 45.7 %all-to-all-start.1 = ((bf16[16,2,1,64,384]{4,3,2,1,0:T(8,128)(2,1)}), bf16[16,2,1,64,384]{4,3,2,1,0:T(8,128)(2,1)}, u32[]{:S(2)}, u32[]{:S(2)}) async-start(bf16[16,2,1,64,384]{4,3,2,1,0:T(8,128)(2,1)} %bitcast_select_fusion.2), calls=%async_computation.1 | async-start | bytes 3145728 | tf_op jit(solution)/shard_map/all_to_all | solution.py:156
  108.2 1.3 copy-start.8
  131.6 0.8 copy-start.3
  154.9 0.8 copy-start.4
  161.5 42.5 %all-to-all-start.2 = ((bf16[16,2,1,64,384]{4,3,2,1,0:T(8,128)(2,1)}), bf16[16,2,1,64,384]{4,3,2,1,0:T(8,128)(2,1)}, u32[]{:S(2)}, u32[]{:S(2)}) async-start(bf16[16,2,1,64,384]{4,3,2,1,0:T(8,128)(2,1)} %get-tuple-element.15), calls=%async_computation.2 | async-start | bytes 3145728 | tf_op jit(solution)/shard_map/all_to_all | solution.py:156
  166.1 37.1 %collective-permute-start.1 = (bf16[256,3072]{1,0:T(8,128)(2,1)}, bf16[256,3072]{1,0:T(8,128)(2,1)}, u32[]{:S(2)}, u32[]{:S(2)}) collective-permute-start(bf16[256,3072]{1,0:T(8,128)(2,1)} %convolution_convert_fusion.3), channel_id=1, source_target_pairs={{0,8},{8,0},{16,24},{24,16},{1,9},{9,1},{17,25},{25,17},{2,10},{10... | collective-permute-start | bytes 4718600 | tf_op jit(solution)/shard_map/ppermute | solution.py:167
  204.1 42.1 %all-to-all-start.3 = ((bf16[16,2,1,64,384]{4,3,2,1,0:T(8,128)(2,1)}), bf16[16,2,1,64,384]{4,3,2,1,0:T(8,128)(2,1)}, u32[]{:S(2)}, u32[]{:S(2)}) async-start(bf16[16,2,1,64,384]{4,3,2,1,0:T(8,128)(2,1)} %get-tuple-element.18), calls=%async_computation.3 | async-start | bytes 3145728 | tf_op jit(solution)/shard_map/all_to_all | solution.py:156
  210.2 38.9 %collective-permute-start.3 = (bf16[256,3072]{1,0:T(8,128)(2,1)}, bf16[256,3072]{1,0:T(8,128)(2,1)}, u32[]{:S(2)}, u32[]{:S(2)}) collective-permute-start(bf16[256,3072]{1,0:T(8,128)(2,1)} %convolution_convert_fusion.2), channel_id=1, source_target_pairs={{0,24},{8,16},{16,8},{24,0},{1,25},{9,17},{17,9},{25,1},{2,26},{10... | collective-permute-start | bytes 4718600 | tf_op jit(solution)/shard_map/ppermute | solution.py:167
  226.4 55.2 %collective-permute-start.5 = (bf16[256,3072]{1,0:T(8,128)(2,1)}, bf16[256,3072]{1,0:T(8,128)(2,1)}, u32[]{:S(2)}, u32[]{:S(2)}) collective-permute-start(bf16[256,3072]{1,0:T(8,128)(2,1)} %convolution_convert_fusion.1), channel_id=1, source_target_pairs={{0,16},{8,24},{16,0},{24,8},{1,17},{9,25},{17,1},{25,9},{2,18},{10... | collective-permute-start | bytes 4718600 | tf_op jit(solution)/shard_map/ppermute | solution.py:167

commit v7 on v6

--- a/solution.py
+++ b/solution.py
@@ -129,7 +129,7 @@
     live_counts = counts.astype(jnp.int32)
 
     own_tokens = clip_tokens[0]
-    order = [1, 3, 2, 0] if n_dp == 4 else list(range(1, n_dp)) + [0]
+    order = [3, 1, 2, 0] if n_dp == 4 else list(range(1, n_dp)) + [0]
     arrived = {0: own_tokens}
     for step in range(1, n_dp):
         arrived[step] = lax.ppermute(own_tokens, "dp", partner_pairs(n_dp, step))

time: 287 us -> 266 us (0.927)
  waiting for transfers between devices: 127 us -> 104 us
    ppermute x3, waiting for transfers between devices: 42.8 us -> 23.7 us  [local(): partial_out = lax.ppermute(partial_out, 'dp', partner_pairs(n_dp, step))]
    ppermute x3, waiting for transfers between devices: 67.2 us -> 53.5 us  [local(): arrived[step] = lax.ppermute(own_tokens, 'dp', partner_pairs(n_dp, step))]
    all_to_all x4, waiting for transfers between devices: 17.4 us -> 26.9 us  [local(): incoming = lax.all_to_all(payload, 'ctx', 0, 0, tiled=True)]
  transfers between devices with their start and end apart: 10 -> 10, of which waited for: 7 -> 7; matrix products, arithmetic and copies ran while one was open for 18% -> 19% of each run, Pallas kernels for 12% -> 13%
where the time goes in v7:
time: 266 us; the launch traced here: 265 us
  waiting for transfers between devices  104 us (39%)
  matrix products  36.7 us (14%)
  Pallas kernels  35.4 us (13%)
  starting transfers between devices  31.2 us (12%)
  other arithmetic  23.9 us (9%)
  local copies, waits for them, and re-layouts  20.3 us (8%)
  blocking collectives  12.9 us (5%)
    ppermute x3, waiting for transfers between devices, local(): arrived[step] = lax.ppermute(own_tokens, 'dp', partner_pairs(n_dp, step))  53.5 us
    pallas_call x4, Pallas kernels, attend(): pl.pallas_call(kernel, out_shape=jax.ShapeDtypeStruct(queries.shape, jnp....  35.4 us
    all_to_all x4, waiting for transfers between devices, local(): incoming = lax.all_to_all(payload, 'ctx', 0, 0, tiled=True)  26.9 us
    ppermute x3, waiting for transfers between devices, local(): partial_out = lax.ppermute(partial_out, 'dp', partner_pairs(n_dp, step))  23.7 us
    dot_general x4, matrix products, local(): jnp.einsum('td,sdh->sth', tokens, qkv_weight, preferred_element_type=jnp....  22.8 us
    all_to_all x4, starting transfers between devices, local(): incoming = lax.all_to_all(payload, 'ctx', 0, 0, tiled=True)  18.8 us
    dot_general x4, matrix products, local(): jnp.dot(attended[0], out_weight, preferred_element_type=jnp.float32)  13.9 us
    all_gather x1, blocking collectives, local(): lax.all_gather(table, 'ctx', axis=0, tiled=True).astype(jnp.int32)  12.9 us
  transfers between devices with their start and end apart: 10, of which 7 were waited for; matrix products, arithmetic and copies ran while one was open for 19% of the time, Pallas kernels for 13%

profile of v7, /device:TPU:0, one launch (start us, length us, event | category | flops | bytes accessed | tf_op | source)
XLA Modules:
  0.0 264.8 jit_solution(16048967044081814591)
XLA Ops:
  0.0 3.9 %collective-permute-start = (bf16[256,3072]{1,0:T(8,128)(2,1)}, bf16[256,3072]{1,0:T(8,128)(2,1)}, u32[]{:S(2)}, u32[]{:S(2)}) collective-permute-start(bf16[256,3072]{1,0:T(8,128)(2,1)} %bitcast.133), channel_id=1, source_target_pairs={{0,24},{8,16},{16,8},{24,0},{1,25},{9,17},{17,9},{25,1},{2,26},{10... | collective-permute-start | bytes 4718600 | tf_op jit(solution)/shard_map/ppermute | solution.py:135
  5.4 12.9 %all-gather = f32[8,4,11]{2,1,0:T(4,128)S(1)} all-gather(f32[1,4,11]{2,1,0:T(4,128)S(1)} %fusion.42), channel_id=1, replica_groups=mesh['dp'=4,'ctx'=8] {'ctx'}, dimensions={0}, use_global_device_ids=true | all-gather | bytes 1584 | tf_op jit(solution)/shard_map/all_gather | solution.py:109
  19.1 19.5 %collective-permute-done = bf16[256,3072]{1,0:T(8,128)(2,1)} collective-permute-done((bf16[256,3072]{1,0:T(8,128)(2,1)}, bf16[256,3072]{1,0:T(8,128)(2,1)}, u32[]{:S(2)}, u32[]{:S(2)}) %collective-permute-start) | collective-permute-done | bytes 1572896 | tf_op jit(solution)/shard_map/ppermute | solution.py:135
  38.6 5.7 %fusion.31 = bf16[3,256,384]{2,1,0:T(8,128)(2,1)S(1)} fusion(bf16[3,3072,384]{2,1,0:T(8,128)(2,1)} %param.10, bf16[256,3072]{1,0:T(8,128)(2,1)} %collective-permute-done), kind=kOutput, calls=%fused_computation.36 | convolution fusion | flops 1812234240 | bytes 9240576 | tf_op jit(solution)/shard_map/td,sdh->sth/dot_general | solution.py:144
  49.8 5.2 %all-to-all-start = ((bf16[16,2,1,64,384]{4,3,2,1,0:T(8,128)(2,1)}), bf16[16,2,1,64,384]{4,3,2,1,0:T(8,128)(2,1)}, u32[]{:S(2)}, u32[]{:S(2)}) async-start(bf16[16,2,1,64,384]{4,3,2,1,0:T(8,128)(2,1)} %bitcast_select_fusion.3), calls=%async_computation | async-start | bytes 3145728 | tf_op jit(solution)/shard_map/all_to_all | solution.py:156
  58.2 34.0 %collective-permute-done.2 = bf16[256,3072]{1,0:T(8,128)(2,1)} collective-permute-done((bf16[256,3072]{1,0:T(8,128)(2,1)}, bf16[256,3072]{1,0:T(8,128)(2,1)}, u32[]{:S(2)}, u32[]{:S(2)}) %collective-permute-start.2) | collective-permute-done | bytes 1572896 | tf_op jit(solution)/shard_map/ppermute | solution.py:135
  93.0 5.7 %fusion.28 = bf16[3,256,384]{2,1,0:T(8,128)(2,1)S(1)} fusion(bf16[3,3072,384]{2,1,0:T(8,128)(2,1)} %param.10, bf16[256,3072]{1,0:T(8,128)(2,1)} %collective-permute-done.2), kind=kOutput, calls=%fused_computation.35 | convolution fusion | flops 1812234240 | bytes 9240576 | tf_op jit(solution)/shard_map/td,sdh->sth/dot_general | solution.py:144
  104.2 4.5 %all-to-all-start.1 = ((bf16[16,2,1,64,384]{4,3,2,1,0:T(8,128)(2,1)}), bf16[16,2,1,64,384]{4,3,2,1,0:T(8,128)(2,1)}, u32[]{:S(2)}, u32[]{:S(2)}) async-start(bf16[16,2,1,64,384]{4,3,2,1,0:T(8,128)(2,1)} %bitcast_select_fusion.2), calls=%async_computation.1 | async-start | bytes 3145728 | tf_op jit(solution)/shard_map/all_to_all | solution.py:156
  113.7 5.7 %fusion.25 = bf16[3,256,384]{2,1,0:T(8,128)(2,1)S(1)} fusion(bf16[3,3072,384]{2,1,0:T(8,128)(2,1)} %param.10, bf16[256,3072]{1,0:T(8,128)(2,1)} %collective-permute-done.4), kind=kOutput, calls=%fused_computation.34 | convolution fusion | flops 1812234240 | bytes 9240576 | tf_op jit(solution)/shard_map/td,sdh->sth/dot_general | solution.py:144
  125.1 8.8 %shard_map.73 = bf16[1,256,384]{2,1,0:T(8,128)(2,1)} custom-call(s32[4,10]{1,0:T(4,128)} %add_select_fusion.2.pos_ref, s32[4]{0:T(128)} %count_ref.7, f32[4,3,10]{2,1,0:T(4,128)} %fusion.40.bias_ref, bf16[1,256,384]{2,1,0:T(8,128)(2,1)} %slice.52.q_ref, ...), custom_call_target="tpu_custom_call" | custom-call | tf_op jit(solution)/shard_map/pallas_call | solution.py:79
  133.9 3.1 %convolution_convert_fusion.3 = bf16[256,3072]{1,0:T(8,128)(2,1)} fusion(bf16[384,3072]{1,0:T(8,128)(2,1)S(1)} %copy-done, bf16[1,256,384]{2,1,0:T(8,128)(2,1)} %shard_map.73), kind=kOutput, calls=%fused_computation.10 | convolution fusion | flops 604766208 | bytes 4128768 | tf_op jit(solution)/shard_map/dot_general | solution.py:162
  137.1 9.3 %all-to-all-done.1 = bf16[16,2,1,64,384]{4,3,2,1,0:T(8,128)(2,1)} async-done(((bf16[16,2,1,64,384]{4,3,2,1,0:T(8,128)(2,1)}), bf16[16,2,1,64,384]{4,3,2,1,0:T(8,128)(2,1)}, u32[]{:S(2)}, u32[]{:S(2)}) %all-to-all-start.1) | async-done | bytes 1572896 | tf_op jit(solution)/shard_map/all_to_all | solution.py:156
  146.3 5.7 %fusion.22 = bf16[3,256,384]{2,1,0:T(8,128)(2,1)S(1)} fusion(bf16[3,3072,384]{2,1,0:T(8,128)(2,1)} %param.10, bf16[256,3072]{1,0:T(8,128)(2,1)} %bitcast.136), kind=kOutput, calls=%fused_computation.33 | convolution fusion | flops 1812234240 | bytes 9240576 | tf_op jit(solution)/shard_map/td,sdh->sth/dot_general | solution.py:144
  154.7 4.0 %bitcast_select_fusion = (bf16[16,2,1,64,384]{4,3,2,1,0:T(8,128)(2,1)}, bf16[16,2,1,64,384]{4,3,2,1,0:T(8,128)(2,1)}) fusion(bf16[16,2,64,384]{3,2,1,0:T(8,128)(2,1)} %gather_fusion.5, pred[16]{0:T(512)(128)(4,1)S(1)} %compare_and_fusion, bf16[16,2,64,384]{3,2,1,0:T(8,128)(2,1)} %gather_fusion.4), kind=kLoop, calls=%fused_computation.17 | loop fusion | flops 1572864 | bytes 6291472 | tf_op jit(solution)/shard_map/jit(_take)/select_n | solution.py:151
  158.7 4.3 %all-to-all-start.2 = ((bf16[16,2,1,64,384]{4,3,2,1,0:T(8,128)(2,1)}), bf16[16,2,1,64,384]{4,3,2,1,0:T(8,128)(2,1)}, u32[]{:S(2)}, u32[]{:S(2)}) async-start(bf16[16,2,1,64,384]{4,3,2,1,0:T(8,128)(2,1)} %get-tuple-element.15), calls=%async_computation.2 | async-start | bytes 3145728 | tf_op jit(solution)/shard_map/all_to_all | solution.py:156
  170.1 8.9 %shard_map.74 = bf16[1,256,384]{2,1,0:T(8,128)(2,1)} custom-call(s32[4,10]{1,0:T(4,128)} %add_select_fusion.2.pos_ref, s32[4]{0:T(128)} %count_ref.7, f32[4,3,10]{2,1,0:T(4,128)} %fusion.40.bias_ref, bf16[1,256,384]{2,1,0:T(8,128)(2,1)} %slice.56.q_ref, ...), custom_call_target="tpu_custom_call" | custom-call | tf_op jit(solution)/shard_map/pallas_call | solution.py:79
  179.0 3.1 %convolution_convert_fusion.2 = bf16[256,3072]{1,0:T(8,128)(2,1)} fusion(bf16[384,3072]{1,0:T(8,128)(2,1)S(1)} %copy-done, bf16[1,256,384]{2,1,0:T(8,128)(2,1)} %shard_map.74), kind=kOutput, calls=%fused_computation.9 | convolution fusion | flops 604766208 | bytes 4128768 | tf_op jit(solution)/shard_map/dot_general | solution.py:162
  182.1 18.8 %collective-permute-done.1 = bf16[256,3072]{1,0:T(8,128)(2,1)} collective-permute-done((bf16[256,3072]{1,0:T(8,128)(2,1)}, bf16[256,3072]{1,0:T(8,128)(2,1)}, u32[]{:S(2)}, u32[]{:S(2)}) %collective-permute-start.1) | collective-permute-done | bytes 1572896 | tf_op jit(solution)/shard_map/ppermute | solution.py:167
  200.9 4.8 %all-to-all-start.3 = ((bf16[16,2,1,64,384]{4,3,2,1,0:T(8,128)(2,1)}), bf16[16,2,1,64,384]{4,3,2,1,0:T(8,128)(2,1)}, u32[]{:S(2)}, u32[]{:S(2)}) async-start(bf16[16,2,1,64,384]{4,3,2,1,0:T(8,128)(2,1)} %get-tuple-element.18), calls=%async_computation.3 | async-start | bytes 3145728 | tf_op jit(solution)/shard_map/all_to_all | solution.py:156
  211.7 8.8 %shard_map.75 = bf16[1,256,384]{2,1,0:T(8,128)(2,1)} custom-call(s32[4,10]{1,0:T(4,128)} %add_select_fusion.2.pos_ref, s32[4]{0:T(128)} %count_ref.7, f32[4,3,10]{2,1,0:T(4,128)} %fusion.40.bias_ref, bf16[1,256,384]{2,1,0:T(8,128)(2,1)} %slice.58.q_ref, ...), custom_call_target="tpu_custom_call" | custom-call | tf_op jit(solution)/shard_map/pallas_call | solution.py:79
  226.8 16.9 %all-to-all-done.3 = bf16[16,2,1,64,384]{4,3,2,1,0:T(8,128)(2,1)} async-done(((bf16[16,2,1,64,384]{4,3,2,1,0:T(8,128)(2,1)}), bf16[16,2,1,64,384]{4,3,2,1,0:T(8,128)(2,1)}, u32[]{:S(2)}, u32[]{:S(2)}) %all-to-all-start.3) | async-done | bytes 1572896 | tf_op jit(solution)/shard_map/all_to_all | solution.py:156
  246.5 8.8 %shard_map.76 = bf16[1,256,384]{2,1,0:T(8,128)(2,1)} custom-call(s32[4,10]{1,0:T(4,128)} %add_select_fusion.2.pos_ref, s32[4]{0:T(128)} %count_ref.7, f32[4,3,10]{2,1,0:T(4,128)} %fusion.40.bias_ref, bf16[1,256,384]{2,1,0:T(8,128)(2,1)} %slice.60.q_ref, ...), custom_call_target="tpu_custom_call" | custom-call | tf_op jit(solution)/shard_map/pallas_call | solution.py:79
  255.4 4.9 %collective-permute-done.5 = bf16[256,3072]{1,0:T(8,128)(2,1)} collective-permute-done((bf16[256,3072]{1,0:T(8,128)(2,1)}, bf16[256,3072]{1,0:T(8,128)(2,1)}, u32[]{:S(2)}, u32[]{:S(2)}) %collective-permute-start.5) | collective-permute-done | bytes 1572896 | tf_op jit(solution)/shard_map/ppermute | solution.py:167
  260.2 4.6 %fusion.1 = bf16[1,256,3072]{2,1,0:T(8,128)(2,1)} fusion(bf16[256,3072]{1,0:T(8,128)(2,1)} %collective-permute-done.5, bf16[256,3072]{1,0:T(8,128)(2,1)} %collective-permute-done.3, bf16[256,3072]{1,0:T(8,128)(2,1)} %collective-permute-done.1, bf16[384,3072]{1,0:T(8,128)(2,1)S(1)} %copy-done, bf16[1,256,384]{2,1,0:T(8,128)(2,1)} %shard_map.76), kind=kOutput, calls=%fused_computation.16 | convolution fusion | flops 611057664 | bytes 8847360 | tf_op jit(solution)/shard_map/dot_general | solution.py:162
  (89 shorter events, 52.7 us)
Async XLA Ops:
  0.0 133.9 %copy-start = (bf16[384,3072]{1,0:T(8,128)(2,1)S(1)}, bf16[384,3072]{1,0:T(8,128)(2,1)}, u32[]{:S(2)}) copy-start(bf16[384,3072]{1,0:T(8,128)(2,1)} %param.11) | copy-start | bytes 7077892
  0.0 38.6 %collective-permute-start = (bf16[256,3072]{1,0:T(8,128)(2,1)}, bf16[256,3072]{1,0:T(8,128)(2,1)}, u32[]{:S(2)}, u32[]{:S(2)}) collective-permute-start(bf16[256,3072]{1,0:T(8,128)(2,1)} %bitcast.133), channel_id=1, source_target_pairs={{0,24},{8,16},{16,8},{24,0},{1,25},{9,17},{17,9},{25,1},{2,26},{10... | collective-permute-start | bytes 4718600 | tf_op jit(solution)/shard_map/ppermute | solution.py:135
  44.3 0.8 copy-start.2
  49.8 8.2 %copy-start.6 = (s32[4]{0:T(128)S(1)}, s32[4]{0:T(128)}, u32[]{:S(2)}) copy-start(s32[4]{0:T(128)} %count_ref.7) | copy-start | bytes 52
  49.8 8.3 %copy-start.5 = (s32[4,10]{1,0:T(4,128)S(1)}, s32[4,10]{1,0:T(4,128)}, u32[]{:S(2)}) copy-start(s32[4,10]{1,0:T(4,128)} %param.12) | copy-start | bytes 484
  49.8 8.3 %copy-start.7 = (s32[4,10]{1,0:T(4,128)S(1)}, s32[4,10]{1,0:T(4,128)}, u32[]{:S(2)}) copy-start(s32[4,10]{1,0:T(4,128)} %param.14) | copy-start | bytes 484
  49.8 43.1 %all-to-all-start = ((bf16[16,2,1,64,384]{4,3,2,1,0:T(8,128)(2,1)}), bf16[16,2,1,64,384]{4,3,2,1,0:T(8,128)(2,1)}, u32[]{:S(2)}, u32[]{:S(2)}) async-start(bf16[16,2,1,64,384]{4,3,2,1,0:T(8,128)(2,1)} %bitcast_select_fusion.3), calls=%async_computation | async-start | bytes 3145728 | tf_op jit(solution)/shard_map/all_to_all | solution.py:156
  55.0 37.1 %collective-permute-start.2 = (bf16[256,3072]{1,0:T(8,128)(2,1)}, bf16[256,3072]{1,0:T(8,128)(2,1)}, u32[]{:S(2)}, u32[]{:S(2)}) collective-permute-start(bf16[256,3072]{1,0:T(8,128)(2,1)} %bitcast.134), channel_id=1, source_target_pairs={{0,8},{8,0},{16,24},{24,16},{1,9},{9,1},{17,25},{25,17},{2,10},{10... | collective-permute-start | bytes 4718600 | tf_op jit(solution)/shard_map/ppermute | solution.py:135
  56.5 57.2 %collective-permute-start.4 = (bf16[256,3072]{1,0:T(8,128)(2,1)}, bf16[256,3072]{1,0:T(8,128)(2,1)}, u32[]{:S(2)}, u32[]{:S(2)}) collective-permute-start(bf16[256,3072]{1,0:T(8,128)(2,1)} %bitcast.135), channel_id=1, source_target_pairs={{0,16},{8,24},{16,0},{24,8},{1,17},{9,25},{17,1},{25,9},{2,18},{10... | collective-permute-start | bytes 4718600 | tf_op jit(solution)/shard_map/ppermute | solution.py:135
  98.7 0.8 copy-start.1
  104.2 42.1 %all-to-all-start.1 = ((bf16[16,2,1,64,384]{4,3,2,1,0:T(8,128)(2,1)}), bf16[16,2,1,64,384]{4,3,2,1,0:T(8,128)(2,1)}, u32[]{:S(2)}, u32[]{:S(2)}) async-start(bf16[16,2,1,64,384]{4,3,2,1,0:T(8,128)(2,1)} %bitcast_select_fusion.2), calls=%async_computation.1 | async-start | bytes 3145728 | tf_op jit(solution)/shard_map/all_to_all | solution.py:156
  108.7 1.3 copy-start.8
  119.4 0.8 copy-start.3
  152.0 0.8 copy-start.4
  158.7 42.2 %all-to-all-start.2 = ((bf16[16,2,1,64,384]{4,3,2,1,0:T(8,128)(2,1)}), bf16[16,2,1,64,384]{4,3,2,1,0:T(8,128)(2,1)}, u32[]{:S(2)}, u32[]{:S(2)}) async-start(bf16[16,2,1,64,384]{4,3,2,1,0:T(8,128)(2,1)} %get-tuple-element.15), calls=%async_computation.2 | async-start | bytes 3145728 | tf_op jit(solution)/shard_map/all_to_all | solution.py:156
  163.0 37.9 %collective-permute-start.1 = (bf16[256,3072]{1,0:T(8,128)(2,1)}, bf16[256,3072]{1,0:T(8,128)(2,1)}, u32[]{:S(2)}, u32[]{:S(2)}) collective-permute-start(bf16[256,3072]{1,0:T(8,128)(2,1)} %convolution_convert_fusion.3), channel_id=1, source_target_pairs={{0,24},{8,16},{16,8},{24,0},{1,25},{9,17},{17,9},{25,1},{2,26},{10... | collective-permute-start | bytes 4718600 | tf_op jit(solution)/shard_map/ppermute | solution.py:167
  200.9 42.7 %all-to-all-start.3 = ((bf16[16,2,1,64,384]{4,3,2,1,0:T(8,128)(2,1)}), bf16[16,2,1,64,384]{4,3,2,1,0:T(8,128)(2,1)}, u32[]{:S(2)}, u32[]{:S(2)}) async-start(bf16[16,2,1,64,384]{4,3,2,1,0:T(8,128)(2,1)} %get-tuple-element.18), calls=%async_computation.3 | async-start | bytes 3145728 | tf_op jit(solution)/shard_map/all_to_all | solution.py:156
  207.3 39.2 %collective-permute-start.3 = (bf16[256,3072]{1,0:T(8,128)(2,1)}, bf16[256,3072]{1,0:T(8,128)(2,1)}, u32[]{:S(2)}, u32[]{:S(2)}) collective-permute-start(bf16[256,3072]{1,0:T(8,128)(2,1)} %convolution_convert_fusion.2), channel_id=1, source_target_pairs={{0,8},{8,0},{16,24},{24,16},{1,9},{9,1},{17,25},{25,17},{2,10},{10... | collective-permute-start | bytes 4718600 | tf_op jit(solution)/shard_map/ppermute | solution.py:167
  223.6 36.6 %collective-permute-start.5 = (bf16[256,3072]{1,0:T(8,128)(2,1)}, bf16[256,3072]{1,0:T(8,128)(2,1)}, u32[]{:S(2)}, u32[]{:S(2)}) collective-permute-start(bf16[256,3072]{1,0:T(8,128)(2,1)} %convolution_convert_fusion.1), channel_id=1, source_target_pairs={{0,16},{8,24},{16,0},{24,8},{1,17},{9,25},{17,1},{25,9},{2,18},{10... | collective-permute-start | bytes 4718600 | tf_op jit(solution)/shard_map/ppermute | solution.py:167

commit v8 on v7

--- a/solution.py
+++ b/solution.py
@@ -64,7 +64,8 @@
 
 
 def attend(positions, live_counts, bias, queries, key_values, heads, head_size):
-    clip_count, token_count, width = queries.shape
+    _, token_count, width = queries.shape
+    clip_count = 1
     tile_count = token_count // TILE
 
     def kv_spec(slot):
@@ -78,7 +79,7 @@
     )
     return pl.pallas_call(
         kernel,
-        out_shape=jax.ShapeDtypeStruct(queries.shape, jnp.bfloat16),
+        out_shape=jax.ShapeDtypeStruct((clip_count, token_count, width), jnp.bfloat16),
         grid_spec=pltpu.PrefetchScalarGridSpec(
             num_scalar_prefetch=2,
             grid=(tile_count,),
@@ -144,11 +145,10 @@
         projected = jnp.einsum(
             "td,sdh->sth", tokens, qkv_weight, preferred_element_type=jnp.float32
         ).astype(jnp.bfloat16)
-        queries = projected[0][None]
         by_tile = jnp.transpose(
             projected[1:3].reshape(2, tile_count, TILE, width_here), (1, 0, 2, 3)
         )[:, :, None]
-        payload = jnp.take(by_tile, send_picks, axis=0)
+        payload = by_tile.at[send_picks].get(mode="promise_in_bounds")
         if index >= 2:
             payload, _ = lax.optimization_barrier((payload, partials[index - 2]))
         if index == len(order) - 1 and len(sent) >= 2:
@@ -158,7 +158,7 @@
         key_values = jnp.concatenate([by_tile, incoming], axis=0)
         if index == len(order) - 1 and len(sent) >= 2:
             key_values, _ = lax.optimization_barrier((key_values, sent[-2]))
-        attended = attend(positions, live_counts, bias, queries, key_values, heads_here, head_size)
+        attended = attend(positions, live_counts, bias, projected, key_values, heads_here, head_size)
         partial_out = jnp.dot(
             attended[0], out_weight, preferred_element_type=jnp.float32
         ).astype(jnp.bfloat16)

time: 266 us -> 247 us (0.929)
  other arithmetic: 23.9 us -> 14.4 us
  local copies, waits for them, and re-layouts: 20.3 us -> 14.1 us
    select_n x4 -> x1, other arithmetic: 9.56 us -> 0.01 us  [local(): payload = by_tile.at[send_picks].get(mode='promise_in_bounds')]
    ppermute x3, waiting for transfers between devices: 23.7 us -> 16.3 us  [local(): partial_out = lax.ppermute(partial_out, 'dp', partner_pairs(n_dp, step))]
    slice x4 -> x0, local copies, waits for them, and re-layouts: 6.51 us -> none  [local(): queries = projected[0][None]]
    all_to_all x4, waiting for transfers between devices: 26.9 us -> 31.8 us  [local(): incoming = lax.all_to_all(payload, 'ctx', 0, 0, tiled=True)]
  transfers between devices with their start and end apart: 10 -> 10, of which waited for: 7 -> 7; matrix products, arithmetic and copies ran while one was open for 19% -> 20% of each run, Pallas kernels for 13% -> 14%
where the time goes in v8:
time: 247 us; the launch traced here: 246 us
  waiting for transfers between devices  102 us (41%)
  matrix products  35.7 us (14%)
  Pallas kernels  35.6 us (14%)
  starting transfers between devices  31.3 us (13%)
  other arithmetic  14.4 us (6%)
  local copies, waits for them, and re-layouts  14.1 us (6%)
  blocking collectives  12.9 us (5%)
    ppermute x3, waiting for transfers between devices, local(): arrived[step] = lax.ppermute(own_tokens, 'dp', partner_pairs(n_dp, step))  53.6 us
    pallas_call x4, Pallas kernels, attend(): pl.pallas_call(kernel, out_shape=jax.ShapeDtypeStruct((clip_count, token_...  35.6 us
    all_to_all x4, waiting for transfers between devices, local(): incoming = lax.all_to_all(payload, 'ctx', 0, 0, tiled=True)  31.8 us
    dot_general x4, matrix products, local(): jnp.einsum('td,sdh->sth', tokens, qkv_weight, preferred_element_type=jnp....  22.8 us
    all_to_all x4, starting transfers between devices, local(): incoming = lax.all_to_all(payload, 'ctx', 0, 0, tiled=True)  18.9 us
    ppermute x3, waiting for transfers between devices, local(): partial_out = lax.ppermute(partial_out, 'dp', partner_pairs(n_dp, step))  16.3 us
    all_gather x1, blocking collectives, local(): lax.all_gather(table, 'ctx', axis=0, tiled=True).astype(jnp.int32)  12.9 us
    dot_general x4, matrix products, local(): jnp.dot(attended[0], out_weight, preferred_element_type=jnp.float32)  12.9 us
  transfers between devices with their start and end apart: 10, of which 7 were waited for; matrix products, arithmetic and copies ran while one was open for 20% of the time, Pallas kernels for 14%

profile of v8, /device:TPU:0, one launch (start us, length us, event | category | flops | bytes accessed | tf_op | source)
XLA Modules:
  0.0 245.8 jit_solution(9904944253180153984)
XLA Ops:
  0.0 3.9 %collective-permute-start = (bf16[256,3072]{1,0:T(8,128)(2,1)}, bf16[256,3072]{1,0:T(8,128)(2,1)}, u32[]{:S(2)}, u32[]{:S(2)}) collective-permute-start(bf16[256,3072]{1,0:T(8,128)(2,1)} %bitcast.127), channel_id=1, source_target_pairs={{0,24},{8,16},{16,8},{24,0},{1,25},{9,17},{17,9},{25,1},{2,26},{10... | collective-permute-start | bytes 4718600 | tf_op jit(solution)/shard_map/ppermute | solution.py:136
  5.4 12.9 %all-gather = f32[8,4,11]{2,1,0:T(4,128)S(1)} all-gather(f32[1,4,11]{2,1,0:T(4,128)S(1)} %fusion.42), channel_id=1, replica_groups=mesh['dp'=4,'ctx'=8] {'ctx'}, dimensions={0}, use_global_device_ids=true | all-gather | bytes 1584 | tf_op jit(solution)/shard_map/all_gather | solution.py:110
  19.1 19.5 %collective-permute-done = bf16[256,3072]{1,0:T(8,128)(2,1)} collective-permute-done((bf16[256,3072]{1,0:T(8,128)(2,1)}, bf16[256,3072]{1,0:T(8,128)(2,1)}, u32[]{:S(2)}, u32[]{:S(2)}) %collective-permute-start) | collective-permute-done | bytes 1572896 | tf_op jit(solution)/shard_map/ppermute | solution.py:136
  38.6 5.7 %fusion.31.q_ref = bf16[3,256,384]{2,1,0:T(8,128)(2,1)S(1)} fusion(bf16[3,3072,384]{2,1,0:T(8,128)(2,1)} %param.8, bf16[256,3072]{1,0:T(8,128)(2,1)} %collective-permute-done), kind=kOutput, calls=%fused_computation.32 | convolution fusion | flops 1812234240 | bytes 9240576 | tf_op jit(solution)/shard_map/td,sdh->sth/dot_general | solution.py:145
  47.1 5.2 %all-to-all-start = ((bf16[16,2,1,64,384]{4,3,2,1,0:T(8,128)(2,1)}), bf16[16,2,1,64,384]{4,3,2,1,0:T(8,128)(2,1)}, u32[]{:S(2)}, u32[]{:S(2)}) async-start(bf16[16,2,1,64,384]{4,3,2,1,0:T(8,128)(2,1)} %bitcast.119), calls=%async_computation | async-start | bytes 3145728 | tf_op jit(solution)/shard_map/all_to_all | solution.py:156
  55.3 34.1 %collective-permute-done.2 = bf16[256,3072]{1,0:T(8,128)(2,1)} collective-permute-done((bf16[256,3072]{1,0:T(8,128)(2,1)}, bf16[256,3072]{1,0:T(8,128)(2,1)}, u32[]{:S(2)}, u32[]{:S(2)}) %collective-permute-start.2) | collective-permute-done | bytes 1572896 | tf_op jit(solution)/shard_map/ppermute | solution.py:136
  90.2 5.7 %fusion.28.q_ref = bf16[3,256,384]{2,1,0:T(8,128)(2,1)S(1)} fusion(bf16[3,3072,384]{2,1,0:T(8,128)(2,1)} %param.8, bf16[256,3072]{1,0:T(8,128)(2,1)} %collective-permute-done.2), kind=kOutput, calls=%fused_computation.31 | convolution fusion | flops 1812234240 | bytes 9240576 | tf_op jit(solution)/shard_map/td,sdh->sth/dot_general | solution.py:145
  98.7 4.4 %all-to-all-start.1 = ((bf16[16,2,1,64,384]{4,3,2,1,0:T(8,128)(2,1)}), bf16[16,2,1,64,384]{4,3,2,1,0:T(8,128)(2,1)}, u32[]{:S(2)}, u32[]{:S(2)}) async-start(bf16[16,2,1,64,384]{4,3,2,1,0:T(8,128)(2,1)} %bitcast.116), calls=%async_computation.1 | async-start | bytes 3145728 | tf_op jit(solution)/shard_map/all_to_all | solution.py:156
  106.6 5.7 %fusion.25.q_ref = bf16[3,256,384]{2,1,0:T(8,128)(2,1)S(1)} fusion(bf16[3,3072,384]{2,1,0:T(8,128)(2,1)} %param.8, bf16[256,3072]{1,0:T(8,128)(2,1)} %collective-permute-done.4), kind=kOutput, calls=%fused_computation.30 | convolution fusion | flops 1812234240 | bytes 9240576 | tf_op jit(solution)/shard_map/td,sdh->sth/dot_general | solution.py:145
  118.0 8.9 %shard_map.73 = bf16[1,256,384]{2,1,0:T(8,128)(2,1)} custom-call(s32[4,10]{1,0:T(4,128)} %add_select_fusion.2.pos_ref, s32[4]{0:T(128)} %count_ref.7, f32[4,3,10]{2,1,0:T(4,128)} %fusion.40.bias_ref, bf16[3,256,384]{2,1,0:T(8,128)(2,1)} %copy-done.1, ...), custom_call_target="tpu_custom_call" | custom-call | tf_op jit(solution)/shard_map/pallas_call | solution.py:80
  126.9 3.1 %convolution_convert_fusion.3 = bf16[256,3072]{1,0:T(8,128)(2,1)} fusion(bf16[384,3072]{1,0:T(8,128)(2,1)S(1)} %copy-done, bf16[1,256,384]{2,1,0:T(8,128)(2,1)} %shard_map.73), kind=kOutput, calls=%fused_computation.10 | convolution fusion | flops 604766208 | bytes 4128768 | tf_op jit(solution)/shard_map/dot_general | solution.py:162
  130.1 10.9 %all-to-all-done.1 = bf16[16,2,1,64,384]{4,3,2,1,0:T(8,128)(2,1)} async-done(((bf16[16,2,1,64,384]{4,3,2,1,0:T(8,128)(2,1)}), bf16[16,2,1,64,384]{4,3,2,1,0:T(8,128)(2,1)}, u32[]{:S(2)}, u32[]{:S(2)}) %all-to-all-start.1) | async-done | bytes 1572896 | tf_op jit(solution)/shard_map/all_to_all | solution.py:156
  141.0 4.5 %all-to-all-start.2 = ((bf16[16,2,1,64,384]{4,3,2,1,0:T(8,128)(2,1)}), bf16[16,2,1,64,384]{4,3,2,1,0:T(8,128)(2,1)}, u32[]{:S(2)}, u32[]{:S(2)}) async-start(bf16[16,2,1,64,384]{4,3,2,1,0:T(8,128)(2,1)} %bitcast.117), calls=%async_computation.2 | async-start | bytes 3145728 | tf_op jit(solution)/shard_map/all_to_all | solution.py:156
  150.9 8.9 %shard_map.74 = bf16[1,256,384]{2,1,0:T(8,128)(2,1)} custom-call(s32[4,10]{1,0:T(4,128)} %add_select_fusion.2.pos_ref, s32[4]{0:T(128)} %count_ref.7, f32[4,3,10]{2,1,0:T(4,128)} %fusion.40.bias_ref, bf16[3,256,384]{2,1,0:T(8,128)(2,1)} %copy-done.2, ...), custom_call_target="tpu_custom_call" | custom-call | tf_op jit(solution)/shard_map/pallas_call | solution.py:80
  159.8 5.7 %fusion.22.q_ref = bf16[3,256,384]{2,1,0:T(8,128)(2,1)S(1)} fusion(bf16[3,3072,384]{2,1,0:T(8,128)(2,1)} %param.8, bf16[256,3072]{1,0:T(8,128)(2,1)} %bitcast.130), kind=kOutput, calls=%fused_computation.29 | convolution fusion | flops 1812234240 | bytes 9240576 | tf_op jit(solution)/shard_map/td,sdh->sth/dot_general | solution.py:145
  170.4 12.7 %collective-permute-done.1 = bf16[256,3072]{1,0:T(8,128)(2,1)} collective-permute-done((bf16[256,3072]{1,0:T(8,128)(2,1)}, bf16[256,3072]{1,0:T(8,128)(2,1)}, u32[]{:S(2)}, u32[]{:S(2)}) %collective-permute-start.1) | collective-permute-done | bytes 1572896 | tf_op jit(solution)/shard_map/ppermute | solution.py:167
  183.2 4.8 %all-to-all-start.3 = ((bf16[16,2,1,64,384]{4,3,2,1,0:T(8,128)(2,1)}), bf16[16,2,1,64,384]{4,3,2,1,0:T(8,128)(2,1)}, u32[]{:S(2)}, u32[]{:S(2)}) async-start(bf16[16,2,1,64,384]{4,3,2,1,0:T(8,128)(2,1)} %bitcast.118), calls=%async_computation.3 | async-start | bytes 3145728 | tf_op jit(solution)/shard_map/all_to_all | solution.py:156
  192.4 8.9 %shard_map.75 = bf16[1,256,384]{2,1,0:T(8,128)(2,1)} custom-call(s32[4,10]{1,0:T(4,128)} %add_select_fusion.2.pos_ref, s32[4]{0:T(128)} %count_ref.7, f32[4,3,10]{2,1,0:T(4,128)} %fusion.40.bias_ref, bf16[3,256,384]{2,1,0:T(8,128)(2,1)} %copy-done.3, ...), custom_call_target="tpu_custom_call" | custom-call | tf_op jit(solution)/shard_map/pallas_call | solution.py:80
  201.3 3.1 %convolution_convert_fusion.1 = bf16[256,3072]{1,0:T(8,128)(2,1)} fusion(bf16[384,3072]{1,0:T(8,128)(2,1)S(1)} %copy-done, bf16[1,256,384]{2,1,0:T(8,128)(2,1)} %shard_map.75), kind=kOutput, calls=%fused_computation.8 | convolution fusion | flops 604766208 | bytes 4128768 | tf_op jit(solution)/shard_map/dot_general | solution.py:162
  205.8 20.1 %all-to-all-done.3 = bf16[16,2,1,64,384]{4,3,2,1,0:T(8,128)(2,1)} async-done(((bf16[16,2,1,64,384]{4,3,2,1,0:T(8,128)(2,1)}), bf16[16,2,1,64,384]{4,3,2,1,0:T(8,128)(2,1)}, u32[]{:S(2)}, u32[]{:S(2)}) %all-to-all-start.3) | async-done | bytes 1572896 | tf_op jit(solution)/shard_map/all_to_all | solution.py:156
  225.9 2.9 %pad_maximum_fusion.3.refs_0_.refs_1_.refs_2_.refs_3_.refs_4_.refs_5_.refs_6_.refs_7_.refs_8_.refs_9_ = bf16[20,2,1,64,384]{4,3,2,1,0:T(8,128)(2,1)} fusion(bf16[16,2,1,64,384]{4,3,2,1,0:T(8,128)(2,1)} %all-to-all-done.3, bf16[4,2,1,64,384]{4,3,2,1,0:T(8,128)(2,1)S(1)} %bitcast.115), kind=kLoop, calls=%fused_computation.15 | loop fusion | flops 983040 | bytes 3932160 | tf_op jit(solution)/shard_map/concatenate | solution.py:158
  228.8 8.9 %shard_map.76 = bf16[1,256,384]{2,1,0:T(8,128)(2,1)} custom-call(s32[4,10]{1,0:T(4,128)} %add_select_fusion.2.pos_ref, s32[4]{0:T(128)} %count_ref.7, f32[4,3,10]{2,1,0:T(4,128)} %fusion.40.bias_ref, bf16[3,256,384]{2,1,0:T(8,128)(2,1)} %copy-done.4, ...), custom_call_target="tpu_custom_call" | custom-call | tf_op jit(solution)/shard_map/pallas_call | solution.py:80
  237.7 3.5 %collective-permute-done.5 = bf16[256,3072]{1,0:T(8,128)(2,1)} collective-permute-done((bf16[256,3072]{1,0:T(8,128)(2,1)}, bf16[256,3072]{1,0:T(8,128)(2,1)}, u32[]{:S(2)}, u32[]{:S(2)}) %collective-permute-start.5) | collective-permute-done | bytes 1572896 | tf_op jit(solution)/shard_map/ppermute | solution.py:167
  241.2 4.6 %fusion.1 = bf16[1,256,3072]{2,1,0:T(8,128)(2,1)} fusion(bf16[256,3072]{1,0:T(8,128)(2,1)} %collective-permute-done.5, bf16[256,3072]{1,0:T(8,128)(2,1)} %collective-permute-done.3, bf16[256,3072]{1,0:T(8,128)(2,1)} %collective-permute-done.1, bf16[384,3072]{1,0:T(8,128)(2,1)S(1)} %copy-done, bf16[1,256,384]{2,1,0:T(8,128)(2,1)} %shard_map.76), kind=kOutput, calls=%fused_computation.16 | convolution fusion | flops 611057664 | bytes 8847360 | tf_op jit(solution)/shard_map/dot_general | solution.py:162
  (83 shorter events, 37.0 us)
Async XLA Ops:
  0.0 126.9 %copy-start = (bf16[384,3072]{1,0:T(8,128)(2,1)S(1)}, bf16[384,3072]{1,0:T(8,128)(2,1)}, u32[]{:S(2)}) copy-start(bf16[384,3072]{1,0:T(8,128)(2,1)} %param.9) | copy-start | bytes 7077892
  0.0 38.6 %collective-permute-start = (bf16[256,3072]{1,0:T(8,128)(2,1)}, bf16[256,3072]{1,0:T(8,128)(2,1)}, u32[]{:S(2)}, u32[]{:S(2)}) collective-permute-start(bf16[256,3072]{1,0:T(8,128)(2,1)} %bitcast.127), channel_id=1, source_target_pairs={{0,24},{8,16},{16,8},{24,0},{1,25},{9,17},{17,9},{25,1},{2,26},{10... | collective-permute-start | bytes 4718600 | tf_op jit(solution)/shard_map/ppermute | solution.py:136
  44.3 0.8 copy-start.1
  47.1 8.2 %copy-start.6 = (s32[4,10]{1,0:T(4,128)S(1)}, s32[4,10]{1,0:T(4,128)}, u32[]{:S(2)}) copy-start(s32[4,10]{1,0:T(4,128)} %param.10) | copy-start | bytes 484
  47.1 43.1 %all-to-all-start = ((bf16[16,2,1,64,384]{4,3,2,1,0:T(8,128)(2,1)}), bf16[16,2,1,64,384]{4,3,2,1,0:T(8,128)(2,1)}, u32[]{:S(2)}, u32[]{:S(2)}) async-start(bf16[16,2,1,64,384]{4,3,2,1,0:T(8,128)(2,1)} %bitcast.119), calls=%async_computation | async-start | bytes 3145728 | tf_op jit(solution)/shard_map/all_to_all | solution.py:156
  52.3 37.1 %collective-permute-start.2 = (bf16[256,3072]{1,0:T(8,128)(2,1)}, bf16[256,3072]{1,0:T(8,128)(2,1)}, u32[]{:S(2)}, u32[]{:S(2)}) collective-permute-start(bf16[256,3072]{1,0:T(8,128)(2,1)} %bitcast.128), channel_id=1, source_target_pairs={{0,8},{8,0},{16,24},{24,16},{1,9},{9,1},{17,25},{25,17},{2,10},{10... | collective-permute-start | bytes 4718600 | tf_op jit(solution)/shard_map/ppermute | solution.py:136
  53.8 52.9 %collective-permute-start.4 = (bf16[256,3072]{1,0:T(8,128)(2,1)}, bf16[256,3072]{1,0:T(8,128)(2,1)}, u32[]{:S(2)}, u32[]{:S(2)}) collective-permute-start(bf16[256,3072]{1,0:T(8,128)(2,1)} %bitcast.129), channel_id=1, source_target_pairs={{0,16},{8,24},{16,0},{24,8},{1,17},{9,25},{17,1},{25,9},{2,18},{10... | collective-permute-start | bytes 4718600 | tf_op jit(solution)/shard_map/ppermute | solution.py:136
  95.9 0.8 copy-start.2
  98.7 4.4 %copy-start.7 = (s32[4]{0:T(128)S(1)}, s32[4]{0:T(128)}, u32[]{:S(2)}) copy-start(s32[4]{0:T(128)} %count_ref.7) | copy-start | bytes 52
  98.7 42.3 %all-to-all-start.1 = ((bf16[16,2,1,64,384]{4,3,2,1,0:T(8,128)(2,1)}), bf16[16,2,1,64,384]{4,3,2,1,0:T(8,128)(2,1)}, u32[]{:S(2)}, u32[]{:S(2)}) async-start(bf16[16,2,1,64,384]{4,3,2,1,0:T(8,128)(2,1)} %bitcast.116), calls=%async_computation.1 | async-start | bytes 3145728 | tf_op jit(solution)/shard_map/all_to_all | solution.py:156
  103.2 1.3 copy-start.9
  103.2 1.5 copy-start.8
  112.3 0.8 copy-start.3
  141.0 42.2 %all-to-all-start.2 = ((bf16[16,2,1,64,384]{4,3,2,1,0:T(8,128)(2,1)}), bf16[16,2,1,64,384]{4,3,2,1,0:T(8,128)(2,1)}, u32[]{:S(2)}, u32[]{:S(2)}) async-start(bf16[16,2,1,64,384]{4,3,2,1,0:T(8,128)(2,1)} %bitcast.117), calls=%async_computation.2 | async-start | bytes 3145728 | tf_op jit(solution)/shard_map/all_to_all | solution.py:156
  145.5 37.7 %collective-permute-start.1 = (bf16[256,3072]{1,0:T(8,128)(2,1)}, bf16[256,3072]{1,0:T(8,128)(2,1)}, u32[]{:S(2)}, u32[]{:S(2)}) collective-permute-start(bf16[256,3072]{1,0:T(8,128)(2,1)} %convolution_convert_fusion.3), channel_id=1, source_target_pairs={{0,24},{8,16},{16,8},{24,0},{1,25},{9,17},{17,9},{25,1},{2,26},{10... | collective-permute-start | bytes 4718600 | tf_op jit(solution)/shard_map/ppermute | solution.py:167
  165.5 0.8 copy-start.4
  166.4 1.9 copy-start.5
  183.2 42.7 %all-to-all-start.3 = ((bf16[16,2,1,64,384]{4,3,2,1,0:T(8,128)(2,1)}), bf16[16,2,1,64,384]{4,3,2,1,0:T(8,128)(2,1)}, u32[]{:S(2)}, u32[]{:S(2)}) async-start(bf16[16,2,1,64,384]{4,3,2,1,0:T(8,128)(2,1)} %bitcast.118), calls=%async_computation.3 | async-start | bytes 3145728 | tf_op jit(solution)/shard_map/all_to_all | solution.py:156
  188.0 40.9 %collective-permute-start.3 = (bf16[256,3072]{1,0:T(8,128)(2,1)}, bf16[256,3072]{1,0:T(8,128)(2,1)}, u32[]{:S(2)}, u32[]{:S(2)}) collective-permute-start(bf16[256,3072]{1,0:T(8,128)(2,1)} %convolution_convert_fusion.2), channel_id=1, source_target_pairs={{0,8},{8,0},{16,24},{24,16},{1,9},{9,1},{17,25},{25,17},{2,10},{10... | collective-permute-start | bytes 4718600 | tf_op jit(solution)/shard_map/ppermute | solution.py:167
  204.3 36.9 %collective-permute-start.5 = (bf16[256,3072]{1,0:T(8,128)(2,1)}, bf16[256,3072]{1,0:T(8,128)(2,1)}, u32[]{:S(2)}, u32[]{:S(2)}) collective-permute-start(bf16[256,3072]{1,0:T(8,128)(2,1)} %convolution_convert_fusion.1), channel_id=1, source_target_pairs={{0,16},{8,24},{16,0},{24,8},{1,17},{9,25},{17,1},{25,9},{2,18},{10... | collective-permute-start | bytes 4718600 | tf_op jit(solution)/shard_map/ppermute | solution.py:167

commit v9 on v8

--- a/solution.py
+++ b/solution.py
@@ -130,15 +130,19 @@
     live_counts = counts.astype(jnp.int32)
 
     own_tokens = clip_tokens[0]
-    order = [3, 1, 2, 0] if n_dp == 4 else list(range(1, n_dp)) + [0]
+    order = [0, 3, 1, 2] if n_dp == 4 else list(range(n_dp))
     arrived = {0: own_tokens}
     for step in range(1, n_dp):
         arrived[step] = lax.ppermute(own_tokens, "dp", partner_pairs(n_dp, step))
+    last = order[-1]
+    if last > 0:
+        far_weight = lax.ppermute(out_weight, "dp", partner_pairs(n_dp, last))
     total = None
     received = []
     partials = []
     sent = []
     for index, step in enumerate(order):
+        final = index == len(order) - 1
         tokens = arrived[step]
         if index >= 1:
             tokens, _ = lax.optimization_barrier((tokens, received[max(index - 2, 0)]))
@@ -151,21 +155,29 @@
         payload = by_tile.at[send_picks].get(mode="promise_in_bounds")
         if index >= 2:
             payload, _ = lax.optimization_barrier((payload, partials[index - 2]))
-        if index == len(order) - 1 and len(sent) >= 2:
-            payload, _ = lax.optimization_barrier((payload, sent[-3]))
+        if final and last > 0:
+            payload, far_weight = lax.optimization_barrier((payload, far_weight))
+        if final and len(sent) >= 2:
+            payload, _ = lax.optimization_barrier((payload, sent[-2]))
         incoming = lax.all_to_all(payload, "ctx", 0, 0, tiled=True)
         received.append(incoming)
         key_values = jnp.concatenate([by_tile, incoming], axis=0)
-        if index == len(order) - 1 and len(sent) >= 2:
-            key_values, _ = lax.optimization_barrier((key_values, sent[-2]))
+        if final and len(sent) >= 1:
+            key_values, _ = lax.optimization_barrier((key_values, sent[-1]))
         attended = attend(positions, live_counts, bias, projected, key_values, heads_here, head_size)
-        partial_out = jnp.dot(
-            attended[0], out_weight, preferred_element_type=jnp.float32
-        ).astype(jnp.bfloat16)
-        partials.append(partial_out)
-        if step > 0:
-            partial_out = lax.ppermute(partial_out, "dp", partner_pairs(n_dp, step))
-            sent.append(partial_out)
+        if final and step > 0:
+            came = lax.ppermute(attended[0], "dp", partner_pairs(n_dp, step))
+            partial_out = jnp.dot(
+                came, far_weight, preferred_element_type=jnp.float32
+            ).astype(jnp.bfloat16)
+        else:
+            partial_out = jnp.dot(
+                attended[0], out_weight, preferred_element_type=jnp.float32
+            ).astype(jnp.bfloat16)
+            partials.append(partial_out)
+            if step > 0:
+                partial_out = lax.ppermute(partial_out, "dp", partner_pairs(n_dp, step))
+                sent.append(partial_out)
         contribution = partial_out.astype(jnp.float32)
         total = contribution if total is None else total + contribution
     return total.astype(jnp.bfloat16)[None]

time: 247 us -> 334 us (1.35)
  waiting for transfers between devices: 102 us -> 193 us
  starting transfers between devices: 31.3 us -> 26.5 us
    ppermute x3, waiting for transfers between devices: 53.6 us -> 154 us  [local(): arrived[step] = lax.ppermute(own_tokens, 'dp', partner_pairs(n_dp, step))]
    all_to_all x4, waiting for transfers between devices: 31.8 us -> 21.6 us  [local(): incoming = lax.all_to_all(payload, 'ctx', 0, 0, tiled=True)]
    ppermute x0 -> x2, waiting for transfers between devices: none -> 6.14 us  [the longest x1 6.14 us: local(): came = lax.ppermute(attended[0], 'dp', partner_pairs(n_dp, step))]
    ppermute x3 -> x2, waiting for transfers between devices: 16.3 us -> 11.1 us  [local(): partial_out = lax.ppermute(partial_out, 'dp', partner_pairs(n_dp, step))]
    dot_general x0 -> x1, matrix products: none -> 4.82 us  [local(): jnp.dot(came, far_weight, preferred_element_type=jnp.float32)]
    dot_general x4 -> x3, matrix products: 12.9 us -> 9.21 us  [local(): jnp.dot(attended[0], out_weight, preferred_element_type=jnp.float32)]
  transfers between devices with their start and end apart: 10 -> 11, of which waited for: 7 -> 6; matrix products, arithmetic and copies ran while one was open for 20% -> 14% of each run, Pallas kernels for 14% -> 8%
where the time goes in v9:
time: 334 us
  waiting for transfers between devices  193 us (58%)
  matrix products  36.8 us (11%)
  Pallas kernels  35.8 us (11%)
  starting transfers between devices  26.5 us (8%)
  blocking collectives  14.4 us (4%)
  local copies, waits for them, and re-layouts  14.1 us (4%)
  other arithmetic  12.9 us (4%)
    ppermute x3, waiting for transfers between devices, local(): arrived[step] = lax.ppermute(own_tokens, 'dp', partner_pairs(n_dp, step))  154 us
    pallas_call x4, Pallas kernels, attend(): pl.pallas_call(kernel, out_shape=jax.ShapeDtypeStruct((clip_count, token_...  35.8 us
    dot_general x4, matrix products, local(): jnp.einsum('td,sdh->sth', tokens, qkv_weight, preferred_element_type=jnp....  22.8 us
    all_to_all x4, waiting for transfers between devices, local(): incoming = lax.all_to_all(payload, 'ctx', 0, 0, tiled=True)  21.6 us
    all_to_all x4, starting transfers between devices, local(): incoming = lax.all_to_all(payload, 'ctx', 0, 0, tiled=True)  18 us
    all_gather x1, blocking collectives, local(): lax.all_gather(table, 'ctx', axis=0, tiled=True).astype(jnp.int32)  14.4 us
    ppermute x2, waiting for transfers between devices, local(): partial_out = lax.ppermute(partial_out, 'dp', partner_pairs(n_dp, step))  11.1 us
    concatenate x4, other arithmetic, local(): key_values = jnp.concatenate([by_tile, incoming], axis=0)  10.2 us
  transfers between devices with their start and end apart: 11, of which 6 were waited for; matrix products, arithmetic and copies ran while one was open for 14% of the time, Pallas kernels for 8%

profile of v9, /device:TPU:0, one launch (start us, length us, event | category | flops | bytes accessed | tf_op | source)
XLA Modules:
  0.0 333.7 jit_solution(3158354771696568061)
XLA Ops:
  1.5 14.4 %all-gather = f32[8,4,11]{2,1,0:T(4,128)S(1)} all-gather(f32[1,4,11]{2,1,0:T(4,128)S(1)} %fusion.39), channel_id=1, replica_groups=mesh['dp'=4,'ctx'=8] {'ctx'}, dimensions={0}, use_global_device_ids=true | all-gather | bytes 1584 | tf_op jit(solution)/shard_map/all_gather | solution.py:110
  16.6 5.7 %fusion.31.q_ref = bf16[3,256,384]{2,1,0:T(8,128)(2,1)S(1)} fusion(bf16[3,3072,384]{2,1,0:T(8,128)(2,1)} %param.8, bf16[1,256,3072]{2,1,0:T(8,128)(2,1)} %param.7), kind=kOutput, calls=%fused_computation.32 | convolution fusion | flops 1812234240 | bytes 9240576 | tf_op jit(solution)/shard_map/td,sdh->sth/dot_general | solution.py:149
  25.1 3.7 %all-to-all-start = ((bf16[16,2,1,64,384]{4,3,2,1,0:T(8,128)(2,1)}), bf16[16,2,1,64,384]{4,3,2,1,0:T(8,128)(2,1)S(1)}, u32[]{:S(2)}, u32[]{:S(2)}) async-start(bf16[16,2,1,64,384]{4,3,2,1,0:T(8,128)(2,1)} %bitcast.13), calls=%async_computation | async-start | bytes 3145728 | tf_op jit(solution)/shard_map/all_to_all | solution.py:162
  32.0 35.3 %collective-permute-done = bf16[256,3072]{1,0:T(8,128)(2,1)} collective-permute-done((bf16[256,3072]{1,0:T(8,128)(2,1)}, bf16[256,3072]{1,0:T(8,128)(2,1)}, u32[]{:S(2)}, u32[]{:S(2)}) %collective-permute-start) | collective-permute-done | bytes 1572896 | tf_op jit(solution)/shard_map/ppermute | solution.py:136
  67.3 5.7 %fusion.28.q_ref = bf16[3,256,384]{2,1,0:T(8,128)(2,1)S(1)} fusion(bf16[3,3072,384]{2,1,0:T(8,128)(2,1)} %param.8, bf16[256,3072]{1,0:T(8,128)(2,1)} %collective-permute-done), kind=kOutput, calls=%fused_computation.31 | convolution fusion | flops 1812234240 | bytes 9240576 | tf_op jit(solution)/shard_map/td,sdh->sth/dot_general | solution.py:149
  75.8 5.0 %all-to-all-start.1 = ((bf16[16,2,1,64,384]{4,3,2,1,0:T(8,128)(2,1)}), bf16[16,2,1,64,384]{4,3,2,1,0:T(8,128)(2,1)}, u32[]{:S(2)}, u32[]{:S(2)}) async-start(bf16[16,2,1,64,384]{4,3,2,1,0:T(8,128)(2,1)} %bitcast.113), calls=%async_computation.1 | async-start | bytes 3145728 | tf_op jit(solution)/shard_map/all_to_all | solution.py:162
  84.2 16.3 %collective-permute-done.2 = bf16[256,3072]{1,0:T(8,128)(2,1)} collective-permute-done((bf16[256,3072]{1,0:T(8,128)(2,1)}, bf16[256,3072]{1,0:T(8,128)(2,1)}, u32[]{:S(2)}, u32[]{:S(2)}) %collective-permute-start.2) | collective-permute-done | bytes 1572896 | tf_op jit(solution)/shard_map/ppermute | solution.py:136
  100.5 5.7 %fusion.25.q_ref = bf16[3,256,384]{2,1,0:T(8,128)(2,1)S(1)} fusion(bf16[3,3072,384]{2,1,0:T(8,128)(2,1)} %param.8, bf16[256,3072]{1,0:T(8,128)(2,1)} %collective-permute-done.2), kind=kOutput, calls=%fused_computation.30 | convolution fusion | flops 1812234240 | bytes 9240576 | tf_op jit(solution)/shard_map/td,sdh->sth/dot_general | solution.py:149
  110.5 9.1 %shard_map.73 = bf16[1,256,384]{2,1,0:T(8,128)(2,1)} custom-call(s32[4,10]{1,0:T(4,128)} %add_select_fusion.2.pos_ref, s32[4]{0:T(128)} %count_ref.7, f32[4,3,10]{2,1,0:T(4,128)} %fusion.37.bias_ref, bf16[3,256,384]{2,1,0:T(8,128)(2,1)} %copy-done.2, ...), custom_call_target="tpu_custom_call" | custom-call | tf_op jit(solution)/shard_map/pallas_call | solution.py:80
  119.7 3.1 convolution_convert_fusion.3
  122.8 4.5 %all-to-all-start.2 = ((bf16[16,2,1,64,384]{4,3,2,1,0:T(8,128)(2,1)}), bf16[16,2,1,64,384]{4,3,2,1,0:T(8,128)(2,1)}, u32[]{:S(2)}, u32[]{:S(2)}) async-start(bf16[16,2,1,64,384]{4,3,2,1,0:T(8,128)(2,1)} %bitcast.114), calls=%async_computation.2 | async-start | bytes 3145728 | tf_op jit(solution)/shard_map/all_to_all | solution.py:162
  132.3 8.9 %shard_map.74 = bf16[1,256,384]{2,1,0:T(8,128)(2,1)} custom-call(s32[4,10]{1,0:T(4,128)} %add_select_fusion.2.pos_ref, s32[4]{0:T(128)} %count_ref.7, f32[4,3,10]{2,1,0:T(4,128)} %fusion.37.bias_ref, bf16[3,256,384]{2,1,0:T(8,128)(2,1)} %copy-done.3, ...), custom_call_target="tpu_custom_call" | custom-call | tf_op jit(solution)/shard_map/pallas_call | solution.py:80
  141.2 3.0 convolution_convert_fusion.2
  145.7 102.5 %collective-permute-done.4 = bf16[256,3072]{1,0:T(8,128)(2,1)} collective-permute-done((bf16[256,3072]{1,0:T(8,128)(2,1)}, bf16[256,3072]{1,0:T(8,128)(2,1)}, u32[]{:S(2)}, u32[]{:S(2)}) %collective-permute-start.4) | collective-permute-done | bytes 1572896 | tf_op jit(solution)/shard_map/ppermute | solution.py:136
  248.1 5.7 %fusion.22.q_ref = bf16[3,256,384]{2,1,0:T(8,128)(2,1)S(1)} fusion(bf16[3,3072,384]{2,1,0:T(8,128)(2,1)} %param.8, bf16[256,3072]{1,0:T(8,128)(2,1)} %collective-permute-done.4), kind=kOutput, calls=%fused_computation.29 | convolution fusion | flops 1812234240 | bytes 9240576 | tf_op jit(solution)/shard_map/td,sdh->sth/dot_general | solution.py:149
  256.6 4.8 %all-to-all-start.3 = ((bf16[16,2,1,64,384]{4,3,2,1,0:T(8,128)(2,1)}), bf16[16,2,1,64,384]{4,3,2,1,0:T(8,128)(2,1)}, u32[]{:S(2)}, u32[]{:S(2)}) async-start(bf16[16,2,1,64,384]{4,3,2,1,0:T(8,128)(2,1)} %bitcast.115), calls=%async_computation.3 | async-start | bytes 3145728 | tf_op jit(solution)/shard_map/all_to_all | solution.py:162
  264.3 8.9 %shard_map.75 = bf16[1,256,384]{2,1,0:T(8,128)(2,1)} custom-call(s32[4,10]{1,0:T(4,128)} %add_select_fusion.2.pos_ref, s32[4]{0:T(128)} %count_ref.7, f32[4,3,10]{2,1,0:T(4,128)} %fusion.37.bias_ref, bf16[3,256,384]{2,1,0:T(8,128)(2,1)} %copy-done.4, ...), custom_call_target="tpu_custom_call" | custom-call | tf_op jit(solution)/shard_map/pallas_call | solution.py:80
  273.2 3.1 convolution_convert_fusion.1
  277.8 21.6 %all-to-all-done.3 = bf16[16,2,1,64,384]{4,3,2,1,0:T(8,128)(2,1)} async-done(((bf16[16,2,1,64,384]{4,3,2,1,0:T(8,128)(2,1)}), bf16[16,2,1,64,384]{4,3,2,1,0:T(8,128)(2,1)}, u32[]{:S(2)}, u32[]{:S(2)}) %all-to-all-start.3) | async-done | bytes 1572896 | tf_op jit(solution)/shard_map/all_to_all | solution.py:162
  299.4 2.9 pad_maximum_fusion.3.refs_0_.refs_1_.refs_2_.refs_3_.refs_4_.refs_5_.refs_6_.refs_7_.refs_8_.refs_9_
  302.3 11.1 %collective-permute-done.3 = bf16[256,3072]{1,0:T(8,128)(2,1)} collective-permute-done((bf16[256,3072]{1,0:T(8,128)(2,1)}, bf16[256,3072]{1,0:T(8,128)(2,1)}, u32[]{:S(2)}, u32[]{:S(2)}) %collective-permute-start.3) | collective-permute-done | bytes 1572896 | tf_op jit(solution)/shard_map/ppermute | solution.py:179
  313.3 8.9 %shard_map.76 = bf16[1,256,384]{2,1,0:T(8,128)(2,1)} custom-call(s32[4,10]{1,0:T(4,128)} %add_select_fusion.2.pos_ref, s32[4]{0:T(128)} %count_ref.7, f32[4,3,10]{2,1,0:T(4,128)} %fusion.37.bias_ref, bf16[3,256,384]{2,1,0:T(8,128)(2,1)} %copy-done.5, ...), custom_call_target="tpu_custom_call" | custom-call | tf_op jit(solution)/shard_map/pallas_call | solution.py:80
  322.7 6.1 %collective-permute-done.6 = bf16[256,384]{1,0:T(8,128)(2,1)S(1)} collective-permute-done((bf16[256,384]{1,0:T(8,128)(2,1)}, bf16[256,384]{1,0:T(8,128)(2,1)S(1)}, u32[]{:S(2)}, u32[]{:S(2)}) %collective-permute-start.6) | collective-permute-done | bytes 196640 | tf_op jit(solution)/shard_map/ppermute | solution.py:169
  328.8 4.8 %fusion.1 = bf16[1,256,3072]{2,1,0:T(8,128)(2,1)} fusion(bf16[256,3072]{1,0:T(8,128)(2,1)} %collective-permute-done.3, bf16[256,3072]{1,0:T(8,128)(2,1)} %collective-permute-done.1, bf16[256,3072]{1,0:T(8,128)(2,1)S(1)} %copy-done.1, bf16[256,384]{1,0:T(8,128)(2,1)S(1)} %collective-permute-done.6, bf16[384,3072]{1,0:T(8,128)(2,1)} %collective-permute-done.5), kind=kOutput, calls=%fused_computation.16 | convolution fusion | flops 611057664 | bytes 8847360 | tf_op jit(solution)/shard_map/dot_general | solution.py:170
  (85 shorter events, 32.7 us)
Async XLA Ops:
  22.3 0.8 copy-start.2
  25.1 6.8 %copy-start.7 = (s32[4]{0:T(128)S(1)}, s32[4]{0:T(128)}, u32[]{:S(2)}) copy-start(s32[4]{0:T(128)} %count_ref.7) | copy-start | bytes 52
  25.1 6.9 %copy-start.6 = (s32[4,10]{1,0:T(4,128)S(1)}, s32[4,10]{1,0:T(4,128)}, u32[]{:S(2)}) copy-start(s32[4,10]{1,0:T(4,128)} %param.10) | copy-start | bytes 484
  25.1 6.9 %copy-start.8 = (s32[4,10]{1,0:T(4,128)S(1)}, s32[4,10]{1,0:T(4,128)}, u32[]{:S(2)}) copy-start(s32[4,10]{1,0:T(4,128)} %param.12) | copy-start | bytes 484
  25.1 42.2 %all-to-all-start = ((bf16[16,2,1,64,384]{4,3,2,1,0:T(8,128)(2,1)}), bf16[16,2,1,64,384]{4,3,2,1,0:T(8,128)(2,1)S(1)}, u32[]{:S(2)}, u32[]{:S(2)}) async-start(bf16[16,2,1,64,384]{4,3,2,1,0:T(8,128)(2,1)} %bitcast.13), calls=%async_computation | async-start | bytes 3145728 | tf_op jit(solution)/shard_map/all_to_all | solution.py:162
  28.8 38.5 %collective-permute-start = (bf16[256,3072]{1,0:T(8,128)(2,1)}, bf16[256,3072]{1,0:T(8,128)(2,1)}, u32[]{:S(2)}, u32[]{:S(2)}) collective-permute-start(bf16[256,3072]{1,0:T(8,128)(2,1)} %bitcast.124), channel_id=1, source_target_pairs={{0,24},{8,16},{16,8},{24,0},{1,25},{9,17},{17,9},{25,1},{2,26},{10... | collective-permute-start | bytes 4718600 | tf_op jit(solution)/shard_map/ppermute | solution.py:136
  31.3 69.2 %collective-permute-start.2 = (bf16[256,3072]{1,0:T(8,128)(2,1)}, bf16[256,3072]{1,0:T(8,128)(2,1)}, u32[]{:S(2)}, u32[]{:S(2)}) collective-permute-start(bf16[256,3072]{1,0:T(8,128)(2,1)} %bitcast.125), channel_id=1, source_target_pairs={{0,8},{8,0},{16,24},{24,16},{1,9},{9,1},{17,25},{25,17},{2,10},{10... | collective-permute-start | bytes 4718600 | tf_op jit(solution)/shard_map/ppermute | solution.py:136
  73.0 0.8 copy-start.3
  75.8 47.0 %all-to-all-start.1 = ((bf16[16,2,1,64,384]{4,3,2,1,0:T(8,128)(2,1)}), bf16[16,2,1,64,384]{4,3,2,1,0:T(8,128)(2,1)}, u32[]{:S(2)}, u32[]{:S(2)}) async-start(bf16[16,2,1,64,384]{4,3,2,1,0:T(8,128)(2,1)} %bitcast.113), calls=%async_computation.1 | async-start | bytes 3145728 | tf_op jit(solution)/shard_map/all_to_all | solution.py:162
  80.8 1.3 copy-start.9
  106.2 0.8 copy-start.4
  110.5 9.1 %copy-start = (bf16[384,3072]{1,0:T(8,128)(2,1)S(1)}, bf16[384,3072]{1,0:T(8,128)(2,1)}, u32[]{:S(2)}) copy-start(bf16[384,3072]{1,0:T(8,128)(2,1)} %param.9) | copy-start | bytes 7077892
  122.8 133.9 %all-to-all-start.2 = ((bf16[16,2,1,64,384]{4,3,2,1,0:T(8,128)(2,1)}), bf16[16,2,1,64,384]{4,3,2,1,0:T(8,128)(2,1)}, u32[]{:S(2)}, u32[]{:S(2)}) async-start(bf16[16,2,1,64,384]{4,3,2,1,0:T(8,128)(2,1)} %bitcast.114), calls=%async_computation.2 | async-start | bytes 3145728 | tf_op jit(solution)/shard_map/all_to_all | solution.py:162
  127.3 129.4 %collective-permute-start.5 = (bf16[384,3072]{1,0:T(8,128)(2,1)S(1)}, bf16[384,3072]{1,0:T(8,128)(2,1)}, u32[]{:S(2)}, u32[]{:S(2)}) collective-permute-start(bf16[384,3072]{1,0:T(8,128)(2,1)S(1)} %copy-done), channel_id=1, source_target_pairs={{0,16},{8,24},{16,0},{24,8},{1,17},{9,25},{17,1},{25,9},{2,18},{10... | collective-permute-start | bytes 7077896 | tf_op jit(solution)/shard_map/ppermute | solution.py:139
  127.8 120.3 %collective-permute-start.4 = (bf16[256,3072]{1,0:T(8,128)(2,1)}, bf16[256,3072]{1,0:T(8,128)(2,1)}, u32[]{:S(2)}, u32[]{:S(2)}) collective-permute-start(bf16[256,3072]{1,0:T(8,128)(2,1)} %bitcast.126), channel_id=1, source_target_pairs={{0,16},{8,24},{16,0},{24,8},{1,17},{9,25},{17,1},{25,9},{2,18},{10... | collective-permute-start | bytes 4718600 | tf_op jit(solution)/shard_map/ppermute | solution.py:136
  144.2 112.4 %collective-permute-start.1 = (bf16[256,3072]{1,0:T(8,128)(2,1)}, bf16[256,3072]{1,0:T(8,128)(2,1)}, u32[]{:S(2)}, u32[]{:S(2)}) collective-permute-start(bf16[256,3072]{1,0:T(8,128)(2,1)} %convolution_convert_fusion.2), channel_id=1, source_target_pairs={{0,24},{8,16},{16,8},{24,0},{1,25},{9,17},{17,9},{25,1},{2,26},{10... | collective-permute-start | bytes 4718600 | tf_op jit(solution)/shard_map/ppermute | solution.py:179
  253.8 0.9 copy-start.5
  256.6 42.7 %all-to-all-start.3 = ((bf16[16,2,1,64,384]{4,3,2,1,0:T(8,128)(2,1)}), bf16[16,2,1,64,384]{4,3,2,1,0:T(8,128)(2,1)}, u32[]{:S(2)}, u32[]{:S(2)}) async-start(bf16[16,2,1,64,384]{4,3,2,1,0:T(8,128)(2,1)} %bitcast.115), calls=%async_computation.3 | async-start | bytes 3145728 | tf_op jit(solution)/shard_map/all_to_all | solution.py:162
  276.3 37.1 %collective-permute-start.3 = (bf16[256,3072]{1,0:T(8,128)(2,1)}, bf16[256,3072]{1,0:T(8,128)(2,1)}, u32[]{:S(2)}, u32[]{:S(2)}) collective-permute-start(bf16[256,3072]{1,0:T(8,128)(2,1)} %convolution_convert_fusion.1), channel_id=1, source_target_pairs={{0,8},{8,0},{16,24},{24,16},{1,9},{9,1},{17,25},{25,17},{2,10},{10... | collective-permute-start | bytes 4718600 | tf_op jit(solution)/shard_map/ppermute | solution.py:179
  302.3 26.6 %copy-start.1 = (bf16[256,3072]{1,0:T(8,128)(2,1)S(1)}, bf16[256,3072]{1,0:T(8,128)(2,1)}, u32[]{:S(2)}) copy-start(bf16[256,3072]{1,0:T(8,128)(2,1)} %convolution_convert_fusion.3) | copy-start | bytes 4718596
  322.2 6.6 %collective-permute-start.6 = (bf16[256,384]{1,0:T(8,128)(2,1)}, bf16[256,384]{1,0:T(8,128)(2,1)S(1)}, u32[]{:S(2)}, u32[]{:S(2)}) collective-permute-start(bf16[256,384]{1,0:T(8,128)(2,1)} %bitcast.120), channel_id=1, source_target_pairs={{0,16},{8,24},{16,0},{24,8},{1,17},{9,25},{17,1},{25,9},{2,18},{10... | collective-permute-start | bytes 589832 | tf_op jit(solution)/shard_map/ppermute | solution.py:169

commit v10 on v8

--- a/solution.py
+++ b/solution.py
@@ -153,7 +153,10 @@
             payload, _ = lax.optimization_barrier((payload, partials[index - 2]))
         if index == len(order) - 1 and len(sent) >= 2:
             payload, _ = lax.optimization_barrier((payload, sent[-3]))
-        incoming = lax.all_to_all(payload, "ctx", 0, 0, tiled=True)
+        incoming = jnp.concatenate(
+            [lax.all_to_all(payload[:, part:part + 1], "ctx", 0, 0, tiled=True) for part in range(2)],
+            axis=1,
+        )
         received.append(incoming)
         key_values = jnp.concatenate([by_tile, incoming], axis=0)
         if index == len(order) - 1 and len(sent) >= 2:

time: 247 us -> 290 us (1.17)
  blocking collectives: 12.9 us -> 36.3 us
  local copies, waits for them, and re-layouts: 14.1 us -> 30.6 us
  starting transfers between devices: 31.3 us -> 44.1 us
  waiting for transfers between devices: 102 us -> 90.7 us
    all_to_all x4 -> x7, waiting for transfers between devices: 31.8 us -> 71.1 us  [local(): lax.all_to_all(payload[:, part:part + 1], 'ctx', 0, 0, tiled=True)]
    ppermute x3, waiting for transfers between devices: 53.6 us -> 19.5 us  [local(): arrived[step] = lax.ppermute(own_tokens, 'dp', partner_pairs(n_dp, step))]
    all_to_all x0 -> x1, blocking collectives: none -> 23.4 us  [local(): lax.all_to_all(payload[:, part:part + 1], 'ctx', 0, 0, tiled=True)]
    ppermute x3, waiting for transfers between devices: 16.3 us -> 0.01 us  [local(): partial_out = lax.ppermute(partial_out, 'dp', partner_pairs(n_dp, step))]
    all_to_all x4 -> x7, starting transfers between devices: 18.9 us -> 31.7 us  [local(): lax.all_to_all(payload[:, part:part + 1], 'ctx', 0, 0, tiled=True)]
    slice x0 -> x4, local copies, waits for them, and re-layouts: none -> 8.12 us  [local(): payload[:, part:part + 1]]
    concatenate x0 -> x2, local copies, waits for them, and re-layouts: none -> 4.25 us  [local(): jnp.concatenate([lax.all_to_all(payload[:, part:part + 1], 'ctx', 0, 0, t...]
    unnamed x21 -> x35, local copies, waits for them, and re-layouts: 3.22 us -> 6.34 us
  transfers between devices with their start and end apart: 10 -> 13, of which waited for: 7 -> 6; matrix products, arithmetic and copies ran while one was open for 20% -> 22% of each run, Pallas kernels for 14% -> 12%
where the time goes in v10:
time: 290 us; the launch traced here: 288 us
  waiting for transfers between devices  90.7 us (31%)
  starting transfers between devices  44.1 us (15%)
  blocking collectives  36.3 us (13%)
  matrix products  35.8 us (12%)
  Pallas kernels  35.8 us (12%)
  local copies, waits for them, and re-layouts  30.6 us (11%)
  other arithmetic  14.8 us (5%)
    all_to_all x7, waiting for transfers between devices, local(): lax.all_to_all(payload[:, part:part + 1], 'ctx', 0, 0, tiled=True)  71.1 us
    pallas_call x4, Pallas kernels, attend(): pl.pallas_call(kernel, out_shape=jax.ShapeDtypeStruct((clip_count, token_...  35.8 us
    all_to_all x7, starting transfers between devices, local(): lax.all_to_all(payload[:, part:part + 1], 'ctx', 0, 0, tiled=True)  31.7 us
    all_to_all x1, blocking collectives, local(): lax.all_to_all(payload[:, part:part + 1], 'ctx', 0, 0, tiled=True)  23.4 us
    dot_general x4, matrix products, local(): jnp.einsum('td,sdh->sth', tokens, qkv_weight, preferred_element_type=jnp....  22.8 us
    ppermute x3, waiting for transfers between devices, local(): arrived[step] = lax.ppermute(own_tokens, 'dp', partner_pairs(n_dp, step))  19.5 us
    dot_general x4, matrix products, local(): jnp.dot(attended[0], out_weight, preferred_element_type=jnp.float32)  13 us
    all_gather x1, blocking collectives, local(): lax.all_gather(table, 'ctx', axis=0, tiled=True).astype(jnp.int32)  12.9 us
  transfers between devices with their start and end apart: 13, of which 6 were waited for; matrix products, arithmetic and copies ran while one was open for 22% of the time, Pallas kernels for 12%

profile of v10, /device:TPU:0, one launch (start us, length us, event | category | flops | bytes accessed | tf_op | source)
XLA Modules:
  0.0 288.5 jit_solution(7284107378416558828)
XLA Ops:
  0.0 3.9 %collective-permute-start = (bf16[256,3072]{1,0:T(8,128)(2,1)}, bf16[256,3072]{1,0:T(8,128)(2,1)}, u32[]{:S(2)}, u32[]{:S(2)}) collective-permute-start(bf16[256,3072]{1,0:T(8,128)(2,1)} %bitcast.127), channel_id=1, source_target_pairs={{0,24},{8,16},{16,8},{24,0},{1,25},{9,17},{17,9},{25,1},{2,26},{10... | collective-permute-start | bytes 4718600 | tf_op jit(solution)/shard_map/ppermute | solution.py:136
  5.4 12.9 %all-gather = f32[8,4,11]{2,1,0:T(4,128)S(1)} all-gather(f32[1,4,11]{2,1,0:T(4,128)S(1)} %fusion.42), channel_id=1, replica_groups=mesh['dp'=4,'ctx'=8] {'ctx'}, dimensions={0}, use_global_device_ids=true | all-gather | bytes 1584 | tf_op jit(solution)/shard_map/all_gather | solution.py:110
  19.1 19.5 %collective-permute-done = bf16[256,3072]{1,0:T(8,128)(2,1)} collective-permute-done((bf16[256,3072]{1,0:T(8,128)(2,1)}, bf16[256,3072]{1,0:T(8,128)(2,1)}, u32[]{:S(2)}, u32[]{:S(2)}) %collective-permute-start) | collective-permute-done | bytes 1572896 | tf_op jit(solution)/shard_map/ppermute | solution.py:136
  38.6 5.7 %fusion.31.q_ref = bf16[3,256,384]{2,1,0:T(8,128)(2,1)S(1)} fusion(bf16[3,3072,384]{2,1,0:T(8,128)(2,1)} %param.8, bf16[256,3072]{1,0:T(8,128)(2,1)} %collective-permute-done), kind=kOutput, calls=%fused_computation.32 | convolution fusion | flops 1812234240 | bytes 9240576 | tf_op jit(solution)/shard_map/td,sdh->sth/dot_general | solution.py:145
  49.8 5.2 %all-to-all-start = ((bf16[16,1,1,64,384]{4,3,2,1,0:T(8,128)(2,1)}), bf16[16,1,1,64,384]{4,3,2,1,0:T(8,128)(2,1)S(1)}, u32[]{:S(2)}, u32[]{:S(2)}) async-start(bf16[16,1,1,64,384]{4,3,2,1,0:T(8,128)(2,1)} %get-tuple-element.26), calls=%async_computation | async-start | bytes 1572864 | tf_op jit(solution)/shard_map/all_to_all | solution.py:157
  56.5 19.5 %all-to-all-done = bf16[16,1,1,64,384]{4,3,2,1,0:T(8,128)(2,1)S(1)} async-done(((bf16[16,1,1,64,384]{4,3,2,1,0:T(8,128)(2,1)}), bf16[16,1,1,64,384]{4,3,2,1,0:T(8,128)(2,1)S(1)}, u32[]{:S(2)}, u32[]{:S(2)}) %all-to-all-start) | async-done | bytes 786464 | tf_op jit(solution)/shard_map/all_to_all | solution.py:157
  76.0 4.2 %all-to-all-start.1 = ((bf16[16,1,1,64,384]{4,3,2,1,0:T(8,128)(2,1)}), bf16[16,1,1,64,384]{4,3,2,1,0:T(8,128)(2,1)}, u32[]{:S(2)}, u32[]{:S(2)}) async-start(bf16[16,1,1,64,384]{4,3,2,1,0:T(8,128)(2,1)} %get-tuple-element.25), calls=%async_computation.1 | async-start | bytes 1572864 | tf_op jit(solution)/shard_map/all_to_all | solution.py:157
  84.7 16.5 %all-to-all-done.1 = bf16[16,1,1,64,384]{4,3,2,1,0:T(8,128)(2,1)} async-done(((bf16[16,1,1,64,384]{4,3,2,1,0:T(8,128)(2,1)}), bf16[16,1,1,64,384]{4,3,2,1,0:T(8,128)(2,1)}, u32[]{:S(2)}, u32[]{:S(2)}) %all-to-all-start.1) | async-done | bytes 786464 | tf_op jit(solution)/shard_map/all_to_all | solution.py:157
  103.3 5.7 %fusion.28.q_ref = bf16[3,256,384]{2,1,0:T(8,128)(2,1)S(1)} fusion(bf16[3,3072,384]{2,1,0:T(8,128)(2,1)} %param.8, bf16[256,3072]{1,0:T(8,128)(2,1)} %collective-permute-done.2), kind=kOutput, calls=%fused_computation.31 | convolution fusion | flops 1812234240 | bytes 9240576 | tf_op jit(solution)/shard_map/td,sdh->sth/dot_general | solution.py:145
  114.5 4.4 %all-to-all-start.2 = ((bf16[16,1,1,64,384]{4,3,2,1,0:T(8,128)(2,1)}), bf16[16,1,1,64,384]{4,3,2,1,0:T(8,128)(2,1)}, u32[]{:S(2)}, u32[]{:S(2)}) async-start(bf16[16,1,1,64,384]{4,3,2,1,0:T(8,128)(2,1)} %get-tuple-element.22), calls=%async_computation.2 | async-start | bytes 1572864 | tf_op jit(solution)/shard_map/all_to_all | solution.py:157
  122.3 17.6 %all-to-all-done.2 = bf16[16,1,1,64,384]{4,3,2,1,0:T(8,128)(2,1)} async-done(((bf16[16,1,1,64,384]{4,3,2,1,0:T(8,128)(2,1)}), bf16[16,1,1,64,384]{4,3,2,1,0:T(8,128)(2,1)}, u32[]{:S(2)}, u32[]{:S(2)}) %all-to-all-start.2) | async-done | bytes 786464 | tf_op jit(solution)/shard_map/all_to_all | solution.py:157
  139.9 4.2 %all-to-all-start.3 = ((bf16[16,1,1,64,384]{4,3,2,1,0:T(8,128)(2,1)}), bf16[16,1,1,64,384]{4,3,2,1,0:T(8,128)(2,1)}, u32[]{:S(2)}, u32[]{:S(2)}) async-start(bf16[16,1,1,64,384]{4,3,2,1,0:T(8,128)(2,1)} %get-tuple-element.21), calls=%async_computation.3 | async-start | bytes 1572864 | tf_op jit(solution)/shard_map/all_to_all | solution.py:157
  144.1 5.7 %fusion.25.q_ref = bf16[3,256,384]{2,1,0:T(8,128)(2,1)S(1)} fusion(bf16[3,3072,384]{2,1,0:T(8,128)(2,1)} %param.8, bf16[256,3072]{1,0:T(8,128)(2,1)} %collective-permute-done.4), kind=kOutput, calls=%fused_computation.30 | convolution fusion | flops 1812234240 | bytes 9240576 | tf_op jit(solution)/shard_map/td,sdh->sth/dot_general | solution.py:145
  155.5 9.0 %shard_map.73 = bf16[1,256,384]{2,1,0:T(8,128)(2,1)} custom-call(s32[4,10]{1,0:T(4,128)} %add_select_fusion.2.pos_ref, s32[4]{0:T(128)} %count_ref.7, f32[4,3,10]{2,1,0:T(4,128)} %fusion.40.bias_ref, bf16[3,256,384]{2,1,0:T(8,128)(2,1)} %copy-done.4, ...), custom_call_target="tpu_custom_call" | custom-call | tf_op jit(solution)/shard_map/pallas_call | solution.py:80
  169.1 4.7 %all-to-all-start.5 = ((bf16[16,1,1,64,384]{4,3,2,1,0:T(8,128)(2,1)}), bf16[16,1,1,64,384]{4,3,2,1,0:T(8,128)(2,1)}, u32[]{:S(2)}, u32[]{:S(2)}) async-start(bf16[16,1,1,64,384]{4,3,2,1,0:T(8,128)(2,1)} %get-tuple-element.24), calls=%async_computation.5 | async-start | bytes 1572864 | tf_op jit(solution)/shard_map/all_to_all | solution.py:157
  180.4 14.4 %all-to-all-done.5 = bf16[16,1,1,64,384]{4,3,2,1,0:T(8,128)(2,1)} async-done(((bf16[16,1,1,64,384]{4,3,2,1,0:T(8,128)(2,1)}), bf16[16,1,1,64,384]{4,3,2,1,0:T(8,128)(2,1)}, u32[]{:S(2)}, u32[]{:S(2)}) %all-to-all-start.5) | async-done | bytes 786464 | tf_op jit(solution)/shard_map/all_to_all | solution.py:157
  194.9 4.4 %all-to-all-start.4 = ((bf16[16,1,1,64,384]{4,3,2,1,0:T(8,128)(2,1)}), bf16[16,1,1,64,384]{4,3,2,1,0:T(8,128)(2,1)}, u32[]{:S(2)}, u32[]{:S(2)}) async-start(bf16[16,1,1,64,384]{4,3,2,1,0:T(8,128)(2,1)} %get-tuple-element.23), calls=%async_computation.4 | async-start | bytes 1572864 | tf_op jit(solution)/shard_map/all_to_all | solution.py:157
  202.2 8.9 %shard_map.74 = bf16[1,256,384]{2,1,0:T(8,128)(2,1)} custom-call(s32[4,10]{1,0:T(4,128)} %add_select_fusion.2.pos_ref, s32[4]{0:T(128)} %count_ref.7, f32[4,3,10]{2,1,0:T(4,128)} %fusion.40.bias_ref, bf16[3,256,384]{2,1,0:T(8,128)(2,1)} %copy-done.5, ...), custom_call_target="tpu_custom_call" | custom-call | tf_op jit(solution)/shard_map/pallas_call | solution.py:80
  211.1 5.7 %fusion.22.q_ref = bf16[3,256,384]{2,1,0:T(8,128)(2,1)S(1)} fusion(bf16[3,3072,384]{2,1,0:T(8,128)(2,1)} %param.8, bf16[256,3072]{1,0:T(8,128)(2,1)} %bitcast.130), kind=kOutput, calls=%fused_computation.29 | convolution fusion | flops 1812234240 | bytes 9240576 | tf_op jit(solution)/shard_map/td,sdh->sth/dot_general | solution.py:145
  223.1 4.6 %all-to-all-start.7 = ((bf16[16,1,1,64,384]{4,3,2,1,0:T(8,128)(2,1)}), bf16[16,1,1,64,384]{4,3,2,1,0:T(8,128)(2,1)}, u32[]{:S(2)}, u32[]{:S(2)}) async-start(bf16[16,1,1,64,384]{4,3,2,1,0:T(8,128)(2,1)} %get-tuple-element.20), calls=%async_computation.7 | async-start | bytes 1572864 | tf_op jit(solution)/shard_map/all_to_all | solution.py:157
  232.2 8.9 %shard_map.75 = bf16[1,256,384]{2,1,0:T(8,128)(2,1)} custom-call(s32[4,10]{1,0:T(4,128)} %add_select_fusion.2.pos_ref, s32[4]{0:T(128)} %count_ref.7, f32[4,3,10]{2,1,0:T(4,128)} %fusion.40.bias_ref, bf16[3,256,384]{2,1,0:T(8,128)(2,1)} %copy-done.6, ...), custom_call_target="tpu_custom_call" | custom-call | tf_op jit(solution)/shard_map/pallas_call | solution.py:80
  248.8 23.4 %all_to_all.40 = bf16[16,1,1,64,384]{4,3,2,1,0:T(8,128)(2,1)S(1)} all-to-all(bf16[16,1,1,64,384]{4,3,2,1,0:T(8,128)(2,1)S(1)} %copy-done.3), channel_id=1, replica_groups=mesh['dp'=4,'ctx'=8] {'ctx'}, dimensions={0} | all-to-all | bytes 1572864 | tf_op jit(solution)/shard_map/all_to_all | solution.py:157
  274.9 8.9 %shard_map.76 = bf16[1,256,384]{2,1,0:T(8,128)(2,1)} custom-call(s32[4,10]{1,0:T(4,128)} %add_select_fusion.2.pos_ref, s32[4]{0:T(128)} %count_ref.7, f32[4,3,10]{2,1,0:T(4,128)} %fusion.40.bias_ref, bf16[3,256,384]{2,1,0:T(8,128)(2,1)} %copy-done.7, ...), custom_call_target="tpu_custom_call" | custom-call | tf_op jit(solution)/shard_map/pallas_call | solution.py:80
  283.9 4.6 %fusion.1 = bf16[1,256,3072]{2,1,0:T(8,128)(2,1)} fusion(bf16[256,3072]{1,0:T(8,128)(2,1)} %collective-permute-done.5, bf16[256,3072]{1,0:T(8,128)(2,1)} %collective-permute-done.3, bf16[256,3072]{1,0:T(8,128)(2,1)} %collective-permute-done.1, bf16[384,3072]{1,0:T(8,128)(2,1)S(1)} %copy-done, bf16[1,256,384]{2,1,0:T(8,128)(2,1)} %shard_map.76), kind=kOutput, calls=%fused_computation.16 | convolution fusion | flops 611057664 | bytes 8847360 | tf_op jit(solution)/shard_map/dot_general | solution.py:165
  (109 shorter events, 65.5 us)
Async XLA Ops:
  0.0 164.5 %copy-start = (bf16[384,3072]{1,0:T(8,128)(2,1)S(1)}, bf16[384,3072]{1,0:T(8,128)(2,1)}, u32[]{:S(2)}) copy-start(bf16[384,3072]{1,0:T(8,128)(2,1)} %param.9) | copy-start | bytes 7077892
  0.0 38.6 %collective-permute-start = (bf16[256,3072]{1,0:T(8,128)(2,1)}, bf16[256,3072]{1,0:T(8,128)(2,1)}, u32[]{:S(2)}, u32[]{:S(2)}) collective-permute-start(bf16[256,3072]{1,0:T(8,128)(2,1)} %bitcast.127), channel_id=1, source_target_pairs={{0,24},{8,16},{16,8},{24,0},{1,25},{9,17},{17,9},{25,1},{2,26},{10... | collective-permute-start | bytes 4718600 | tf_op jit(solution)/shard_map/ppermute | solution.py:136
  49.8 32.0 %copy-start.11 = (s32[4,10]{1,0:T(4,128)S(1)}, s32[4,10]{1,0:T(4,128)}, u32[]{:S(2)}) copy-start(s32[4,10]{1,0:T(4,128)} %param.12) | copy-start | bytes 484
  49.8 32.6 %copy-start.9 = (s32[4,10]{1,0:T(4,128)S(1)}, s32[4,10]{1,0:T(4,128)}, u32[]{:S(2)}) copy-start(s32[4,10]{1,0:T(4,128)} %param.10) | copy-start | bytes 484
  49.8 26.2 %all-to-all-start = ((bf16[16,1,1,64,384]{4,3,2,1,0:T(8,128)(2,1)}), bf16[16,1,1,64,384]{4,3,2,1,0:T(8,128)(2,1)S(1)}, u32[]{:S(2)}, u32[]{:S(2)}) async-start(bf16[16,1,1,64,384]{4,3,2,1,0:T(8,128)(2,1)} %get-tuple-element.26), calls=%async_computation | async-start | bytes 1572864 | tf_op jit(solution)/shard_map/all_to_all | solution.py:157
  55.0 48.3 %collective-permute-start.2 = (bf16[256,3072]{1,0:T(8,128)(2,1)}, bf16[256,3072]{1,0:T(8,128)(2,1)}, u32[]{:S(2)}, u32[]{:S(2)}) collective-permute-start(bf16[256,3072]{1,0:T(8,128)(2,1)} %bitcast.128), channel_id=1, source_target_pairs={{0,8},{8,0},{16,24},{24,16},{1,9},{9,1},{17,25},{25,17},{2,10},{10... | collective-permute-start | bytes 4718600 | tf_op jit(solution)/shard_map/ppermute | solution.py:136
  76.0 25.2 %all-to-all-start.1 = ((bf16[16,1,1,64,384]{4,3,2,1,0:T(8,128)(2,1)}), bf16[16,1,1,64,384]{4,3,2,1,0:T(8,128)(2,1)}, u32[]{:S(2)}, u32[]{:S(2)}) async-start(bf16[16,1,1,64,384]{4,3,2,1,0:T(8,128)(2,1)} %get-tuple-element.25), calls=%async_computation.1 | async-start | bytes 1572864 | tf_op jit(solution)/shard_map/all_to_all | solution.py:157
  80.2 42.1 %collective-permute-start.4 = (bf16[256,3072]{1,0:T(8,128)(2,1)}, bf16[256,3072]{1,0:T(8,128)(2,1)}, u32[]{:S(2)}, u32[]{:S(2)}) collective-permute-start(bf16[256,3072]{1,0:T(8,128)(2,1)} %bitcast.129), channel_id=1, source_target_pairs={{0,16},{8,24},{16,0},{24,8},{1,17},{9,25},{17,1},{25,9},{2,18},{10... | collective-permute-start | bytes 4718600 | tf_op jit(solution)/shard_map/ppermute | solution.py:136
  114.5 4.4 %copy-start.10 = (s32[4]{0:T(128)S(1)}, s32[4]{0:T(128)}, u32[]{:S(2)}) copy-start(s32[4]{0:T(128)} %count_ref.7) | copy-start | bytes 52
  114.5 4.5 %copy-start.12 = (s32[8,4]{0,1:T(4,128)S(1)}, s32[8,4]{0,1:T(4,128)}, u32[]{:S(2)}) copy-start(s32[8,4]{0,1:T(4,128)} %iota_add_fusion) | copy-start | bytes 388
  114.5 4.7 %copy-start.14 = (s32[40]{0:T(128)S(1)}, s32[40]{0:T(128)}, u32[]{:S(2)}) copy-start(s32[40]{0:T(128)} %reshape.125) | copy-start | bytes 484
  114.5 4.7 %copy-start.15 = (s32[40]{0:T(128)S(1)}, s32[40]{0:T(128)}, u32[]{:S(2)}) copy-start(s32[40]{0:T(128)} %reshape.117) | copy-start | bytes 484
  114.5 5.6 %copy-start.13 = (f32[3,343]{1,0:T(4,128)S(1)}, f32[3,343]{1,0:T(4,128)}, u32[]{:S(2)}) copy-start(f32[3,343]{1,0:T(4,128)} %param.13) | copy-start | bytes 12352
  114.5 25.4 %all-to-all-start.2 = ((bf16[16,1,1,64,384]{4,3,2,1,0:T(8,128)(2,1)}), bf16[16,1,1,64,384]{4,3,2,1,0:T(8,128)(2,1)}, u32[]{:S(2)}, u32[]{:S(2)}) async-start(bf16[16,1,1,64,384]{4,3,2,1,0:T(8,128)(2,1)} %get-tuple-element.22), calls=%async_computation.2 | async-start | bytes 1572864 | tf_op jit(solution)/shard_map/all_to_all | solution.py:157
  139.9 29.2 %all-to-all-start.3 = ((bf16[16,1,1,64,384]{4,3,2,1,0:T(8,128)(2,1)}), bf16[16,1,1,64,384]{4,3,2,1,0:T(8,128)(2,1)}, u32[]{:S(2)}, u32[]{:S(2)}) async-start(bf16[16,1,1,64,384]{4,3,2,1,0:T(8,128)(2,1)} %get-tuple-element.21), calls=%async_computation.3 | async-start | bytes 1572864 | tf_op jit(solution)/shard_map/all_to_all | solution.py:157
  164.5 3.2 %copy-start.1 = (bf16[16,2,64,384]{3,2,1,0:T(8,128)(2,1)S(1)}, bf16[16,2,64,384]{3,2,1,0:T(8,128)(2,1)}, u32[]{:S(2)}) copy-start(bf16[16,2,64,384]{3,2,1,0:T(8,128)(2,1)} %gather_fusion.4) | copy-start | bytes 4718596
  169.1 25.8 %all-to-all-start.5 = ((bf16[16,1,1,64,384]{4,3,2,1,0:T(8,128)(2,1)}), bf16[16,1,1,64,384]{4,3,2,1,0:T(8,128)(2,1)}, u32[]{:S(2)}, u32[]{:S(2)}) async-start(bf16[16,1,1,64,384]{4,3,2,1,0:T(8,128)(2,1)} %get-tuple-element.24), calls=%async_computation.5 | async-start | bytes 1572864 | tf_op jit(solution)/shard_map/all_to_all | solution.py:157
  173.8 48.0 %collective-permute-start.1 = (bf16[256,3072]{1,0:T(8,128)(2,1)}, bf16[256,3072]{1,0:T(8,128)(2,1)}, u32[]{:S(2)}, u32[]{:S(2)}) collective-permute-start(bf16[256,3072]{1,0:T(8,128)(2,1)} %convolution_convert_fusion.3), channel_id=1, source_target_pairs={{0,24},{8,16},{16,8},{24,0},{1,25},{9,17},{17,9},{25,1},{2,26},{10... | collective-permute-start | bytes 4718600 | tf_op jit(solution)/shard_map/ppermute | solution.py:170
  194.9 28.3 %all-to-all-start.4 = ((bf16[16,1,1,64,384]{4,3,2,1,0:T(8,128)(2,1)}), bf16[16,1,1,64,384]{4,3,2,1,0:T(8,128)(2,1)}, u32[]{:S(2)}, u32[]{:S(2)}) async-start(bf16[16,1,1,64,384]{4,3,2,1,0:T(8,128)(2,1)} %get-tuple-element.23), calls=%async_computation.4 | async-start | bytes 1572864 | tf_op jit(solution)/shard_map/all_to_all | solution.py:157
  219.6 2.2 copy-start.2
  223.1 25.7 %all-to-all-start.7 = ((bf16[16,1,1,64,384]{4,3,2,1,0:T(8,128)(2,1)}), bf16[16,1,1,64,384]{4,3,2,1,0:T(8,128)(2,1)}, u32[]{:S(2)}, u32[]{:S(2)}) async-start(bf16[16,1,1,64,384]{4,3,2,1,0:T(8,128)(2,1)} %get-tuple-element.20), calls=%async_computation.7 | async-start | bytes 1572864 | tf_op jit(solution)/shard_map/all_to_all | solution.py:157
  227.7 47.2 %collective-permute-start.3 = (bf16[256,3072]{1,0:T(8,128)(2,1)}, bf16[256,3072]{1,0:T(8,128)(2,1)}, u32[]{:S(2)}, u32[]{:S(2)}) collective-permute-start(bf16[256,3072]{1,0:T(8,128)(2,1)} %convolution_convert_fusion.2), channel_id=1, source_target_pairs={{0,8},{8,0},{16,24},{24,16},{1,9},{9,1},{17,25},{25,17},{2,10},{10... | collective-permute-start | bytes 4718600 | tf_op jit(solution)/shard_map/ppermute | solution.py:170
  241.1 7.7 %copy-start.3 = (bf16[16,1,1,64,384]{4,3,2,1,0:T(8,128)(2,1)S(1)}, bf16[16,1,1,64,384]{4,3,2,1,0:T(8,128)(2,1)}, u32[]{:S(2)}) copy-start(bf16[16,1,1,64,384]{4,3,2,1,0:T(8,128)(2,1)} %get-tuple-element.19) | copy-start | bytes 2359300
  244.3 39.6 %collective-permute-start.5 = (bf16[256,3072]{1,0:T(8,128)(2,1)}, bf16[256,3072]{1,0:T(8,128)(2,1)}, u32[]{:S(2)}, u32[]{:S(2)}) collective-permute-start(bf16[256,3072]{1,0:T(8,128)(2,1)} %convolution_convert_fusion.1), channel_id=1, source_target_pairs={{0,16},{8,24},{16,0},{24,8},{1,17},{9,25},{17,1},{25,9},{2,18},{10... | collective-permute-start | bytes 4718600 | tf_op jit(solution)/shard_map/ppermute | solution.py:170
  (5 other events, 5.2 us)

commit v11 on v8

--- a/solution.py
+++ b/solution.py
@@ -28,67 +28,72 @@
     return first.astype(jnp.int32), second.astype(jnp.int32)
 
 
-def attention_kernel(pos_ref, count_ref, bias_ref, q_ref, *refs, heads, head_size, scale):
-    kv_refs = refs[:KMAX]
-    out_ref = refs[KMAX]
+def attention_kernel(pos_ref, count_ref, bias_ref, q_ref, own_ref, far_ref, out_ref, *, heads, head_size, scale):
     tile = pl.program_id(0)
+    own_tiles = own_ref.shape[0]
     live_count = count_ref[tile]
-    queries = q_ref[...]
-    clip_count = queries.shape[0]
+    queries = q_ref[0]
+    picks = []
+    for slot in range(KMAX):
+        where = pos_ref[tile, slot]
+        picks.append((
+            where < own_tiles,
+            jnp.minimum(where, own_tiles - 1),
+            jnp.maximum(where - own_tiles, 0),
+        ))
+
+    def rows(part, slot, cols):
+        mine, near, far = picks[slot]
+        return jnp.where(mine, own_ref[near, part, 0, :, cols], far_ref[far, part, 0, :, cols])
+
     for head in range(heads):
-        cols = slice(head * head_size, (head + 1) * head_size)
-        q_head = queries[:, :, cols]
+        cols = pl.ds(head * head_size, head_size)
+        q_head = queries[:, head * head_size:(head + 1) * head_size]
         scores = []
         for slot in range(KMAX):
-            k_head = kv_refs[slot][0, :, :, cols]
             s = lax.dot_general(
-                q_head, k_head, (((2,), (2,)), ((0,), (0,))), preferred_element_type=jnp.float32
+                q_head, rows(0, slot, cols), (((1,), (1,)), ((), ())),
+                preferred_element_type=jnp.float32,
             )
             s = s * scale + bias_ref[tile, head, slot]
             s = jnp.where(slot < live_count, s, -1e30)
             scores.append(s)
-        row_max = scores[0].max(axis=2, keepdims=True)
+        row_max = scores[0].max(axis=1, keepdims=True)
         for s in scores[1:]:
-            row_max = jnp.maximum(row_max, s.max(axis=2, keepdims=True))
-        total = jnp.zeros((clip_count, TILE, head_size), jnp.float32)
-        weight_sum = jnp.zeros((clip_count, TILE, 1), jnp.float32)
+            row_max = jnp.maximum(row_max, s.max(axis=1, keepdims=True))
+        total = jnp.zeros((TILE, head_size), jnp.float32)
+        weight_sum = jnp.zeros((TILE, 1), jnp.float32)
         for slot in range(KMAX):
             w = jnp.exp(scores[slot] - row_max)
-            weight_sum = weight_sum + w.sum(axis=2, keepdims=True)
-            v_head = kv_refs[slot][1, :, :, cols]
-            total = total + lax.dot_general(
-                w.astype(jnp.bfloat16), v_head, (((2,), (1,)), ((0,), (0,))),
-                preferred_element_type=jnp.float32,
+            weight_sum = weight_sum + w.sum(axis=1, keepdims=True)
+            total = total + jnp.dot(
+                w.astype(jnp.bfloat16), rows(1, slot, cols), preferred_element_type=jnp.float32
             )
-        out_ref[:, :, cols] = (total / weight_sum).astype(out_ref.dtype)
+        out_ref[0, :, head * head_size:(head + 1) * head_size] = (total / weight_sum).astype(out_ref.dtype)
 
 
-def attend(positions, live_counts, bias, queries, key_values, heads, head_size):
+def attend(positions, live_counts, bias, queries, own_tiles, far_tiles, heads, head_size):
     _, token_count, width = queries.shape
-    clip_count = 1
     tile_count = token_count // TILE
 
-    def kv_spec(slot):
-        return pl.BlockSpec(
-            (None, 2, clip_count, TILE, width),
-            lambda t, pos, cnt, slot=slot: (pos[t, slot], 0, 0, 0, 0),
-        )
+    def whole(array):
+        return pl.BlockSpec(array.shape, lambda t, pos, cnt: (0,) * array.ndim)
 
     kernel = functools.partial(
         attention_kernel, heads=heads, head_size=head_size, scale=1.0 / math.sqrt(head_size)
     )
     return pl.pallas_call(
         kernel,
-        out_shape=jax.ShapeDtypeStruct((clip_count, token_count, width), jnp.bfloat16),
+        out_shape=jax.ShapeDtypeStruct((1, token_count, width), jnp.bfloat16),
         grid_spec=pltpu.PrefetchScalarGridSpec(
             num_scalar_prefetch=2,
             grid=(tile_count,),
             in_specs=[pl.BlockSpec(memory_space=pltpu.SMEM),
-                      pl.BlockSpec((clip_count, TILE, width), lambda t, pos, cnt: (0, t, 0))]
-            + [kv_spec(slot) for slot in range(KMAX)],
-            out_specs=pl.BlockSpec((clip_count, TILE, width), lambda t, pos, cnt: (0, t, 0)),
+                      pl.BlockSpec((1, TILE, width), lambda t, pos, cnt: (0, t, 0)),
+                      whole(own_tiles), whole(far_tiles)],
+            out_specs=pl.BlockSpec((1, TILE, width), lambda t, pos, cnt: (0, t, 0)),
         ),
-    )(positions, live_counts, bias, queries, *([key_values] * KMAX))
+    )(positions, live_counts, bias, queries, own_tiles, far_tiles)
 
 
 def partner_pairs(count, step):
@@ -155,10 +160,9 @@
             payload, _ = lax.optimization_barrier((payload, sent[-3]))
         incoming = lax.all_to_all(payload, "ctx", 0, 0, tiled=True)
         received.append(incoming)
-        key_values = jnp.concatenate([by_tile, incoming], axis=0)
         if index == len(order) - 1 and len(sent) >= 2:
-            key_values, _ = lax.optimization_barrier((key_values, sent[-2]))
-        attended = attend(positions, live_counts, bias, projected, key_values, heads_here, head_size)
+            incoming, _ = lax.optimization_barrier((incoming, sent[-2]))
+        attended = attend(positions, live_counts, bias, projected, by_tile, incoming, heads_here, head_size)
         partial_out = jnp.dot(
             attended[0], out_weight, preferred_element_type=jnp.float32
         ).astype(jnp.bfloat16)

time: 247 us -> 241 us (0.976)
  waiting for transfers between devices: 102 us -> 114 us
  other arithmetic: 14.4 us -> 2.67 us
  Pallas kernels: 35.6 us -> 31.9 us
  local copies, waits for them, and re-layouts: 14.1 us -> 11.1 us
    ppermute x3, waiting for transfers between devices: 16.3 us -> 42.8 us  [local(): partial_out = lax.ppermute(partial_out, 'dp', partner_pairs(n_dp, step))]
    all_to_all x4, waiting for transfers between devices: 31.8 us -> 17.2 us  [local(): incoming = lax.all_to_all(payload, 'ctx', 0, 0, tiled=True)]
    concatenate x4 -> x0, other arithmetic: 11.7 us -> none  [local(): key_values = jnp.concatenate([by_tile, incoming], axis=0)]
    pallas_call x4, Pallas kernels: 35.6 us -> 31.9 us  [attend(): pl.pallas_call(kernel, out_shape=jax.ShapeDtypeStruct((1, token_count, wi...]
    unnamed x21 -> x27, local copies, waits for them, and re-layouts: 3.22 us -> 0.2 us
  transfers between devices with their start and end apart: 10 -> 10, of which waited for: 7 -> 8; matrix products, arithmetic and copies ran while one was open for 20% -> 16% of each run, Pallas kernels for 14% -> 13%
where the time goes in v11:
time: 241 us; the launch traced here: 240 us
  waiting for transfers between devices  114 us (47%)
  matrix products  36.7 us (15%)
  Pallas kernels  31.9 us (13%)
  starting transfers between devices  31.3 us (13%)
  blocking collectives  12.9 us (5%)
  local copies, waits for them, and re-layouts  11.1 us (5%)
  other arithmetic  2.67 us (1%)
    ppermute x3, waiting for transfers between devices, local(): arrived[step] = lax.ppermute(own_tokens, 'dp', partner_pairs(n_dp, step))  53.6 us
    ppermute x3, waiting for transfers between devices, local(): partial_out = lax.ppermute(partial_out, 'dp', partner_pairs(n_dp, step))  42.8 us
    pallas_call x4, Pallas kernels, attend(): pl.pallas_call(kernel, out_shape=jax.ShapeDtypeStruct((1, token_count, wi...  31.9 us
    dot_general x4, matrix products, local(): jnp.einsum('td,sdh->sth', tokens, qkv_weight, preferred_element_type=jnp....  22.8 us
    all_to_all x4, starting transfers between devices, local(): incoming = lax.all_to_all(payload, 'ctx', 0, 0, tiled=True)  18.9 us
    all_to_all x4, waiting for transfers between devices, local(): incoming = lax.all_to_all(payload, 'ctx', 0, 0, tiled=True)  17.2 us
    dot_general x4, matrix products, local(): jnp.dot(attended[0], out_weight, preferred_element_type=jnp.float32)  13.8 us
    all_gather x1, blocking collectives, local(): lax.all_gather(table, 'ctx', axis=0, tiled=True).astype(jnp.int32)  12.9 us
  transfers between devices with their start and end apart: 10, of which 8 were waited for; matrix products, arithmetic and copies ran while one was open for 16% of the time, Pallas kernels for 13%

profile of v11, /device:TPU:0, one launch (start us, length us, event | category | flops | bytes accessed | tf_op | source)
XLA Modules:
  0.0 240.4 jit_solution(14152558461007453526)
XLA Ops:
  0.0 3.9 %collective-permute-start = (bf16[256,3072]{1,0:T(8,128)(2,1)}, bf16[256,3072]{1,0:T(8,128)(2,1)}, u32[]{:S(2)}, u32[]{:S(2)}) collective-permute-start(bf16[256,3072]{1,0:T(8,128)(2,1)} %bitcast.127), channel_id=1, source_target_pairs={{0,24},{8,16},{16,8},{24,0},{1,25},{9,17},{17,9},{25,1},{2,26},{10... | collective-permute-start | bytes 4718600 | tf_op jit(solution)/shard_map/ppermute | solution.py:141
  5.4 12.9 %all-gather = f32[8,4,11]{2,1,0:T(4,128)S(1)} all-gather(f32[1,4,11]{2,1,0:T(4,128)S(1)} %fusion.42), channel_id=1, replica_groups=mesh['dp'=4,'ctx'=8] {'ctx'}, dimensions={0}, use_global_device_ids=true | all-gather | bytes 1584 | tf_op jit(solution)/shard_map/all_gather | solution.py:115
  19.1 19.5 %collective-permute-done = bf16[256,3072]{1,0:T(8,128)(2,1)} collective-permute-done((bf16[256,3072]{1,0:T(8,128)(2,1)}, bf16[256,3072]{1,0:T(8,128)(2,1)}, u32[]{:S(2)}, u32[]{:S(2)}) %collective-permute-start) | collective-permute-done | bytes 1572896 | tf_op jit(solution)/shard_map/ppermute | solution.py:141
  38.6 5.7 %fusion.31.q_ref = bf16[3,256,384]{2,1,0:T(8,128)(2,1)S(1)} fusion(bf16[3,3072,384]{2,1,0:T(8,128)(2,1)} %param.8, bf16[256,3072]{1,0:T(8,128)(2,1)} %collective-permute-done), kind=kOutput, calls=%fused_computation.28 | convolution fusion | flops 1812234240 | bytes 9240576 | tf_op jit(solution)/shard_map/td,sdh->sth/dot_general | solution.py:150
  46.3 5.2 %all-to-all-start = ((bf16[16,2,1,64,384]{4,3,2,1,0:T(8,128)(2,1)}), bf16[16,2,1,64,384]{4,3,2,1,0:T(8,128)(2,1)}, u32[]{:S(2)}, u32[]{:S(2)}) async-start(bf16[16,2,1,64,384]{4,3,2,1,0:T(8,128)(2,1)} %bitcast.119), calls=%async_computation | async-start | bytes 3145728 | tf_op jit(solution)/shard_map/all_to_all | solution.py:161
  54.6 34.1 %collective-permute-done.2 = bf16[256,3072]{1,0:T(8,128)(2,1)} collective-permute-done((bf16[256,3072]{1,0:T(8,128)(2,1)}, bf16[256,3072]{1,0:T(8,128)(2,1)}, u32[]{:S(2)}, u32[]{:S(2)}) %collective-permute-start.2) | collective-permute-done | bytes 1572896 | tf_op jit(solution)/shard_map/ppermute | solution.py:141
  89.5 5.7 %fusion.28.q_ref = bf16[3,256,384]{2,1,0:T(8,128)(2,1)S(1)} fusion(bf16[3,3072,384]{2,1,0:T(8,128)(2,1)} %param.8, bf16[256,3072]{1,0:T(8,128)(2,1)} %collective-permute-done.2), kind=kOutput, calls=%fused_computation.27 | convolution fusion | flops 1812234240 | bytes 9240576 | tf_op jit(solution)/shard_map/td,sdh->sth/dot_general | solution.py:150
  97.3 4.4 %all-to-all-start.1 = ((bf16[16,2,1,64,384]{4,3,2,1,0:T(8,128)(2,1)}), bf16[16,2,1,64,384]{4,3,2,1,0:T(8,128)(2,1)}, u32[]{:S(2)}, u32[]{:S(2)}) async-start(bf16[16,2,1,64,384]{4,3,2,1,0:T(8,128)(2,1)} %bitcast.116), calls=%async_computation.1 | async-start | bytes 3145728 | tf_op jit(solution)/shard_map/all_to_all | solution.py:161
  105.2 5.7 %fusion.25.q_ref = bf16[3,256,384]{2,1,0:T(8,128)(2,1)S(1)} fusion(bf16[3,3072,384]{2,1,0:T(8,128)(2,1)} %param.8, bf16[256,3072]{1,0:T(8,128)(2,1)} %collective-permute-done.4), kind=kOutput, calls=%fused_computation.26 | convolution fusion | flops 1812234240 | bytes 9240576 | tf_op jit(solution)/shard_map/td,sdh->sth/dot_general | solution.py:150
  112.9 8.0 %shard_map.73 = bf16[1,256,384]{2,1,0:T(8,128)(2,1)} custom-call(s32[4,10]{1,0:T(4,128)} %add_select_fusion.2.pos_ref, s32[4]{0:T(128)} %count_ref.7, f32[4,3,10]{2,1,0:T(4,128)} %fusion.40.bias_ref, bf16[3,256,384]{2,1,0:T(8,128)(2,1)} %copy-done.5, bf16[4,2,1,64,384]{4,3,2,1,0:T(8,128)(2,1)} %bitcast.109, bf16[16,2,1,64,384]{4,3,2,1,0:T(8,128)(2,1)} %all-to-all-done.far_ref), custom_call_target="tpu_custom_call" | custom-call | tf_op jit(solution)/shard_map/pallas_call | solution.py:85
  120.9 3.1 %convolution_convert_fusion.3 = bf16[256,3072]{1,0:T(8,128)(2,1)} fusion(bf16[384,3072]{1,0:T(8,128)(2,1)S(1)} %copy-done, bf16[1,256,384]{2,1,0:T(8,128)(2,1)} %shard_map.73), kind=kOutput, calls=%fused_computation.10 | convolution fusion | flops 604766208 | bytes 4128768 | tf_op jit(solution)/shard_map/dot_general | solution.py:166
  124.0 15.6 %all-to-all-done.1.far_ref = bf16[16,2,1,64,384]{4,3,2,1,0:T(8,128)(2,1)} async-done(((bf16[16,2,1,64,384]{4,3,2,1,0:T(8,128)(2,1)}), bf16[16,2,1,64,384]{4,3,2,1,0:T(8,128)(2,1)}, u32[]{:S(2)}, u32[]{:S(2)}) %all-to-all-start.1) | async-done | bytes 1572896 | tf_op jit(solution)/shard_map/all_to_all | solution.py:161
  139.5 4.5 %all-to-all-start.2 = ((bf16[16,2,1,64,384]{4,3,2,1,0:T(8,128)(2,1)}), bf16[16,2,1,64,384]{4,3,2,1,0:T(8,128)(2,1)}, u32[]{:S(2)}, u32[]{:S(2)}) async-start(bf16[16,2,1,64,384]{4,3,2,1,0:T(8,128)(2,1)} %bitcast.118), calls=%async_computation.2 | async-start | bytes 3145728 | tf_op jit(solution)/shard_map/all_to_all | solution.py:161
  146.5 5.7 %fusion.22.q_ref = bf16[3,256,384]{2,1,0:T(8,128)(2,1)S(1)} fusion(bf16[3,3072,384]{2,1,0:T(8,128)(2,1)} %param.8, bf16[256,3072]{1,0:T(8,128)(2,1)} %bitcast.130), kind=kOutput, calls=%fused_computation.25 | convolution fusion | flops 1812234240 | bytes 9240576 | tf_op jit(solution)/shard_map/td,sdh->sth/dot_general | solution.py:150
  154.3 8.0 %shard_map.74 = bf16[1,256,384]{2,1,0:T(8,128)(2,1)} custom-call(s32[4,10]{1,0:T(4,128)} %add_select_fusion.2.pos_ref, s32[4]{0:T(128)} %count_ref.7, f32[4,3,10]{2,1,0:T(4,128)} %fusion.40.bias_ref, bf16[3,256,384]{2,1,0:T(8,128)(2,1)} %copy-done.6, bf16[4,2,1,64,384]{4,3,2,1,0:T(8,128)(2,1)} %bitcast.111, bf16[16,2,1,64,384]{4,3,2,1,0:T(8,128)(2,1)} %all-to-all-done.1.far_ref), custom_call_target="tpu_custom_call" | custom-call | tf_op jit(solution)/shard_map/pallas_call | solution.py:85
  162.3 3.2 %convolution_convert_fusion.2 = bf16[256,3072]{1,0:T(8,128)(2,1)} fusion(bf16[384,3072]{1,0:T(8,128)(2,1)S(1)} %copy-done, bf16[1,256,384]{2,1,0:T(8,128)(2,1)} %shard_map.74), kind=kOutput, calls=%fused_computation.9 | convolution fusion | flops 604766208 | bytes 4128768 | tf_op jit(solution)/shard_map/dot_general | solution.py:166
  165.4 16.3 %collective-permute-done.1 = bf16[256,3072]{1,0:T(8,128)(2,1)} collective-permute-done((bf16[256,3072]{1,0:T(8,128)(2,1)}, bf16[256,3072]{1,0:T(8,128)(2,1)}, u32[]{:S(2)}, u32[]{:S(2)}) %collective-permute-start.1) | collective-permute-done | bytes 1572896 | tf_op jit(solution)/shard_map/ppermute | solution.py:171
  181.7 4.8 %all-to-all-start.3 = ((bf16[16,2,1,64,384]{4,3,2,1,0:T(8,128)(2,1)}), bf16[16,2,1,64,384]{4,3,2,1,0:T(8,128)(2,1)}, u32[]{:S(2)}, u32[]{:S(2)}) async-start(bf16[16,2,1,64,384]{4,3,2,1,0:T(8,128)(2,1)} %bitcast.117), calls=%async_computation.3 | async-start | bytes 3145728 | tf_op jit(solution)/shard_map/all_to_all | solution.py:161
  188.0 8.0 %shard_map.75 = bf16[1,256,384]{2,1,0:T(8,128)(2,1)} custom-call(s32[4,10]{1,0:T(4,128)} %add_select_fusion.2.pos_ref, s32[4]{0:T(128)} %count_ref.7, f32[4,3,10]{2,1,0:T(4,128)} %fusion.40.bias_ref, bf16[3,256,384]{2,1,0:T(8,128)(2,1)} %copy-done.7, bf16[4,2,1,64,384]{4,3,2,1,0:T(8,128)(2,1)} %bitcast.113, bf16[16,2,1,64,384]{4,3,2,1,0:T(8,128)(2,1)} %all-to-all-done.2.far_ref), custom_call_target="tpu_custom_call" | custom-call | tf_op jit(solution)/shard_map/pallas_call | solution.py:85
  196.0 3.1 %convolution_convert_fusion.1 = bf16[256,3072]{1,0:T(8,128)(2,1)} fusion(bf16[384,3072]{1,0:T(8,128)(2,1)S(1)} %copy-done, bf16[1,256,384]{2,1,0:T(8,128)(2,1)} %shard_map.75), kind=kOutput, calls=%fused_computation.8 | convolution fusion | flops 604766208 | bytes 4128768 | tf_op jit(solution)/shard_map/dot_general | solution.py:166
  200.5 23.1 %collective-permute-done.3 = bf16[256,3072]{1,0:T(8,128)(2,1)} collective-permute-done((bf16[256,3072]{1,0:T(8,128)(2,1)}, bf16[256,3072]{1,0:T(8,128)(2,1)}, u32[]{:S(2)}, u32[]{:S(2)}) %collective-permute-start.3) | collective-permute-done | bytes 1572896 | tf_op jit(solution)/shard_map/ppermute | solution.py:171
  224.4 8.0 %shard_map.76 = bf16[1,256,384]{2,1,0:T(8,128)(2,1)} custom-call(s32[4,10]{1,0:T(4,128)} %add_select_fusion.2.pos_ref, s32[4]{0:T(128)} %count_ref.7, f32[4,3,10]{2,1,0:T(4,128)} %fusion.40.bias_ref, bf16[3,256,384]{2,1,0:T(8,128)(2,1)} %copy-done.8, bf16[4,2,1,64,384]{4,3,2,1,0:T(8,128)(2,1)} %bitcast.115, bf16[16,2,1,64,384]{4,3,2,1,0:T(8,128)(2,1)} %all-to-all-done.3.far_ref), custom_call_target="tpu_custom_call" | custom-call | tf_op jit(solution)/shard_map/pallas_call | solution.py:85
  232.4 3.4 %collective-permute-done.5 = bf16[256,3072]{1,0:T(8,128)(2,1)} collective-permute-done((bf16[256,3072]{1,0:T(8,128)(2,1)}, bf16[256,3072]{1,0:T(8,128)(2,1)}, u32[]{:S(2)}, u32[]{:S(2)}) %collective-permute-start.5) | collective-permute-done | bytes 1572896 | tf_op jit(solution)/shard_map/ppermute | solution.py:171
  235.9 4.6 %fusion.1 = bf16[1,256,3072]{2,1,0:T(8,128)(2,1)} fusion(bf16[256,3072]{1,0:T(8,128)(2,1)} %collective-permute-done.5, bf16[256,3072]{1,0:T(8,128)(2,1)} %collective-permute-done.3, bf16[256,3072]{1,0:T(8,128)(2,1)} %collective-permute-done.1, bf16[384,3072]{1,0:T(8,128)(2,1)S(1)} %copy-done, bf16[1,256,384]{2,1,0:T(8,128)(2,1)} %shard_map.76), kind=kOutput, calls=%fused_computation.12 | convolution fusion | flops 611057664 | bytes 8847360 | tf_op jit(solution)/shard_map/dot_general | solution.py:166
  (85 shorter events, 23.9 us)
Async XLA Ops:
  0.0 120.9 %copy-start = (bf16[384,3072]{1,0:T(8,128)(2,1)S(1)}, bf16[384,3072]{1,0:T(8,128)(2,1)}, u32[]{:S(2)}) copy-start(bf16[384,3072]{1,0:T(8,128)(2,1)} %param.9) | copy-start | bytes 7077892
  0.0 38.6 %collective-permute-start = (bf16[256,3072]{1,0:T(8,128)(2,1)}, bf16[256,3072]{1,0:T(8,128)(2,1)}, u32[]{:S(2)}, u32[]{:S(2)}) collective-permute-start(bf16[256,3072]{1,0:T(8,128)(2,1)} %bitcast.127), channel_id=1, source_target_pairs={{0,24},{8,16},{16,8},{24,0},{1,25},{9,17},{17,9},{25,1},{2,26},{10... | collective-permute-start | bytes 4718600 | tf_op jit(solution)/shard_map/ppermute | solution.py:141
  44.3 2.0 copy-start.5
  44.4 1.9 copy-start.1
  46.3 8.2 %copy-start.9 = (s32[4,10]{1,0:T(4,128)S(1)}, s32[4,10]{1,0:T(4,128)}, u32[]{:S(2)}) copy-start(s32[4,10]{1,0:T(4,128)} %param.10) | copy-start | bytes 484
  46.3 8.3 %copy-start.11 = (s32[4,10]{1,0:T(4,128)S(1)}, s32[4,10]{1,0:T(4,128)}, u32[]{:S(2)}) copy-start(s32[4,10]{1,0:T(4,128)} %param.12) | copy-start | bytes 484
  46.3 43.2 %all-to-all-start = ((bf16[16,2,1,64,384]{4,3,2,1,0:T(8,128)(2,1)}), bf16[16,2,1,64,384]{4,3,2,1,0:T(8,128)(2,1)}, u32[]{:S(2)}, u32[]{:S(2)}) async-start(bf16[16,2,1,64,384]{4,3,2,1,0:T(8,128)(2,1)} %bitcast.119), calls=%async_computation | async-start | bytes 3145728 | tf_op jit(solution)/shard_map/all_to_all | solution.py:161
  51.6 37.1 %collective-permute-start.2 = (bf16[256,3072]{1,0:T(8,128)(2,1)}, bf16[256,3072]{1,0:T(8,128)(2,1)}, u32[]{:S(2)}, u32[]{:S(2)}) collective-permute-start(bf16[256,3072]{1,0:T(8,128)(2,1)} %bitcast.128), channel_id=1, source_target_pairs={{0,8},{8,0},{16,24},{24,16},{1,9},{9,1},{17,25},{25,17},{2,10},{10... | collective-permute-start | bytes 4718600 | tf_op jit(solution)/shard_map/ppermute | solution.py:141
  53.1 52.1 %collective-permute-start.4 = (bf16[256,3072]{1,0:T(8,128)(2,1)}, bf16[256,3072]{1,0:T(8,128)(2,1)}, u32[]{:S(2)}, u32[]{:S(2)}) collective-permute-start(bf16[256,3072]{1,0:T(8,128)(2,1)} %bitcast.129), channel_id=1, source_target_pairs={{0,16},{8,24},{16,0},{24,8},{1,17},{9,25},{17,1},{25,9},{2,18},{10... | collective-permute-start | bytes 4718600 | tf_op jit(solution)/shard_map/ppermute | solution.py:141
  95.2 2.0 copy-start.6
  95.3 1.9 copy-start.2
  97.3 4.4 %copy-start.10 = (s32[4]{0:T(128)S(1)}, s32[4]{0:T(128)}, u32[]{:S(2)}) copy-start(s32[4]{0:T(128)} %count_ref.7) | copy-start | bytes 52
  97.3 42.3 %all-to-all-start.1 = ((bf16[16,2,1,64,384]{4,3,2,1,0:T(8,128)(2,1)}), bf16[16,2,1,64,384]{4,3,2,1,0:T(8,128)(2,1)}, u32[]{:S(2)}, u32[]{:S(2)}) async-start(bf16[16,2,1,64,384]{4,3,2,1,0:T(8,128)(2,1)} %bitcast.116), calls=%async_computation.1 | async-start | bytes 3145728 | tf_op jit(solution)/shard_map/all_to_all | solution.py:161
  101.7 1.4 copy-start.12
  110.9 2.0 copy-start.7
  111.0 1.9 copy-start.3
  139.5 42.2 %all-to-all-start.2 = ((bf16[16,2,1,64,384]{4,3,2,1,0:T(8,128)(2,1)}), bf16[16,2,1,64,384]{4,3,2,1,0:T(8,128)(2,1)}, u32[]{:S(2)}, u32[]{:S(2)}) async-start(bf16[16,2,1,64,384]{4,3,2,1,0:T(8,128)(2,1)} %bitcast.118), calls=%async_computation.2 | async-start | bytes 3145728 | tf_op jit(solution)/shard_map/all_to_all | solution.py:161
  144.0 37.7 %collective-permute-start.1 = (bf16[256,3072]{1,0:T(8,128)(2,1)}, bf16[256,3072]{1,0:T(8,128)(2,1)}, u32[]{:S(2)}, u32[]{:S(2)}) collective-permute-start(bf16[256,3072]{1,0:T(8,128)(2,1)} %convolution_convert_fusion.3), channel_id=1, source_target_pairs={{0,24},{8,16},{16,8},{24,0},{1,25},{9,17},{17,9},{25,1},{2,26},{10... | collective-permute-start | bytes 4718600 | tf_op jit(solution)/shard_map/ppermute | solution.py:171
  152.2 2.1 copy-start.8
  152.3 2.0 copy-start.4
  181.7 42.7 %all-to-all-start.3 = ((bf16[16,2,1,64,384]{4,3,2,1,0:T(8,128)(2,1)}), bf16[16,2,1,64,384]{4,3,2,1,0:T(8,128)(2,1)}, u32[]{:S(2)}, u32[]{:S(2)}) async-start(bf16[16,2,1,64,384]{4,3,2,1,0:T(8,128)(2,1)} %bitcast.117), calls=%async_computation.3 | async-start | bytes 3145728 | tf_op jit(solution)/shard_map/all_to_all | solution.py:161
  186.5 37.1 %collective-permute-start.3 = (bf16[256,3072]{1,0:T(8,128)(2,1)}, bf16[256,3072]{1,0:T(8,128)(2,1)}, u32[]{:S(2)}, u32[]{:S(2)}) collective-permute-start(bf16[256,3072]{1,0:T(8,128)(2,1)} %convolution_convert_fusion.2), channel_id=1, source_target_pairs={{0,8},{8,0},{16,24},{24,16},{1,9},{9,1},{17,25},{25,17},{2,10},{10... | collective-permute-start | bytes 4718600 | tf_op jit(solution)/shard_map/ppermute | solution.py:171
  199.0 36.8 %collective-permute-start.5 = (bf16[256,3072]{1,0:T(8,128)(2,1)}, bf16[256,3072]{1,0:T(8,128)(2,1)}, u32[]{:S(2)}, u32[]{:S(2)}) collective-permute-start(bf16[256,3072]{1,0:T(8,128)(2,1)} %convolution_convert_fusion.1), channel_id=1, source_target_pairs={{0,16},{8,24},{16,0},{24,8},{1,17},{9,25},{17,1},{25,9},{2,18},{10... | collective-permute-start | bytes 4718600 | tf_op jit(solution)/shard_map/ppermute | solution.py:171

commit v12 on v11

--- a/solution.py
+++ b/solution.py
@@ -135,18 +135,24 @@
     live_counts = counts.astype(jnp.int32)
 
     own_tokens = clip_tokens[0]
-    order = [3, 1, 2, 0] if n_dp == 4 else list(range(1, n_dp)) + [0]
+    order = [0, 3, 2, 1] if n_dp == 4 else list(range(n_dp))
     arrived = {0: own_tokens}
     for step in range(1, n_dp):
         arrived[step] = lax.ppermute(own_tokens, "dp", partner_pairs(n_dp, step))
+    last = order[-1]
     total = None
     received = []
     partials = []
     sent = []
+    far_weight = None
     for index, step in enumerate(order):
+        final = index == len(order) - 1
         tokens = arrived[step]
         if index >= 1:
             tokens, _ = lax.optimization_barrier((tokens, received[max(index - 2, 0)]))
+        if index == 1 and last > 0:
+            held, _ = lax.optimization_barrier((out_weight, received[0]))
+            far_weight = lax.ppermute(held, "dp", partner_pairs(n_dp, last))
         projected = jnp.einsum(
             "td,sdh->sth", tokens, qkv_weight, preferred_element_type=jnp.float32
         ).astype(jnp.bfloat16)
@@ -156,20 +162,25 @@
         payload = by_tile.at[send_picks].get(mode="promise_in_bounds")
         if index >= 2:
             payload, _ = lax.optimization_barrier((payload, partials[index - 2]))
-        if index == len(order) - 1 and len(sent) >= 2:
-            payload, _ = lax.optimization_barrier((payload, sent[-3]))
+        if final and len(sent) >= 2:
+            payload, _ = lax.optimization_barrier((payload, sent[-2]))
         incoming = lax.all_to_all(payload, "ctx", 0, 0, tiled=True)
         received.append(incoming)
-        if index == len(order) - 1 and len(sent) >= 2:
-            incoming, _ = lax.optimization_barrier((incoming, sent[-2]))
         attended = attend(positions, live_counts, bias, projected, by_tile, incoming, heads_here, head_size)
-        partial_out = jnp.dot(
-            attended[0], out_weight, preferred_element_type=jnp.float32
-        ).astype(jnp.bfloat16)
-        partials.append(partial_out)
-        if step > 0:
-            partial_out = lax.ppermute(partial_out, "dp", partner_pairs(n_dp, step))
-            sent.append(partial_out)
+        if final and step > 0:
+            came = lax.ppermute(attended[0], "dp", partner_pairs(n_dp, step))
+            weight = far_weight if far_weight is not None else lax.ppermute(
+                out_weight, "dp", partner_pairs(n_dp, step)
+            )
+            partial_out = jnp.dot(came, weight, preferred_element_type=jnp.float32).astype(jnp.bfloat16)
+        else:
+            partial_out = jnp.dot(
+                attended[0], out_weight, preferred_element_type=jnp.float32
+            ).astype(jnp.bfloat16)
+            partials.append(partial_out)
+            if step > 0:
+                partial_out = lax.ppermute(partial_out, "dp", partner_pairs(n_dp, step))
+                sent.append(partial_out)
         contribution = partial_out.astype(jnp.float32)
         total = contribution if total is None else total + contribution
     return total.astype(jnp.bfloat16)[None]

time: 241 us -> 264 us (1.095)
  waiting for transfers between devices: 114 us -> 138 us
  starting transfers between devices: 31.3 us -> 26.9 us
    ppermute x3, waiting for transfers between devices: 53.6 us -> 75.2 us  [local(): arrived[step] = lax.ppermute(own_tokens, 'dp', partner_pairs(n_dp, step))]
    ppermute x3 -> x2, waiting for transfers between devices: 42.8 us -> 26.5 us  [local(): partial_out = lax.ppermute(partial_out, 'dp', partner_pairs(n_dp, step))]
    ppermute x0 -> x2, waiting for transfers between devices: none -> 11.2 us  [the longest x1 7.45 us: local(): far_weight = lax.ppermute(held, 'dp', partner_pairs(n_dp, last))]
    all_to_all x4, waiting for transfers between devices: 17.2 us -> 24.9 us  [local(): incoming = lax.all_to_all(payload, 'ctx', 0, 0, tiled=True)]
    dot_general x0 -> x1, matrix products: none -> 5.28 us  [local(): jnp.dot(came, weight, preferred_element_type=jnp.float32)]
    dot_general x4 -> x3, matrix products: 13.8 us -> 9.24 us  [local(): jnp.dot(attended[0], out_weight, preferred_element_type=jnp.float32)]
    ppermute x3 -> x2, starting transfers between devices: 5.52 us -> 2.69 us  [local(): partial_out = lax.ppermute(partial_out, 'dp', partner_pairs(n_dp, step))]
  transfers between devices with their start and end apart: 10 -> 11, of which waited for: 8 -> 7; matrix products, arithmetic and copies ran while one was open for 16% -> 14% of each run, Pallas kernels for 13% -> 12%
where the time goes in v12:
time: 264 us; the launch traced here: 263 us
  waiting for transfers between devices  138 us (52%)
  matrix products  37.8 us (14%)
  Pallas kernels  32 us (12%)
  starting transfers between devices  26.9 us (10%)
  blocking collectives  14.4 us (5%)
  local copies, waits for them, and re-layouts  11.1 us (4%)
  other arithmetic  2.67 us (1%)
    ppermute x3, waiting for transfers between devices, local(): arrived[step] = lax.ppermute(own_tokens, 'dp', partner_pairs(n_dp, step))  75.2 us
    pallas_call x4, Pallas kernels, attend(): pl.pallas_call(kernel, out_shape=jax.ShapeDtypeStruct((1, token_count, wi...  32 us
    ppermute x2, waiting for transfers between devices, local(): partial_out = lax.ppermute(partial_out, 'dp', partner_pairs(n_dp, step))  26.5 us
    all_to_all x4, waiting for transfers between devices, local(): incoming = lax.all_to_all(payload, 'ctx', 0, 0, tiled=True)  24.9 us
    dot_general x4, matrix products, local(): jnp.einsum('td,sdh->sth', tokens, qkv_weight, preferred_element_type=jnp....  23.3 us
    all_to_all x4, starting transfers between devices, local(): incoming = lax.all_to_all(payload, 'ctx', 0, 0, tiled=True)  18.1 us
    all_gather x1, blocking collectives, local(): lax.all_gather(table, 'ctx', axis=0, tiled=True).astype(jnp.int32)  14.4 us
    dot_general x3, matrix products, local(): jnp.dot(attended[0], out_weight, preferred_element_type=jnp.float32)  9.24 us
  transfers between devices with their start and end apart: 11, of which 7 were waited for; matrix products, arithmetic and copies ran while one was open for 14% of the time, Pallas kernels for 12%

profile of v12, /device:TPU:0, one launch (start us, length us, event | category | flops | bytes accessed | tf_op | source)
XLA Modules:
  0.0 263.1 jit_solution(16276087235070257996)
XLA Ops:
  1.5 14.4 %all-gather = f32[8,4,11]{2,1,0:T(4,128)S(1)} all-gather(f32[1,4,11]{2,1,0:T(4,128)S(1)} %fusion.39), channel_id=1, replica_groups=mesh['dp'=4,'ctx'=8] {'ctx'}, dimensions={0}, use_global_device_ids=true | all-gather | bytes 1584 | tf_op jit(solution)/shard_map/all_gather | solution.py:115
  16.6 5.7 %fusion.31.q_ref = bf16[3,256,384]{2,1,0:T(8,128)(2,1)S(1)} fusion(bf16[3,3072,384]{2,1,0:T(8,128)(2,1)} %param.8, bf16[1,256,3072]{2,1,0:T(8,128)(2,1)} %param.7), kind=kOutput, calls=%fused_computation.28 | convolution fusion | flops 1812234240 | bytes 9240576 | tf_op jit(solution)/shard_map/td,sdh->sth/dot_general | solution.py:156
  24.4 3.7 %all-to-all-start = ((bf16[16,2,1,64,384]{4,3,2,1,0:T(8,128)(2,1)}), bf16[16,2,1,64,384]{4,3,2,1,0:T(8,128)(2,1)S(1)}, u32[]{:S(2)}, u32[]{:S(2)}) async-start(bf16[16,2,1,64,384]{4,3,2,1,0:T(8,128)(2,1)} %bitcast.13), calls=%async_computation | async-start | bytes 3145728 | tf_op jit(solution)/shard_map/all_to_all | solution.py:167
  31.1 35.0 %collective-permute-done = bf16[256,3072]{1,0:T(8,128)(2,1)} collective-permute-done((bf16[256,3072]{1,0:T(8,128)(2,1)}, bf16[256,3072]{1,0:T(8,128)(2,1)}, u32[]{:S(2)}, u32[]{:S(2)}) %collective-permute-start) | collective-permute-done | bytes 1572896 | tf_op jit(solution)/shard_map/ppermute | solution.py:141
  66.1 6.2 %fusion.28.q_ref = bf16[3,256,384]{2,1,0:T(8,128)(2,1)S(1)} fusion(bf16[3,3072,384]{2,1,0:T(8,128)(2,1)} %param.8, bf16[256,3072]{1,0:T(8,128)(2,1)} %collective-permute-done), kind=kOutput, calls=%fused_computation.27 | convolution fusion | flops 1812234240 | bytes 9240576 | tf_op jit(solution)/shard_map/td,sdh->sth/dot_general | solution.py:156
  74.5 4.9 %all-to-all-start.1 = ((bf16[16,2,1,64,384]{4,3,2,1,0:T(8,128)(2,1)}), bf16[16,2,1,64,384]{4,3,2,1,0:T(8,128)(2,1)}, u32[]{:S(2)}, u32[]{:S(2)}) async-start(bf16[16,2,1,64,384]{4,3,2,1,0:T(8,128)(2,1)} %bitcast.20), calls=%async_computation.1 | async-start | bytes 3145728 | tf_op jit(solution)/shard_map/all_to_all | solution.py:167
  82.9 16.8 %collective-permute-done.2 = bf16[256,3072]{1,0:T(8,128)(2,1)} collective-permute-done((bf16[256,3072]{1,0:T(8,128)(2,1)}, bf16[256,3072]{1,0:T(8,128)(2,1)}, u32[]{:S(2)}, u32[]{:S(2)}) %collective-permute-start.2) | collective-permute-done | bytes 1572896 | tf_op jit(solution)/shard_map/ppermute | solution.py:141
  99.7 5.7 %fusion.25.q_ref = bf16[3,256,384]{2,1,0:T(8,128)(2,1)S(1)} fusion(bf16[3,3072,384]{2,1,0:T(8,128)(2,1)} %param.8, bf16[256,3072]{1,0:T(8,128)(2,1)} %collective-permute-done.2), kind=kOutput, calls=%fused_computation.26 | convolution fusion | flops 1812234240 | bytes 9240576 | tf_op jit(solution)/shard_map/td,sdh->sth/dot_general | solution.py:156
  107.5 8.1 %shard_map.73 = bf16[1,256,384]{2,1,0:T(8,128)(2,1)} custom-call(s32[4,10]{1,0:T(4,128)} %add_select_fusion.2.pos_ref, s32[4]{0:T(128)} %count_ref.7, f32[4,3,10]{2,1,0:T(4,128)} %fusion.37.bias_ref, bf16[3,256,384]{2,1,0:T(8,128)(2,1)} %copy-done.6, bf16[4,2,1,64,384]{4,3,2,1,0:T(8,128)(2,1)} %bitcast.106, bf16[16,2,1,64,384]{4,3,2,1,0:T(8,128)(2,1)} %copy-done.5), custom_call_target="tpu_custom_call" | custom-call | tf_op jit(solution)/shard_map/pallas_call | solution.py:85
  115.6 3.0 %convolution_convert_fusion.3 = bf16[256,3072]{1,0:T(8,128)(2,1)} fusion(bf16[384,3072]{1,0:T(8,128)(2,1)S(1)} %copy-done, bf16[1,256,384]{2,1,0:T(8,128)(2,1)} %shard_map.73), kind=kOutput, calls=%fused_computation.10 | convolution fusion | flops 604766208 | bytes 4128768 | tf_op jit(solution)/shard_map/dot_general | solution.py:177
  118.6 4.8 %all-to-all-start.2 = ((bf16[16,2,1,64,384]{4,3,2,1,0:T(8,128)(2,1)}), bf16[16,2,1,64,384]{4,3,2,1,0:T(8,128)(2,1)}, u32[]{:S(2)}, u32[]{:S(2)}) async-start(bf16[16,2,1,64,384]{4,3,2,1,0:T(8,128)(2,1)} %bitcast.113), calls=%async_computation.2 | async-start | bytes 3145728 | tf_op jit(solution)/shard_map/all_to_all | solution.py:167
  124.9 8.0 %shard_map.74 = bf16[1,256,384]{2,1,0:T(8,128)(2,1)} custom-call(s32[4,10]{1,0:T(4,128)} %add_select_fusion.2.pos_ref, s32[4]{0:T(128)} %count_ref.7, f32[4,3,10]{2,1,0:T(4,128)} %fusion.37.bias_ref, bf16[3,256,384]{2,1,0:T(8,128)(2,1)} %copy-done.7, bf16[4,2,1,64,384]{4,3,2,1,0:T(8,128)(2,1)} %bitcast.108, bf16[16,2,1,64,384]{4,3,2,1,0:T(8,128)(2,1)} %all-to-all-done.1.far_ref), custom_call_target="tpu_custom_call" | custom-call | tf_op jit(solution)/shard_map/pallas_call | solution.py:85
  132.8 3.1 %convolution_convert_fusion.2 = bf16[256,3072]{1,0:T(8,128)(2,1)} fusion(bf16[384,3072]{1,0:T(8,128)(2,1)S(1)} %copy-done, bf16[1,256,384]{2,1,0:T(8,128)(2,1)} %shard_map.74), kind=kOutput, calls=%fused_computation.9 | convolution fusion | flops 604766208 | bytes 4128768 | tf_op jit(solution)/shard_map/dot_general | solution.py:177
  137.5 23.4 %collective-permute-done.4 = bf16[256,3072]{1,0:T(8,128)(2,1)} collective-permute-done((bf16[256,3072]{1,0:T(8,128)(2,1)}, bf16[256,3072]{1,0:T(8,128)(2,1)}, u32[]{:S(2)}, u32[]{:S(2)}) %collective-permute-start.4) | collective-permute-done | bytes 1572896 | tf_op jit(solution)/shard_map/ppermute | solution.py:141
  160.9 5.7 %fusion.22.q_ref = bf16[3,256,384]{2,1,0:T(8,128)(2,1)S(1)} fusion(bf16[3,3072,384]{2,1,0:T(8,128)(2,1)} %param.8, bf16[256,3072]{1,0:T(8,128)(2,1)} %collective-permute-done.4), kind=kOutput, calls=%fused_computation.25 | convolution fusion | flops 1812234240 | bytes 9240576 | tf_op jit(solution)/shard_map/td,sdh->sth/dot_general | solution.py:156
  168.7 26.5 %collective-permute-done.1 = bf16[256,3072]{1,0:T(8,128)(2,1)} collective-permute-done((bf16[256,3072]{1,0:T(8,128)(2,1)}, bf16[256,3072]{1,0:T(8,128)(2,1)}, u32[]{:S(2)}, u32[]{:S(2)}) %collective-permute-start.1) | collective-permute-done | bytes 1572896 | tf_op jit(solution)/shard_map/ppermute | solution.py:182
  195.2 4.7 %all-to-all-start.3 = ((bf16[16,2,1,64,384]{4,3,2,1,0:T(8,128)(2,1)}), bf16[16,2,1,64,384]{4,3,2,1,0:T(8,128)(2,1)}, u32[]{:S(2)}, u32[]{:S(2)}) async-start(bf16[16,2,1,64,384]{4,3,2,1,0:T(8,128)(2,1)} %bitcast.114), calls=%async_computation.3 | async-start | bytes 3145728 | tf_op jit(solution)/shard_map/all_to_all | solution.py:167
  200.7 8.0 %shard_map.75 = bf16[1,256,384]{2,1,0:T(8,128)(2,1)} custom-call(s32[4,10]{1,0:T(4,128)} %add_select_fusion.2.pos_ref, s32[4]{0:T(128)} %count_ref.7, f32[4,3,10]{2,1,0:T(4,128)} %fusion.37.bias_ref, bf16[3,256,384]{2,1,0:T(8,128)(2,1)} %copy-done.8, bf16[4,2,1,64,384]{4,3,2,1,0:T(8,128)(2,1)} %bitcast.110, bf16[16,2,1,64,384]{4,3,2,1,0:T(8,128)(2,1)} %all-to-all-done.2.far_ref), custom_call_target="tpu_custom_call" | custom-call | tf_op jit(solution)/shard_map/pallas_call | solution.py:85
  208.7 3.1 %convolution_convert_fusion.1 = bf16[256,3072]{1,0:T(8,128)(2,1)} fusion(bf16[384,3072]{1,0:T(8,128)(2,1)S(1)} %copy-done, bf16[1,256,384]{2,1,0:T(8,128)(2,1)} %shard_map.75), kind=kOutput, calls=%fused_computation.8 | convolution fusion | flops 604766208 | bytes 4128768 | tf_op jit(solution)/shard_map/dot_general | solution.py:177
  212.9 24.9 %all-to-all-done.3.far_ref = bf16[16,2,1,64,384]{4,3,2,1,0:T(8,128)(2,1)} async-done(((bf16[16,2,1,64,384]{4,3,2,1,0:T(8,128)(2,1)}), bf16[16,2,1,64,384]{4,3,2,1,0:T(8,128)(2,1)}, u32[]{:S(2)}, u32[]{:S(2)}) %all-to-all-start.3) | async-done | bytes 1572896 | tf_op jit(solution)/shard_map/all_to_all | solution.py:167
  237.9 8.0 %shard_map.76 = bf16[1,256,384]{2,1,0:T(8,128)(2,1)} custom-call(s32[4,10]{1,0:T(4,128)} %add_select_fusion.2.pos_ref, s32[4]{0:T(128)} %count_ref.7, f32[4,3,10]{2,1,0:T(4,128)} %fusion.37.bias_ref, bf16[3,256,384]{2,1,0:T(8,128)(2,1)} %copy-done.9, bf16[4,2,1,64,384]{4,3,2,1,0:T(8,128)(2,1)} %bitcast.112, bf16[16,2,1,64,384]{4,3,2,1,0:T(8,128)(2,1)} %all-to-all-done.3.far_ref), custom_call_target="tpu_custom_call" | custom-call | tf_op jit(solution)/shard_map/pallas_call | solution.py:85
  246.6 7.5 %collective-permute-done.6 = bf16[384,3072]{1,0:T(8,128)(2,1)} collective-permute-done((bf16[384,3072]{1,0:T(8,128)(2,1)S(1)}, bf16[384,3072]{1,0:T(8,128)(2,1)}, u32[]{:S(2)}, u32[]{:S(2)}) %collective-permute-start.6) | collective-permute-done | bytes 2359328 | tf_op jit(solution)/shard_map/ppermute | solution.py:155
  254.1 3.7 %collective-permute-done.5 = bf16[256,384]{1,0:T(8,128)(2,1)S(1)} collective-permute-done((bf16[256,384]{1,0:T(8,128)(2,1)}, bf16[256,384]{1,0:T(8,128)(2,1)S(1)}, u32[]{:S(2)}, u32[]{:S(2)}) %collective-permute-start.5) | collective-permute-done | bytes 196640 | tf_op jit(solution)/shard_map/ppermute | solution.py:171
  257.8 5.3 %fusion.1 = bf16[1,256,3072]{2,1,0:T(8,128)(2,1)} fusion(bf16[256,3072]{1,0:T(8,128)(2,1)} %collective-permute-done.3, bf16[256,3072]{1,0:T(8,128)(2,1)} %collective-permute-done.1, bf16[256,3072]{1,0:T(8,128)(2,1)} %convolution_convert_fusion.3, bf16[256,384]{1,0:T(8,128)(2,1)S(1)} %collective-permute-done.5, bf16[384,3072]{1,0:T(8,128)(2,1)} %collective-permute-done.6), kind=kOutput, calls=%fused_computation.12 | convolution fusion | flops 611057664 | bytes 8847360 | tf_op jit(solution)/shard_map/dot_general | solution.py:175
  (89 shorter events, 22.6 us)
Async XLA Ops:
  22.3 2.0 copy-start.6
  22.4 1.9 copy-start.1
  24.4 6.8 %copy-start.10 = (s32[4,10]{1,0:T(4,128)S(1)}, s32[4,10]{1,0:T(4,128)}, u32[]{:S(2)}) copy-start(s32[4,10]{1,0:T(4,128)} %param.10) | copy-start | bytes 484
  24.4 41.8 %all-to-all-start = ((bf16[16,2,1,64,384]{4,3,2,1,0:T(8,128)(2,1)}), bf16[16,2,1,64,384]{4,3,2,1,0:T(8,128)(2,1)S(1)}, u32[]{:S(2)}, u32[]{:S(2)}) async-start(bf16[16,2,1,64,384]{4,3,2,1,0:T(8,128)(2,1)} %bitcast.13), calls=%async_computation | async-start | bytes 3145728 | tf_op jit(solution)/shard_map/all_to_all | solution.py:167
  28.1 38.0 %collective-permute-start = (bf16[256,3072]{1,0:T(8,128)(2,1)}, bf16[256,3072]{1,0:T(8,128)(2,1)}, u32[]{:S(2)}, u32[]{:S(2)}) collective-permute-start(bf16[256,3072]{1,0:T(8,128)(2,1)} %bitcast.123), channel_id=1, source_target_pairs={{0,24},{8,16},{16,8},{24,0},{1,25},{9,17},{17,9},{25,1},{2,26},{10... | collective-permute-start | bytes 4718600 | tf_op jit(solution)/shard_map/ppermute | solution.py:141
  30.6 69.1 %collective-permute-start.2 = (bf16[256,3072]{1,0:T(8,128)(2,1)}, bf16[256,3072]{1,0:T(8,128)(2,1)}, u32[]{:S(2)}, u32[]{:S(2)}) collective-permute-start(bf16[256,3072]{1,0:T(8,128)(2,1)} %bitcast.124), channel_id=1, source_target_pairs={{0,16},{8,24},{16,0},{24,8},{1,17},{9,25},{17,1},{25,9},{2,18},{10... | collective-permute-start | bytes 4718600 | tf_op jit(solution)/shard_map/ppermute | solution.py:141
  66.1 6.3 %copy-start.5 = (bf16[16,2,1,64,384]{4,3,2,1,0:T(8,128)(2,1)}, bf16[16,2,1,64,384]{4,3,2,1,0:T(8,128)(2,1)S(1)}, u32[]{:S(2)}) copy-start(bf16[16,2,1,64,384]{4,3,2,1,0:T(8,128)(2,1)S(1)} %all-to-all-done.far_ref) | copy-start | bytes 4718596
  72.4 2.1 copy-start.7
  72.5 2.0 copy-start.2
  74.5 4.9 %copy-start.11 = (s32[4]{0:T(128)S(1)}, s32[4]{0:T(128)}, u32[]{:S(2)}) copy-start(s32[4]{0:T(128)} %count_ref.7) | copy-start | bytes 52
  74.5 44.1 %all-to-all-start.1 = ((bf16[16,2,1,64,384]{4,3,2,1,0:T(8,128)(2,1)}), bf16[16,2,1,64,384]{4,3,2,1,0:T(8,128)(2,1)}, u32[]{:S(2)}, u32[]{:S(2)}) async-start(bf16[16,2,1,64,384]{4,3,2,1,0:T(8,128)(2,1)} %bitcast.20), calls=%async_computation.1 | async-start | bytes 3145728 | tf_op jit(solution)/shard_map/all_to_all | solution.py:167
  79.4 1.5 copy-start.12
  105.4 2.0 copy-start.8
  105.5 1.9 copy-start.3
  107.4 8.1 %copy-start = (bf16[384,3072]{1,0:T(8,128)(2,1)S(1)}, bf16[384,3072]{1,0:T(8,128)(2,1)}, u32[]{:S(2)}) copy-start(bf16[384,3072]{1,0:T(8,128)(2,1)} %param.9) | copy-start | bytes 7077892
  118.6 76.6 %all-to-all-start.2 = ((bf16[16,2,1,64,384]{4,3,2,1,0:T(8,128)(2,1)}), bf16[16,2,1,64,384]{4,3,2,1,0:T(8,128)(2,1)}, u32[]{:S(2)}, u32[]{:S(2)}) async-start(bf16[16,2,1,64,384]{4,3,2,1,0:T(8,128)(2,1)} %bitcast.113), calls=%async_computation.2 | async-start | bytes 3145728 | tf_op jit(solution)/shard_map/all_to_all | solution.py:167
  123.4 37.5 %collective-permute-start.4 = (bf16[256,3072]{1,0:T(8,128)(2,1)}, bf16[256,3072]{1,0:T(8,128)(2,1)}, u32[]{:S(2)}, u32[]{:S(2)}) collective-permute-start(bf16[256,3072]{1,0:T(8,128)(2,1)} %bitcast.125), channel_id=1, source_target_pairs={{0,8},{8,0},{16,24},{24,16},{1,9},{9,1},{17,25},{25,17},{2,10},{10... | collective-permute-start | bytes 4718600 | tf_op jit(solution)/shard_map/ppermute | solution.py:141
  136.0 59.2 %collective-permute-start.1 = (bf16[256,3072]{1,0:T(8,128)(2,1)}, bf16[256,3072]{1,0:T(8,128)(2,1)}, u32[]{:S(2)}, u32[]{:S(2)}) collective-permute-start(bf16[256,3072]{1,0:T(8,128)(2,1)} %convolution_convert_fusion.2), channel_id=1, source_target_pairs={{0,24},{8,16},{16,8},{24,0},{1,25},{9,17},{17,9},{25,1},{2,26},{10... | collective-permute-start | bytes 4718600 | tf_op jit(solution)/shard_map/ppermute | solution.py:182
  166.6 2.1 copy-start.9
  166.7 2.0 copy-start.4
  195.2 42.7 %all-to-all-start.3 = ((bf16[16,2,1,64,384]{4,3,2,1,0:T(8,128)(2,1)}), bf16[16,2,1,64,384]{4,3,2,1,0:T(8,128)(2,1)}, u32[]{:S(2)}, u32[]{:S(2)}) async-start(bf16[16,2,1,64,384]{4,3,2,1,0:T(8,128)(2,1)} %bitcast.114), calls=%async_computation.3 | async-start | bytes 3145728 | tf_op jit(solution)/shard_map/all_to_all | solution.py:167
  199.9 54.1 %collective-permute-start.6 = (bf16[384,3072]{1,0:T(8,128)(2,1)S(1)}, bf16[384,3072]{1,0:T(8,128)(2,1)}, u32[]{:S(2)}, u32[]{:S(2)}) collective-permute-start(bf16[384,3072]{1,0:T(8,128)(2,1)S(1)} %copy-done), channel_id=1, source_target_pairs={{0,8},{8,0},{16,24},{24,16},{1,9},{9,1},{17,25},{25,17},{2,10},{10... | collective-permute-start | bytes 7077896 | tf_op jit(solution)/shard_map/ppermute | solution.py:155
  211.7 42.3 %collective-permute-start.3 = (bf16[256,3072]{1,0:T(8,128)(2,1)}, bf16[256,3072]{1,0:T(8,128)(2,1)}, u32[]{:S(2)}, u32[]{:S(2)}) collective-permute-start(bf16[256,3072]{1,0:T(8,128)(2,1)} %convolution_convert_fusion.1), channel_id=1, source_target_pairs={{0,16},{8,24},{16,0},{24,8},{1,17},{9,25},{17,1},{25,9},{2,18},{10... | collective-permute-start | bytes 4718600 | tf_op jit(solution)/shard_map/ppermute | solution.py:182
  245.8 12.0 %collective-permute-start.5 = (bf16[256,384]{1,0:T(8,128)(2,1)}, bf16[256,384]{1,0:T(8,128)(2,1)S(1)}, u32[]{:S(2)}, u32[]{:S(2)}) collective-permute-start(bf16[256,384]{1,0:T(8,128)(2,1)} %bitcast.119), channel_id=1, source_target_pairs={{0,8},{8,0},{16,24},{24,16},{1,9},{9,1},{17,25},{25,17},{2,10},{10... | collective-permute-start | bytes 589832 | tf_op jit(solution)/shard_map/ppermute | solution.py:171
  (1 other events, 1.3 us)

commit v13 on v11

--- a/solution.py
+++ b/solution.py
@@ -46,29 +46,24 @@
         mine, near, far = picks[slot]
         return jnp.where(mine, own_ref[near, part, 0, :, cols], far_ref[far, part, 0, :, cols])
 
+    column = lax.broadcasted_iota(jnp.int32, (1, KMAX * TILE), 1) // TILE
+    live = column < live_count
     for head in range(heads):
         cols = pl.ds(head * head_size, head_size)
         q_head = queries[:, head * head_size:(head + 1) * head_size]
-        scores = []
+        keys = jnp.concatenate([rows(0, slot, cols) for slot in range(KMAX)], axis=0)
+        values = jnp.concatenate([rows(1, slot, cols) for slot in range(KMAX)], axis=0)
+        bias_row = jnp.zeros((1, KMAX * TILE), jnp.float32)
         for slot in range(KMAX):
-            s = lax.dot_general(
-                q_head, rows(0, slot, cols), (((1,), (1,)), ((), ())),
-                preferred_element_type=jnp.float32,
-            )
-            s = s * scale + bias_ref[tile, head, slot]
-            s = jnp.where(slot < live_count, s, -1e30)
-            scores.append(s)
-        row_max = scores[0].max(axis=1, keepdims=True)
-        for s in scores[1:]:
-            row_max = jnp.maximum(row_max, s.max(axis=1, keepdims=True))
-        total = jnp.zeros((TILE, head_size), jnp.float32)
-        weight_sum = jnp.zeros((TILE, 1), jnp.float32)
-        for slot in range(KMAX):
-            w = jnp.exp(scores[slot] - row_max)
-            weight_sum = weight_sum + w.sum(axis=1, keepdims=True)
-            total = total + jnp.dot(
-                w.astype(jnp.bfloat16), rows(1, slot, cols), preferred_element_type=jnp.float32
-            )
+            bias_row = jnp.where(column == slot, bias_ref[tile, head, slot], bias_row)
+        s = lax.dot_general(
+            q_head, keys, (((1,), (1,)), ((), ())), preferred_element_type=jnp.float32
+        )
+        s = jnp.where(live, s * scale + bias_row, -1e30)
+        row_max = s.max(axis=1, keepdims=True)
+        w = jnp.exp(s - row_max)
+        weight_sum = w.sum(axis=1, keepdims=True)
+        total = jnp.dot(w.astype(jnp.bfloat16), values, preferred_element_type=jnp.float32)
         out_ref[0, :, head * head_size:(head + 1) * head_size] = (total / weight_sum).astype(out_ref.dtype)
 
 

time: 241 us -> 240 us (level)
  Pallas kernels: 31.9 us -> 29.1 us
    pallas_call x4, Pallas kernels: 31.9 us -> 29.1 us  [attend(): pl.pallas_call(kernel, out_shape=jax.ShapeDtypeStruct((1, token_count, wi...]
  transfers between devices with their start and end apart: 10 -> 10, of which waited for: 8 -> 8; matrix products, arithmetic and copies ran while one was open for 16% -> 16% of each run, Pallas kernels for 13% -> 12%
where the time goes in v13:
time: 240 us
  waiting for transfers between devices  116 us (48%)
  matrix products  36.7 us (15%)
  starting transfers between devices  31.3 us (13%)
  Pallas kernels  29.1 us (12%)
  blocking collectives  12.9 us (5%)
  local copies, waits for them, and re-layouts  11.1 us (5%)
  other arithmetic  2.67 us (1%)
    ppermute x3, waiting for transfers between devices, local(): arrived[step] = lax.ppermute(own_tokens, 'dp', partner_pairs(n_dp, step))  53.6 us
    ppermute x3, waiting for transfers between devices, local(): partial_out = lax.ppermute(partial_out, 'dp', partner_pairs(n_dp, step))  44.2 us
    pallas_call x4, Pallas kernels, attend(): pl.pallas_call(kernel, out_shape=jax.ShapeDtypeStruct((1, token_count, wi...  29.1 us
    dot_general x4, matrix products, local(): jnp.einsum('td,sdh->sth', tokens, qkv_weight, preferred_element_type=jnp....  22.8 us
    all_to_all x4, starting transfers between devices, local(): incoming = lax.all_to_all(payload, 'ctx', 0, 0, tiled=True)  18.9 us
    all_to_all x4, waiting for transfers between devices, local(): incoming = lax.all_to_all(payload, 'ctx', 0, 0, tiled=True)  17.9 us
    dot_general x4, matrix products, local(): jnp.dot(attended[0], out_weight, preferred_element_type=jnp.float32)  13.8 us
    all_gather x1, blocking collectives, local(): lax.all_gather(table, 'ctx', axis=0, tiled=True).astype(jnp.int32)  12.9 us
  transfers between devices with their start and end apart: 10, of which 8 were waited for; matrix products, arithmetic and copies ran while one was open for 16% of the time, Pallas kernels for 12%

profile of v13, /device:TPU:0, one launch (start us, length us, event | category | flops | bytes accessed | tf_op | source)
XLA Modules:
  0.0 239.7 jit_solution(177598551009919320)
XLA Ops:
  0.0 3.9 %collective-permute-start = (bf16[256,3072]{1,0:T(8,128)(2,1)}, bf16[256,3072]{1,0:T(8,128)(2,1)}, u32[]{:S(2)}, u32[]{:S(2)}) collective-permute-start(bf16[256,3072]{1,0:T(8,128)(2,1)} %bitcast.127), channel_id=1, source_target_pairs={{0,24},{8,16},{16,8},{24,0},{1,25},{9,17},{17,9},{25,1},{2,26},{10... | collective-permute-start | bytes 4718600 | tf_op jit(solution)/shard_map/ppermute | solution.py:136
  5.4 12.9 %all-gather = f32[8,4,11]{2,1,0:T(4,128)S(1)} all-gather(f32[1,4,11]{2,1,0:T(4,128)S(1)} %fusion.42), channel_id=1, replica_groups=mesh['dp'=4,'ctx'=8] {'ctx'}, dimensions={0}, use_global_device_ids=true | all-gather | bytes 1584 | tf_op jit(solution)/shard_map/all_gather | solution.py:110
  19.1 19.5 %collective-permute-done = bf16[256,3072]{1,0:T(8,128)(2,1)} collective-permute-done((bf16[256,3072]{1,0:T(8,128)(2,1)}, bf16[256,3072]{1,0:T(8,128)(2,1)}, u32[]{:S(2)}, u32[]{:S(2)}) %collective-permute-start) | collective-permute-done | bytes 1572896 | tf_op jit(solution)/shard_map/ppermute | solution.py:136
  38.6 5.7 %fusion.31.q_ref = bf16[3,256,384]{2,1,0:T(8,128)(2,1)S(1)} fusion(bf16[3,3072,384]{2,1,0:T(8,128)(2,1)} %param.8, bf16[256,3072]{1,0:T(8,128)(2,1)} %collective-permute-done), kind=kOutput, calls=%fused_computation.28 | convolution fusion | flops 1812234240 | bytes 9240576 | tf_op jit(solution)/shard_map/td,sdh->sth/dot_general | solution.py:145
  46.3 5.2 %all-to-all-start = ((bf16[16,2,1,64,384]{4,3,2,1,0:T(8,128)(2,1)}), bf16[16,2,1,64,384]{4,3,2,1,0:T(8,128)(2,1)}, u32[]{:S(2)}, u32[]{:S(2)}) async-start(bf16[16,2,1,64,384]{4,3,2,1,0:T(8,128)(2,1)} %bitcast.119), calls=%async_computation | async-start | bytes 3145728 | tf_op jit(solution)/shard_map/all_to_all | solution.py:156
  54.6 34.1 %collective-permute-done.2 = bf16[256,3072]{1,0:T(8,128)(2,1)} collective-permute-done((bf16[256,3072]{1,0:T(8,128)(2,1)}, bf16[256,3072]{1,0:T(8,128)(2,1)}, u32[]{:S(2)}, u32[]{:S(2)}) %collective-permute-start.2) | collective-permute-done | bytes 1572896 | tf_op jit(solution)/shard_map/ppermute | solution.py:136
  89.5 5.7 %fusion.28.q_ref = bf16[3,256,384]{2,1,0:T(8,128)(2,1)S(1)} fusion(bf16[3,3072,384]{2,1,0:T(8,128)(2,1)} %param.8, bf16[256,3072]{1,0:T(8,128)(2,1)} %collective-permute-done.2), kind=kOutput, calls=%fused_computation.27 | convolution fusion | flops 1812234240 | bytes 9240576 | tf_op jit(solution)/shard_map/td,sdh->sth/dot_general | solution.py:145
  97.3 4.4 %all-to-all-start.1 = ((bf16[16,2,1,64,384]{4,3,2,1,0:T(8,128)(2,1)}), bf16[16,2,1,64,384]{4,3,2,1,0:T(8,128)(2,1)}, u32[]{:S(2)}, u32[]{:S(2)}) async-start(bf16[16,2,1,64,384]{4,3,2,1,0:T(8,128)(2,1)} %bitcast.116), calls=%async_computation.1 | async-start | bytes 3145728 | tf_op jit(solution)/shard_map/all_to_all | solution.py:156
  105.2 5.7 %fusion.25.q_ref = bf16[3,256,384]{2,1,0:T(8,128)(2,1)S(1)} fusion(bf16[3,3072,384]{2,1,0:T(8,128)(2,1)} %param.8, bf16[256,3072]{1,0:T(8,128)(2,1)} %collective-permute-done.4), kind=kOutput, calls=%fused_computation.26 | convolution fusion | flops 1812234240 | bytes 9240576 | tf_op jit(solution)/shard_map/td,sdh->sth/dot_general | solution.py:145
  112.9 7.3 %shard_map.73 = bf16[1,256,384]{2,1,0:T(8,128)(2,1)} custom-call(s32[4,10]{1,0:T(4,128)} %add_select_fusion.2.pos_ref, s32[4]{0:T(128)} %count_ref.7, f32[4,3,10]{2,1,0:T(4,128)} %fusion.40.bias_ref, bf16[3,256,384]{2,1,0:T(8,128)(2,1)} %copy-done.5, bf16[4,2,1,64,384]{4,3,2,1,0:T(8,128)(2,1)} %bitcast.109, bf16[16,2,1,64,384]{4,3,2,1,0:T(8,128)(2,1)} %all-to-all-done.far_ref), custom_call_target="tpu_custom_call" | custom-call | tf_op jit(solution)/shard_map/pallas_call | solution.py:80
  120.2 3.1 %convolution_convert_fusion.3 = bf16[256,3072]{1,0:T(8,128)(2,1)} fusion(bf16[384,3072]{1,0:T(8,128)(2,1)S(1)} %copy-done, bf16[1,256,384]{2,1,0:T(8,128)(2,1)} %shard_map.73), kind=kOutput, calls=%fused_computation.10 | convolution fusion | flops 604766208 | bytes 4128768 | tf_op jit(solution)/shard_map/dot_general | solution.py:161
  123.3 16.2 %all-to-all-done.1.far_ref = bf16[16,2,1,64,384]{4,3,2,1,0:T(8,128)(2,1)} async-done(((bf16[16,2,1,64,384]{4,3,2,1,0:T(8,128)(2,1)}), bf16[16,2,1,64,384]{4,3,2,1,0:T(8,128)(2,1)}, u32[]{:S(2)}, u32[]{:S(2)}) %all-to-all-start.1) | async-done | bytes 1572896 | tf_op jit(solution)/shard_map/all_to_all | solution.py:156
  139.5 4.5 %all-to-all-start.2 = ((bf16[16,2,1,64,384]{4,3,2,1,0:T(8,128)(2,1)}), bf16[16,2,1,64,384]{4,3,2,1,0:T(8,128)(2,1)}, u32[]{:S(2)}, u32[]{:S(2)}) async-start(bf16[16,2,1,64,384]{4,3,2,1,0:T(8,128)(2,1)} %bitcast.118), calls=%async_computation.2 | async-start | bytes 3145728 | tf_op jit(solution)/shard_map/all_to_all | solution.py:156
  146.5 5.7 %fusion.22.q_ref = bf16[3,256,384]{2,1,0:T(8,128)(2,1)S(1)} fusion(bf16[3,3072,384]{2,1,0:T(8,128)(2,1)} %param.8, bf16[256,3072]{1,0:T(8,128)(2,1)} %bitcast.130), kind=kOutput, calls=%fused_computation.25 | convolution fusion | flops 1812234240 | bytes 9240576 | tf_op jit(solution)/shard_map/td,sdh->sth/dot_general | solution.py:145
  154.3 7.3 %shard_map.74 = bf16[1,256,384]{2,1,0:T(8,128)(2,1)} custom-call(s32[4,10]{1,0:T(4,128)} %add_select_fusion.2.pos_ref, s32[4]{0:T(128)} %count_ref.7, f32[4,3,10]{2,1,0:T(4,128)} %fusion.40.bias_ref, bf16[3,256,384]{2,1,0:T(8,128)(2,1)} %copy-done.6, bf16[4,2,1,64,384]{4,3,2,1,0:T(8,128)(2,1)} %bitcast.111, bf16[16,2,1,64,384]{4,3,2,1,0:T(8,128)(2,1)} %all-to-all-done.1.far_ref), custom_call_target="tpu_custom_call" | custom-call | tf_op jit(solution)/shard_map/pallas_call | solution.py:80
  161.6 3.2 %convolution_convert_fusion.2 = bf16[256,3072]{1,0:T(8,128)(2,1)} fusion(bf16[384,3072]{1,0:T(8,128)(2,1)S(1)} %copy-done, bf16[1,256,384]{2,1,0:T(8,128)(2,1)} %shard_map.74), kind=kOutput, calls=%fused_computation.9 | convolution fusion | flops 604766208 | bytes 4128768 | tf_op jit(solution)/shard_map/dot_general | solution.py:161
  164.7 17.0 %collective-permute-done.1 = bf16[256,3072]{1,0:T(8,128)(2,1)} collective-permute-done((bf16[256,3072]{1,0:T(8,128)(2,1)}, bf16[256,3072]{1,0:T(8,128)(2,1)}, u32[]{:S(2)}, u32[]{:S(2)}) %collective-permute-start.1) | collective-permute-done | bytes 1572896 | tf_op jit(solution)/shard_map/ppermute | solution.py:166
  181.7 4.8 %all-to-all-start.3 = ((bf16[16,2,1,64,384]{4,3,2,1,0:T(8,128)(2,1)}), bf16[16,2,1,64,384]{4,3,2,1,0:T(8,128)(2,1)}, u32[]{:S(2)}, u32[]{:S(2)}) async-start(bf16[16,2,1,64,384]{4,3,2,1,0:T(8,128)(2,1)} %bitcast.117), calls=%async_computation.3 | async-start | bytes 3145728 | tf_op jit(solution)/shard_map/all_to_all | solution.py:156
  188.0 7.3 %shard_map.75 = bf16[1,256,384]{2,1,0:T(8,128)(2,1)} custom-call(s32[4,10]{1,0:T(4,128)} %add_select_fusion.2.pos_ref, s32[4]{0:T(128)} %count_ref.7, f32[4,3,10]{2,1,0:T(4,128)} %fusion.40.bias_ref, bf16[3,256,384]{2,1,0:T(8,128)(2,1)} %copy-done.7, bf16[4,2,1,64,384]{4,3,2,1,0:T(8,128)(2,1)} %bitcast.113, bf16[16,2,1,64,384]{4,3,2,1,0:T(8,128)(2,1)} %all-to-all-done.2.far_ref), custom_call_target="tpu_custom_call" | custom-call | tf_op jit(solution)/shard_map/pallas_call | solution.py:80
  195.3 3.1 %convolution_convert_fusion.1 = bf16[256,3072]{1,0:T(8,128)(2,1)} fusion(bf16[384,3072]{1,0:T(8,128)(2,1)S(1)} %copy-done, bf16[1,256,384]{2,1,0:T(8,128)(2,1)} %shard_map.75), kind=kOutput, calls=%fused_computation.8 | convolution fusion | flops 604766208 | bytes 4128768 | tf_op jit(solution)/shard_map/dot_general | solution.py:161
  199.8 23.8 %collective-permute-done.3 = bf16[256,3072]{1,0:T(8,128)(2,1)} collective-permute-done((bf16[256,3072]{1,0:T(8,128)(2,1)}, bf16[256,3072]{1,0:T(8,128)(2,1)}, u32[]{:S(2)}, u32[]{:S(2)}) %collective-permute-start.3) | collective-permute-done | bytes 1572896 | tf_op jit(solution)/shard_map/ppermute | solution.py:166
  224.4 7.3 %shard_map.76 = bf16[1,256,384]{2,1,0:T(8,128)(2,1)} custom-call(s32[4,10]{1,0:T(4,128)} %add_select_fusion.2.pos_ref, s32[4]{0:T(128)} %count_ref.7, f32[4,3,10]{2,1,0:T(4,128)} %fusion.40.bias_ref, bf16[3,256,384]{2,1,0:T(8,128)(2,1)} %copy-done.8, bf16[4,2,1,64,384]{4,3,2,1,0:T(8,128)(2,1)} %bitcast.115, bf16[16,2,1,64,384]{4,3,2,1,0:T(8,128)(2,1)} %all-to-all-done.3.far_ref), custom_call_target="tpu_custom_call" | custom-call | tf_op jit(solution)/shard_map/pallas_call | solution.py:80
  231.7 3.4 %collective-permute-done.5 = bf16[256,3072]{1,0:T(8,128)(2,1)} collective-permute-done((bf16[256,3072]{1,0:T(8,128)(2,1)}, bf16[256,3072]{1,0:T(8,128)(2,1)}, u32[]{:S(2)}, u32[]{:S(2)}) %collective-permute-start.5) | collective-permute-done | bytes 1572896 | tf_op jit(solution)/shard_map/ppermute | solution.py:166
  235.2 4.6 %fusion.1 = bf16[1,256,3072]{2,1,0:T(8,128)(2,1)} fusion(bf16[256,3072]{1,0:T(8,128)(2,1)} %collective-permute-done.5, bf16[256,3072]{1,0:T(8,128)(2,1)} %collective-permute-done.3, bf16[256,3072]{1,0:T(8,128)(2,1)} %collective-permute-done.1, bf16[384,3072]{1,0:T(8,128)(2,1)S(1)} %copy-done, bf16[1,256,384]{2,1,0:T(8,128)(2,1)} %shard_map.76), kind=kOutput, calls=%fused_computation.12 | convolution fusion | flops 611057664 | bytes 8847360 | tf_op jit(solution)/shard_map/dot_general | solution.py:161
  (85 shorter events, 23.9 us)
Async XLA Ops:
  0.0 120.2 %copy-start = (bf16[384,3072]{1,0:T(8,128)(2,1)S(1)}, bf16[384,3072]{1,0:T(8,128)(2,1)}, u32[]{:S(2)}) copy-start(bf16[384,3072]{1,0:T(8,128)(2,1)} %param.9) | copy-start | bytes 7077892
  0.0 38.6 %collective-permute-start = (bf16[256,3072]{1,0:T(8,128)(2,1)}, bf16[256,3072]{1,0:T(8,128)(2,1)}, u32[]{:S(2)}, u32[]{:S(2)}) collective-permute-start(bf16[256,3072]{1,0:T(8,128)(2,1)} %bitcast.127), channel_id=1, source_target_pairs={{0,24},{8,16},{16,8},{24,0},{1,25},{9,17},{17,9},{25,1},{2,26},{10... | collective-permute-start | bytes 4718600 | tf_op jit(solution)/shard_map/ppermute | solution.py:136
  44.3 2.0 copy-start.5
  44.4 1.9 copy-start.1
  46.3 8.2 %copy-start.9 = (s32[4,10]{1,0:T(4,128)S(1)}, s32[4,10]{1,0:T(4,128)}, u32[]{:S(2)}) copy-start(s32[4,10]{1,0:T(4,128)} %param.10) | copy-start | bytes 484
  46.3 8.3 %copy-start.11 = (s32[4,10]{1,0:T(4,128)S(1)}, s32[4,10]{1,0:T(4,128)}, u32[]{:S(2)}) copy-start(s32[4,10]{1,0:T(4,128)} %param.12) | copy-start | bytes 484
  46.3 43.2 %all-to-all-start = ((bf16[16,2,1,64,384]{4,3,2,1,0:T(8,128)(2,1)}), bf16[16,2,1,64,384]{4,3,2,1,0:T(8,128)(2,1)}, u32[]{:S(2)}, u32[]{:S(2)}) async-start(bf16[16,2,1,64,384]{4,3,2,1,0:T(8,128)(2,1)} %bitcast.119), calls=%async_computation | async-start | bytes 3145728 | tf_op jit(solution)/shard_map/all_to_all | solution.py:156
  51.6 37.1 %collective-permute-start.2 = (bf16[256,3072]{1,0:T(8,128)(2,1)}, bf16[256,3072]{1,0:T(8,128)(2,1)}, u32[]{:S(2)}, u32[]{:S(2)}) collective-permute-start(bf16[256,3072]{1,0:T(8,128)(2,1)} %bitcast.128), channel_id=1, source_target_pairs={{0,8},{8,0},{16,24},{24,16},{1,9},{9,1},{17,25},{25,17},{2,10},{10... | collective-permute-start | bytes 4718600 | tf_op jit(solution)/shard_map/ppermute | solution.py:136
  53.1 52.1 %collective-permute-start.4 = (bf16[256,3072]{1,0:T(8,128)(2,1)}, bf16[256,3072]{1,0:T(8,128)(2,1)}, u32[]{:S(2)}, u32[]{:S(2)}) collective-permute-start(bf16[256,3072]{1,0:T(8,128)(2,1)} %bitcast.129), channel_id=1, source_target_pairs={{0,16},{8,24},{16,0},{24,8},{1,17},{9,25},{17,1},{25,9},{2,18},{10... | collective-permute-start | bytes 4718600 | tf_op jit(solution)/shard_map/ppermute | solution.py:136
  95.2 2.0 copy-start.6
  95.3 1.9 copy-start.2
  97.3 4.4 %copy-start.10 = (s32[4]{0:T(128)S(1)}, s32[4]{0:T(128)}, u32[]{:S(2)}) copy-start(s32[4]{0:T(128)} %count_ref.7) | copy-start | bytes 52
  97.3 42.3 %all-to-all-start.1 = ((bf16[16,2,1,64,384]{4,3,2,1,0:T(8,128)(2,1)}), bf16[16,2,1,64,384]{4,3,2,1,0:T(8,128)(2,1)}, u32[]{:S(2)}, u32[]{:S(2)}) async-start(bf16[16,2,1,64,384]{4,3,2,1,0:T(8,128)(2,1)} %bitcast.116), calls=%async_computation.1 | async-start | bytes 3145728 | tf_op jit(solution)/shard_map/all_to_all | solution.py:156
  101.7 1.4 copy-start.12
  110.9 2.0 copy-start.7
  111.0 1.9 copy-start.3
  139.5 42.2 %all-to-all-start.2 = ((bf16[16,2,1,64,384]{4,3,2,1,0:T(8,128)(2,1)}), bf16[16,2,1,64,384]{4,3,2,1,0:T(8,128)(2,1)}, u32[]{:S(2)}, u32[]{:S(2)}) async-start(bf16[16,2,1,64,384]{4,3,2,1,0:T(8,128)(2,1)} %bitcast.118), calls=%async_computation.2 | async-start | bytes 3145728 | tf_op jit(solution)/shard_map/all_to_all | solution.py:156
  144.0 37.7 %collective-permute-start.1 = (bf16[256,3072]{1,0:T(8,128)(2,1)}, bf16[256,3072]{1,0:T(8,128)(2,1)}, u32[]{:S(2)}, u32[]{:S(2)}) collective-permute-start(bf16[256,3072]{1,0:T(8,128)(2,1)} %convolution_convert_fusion.3), channel_id=1, source_target_pairs={{0,24},{8,16},{16,8},{24,0},{1,25},{9,17},{17,9},{25,1},{2,26},{10... | collective-permute-start | bytes 4718600 | tf_op jit(solution)/shard_map/ppermute | solution.py:166
  152.2 2.1 copy-start.8
  152.3 2.0 copy-start.4
  181.7 42.7 %all-to-all-start.3 = ((bf16[16,2,1,64,384]{4,3,2,1,0:T(8,128)(2,1)}), bf16[16,2,1,64,384]{4,3,2,1,0:T(8,128)(2,1)}, u32[]{:S(2)}, u32[]{:S(2)}) async-start(bf16[16,2,1,64,384]{4,3,2,1,0:T(8,128)(2,1)} %bitcast.117), calls=%async_computation.3 | async-start | bytes 3145728 | tf_op jit(solution)/shard_map/all_to_all | solution.py:156
  186.5 37.1 %collective-permute-start.3 = (bf16[256,3072]{1,0:T(8,128)(2,1)}, bf16[256,3072]{1,0:T(8,128)(2,1)}, u32[]{:S(2)}, u32[]{:S(2)}) collective-permute-start(bf16[256,3072]{1,0:T(8,128)(2,1)} %convolution_convert_fusion.2), channel_id=1, source_target_pairs={{0,8},{8,0},{16,24},{24,16},{1,9},{9,1},{17,25},{25,17},{2,10},{10... | collective-permute-start | bytes 4718600 | tf_op jit(solution)/shard_map/ppermute | solution.py:166
  198.3 36.8 %collective-permute-start.5 = (bf16[256,3072]{1,0:T(8,128)(2,1)}, bf16[256,3072]{1,0:T(8,128)(2,1)}, u32[]{:S(2)}, u32[]{:S(2)}) collective-permute-start(bf16[256,3072]{1,0:T(8,128)(2,1)} %convolution_convert_fusion.1), channel_id=1, source_target_pairs={{0,16},{8,24},{16,0},{24,8},{1,17},{9,25},{17,1},{25,9},{2,18},{10... | collective-permute-start | bytes 4718600 | tf_op jit(solution)/shard_map/ppermute | solution.py:166

commit v14 on v13

--- a/solution.py
+++ b/solution.py
@@ -142,11 +142,11 @@
         tokens = arrived[step]
         if index >= 1:
             tokens, _ = lax.optimization_barrier((tokens, received[max(index - 2, 0)]))
-        projected = jnp.einsum(
-            "td,sdh->sth", tokens, qkv_weight, preferred_element_type=jnp.float32
+        key_value = jnp.einsum(
+            "td,sdh->sth", tokens, qkv_weight[1:3], preferred_element_type=jnp.float32
         ).astype(jnp.bfloat16)
         by_tile = jnp.transpose(
-            projected[1:3].reshape(2, tile_count, TILE, width_here), (1, 0, 2, 3)
+            key_value.reshape(2, tile_count, TILE, width_here), (1, 0, 2, 3)
         )[:, :, None]
         payload = by_tile.at[send_picks].get(mode="promise_in_bounds")
         if index >= 2:
@@ -157,7 +157,8 @@
         received.append(incoming)
         if index == len(order) - 1 and len(sent) >= 2:
             incoming, _ = lax.optimization_barrier((incoming, sent[-2]))
-        attended = attend(positions, live_counts, bias, projected, by_tile, incoming, heads_here, head_size)
+        queries = jnp.dot(tokens, qkv_weight[0], preferred_element_type=jnp.float32).astype(jnp.bfloat16)
+        attended = attend(positions, live_counts, bias, queries[None], by_tile, incoming, heads_here, head_size)
         partial_out = jnp.dot(
             attended[0], out_weight, preferred_element_type=jnp.float32
         ).astype(jnp.bfloat16)

time: 240 us -> 241 us (level)
  matrix products: 36.7 us -> 45.1 us
  waiting for transfers between devices: 116 us -> 108 us
    dot_general x4 -> x8, matrix products: 22.8 us -> 31.1 us  [the longest x4 16.3 us: local(): jnp.einsum('td,sdh->sth', tokens, qkv_weight[1:3], preferred_element_type...]
    ppermute x3, waiting for transfers between devices: 44.2 us -> 39.9 us  [local(): partial_out = lax.ppermute(partial_out, 'dp', partner_pairs(n_dp, step))]
    all_to_all x4, waiting for transfers between devices: 17.9 us -> 14.9 us  [local(): incoming = lax.all_to_all(payload, 'ctx', 0, 0, tiled=True)]
  transfers between devices with their start and end apart: 10 -> 10, of which waited for: 8 -> 7; matrix products, arithmetic and copies ran while one was open for 16% -> 20% of each run, Pallas kernels for 12% -> 12%
where the time goes in v14:
time: 241 us
  waiting for transfers between devices  108 us (45%)
  matrix products  45.1 us (19%)
  starting transfers between devices  31.3 us (13%)
  Pallas kernels  29.1 us (12%)
  blocking collectives  12.9 us (5%)
  local copies, waits for them, and re-layouts  10.9 us (5%)
  other arithmetic  2.66 us (1%)
    ppermute x3, waiting for transfers between devices, local(): arrived[step] = lax.ppermute(own_tokens, 'dp', partner_pairs(n_dp, step))  53.4 us
    ppermute x3, waiting for transfers between devices, local(): partial_out = lax.ppermute(partial_out, 'dp', partner_pairs(n_dp, step))  39.9 us
    pallas_call x4, Pallas kernels, attend(): pl.pallas_call(kernel, out_shape=jax.ShapeDtypeStruct((1, token_count, wi...  29.1 us
    all_to_all x4, starting transfers between devices, local(): incoming = lax.all_to_all(payload, 'ctx', 0, 0, tiled=True)  18.9 us
    dot_general x4, matrix products, local(): jnp.einsum('td,sdh->sth', tokens, qkv_weight[1:3], preferred_element_type...  16.3 us
    all_to_all x4, waiting for transfers between devices, local(): incoming = lax.all_to_all(payload, 'ctx', 0, 0, tiled=True)  14.9 us
    dot_general x4, matrix products, local(): jnp.dot(tokens, qkv_weight[0], preferred_element_type=jnp.float32)  14.8 us
    dot_general x4, matrix products, local(): jnp.dot(attended[0], out_weight, preferred_element_type=jnp.float32)  14 us
  transfers between devices with their start and end apart: 10, of which 7 were waited for; matrix products, arithmetic and copies ran while one was open for 20% of the time, Pallas kernels for 12%

profile of v14, /device:TPU:0, one launch (start us, length us, event | category | flops | bytes accessed | tf_op | source)
XLA Modules:
  0.0 240.5 jit_solution(415418166492565534)
XLA Ops:
  0.0 3.9 %collective-permute-start = (bf16[256,3072]{1,0:T(8,128)(2,1)}, bf16[256,3072]{1,0:T(8,128)(2,1)}, u32[]{:S(2)}, u32[]{:S(2)}) collective-permute-start(bf16[256,3072]{1,0:T(8,128)(2,1)} %bitcast.152), channel_id=1, source_target_pairs={{0,24},{8,16},{16,8},{24,0},{1,25},{9,17},{17,9},{25,1},{2,26},{10... | collective-permute-start | bytes 4718600 | tf_op jit(solution)/shard_map/ppermute | solution.py:136
  5.4 12.9 %all-gather = f32[8,4,11]{2,1,0:T(4,128)S(1)} all-gather(f32[1,4,11]{2,1,0:T(4,128)S(1)} %fusion.78), channel_id=1, replica_groups=mesh['dp'=4,'ctx'=8] {'ctx'}, dimensions={0}, use_global_device_ids=true | all-gather | bytes 1584 | tf_op jit(solution)/shard_map/all_gather | solution.py:110
  19.1 19.5 %collective-permute-done = bf16[256,3072]{1,0:T(8,128)(2,1)} collective-permute-done((bf16[256,3072]{1,0:T(8,128)(2,1)}, bf16[256,3072]{1,0:T(8,128)(2,1)}, u32[]{:S(2)}, u32[]{:S(2)}) %collective-permute-start) | collective-permute-done | bytes 1572896 | tf_op jit(solution)/shard_map/ppermute | solution.py:136
  38.6 4.2 %fusion.26 = bf16[2,384,256]{1,2,0:T(8,128)(2,1)S(1)} fusion(bf16[3,3072,384]{2,1,0:T(8,128)(2,1)} %param.8, bf16[256,3072]{1,0:T(8,128)(2,1)} %collective-permute-done), kind=kOutput, calls=%fused_computation.37 | convolution fusion | flops 1208156160 | bytes 6684672 | tf_op jit(solution)/shard_map/td,sdh->sth/dot_general | solution.py:145
  44.8 5.2 %all-to-all-start = ((bf16[16,2,1,64,384]{4,3,2,1,0:T(8,128)(2,1)}), bf16[16,2,1,64,384]{4,3,2,1,0:T(8,128)(2,1)}, u32[]{:S(2)}, u32[]{:S(2)}) async-start(bf16[16,2,1,64,384]{4,3,2,1,0:T(8,128)(2,1)} %bitcast.144), calls=%async_computation | async-start | bytes 3145728 | tf_op jit(solution)/shard_map/all_to_all | solution.py:156
  53.2 33.9 %collective-permute-done.2 = bf16[256,3072]{1,0:T(8,128)(2,1)} collective-permute-done((bf16[256,3072]{1,0:T(8,128)(2,1)}, bf16[256,3072]{1,0:T(8,128)(2,1)}, u32[]{:S(2)}, u32[]{:S(2)}) %collective-permute-start.2) | collective-permute-done | bytes 1572896 | tf_op jit(solution)/shard_map/ppermute | solution.py:136
  87.9 4.2 %fusion.31 = bf16[256,2,384]{2,0,1:T(8,128)(2,1)S(1)} fusion(bf16[3,3072,384]{2,1,0:T(8,128)(2,1)} %param.8, bf16[256,3072]{1,0:T(8,128)(2,1)} %collective-permute-done.2), kind=kOutput, calls=%fused_computation.38 | convolution fusion | flops 1208156160 | bytes 6684672 | tf_op jit(solution)/shard_map/td,sdh->sth/dot_general | solution.py:145
  94.1 4.4 %all-to-all-start.1 = ((bf16[16,2,1,64,384]{4,3,2,1,0:T(8,128)(2,1)}), bf16[16,2,1,64,384]{4,3,2,1,0:T(8,128)(2,1)}, u32[]{:S(2)}, u32[]{:S(2)}) async-start(bf16[16,2,1,64,384]{4,3,2,1,0:T(8,128)(2,1)} %bitcast.141), calls=%async_computation.1 | async-start | bytes 3145728 | tf_op jit(solution)/shard_map/all_to_all | solution.py:156
  101.8 3.8 %fusion.67.q_ref = bf16[1,256,384]{2,1,0:T(8,128)(2,1)} fusion(bf16[256,3072]{1,0:T(8,128)(2,1)} %collective-permute-done, bf16[3,3072,384]{2,1,0:T(8,128)(2,1)} %param.8), kind=kOutput, calls=%fused_computation.48 | convolution fusion | flops 604078080 | bytes 4128768 | tf_op jit(solution)/shard_map/dot_general | solution.py:160
  105.6 4.2 %fusion.36 = bf16[256,2,384]{2,0,1:T(8,128)(2,1)S(1)} fusion(bf16[3,3072,384]{2,1,0:T(8,128)(2,1)} %param.8, bf16[256,3072]{1,0:T(8,128)(2,1)} %collective-permute-done.4), kind=kOutput, calls=%fused_computation.39 | convolution fusion | flops 1208156160 | bytes 6684672 | tf_op jit(solution)/shard_map/td,sdh->sth/dot_general | solution.py:145
  111.8 7.3 %shard_map.73 = bf16[1,256,384]{2,1,0:T(8,128)(2,1)} custom-call(s32[4,10]{1,0:T(4,128)} %add_select_fusion.2.pos_ref, s32[4]{0:T(128)} %count_ref.7, f32[4,3,10]{2,1,0:T(4,128)} %fusion.76.bias_ref, bf16[1,256,384]{2,1,0:T(8,128)(2,1)} %fusion.67.q_ref, bf16[4,2,1,64,384]{4,3,2,1,0:T(8,128)(2,1)} %bitcast.134, bf16[16,2,1,64,384]{4,3,2,1,0:T(8,128)(2,1)} %all-to-all-done.far_ref), custom_call_target="tpu_custom_call" | custom-call | tf_op jit(solution)/shard_map/pallas_call | solution.py:80
  122.3 14.1 %all-to-all-done.1.far_ref = bf16[16,2,1,64,384]{4,3,2,1,0:T(8,128)(2,1)} async-done(((bf16[16,2,1,64,384]{4,3,2,1,0:T(8,128)(2,1)}), bf16[16,2,1,64,384]{4,3,2,1,0:T(8,128)(2,1)}, u32[]{:S(2)}, u32[]{:S(2)}) %all-to-all-start.1) | async-done | bytes 1572896 | tf_op jit(solution)/shard_map/all_to_all | solution.py:156
  136.4 4.5 %all-to-all-start.2 = ((bf16[16,2,1,64,384]{4,3,2,1,0:T(8,128)(2,1)}), bf16[16,2,1,64,384]{4,3,2,1,0:T(8,128)(2,1)}, u32[]{:S(2)}, u32[]{:S(2)}) async-start(bf16[16,2,1,64,384]{4,3,2,1,0:T(8,128)(2,1)} %bitcast.143), calls=%async_computation.2 | async-start | bytes 3145728 | tf_op jit(solution)/shard_map/all_to_all | solution.py:156
  143.4 3.8 %fusion.64.q_ref = bf16[1,256,384]{2,1,0:T(8,128)(2,1)} fusion(bf16[256,3072]{1,0:T(8,128)(2,1)} %collective-permute-done.2, bf16[3,3072,384]{2,1,0:T(8,128)(2,1)} %param.8), kind=kOutput, calls=%fused_computation.47 | convolution fusion | flops 604078080 | bytes 4128768 | tf_op jit(solution)/shard_map/dot_general | solution.py:160
  147.2 3.8 %fusion.41 = bf16[256,2,384]{2,0,1:T(8,128)(2,1)S(1)} fusion(bf16[3,3072,384]{2,1,0:T(8,128)(2,1)} %param.8, bf16[256,3072]{1,0:T(8,128)(2,1)S(1)} %bitcast.155), kind=kOutput, calls=%fused_computation.40 | convolution fusion | flops 1208156160 | bytes 6684672 | tf_op jit(solution)/shard_map/td,sdh->sth/dot_general | solution.py:145
  153.0 7.3 %shard_map.74 = bf16[1,256,384]{2,1,0:T(8,128)(2,1)} custom-call(s32[4,10]{1,0:T(4,128)} %add_select_fusion.2.pos_ref, s32[4]{0:T(128)} %count_ref.7, f32[4,3,10]{2,1,0:T(4,128)} %fusion.76.bias_ref, bf16[1,256,384]{2,1,0:T(8,128)(2,1)} %fusion.64.q_ref, bf16[4,2,1,64,384]{4,3,2,1,0:T(8,128)(2,1)} %bitcast.136, ...), custom_call_target="tpu_custom_call" | custom-call | tf_op jit(solution)/shard_map/pallas_call | solution.py:80
  163.3 15.3 %collective-permute-done.1 = bf16[256,3072]{1,0:T(8,128)(2,1)} collective-permute-done((bf16[256,3072]{1,0:T(8,128)(2,1)}, bf16[256,3072]{1,0:T(8,128)(2,1)}, u32[]{:S(2)}, u32[]{:S(2)}) %collective-permute-start.1) | collective-permute-done | bytes 1572896 | tf_op jit(solution)/shard_map/ppermute | solution.py:167
  178.6 4.8 %all-to-all-start.3 = ((bf16[16,2,1,64,384]{4,3,2,1,0:T(8,128)(2,1)}), bf16[16,2,1,64,384]{4,3,2,1,0:T(8,128)(2,1)}, u32[]{:S(2)}, u32[]{:S(2)}) async-start(bf16[16,2,1,64,384]{4,3,2,1,0:T(8,128)(2,1)} %bitcast.142), calls=%async_computation.3 | async-start | bytes 3145728 | tf_op jit(solution)/shard_map/all_to_all | solution.py:156
  183.4 3.8 %fusion.61.q_ref = bf16[1,256,384]{2,1,0:T(8,128)(2,1)} fusion(bf16[256,3072]{1,0:T(8,128)(2,1)} %collective-permute-done.4, bf16[3,3072,384]{2,1,0:T(8,128)(2,1)} %param.8), kind=kOutput, calls=%fused_computation.46 | convolution fusion | flops 604078080 | bytes 4128768 | tf_op jit(solution)/shard_map/dot_general | solution.py:160
  188.7 7.3 %shard_map.75 = bf16[1,256,384]{2,1,0:T(8,128)(2,1)} custom-call(s32[4,10]{1,0:T(4,128)} %add_select_fusion.2.pos_ref, s32[4]{0:T(128)} %count_ref.7, f32[4,3,10]{2,1,0:T(4,128)} %fusion.76.bias_ref, bf16[1,256,384]{2,1,0:T(8,128)(2,1)} %fusion.61.q_ref, bf16[4,2,1,64,384]{4,3,2,1,0:T(8,128)(2,1)} %bitcast.138, ...), custom_call_target="tpu_custom_call" | custom-call | tf_op jit(solution)/shard_map/pallas_call | solution.py:80
  204.0 20.3 %collective-permute-done.3 = bf16[256,3072]{1,0:T(8,128)(2,1)} collective-permute-done((bf16[256,3072]{1,0:T(8,128)(2,1)}, bf16[256,3072]{1,0:T(8,128)(2,1)}, u32[]{:S(2)}, u32[]{:S(2)}) %collective-permute-start.3) | collective-permute-done | bytes 1572896 | tf_op jit(solution)/shard_map/ppermute | solution.py:167
  224.3 7.3 %shard_map.76 = bf16[1,256,384]{2,1,0:T(8,128)(2,1)} custom-call(s32[4,10]{1,0:T(4,128)} %add_select_fusion.2.pos_ref, s32[4]{0:T(128)} %count_ref.7, f32[4,3,10]{2,1,0:T(4,128)} %fusion.76.bias_ref, bf16[1,256,384]{2,1,0:T(8,128)(2,1)} %fusion.58.q_ref, bf16[4,2,1,64,384]{4,3,2,1,0:T(8,128)(2,1)} %bitcast.140, ...), custom_call_target="tpu_custom_call" | custom-call | tf_op jit(solution)/shard_map/pallas_call | solution.py:80
  231.6 4.4 %collective-permute-done.5 = bf16[256,3072]{1,0:T(8,128)(2,1)} collective-permute-done((bf16[256,3072]{1,0:T(8,128)(2,1)}, bf16[256,3072]{1,0:T(8,128)(2,1)}, u32[]{:S(2)}, u32[]{:S(2)}) %collective-permute-start.5) | collective-permute-done | bytes 1572896 | tf_op jit(solution)/shard_map/ppermute | solution.py:167
  235.9 4.6 %fusion.17 = bf16[1,256,3072]{2,1,0:T(8,128)(2,1)} fusion(bf16[256,3072]{1,0:T(8,128)(2,1)} %collective-permute-done.5, bf16[256,3072]{1,0:T(8,128)(2,1)} %collective-permute-done.3, bf16[256,3072]{1,0:T(8,128)(2,1)} %collective-permute-done.1, bf16[384,3072]{1,0:T(8,128)(2,1)S(1)} %copy-done, bf16[1,256,384]{2,1,0:T(8,128)(2,1)} %shard_map.76), kind=kOutput, calls=%fused_computation.28 | convolution fusion | flops 611057664 | bytes 8847360 | tf_op jit(solution)/shard_map/dot_general | solution.py:162
  (81 shorter events, 35.6 us)
Async XLA Ops:
  0.0 119.1 %copy-start = (bf16[384,3072]{1,0:T(8,128)(2,1)S(1)}, bf16[384,3072]{1,0:T(8,128)(2,1)}, u32[]{:S(2)}) copy-start(bf16[384,3072]{1,0:T(8,128)(2,1)} %param.9) | copy-start | bytes 7077892
  0.0 38.6 %collective-permute-start = (bf16[256,3072]{1,0:T(8,128)(2,1)}, bf16[256,3072]{1,0:T(8,128)(2,1)}, u32[]{:S(2)}, u32[]{:S(2)}) collective-permute-start(bf16[256,3072]{1,0:T(8,128)(2,1)} %bitcast.152), channel_id=1, source_target_pairs={{0,24},{8,16},{16,8},{24,0},{1,25},{9,17},{17,9},{25,1},{2,26},{10... | collective-permute-start | bytes 4718600 | tf_op jit(solution)/shard_map/ppermute | solution.py:136
  42.9 1.9 copy-start.1
  44.8 8.2 %copy-start.7 = (s32[4,10]{1,0:T(4,128)S(1)}, s32[4,10]{1,0:T(4,128)}, u32[]{:S(2)}) copy-start(s32[4,10]{1,0:T(4,128)} %param.12) | copy-start | bytes 484
  44.8 8.3 %copy-start.5 = (s32[4,10]{1,0:T(4,128)S(1)}, s32[4,10]{1,0:T(4,128)}, u32[]{:S(2)}) copy-start(s32[4,10]{1,0:T(4,128)} %param.10) | copy-start | bytes 484
  44.8 43.1 %all-to-all-start = ((bf16[16,2,1,64,384]{4,3,2,1,0:T(8,128)(2,1)}), bf16[16,2,1,64,384]{4,3,2,1,0:T(8,128)(2,1)}, u32[]{:S(2)}, u32[]{:S(2)}) async-start(bf16[16,2,1,64,384]{4,3,2,1,0:T(8,128)(2,1)} %bitcast.144), calls=%async_computation | async-start | bytes 3145728 | tf_op jit(solution)/shard_map/all_to_all | solution.py:156
  50.0 37.1 %collective-permute-start.2 = (bf16[256,3072]{1,0:T(8,128)(2,1)}, bf16[256,3072]{1,0:T(8,128)(2,1)}, u32[]{:S(2)}, u32[]{:S(2)}) collective-permute-start(bf16[256,3072]{1,0:T(8,128)(2,1)} %bitcast.153), channel_id=1, source_target_pairs={{0,8},{8,0},{16,24},{24,16},{1,9},{9,1},{17,25},{25,17},{2,10},{10... | collective-permute-start | bytes 4718600 | tf_op jit(solution)/shard_map/ppermute | solution.py:136
  51.5 54.2 %collective-permute-start.4 = (bf16[256,3072]{1,0:T(8,128)(2,1)}, bf16[256,3072]{1,0:T(8,128)(2,1)}, u32[]{:S(2)}, u32[]{:S(2)}) collective-permute-start(bf16[256,3072]{1,0:T(8,128)(2,1)} %bitcast.154), channel_id=1, source_target_pairs={{0,16},{8,24},{16,0},{24,8},{1,17},{9,25},{17,1},{25,9},{2,18},{10... | collective-permute-start | bytes 4718600 | tf_op jit(solution)/shard_map/ppermute | solution.py:136
  92.2 1.9 copy-start.2
  94.1 4.4 %copy-start.6 = (s32[4]{0:T(128)S(1)}, s32[4]{0:T(128)}, u32[]{:S(2)}) copy-start(s32[4]{0:T(128)} %count_ref.7) | copy-start | bytes 52
  94.1 42.3 %all-to-all-start.1 = ((bf16[16,2,1,64,384]{4,3,2,1,0:T(8,128)(2,1)}), bf16[16,2,1,64,384]{4,3,2,1,0:T(8,128)(2,1)}, u32[]{:S(2)}, u32[]{:S(2)}) async-start(bf16[16,2,1,64,384]{4,3,2,1,0:T(8,128)(2,1)} %bitcast.141), calls=%async_computation.1 | async-start | bytes 3145728 | tf_op jit(solution)/shard_map/all_to_all | solution.py:156
  98.6 1.2 copy-start.8
  109.9 1.9 copy-start.3
  136.4 42.2 %all-to-all-start.2 = ((bf16[16,2,1,64,384]{4,3,2,1,0:T(8,128)(2,1)}), bf16[16,2,1,64,384]{4,3,2,1,0:T(8,128)(2,1)}, u32[]{:S(2)}, u32[]{:S(2)}) async-start(bf16[16,2,1,64,384]{4,3,2,1,0:T(8,128)(2,1)} %bitcast.143), calls=%async_computation.2 | async-start | bytes 3145728 | tf_op jit(solution)/shard_map/all_to_all | solution.py:156
  140.9 6.3 %copy-start.9 = (bf16[1,256,3072]{2,1,0:T(8,128)(2,1)S(1)}, bf16[1,256,3072]{2,1,0:T(8,128)(2,1)}, u32[]{:S(2)}) copy-start(bf16[1,256,3072]{2,1,0:T(8,128)(2,1)} %param.7) | copy-start | bytes 4718596
  140.9 37.7 %collective-permute-start.1 = (bf16[256,3072]{1,0:T(8,128)(2,1)}, bf16[256,3072]{1,0:T(8,128)(2,1)}, u32[]{:S(2)}, u32[]{:S(2)}) collective-permute-start(bf16[256,3072]{1,0:T(8,128)(2,1)} %convolution_convert_fusion.3), channel_id=1, source_target_pairs={{0,24},{8,16},{16,8},{24,0},{1,25},{9,17},{17,9},{25,1},{2,26},{10... | collective-permute-start | bytes 4718600 | tf_op jit(solution)/shard_map/ppermute | solution.py:167
  151.0 1.9 copy-start.4
  178.6 45.7 %all-to-all-start.3 = ((bf16[16,2,1,64,384]{4,3,2,1,0:T(8,128)(2,1)}), bf16[16,2,1,64,384]{4,3,2,1,0:T(8,128)(2,1)}, u32[]{:S(2)}, u32[]{:S(2)}) async-start(bf16[16,2,1,64,384]{4,3,2,1,0:T(8,128)(2,1)} %bitcast.142), calls=%async_computation.3 | async-start | bytes 3145728 | tf_op jit(solution)/shard_map/all_to_all | solution.py:156
  187.2 37.1 %collective-permute-start.3 = (bf16[256,3072]{1,0:T(8,128)(2,1)}, bf16[256,3072]{1,0:T(8,128)(2,1)}, u32[]{:S(2)}, u32[]{:S(2)}) collective-permute-start(bf16[256,3072]{1,0:T(8,128)(2,1)} %convolution_convert_fusion.2), channel_id=1, source_target_pairs={{0,8},{8,0},{16,24},{24,16},{1,9},{9,1},{17,25},{25,17},{2,10},{10... | collective-permute-start | bytes 4718600 | tf_op jit(solution)/shard_map/ppermute | solution.py:167
  195.9 4.7 %copy-start.10 = (bf16[1,256,3072]{2,1,0:T(8,128)(2,1)S(1)}, bf16[1,256,3072]{2,1,0:T(8,128)(2,1)}, u32[]{:S(2)}) copy-start(bf16[1,256,3072]{2,1,0:T(8,128)(2,1)} %param.7) | copy-start | bytes 4718596
  199.1 36.8 %collective-permute-start.5 = (bf16[256,3072]{1,0:T(8,128)(2,1)}, bf16[256,3072]{1,0:T(8,128)(2,1)}, u32[]{:S(2)}, u32[]{:S(2)}) collective-permute-start(bf16[256,3072]{1,0:T(8,128)(2,1)} %convolution_convert_fusion.1), channel_id=1, source_target_pairs={{0,16},{8,24},{16,0},{24,8},{1,17},{9,25},{17,1},{25,9},{2,18},{10... | collective-permute-start | bytes 4718600 | tf_op jit(solution)/shard_map/ppermute | solution.py:167

commit v15 on v13

--- a/solution.py
+++ b/solution.py
@@ -140,8 +140,8 @@
     sent = []
     for index, step in enumerate(order):
         tokens = arrived[step]
-        if index >= 1:
-            tokens, _ = lax.optimization_barrier((tokens, received[max(index - 2, 0)]))
+        if index >= 2:
+            tokens, _ = lax.optimization_barrier((tokens, received[index - 2]))
         projected = jnp.einsum(
             "td,sdh->sth", tokens, qkv_weight, preferred_element_type=jnp.float32
         ).astype(jnp.bfloat16)

time: 240 us -> 240 us (level)
  transfers between devices with their start and end apart: 10 -> 10, of which waited for: 8 -> 7; matrix products, arithmetic and copies ran while one was open for 16% -> 16% of each run, Pallas kernels for 12% -> 12%
where the time goes in v15:
time: 240 us; the launch traced here: 239 us
  waiting for transfers between devices  115 us (48%)
  matrix products  36.2 us (15%)
  starting transfers between devices  31.7 us (13%)
  Pallas kernels  29.1 us (12%)
  blocking collectives  12.9 us (5%)
  local copies, waits for them, and re-layouts  11.1 us (5%)
  other arithmetic  2.67 us (1%)
    ppermute x3, waiting for transfers between devices, local(): arrived[step] = lax.ppermute(own_tokens, 'dp', partner_pairs(n_dp, step))  53.5 us
    ppermute x3, waiting for transfers between devices, local(): partial_out = lax.ppermute(partial_out, 'dp', partner_pairs(n_dp, step))  44.2 us
    pallas_call x4, Pallas kernels, attend(): pl.pallas_call(kernel, out_shape=jax.ShapeDtypeStruct((1, token_count, wi...  29.1 us
    dot_general x4, matrix products, local(): jnp.einsum('td,sdh->sth', tokens, qkv_weight, preferred_element_type=jnp....  22.4 us
    all_to_all x4, starting transfers between devices, local(): incoming = lax.all_to_all(payload, 'ctx', 0, 0, tiled=True)  19.2 us
    all_to_all x4, waiting for transfers between devices, local(): incoming = lax.all_to_all(payload, 'ctx', 0, 0, tiled=True)  17.2 us
    dot_general x4, matrix products, local(): jnp.dot(attended[0], out_weight, preferred_element_type=jnp.float32)  13.8 us
    all_gather x1, blocking collectives, local(): lax.all_gather(table, 'ctx', axis=0, tiled=True).astype(jnp.int32)  12.9 us
  transfers between devices with their start and end apart: 10, of which 7 were waited for; matrix products, arithmetic and copies ran while one was open for 16% of the time, Pallas kernels for 12%

profile of v15, /device:TPU:0, one launch (start us, length us, event | category | flops | bytes accessed | tf_op | source)
XLA Modules:
  0.0 238.8 jit_solution(14765090379058575357)
XLA Ops:
  0.0 3.9 %collective-permute-start = (bf16[256,3072]{1,0:T(8,128)(2,1)}, bf16[256,3072]{1,0:T(8,128)(2,1)}, u32[]{:S(2)}, u32[]{:S(2)}) collective-permute-start(bf16[256,3072]{1,0:T(8,128)(2,1)} %bitcast.127), channel_id=1, source_target_pairs={{0,24},{8,16},{16,8},{24,0},{1,25},{9,17},{17,9},{25,1},{2,26},{10... | collective-permute-start | bytes 4718600 | tf_op jit(solution)/shard_map/ppermute | solution.py:136
  5.4 12.9 %all-gather = f32[8,4,11]{2,1,0:T(4,128)S(1)} all-gather(f32[1,4,11]{2,1,0:T(4,128)S(1)} %fusion.42), channel_id=1, replica_groups=mesh['dp'=4,'ctx'=8] {'ctx'}, dimensions={0}, use_global_device_ids=true | all-gather | bytes 1584 | tf_op jit(solution)/shard_map/all_gather | solution.py:110
  19.1 19.5 %collective-permute-done = bf16[256,3072]{1,0:T(8,128)(2,1)} collective-permute-done((bf16[256,3072]{1,0:T(8,128)(2,1)}, bf16[256,3072]{1,0:T(8,128)(2,1)}, u32[]{:S(2)}, u32[]{:S(2)}) %collective-permute-start) | collective-permute-done | bytes 1572896 | tf_op jit(solution)/shard_map/ppermute | solution.py:136
  38.6 5.7 %fusion.31.q_ref = bf16[3,256,384]{2,1,0:T(8,128)(2,1)S(1)} fusion(bf16[3,3072,384]{2,1,0:T(8,128)(2,1)} %param.8, bf16[256,3072]{1,0:T(8,128)(2,1)} %collective-permute-done), kind=kOutput, calls=%fused_computation.28 | convolution fusion | flops 1812234240 | bytes 9240576 | tf_op jit(solution)/shard_map/td,sdh->sth/dot_general | solution.py:145
  46.3 5.2 %all-to-all-start = ((bf16[16,2,1,64,384]{4,3,2,1,0:T(8,128)(2,1)}), bf16[16,2,1,64,384]{4,3,2,1,0:T(8,128)(2,1)}, u32[]{:S(2)}, u32[]{:S(2)}) async-start(bf16[16,2,1,64,384]{4,3,2,1,0:T(8,128)(2,1)} %bitcast.119), calls=%async_computation | async-start | bytes 3145728 | tf_op jit(solution)/shard_map/all_to_all | solution.py:156
  54.6 34.0 %collective-permute-done.2 = bf16[256,3072]{1,0:T(8,128)(2,1)S(1)} collective-permute-done((bf16[256,3072]{1,0:T(8,128)(2,1)}, bf16[256,3072]{1,0:T(8,128)(2,1)S(1)}, u32[]{:S(2)}, u32[]{:S(2)}) %collective-permute-start.2) | collective-permute-done | bytes 1572896 | tf_op jit(solution)/shard_map/ppermute | solution.py:136
  88.6 5.3 %fusion.28.q_ref = bf16[3,256,384]{2,1,0:T(8,128)(2,1)S(1)} fusion(bf16[3,3072,384]{2,1,0:T(8,128)(2,1)} %param.8, bf16[256,3072]{1,0:T(8,128)(2,1)S(1)} %collective-permute-done.2), kind=kOutput, calls=%fused_computation.27 | convolution fusion | flops 1812234240 | bytes 9240576 | tf_op jit(solution)/shard_map/td,sdh->sth/dot_general | solution.py:145
  95.9 4.7 %all-to-all-start.1 = ((bf16[16,2,1,64,384]{4,3,2,1,0:T(8,128)(2,1)}), bf16[16,2,1,64,384]{4,3,2,1,0:T(8,128)(2,1)}, u32[]{:S(2)}, u32[]{:S(2)}) async-start(bf16[16,2,1,64,384]{4,3,2,1,0:T(8,128)(2,1)} %bitcast.116), calls=%async_computation.1 | async-start | bytes 3145728 | tf_op jit(solution)/shard_map/all_to_all | solution.py:156
  104.1 5.7 %fusion.25.q_ref = bf16[3,256,384]{2,1,0:T(8,128)(2,1)S(1)} fusion(bf16[3,3072,384]{2,1,0:T(8,128)(2,1)} %param.8, bf16[256,3072]{1,0:T(8,128)(2,1)} %collective-permute-done.4), kind=kOutput, calls=%fused_computation.26 | convolution fusion | flops 1812234240 | bytes 9240576 | tf_op jit(solution)/shard_map/td,sdh->sth/dot_general | solution.py:145
  111.9 7.3 %shard_map.73 = bf16[1,256,384]{2,1,0:T(8,128)(2,1)} custom-call(s32[4,10]{1,0:T(4,128)} %add_select_fusion.2.pos_ref, s32[4]{0:T(128)} %count_ref.7, f32[4,3,10]{2,1,0:T(4,128)} %fusion.40.bias_ref, bf16[3,256,384]{2,1,0:T(8,128)(2,1)} %copy-done.5, bf16[4,2,1,64,384]{4,3,2,1,0:T(8,128)(2,1)} %bitcast.109, bf16[16,2,1,64,384]{4,3,2,1,0:T(8,128)(2,1)} %all-to-all-done.far_ref), custom_call_target="tpu_custom_call" | custom-call | tf_op jit(solution)/shard_map/pallas_call | solution.py:80
  119.2 3.1 %convolution_convert_fusion.3 = bf16[256,3072]{1,0:T(8,128)(2,1)} fusion(bf16[384,3072]{1,0:T(8,128)(2,1)S(1)} %copy-done, bf16[1,256,384]{2,1,0:T(8,128)(2,1)} %shard_map.73), kind=kOutput, calls=%fused_computation.10 | convolution fusion | flops 604766208 | bytes 4128768 | tf_op jit(solution)/shard_map/dot_general | solution.py:161
  122.2 16.3 %all-to-all-done.1.far_ref = bf16[16,2,1,64,384]{4,3,2,1,0:T(8,128)(2,1)} async-done(((bf16[16,2,1,64,384]{4,3,2,1,0:T(8,128)(2,1)}), bf16[16,2,1,64,384]{4,3,2,1,0:T(8,128)(2,1)}, u32[]{:S(2)}, u32[]{:S(2)}) %all-to-all-start.1) | async-done | bytes 1572896 | tf_op jit(solution)/shard_map/all_to_all | solution.py:156
  138.6 4.5 %all-to-all-start.2 = ((bf16[16,2,1,64,384]{4,3,2,1,0:T(8,128)(2,1)}), bf16[16,2,1,64,384]{4,3,2,1,0:T(8,128)(2,1)}, u32[]{:S(2)}, u32[]{:S(2)}) async-start(bf16[16,2,1,64,384]{4,3,2,1,0:T(8,128)(2,1)} %bitcast.118), calls=%async_computation.2 | async-start | bytes 3145728 | tf_op jit(solution)/shard_map/all_to_all | solution.py:156
  145.6 5.7 %fusion.22.q_ref = bf16[3,256,384]{2,1,0:T(8,128)(2,1)S(1)} fusion(bf16[3,3072,384]{2,1,0:T(8,128)(2,1)} %param.8, bf16[256,3072]{1,0:T(8,128)(2,1)} %bitcast.130), kind=kOutput, calls=%fused_computation.25 | convolution fusion | flops 1812234240 | bytes 9240576 | tf_op jit(solution)/shard_map/td,sdh->sth/dot_general | solution.py:145
  153.4 7.3 %shard_map.74 = bf16[1,256,384]{2,1,0:T(8,128)(2,1)} custom-call(s32[4,10]{1,0:T(4,128)} %add_select_fusion.2.pos_ref, s32[4]{0:T(128)} %count_ref.7, f32[4,3,10]{2,1,0:T(4,128)} %fusion.40.bias_ref, bf16[3,256,384]{2,1,0:T(8,128)(2,1)} %copy-done.6, bf16[4,2,1,64,384]{4,3,2,1,0:T(8,128)(2,1)} %bitcast.111, bf16[16,2,1,64,384]{4,3,2,1,0:T(8,128)(2,1)} %all-to-all-done.1.far_ref), custom_call_target="tpu_custom_call" | custom-call | tf_op jit(solution)/shard_map/pallas_call | solution.py:80
  160.6 3.2 %convolution_convert_fusion.2 = bf16[256,3072]{1,0:T(8,128)(2,1)} fusion(bf16[384,3072]{1,0:T(8,128)(2,1)S(1)} %copy-done, bf16[1,256,384]{2,1,0:T(8,128)(2,1)} %shard_map.74), kind=kOutput, calls=%fused_computation.9 | convolution fusion | flops 604766208 | bytes 4128768 | tf_op jit(solution)/shard_map/dot_general | solution.py:161
  163.8 17.0 %collective-permute-done.1 = bf16[256,3072]{1,0:T(8,128)(2,1)} collective-permute-done((bf16[256,3072]{1,0:T(8,128)(2,1)}, bf16[256,3072]{1,0:T(8,128)(2,1)}, u32[]{:S(2)}, u32[]{:S(2)}) %collective-permute-start.1) | collective-permute-done | bytes 1572896 | tf_op jit(solution)/shard_map/ppermute | solution.py:166
  180.8 4.8 %all-to-all-start.3 = ((bf16[16,2,1,64,384]{4,3,2,1,0:T(8,128)(2,1)}), bf16[16,2,1,64,384]{4,3,2,1,0:T(8,128)(2,1)}, u32[]{:S(2)}, u32[]{:S(2)}) async-start(bf16[16,2,1,64,384]{4,3,2,1,0:T(8,128)(2,1)} %bitcast.117), calls=%async_computation.3 | async-start | bytes 3145728 | tf_op jit(solution)/shard_map/all_to_all | solution.py:156
  187.1 7.3 %shard_map.75 = bf16[1,256,384]{2,1,0:T(8,128)(2,1)} custom-call(s32[4,10]{1,0:T(4,128)} %add_select_fusion.2.pos_ref, s32[4]{0:T(128)} %count_ref.7, f32[4,3,10]{2,1,0:T(4,128)} %fusion.40.bias_ref, bf16[3,256,384]{2,1,0:T(8,128)(2,1)} %copy-done.7, bf16[4,2,1,64,384]{4,3,2,1,0:T(8,128)(2,1)} %bitcast.113, bf16[16,2,1,64,384]{4,3,2,1,0:T(8,128)(2,1)} %all-to-all-done.2.far_ref), custom_call_target="tpu_custom_call" | custom-call | tf_op jit(solution)/shard_map/pallas_call | solution.py:80
  194.3 3.1 %convolution_convert_fusion.1 = bf16[256,3072]{1,0:T(8,128)(2,1)} fusion(bf16[384,3072]{1,0:T(8,128)(2,1)S(1)} %copy-done, bf16[1,256,384]{2,1,0:T(8,128)(2,1)} %shard_map.75), kind=kOutput, calls=%fused_computation.8 | convolution fusion | flops 604766208 | bytes 4128768 | tf_op jit(solution)/shard_map/dot_general | solution.py:161
  198.9 23.8 %collective-permute-done.3 = bf16[256,3072]{1,0:T(8,128)(2,1)} collective-permute-done((bf16[256,3072]{1,0:T(8,128)(2,1)}, bf16[256,3072]{1,0:T(8,128)(2,1)}, u32[]{:S(2)}, u32[]{:S(2)}) %collective-permute-start.3) | collective-permute-done | bytes 1572896 | tf_op jit(solution)/shard_map/ppermute | solution.py:166
  223.5 7.3 %shard_map.76 = bf16[1,256,384]{2,1,0:T(8,128)(2,1)} custom-call(s32[4,10]{1,0:T(4,128)} %add_select_fusion.2.pos_ref, s32[4]{0:T(128)} %count_ref.7, f32[4,3,10]{2,1,0:T(4,128)} %fusion.40.bias_ref, bf16[3,256,384]{2,1,0:T(8,128)(2,1)} %copy-done.8, bf16[4,2,1,64,384]{4,3,2,1,0:T(8,128)(2,1)} %bitcast.115, bf16[16,2,1,64,384]{4,3,2,1,0:T(8,128)(2,1)} %all-to-all-done.3.far_ref), custom_call_target="tpu_custom_call" | custom-call | tf_op jit(solution)/shard_map/pallas_call | solution.py:80
  230.8 3.4 %collective-permute-done.5 = bf16[256,3072]{1,0:T(8,128)(2,1)} collective-permute-done((bf16[256,3072]{1,0:T(8,128)(2,1)}, bf16[256,3072]{1,0:T(8,128)(2,1)}, u32[]{:S(2)}, u32[]{:S(2)}) %collective-permute-start.5) | collective-permute-done | bytes 1572896 | tf_op jit(solution)/shard_map/ppermute | solution.py:166
  234.2 4.6 %fusion.1 = bf16[1,256,3072]{2,1,0:T(8,128)(2,1)} fusion(bf16[256,3072]{1,0:T(8,128)(2,1)} %collective-permute-done.5, bf16[256,3072]{1,0:T(8,128)(2,1)} %collective-permute-done.3, bf16[256,3072]{1,0:T(8,128)(2,1)} %collective-permute-done.1, bf16[384,3072]{1,0:T(8,128)(2,1)S(1)} %copy-done, bf16[1,256,384]{2,1,0:T(8,128)(2,1)} %shard_map.76), kind=kOutput, calls=%fused_computation.12 | convolution fusion | flops 611057664 | bytes 8847360 | tf_op jit(solution)/shard_map/dot_general | solution.py:161
  (85 shorter events, 23.1 us)
Async XLA Ops:
  0.0 119.2 %copy-start = (bf16[384,3072]{1,0:T(8,128)(2,1)S(1)}, bf16[384,3072]{1,0:T(8,128)(2,1)}, u32[]{:S(2)}) copy-start(bf16[384,3072]{1,0:T(8,128)(2,1)} %param.9) | copy-start | bytes 7077892
  0.0 38.6 %collective-permute-start = (bf16[256,3072]{1,0:T(8,128)(2,1)}, bf16[256,3072]{1,0:T(8,128)(2,1)}, u32[]{:S(2)}, u32[]{:S(2)}) collective-permute-start(bf16[256,3072]{1,0:T(8,128)(2,1)} %bitcast.127), channel_id=1, source_target_pairs={{0,24},{8,16},{16,8},{24,0},{1,25},{9,17},{17,9},{25,1},{2,26},{10... | collective-permute-start | bytes 4718600 | tf_op jit(solution)/shard_map/ppermute | solution.py:136
  44.3 2.0 copy-start.5
  44.4 1.9 copy-start.1
  46.3 8.2 %copy-start.9 = (s32[4,10]{1,0:T(4,128)S(1)}, s32[4,10]{1,0:T(4,128)}, u32[]{:S(2)}) copy-start(s32[4,10]{1,0:T(4,128)} %param.10) | copy-start | bytes 484
  46.3 49.6 %all-to-all-start = ((bf16[16,2,1,64,384]{4,3,2,1,0:T(8,128)(2,1)}), bf16[16,2,1,64,384]{4,3,2,1,0:T(8,128)(2,1)}, u32[]{:S(2)}, u32[]{:S(2)}) async-start(bf16[16,2,1,64,384]{4,3,2,1,0:T(8,128)(2,1)} %bitcast.119), calls=%async_computation | async-start | bytes 3145728 | tf_op jit(solution)/shard_map/all_to_all | solution.py:156
  51.5 37.0 %collective-permute-start.2 = (bf16[256,3072]{1,0:T(8,128)(2,1)}, bf16[256,3072]{1,0:T(8,128)(2,1)S(1)}, u32[]{:S(2)}, u32[]{:S(2)}) collective-permute-start(bf16[256,3072]{1,0:T(8,128)(2,1)} %bitcast.128), channel_id=1, source_target_pairs={{0,8},{8,0},{16,24},{24,16},{1,9},{9,1},{17,25},{25,17},{2,10},{10... | collective-permute-start | bytes 4718600 | tf_op jit(solution)/shard_map/ppermute | solution.py:136
  53.0 51.1 %collective-permute-start.4 = (bf16[256,3072]{1,0:T(8,128)(2,1)}, bf16[256,3072]{1,0:T(8,128)(2,1)}, u32[]{:S(2)}, u32[]{:S(2)}) collective-permute-start(bf16[256,3072]{1,0:T(8,128)(2,1)} %bitcast.129), channel_id=1, source_target_pairs={{0,16},{8,24},{16,0},{24,8},{1,17},{9,25},{17,1},{25,9},{2,18},{10... | collective-permute-start | bytes 4718600 | tf_op jit(solution)/shard_map/ppermute | solution.py:136
  93.8 2.0 copy-start.6
  93.9 1.9 copy-start.2
  95.9 4.8 %copy-start.10 = (s32[4]{0:T(128)S(1)}, s32[4]{0:T(128)}, u32[]{:S(2)}) copy-start(s32[4]{0:T(128)} %count_ref.7) | copy-start | bytes 52
  95.9 42.7 %all-to-all-start.1 = ((bf16[16,2,1,64,384]{4,3,2,1,0:T(8,128)(2,1)}), bf16[16,2,1,64,384]{4,3,2,1,0:T(8,128)(2,1)}, u32[]{:S(2)}, u32[]{:S(2)}) async-start(bf16[16,2,1,64,384]{4,3,2,1,0:T(8,128)(2,1)} %bitcast.116), calls=%async_computation.1 | async-start | bytes 3145728 | tf_op jit(solution)/shard_map/all_to_all | solution.py:156
  100.7 1.3 copy-start.12
  100.7 1.5 copy-start.11
  109.9 2.0 copy-start.7
  110.0 1.9 copy-start.3
  138.6 42.2 %all-to-all-start.2 = ((bf16[16,2,1,64,384]{4,3,2,1,0:T(8,128)(2,1)}), bf16[16,2,1,64,384]{4,3,2,1,0:T(8,128)(2,1)}, u32[]{:S(2)}, u32[]{:S(2)}) async-start(bf16[16,2,1,64,384]{4,3,2,1,0:T(8,128)(2,1)} %bitcast.118), calls=%async_computation.2 | async-start | bytes 3145728 | tf_op jit(solution)/shard_map/all_to_all | solution.py:156
  143.1 37.7 %collective-permute-start.1 = (bf16[256,3072]{1,0:T(8,128)(2,1)}, bf16[256,3072]{1,0:T(8,128)(2,1)}, u32[]{:S(2)}, u32[]{:S(2)}) collective-permute-start(bf16[256,3072]{1,0:T(8,128)(2,1)} %convolution_convert_fusion.3), channel_id=1, source_target_pairs={{0,24},{8,16},{16,8},{24,0},{1,25},{9,17},{17,9},{25,1},{2,26},{10... | collective-permute-start | bytes 4718600 | tf_op jit(solution)/shard_map/ppermute | solution.py:166
  151.3 2.1 copy-start.8
  151.4 2.0 copy-start.4
  180.8 42.7 %all-to-all-start.3 = ((bf16[16,2,1,64,384]{4,3,2,1,0:T(8,128)(2,1)}), bf16[16,2,1,64,384]{4,3,2,1,0:T(8,128)(2,1)}, u32[]{:S(2)}, u32[]{:S(2)}) async-start(bf16[16,2,1,64,384]{4,3,2,1,0:T(8,128)(2,1)} %bitcast.117), calls=%async_computation.3 | async-start | bytes 3145728 | tf_op jit(solution)/shard_map/all_to_all | solution.py:156
  185.6 37.1 %collective-permute-start.3 = (bf16[256,3072]{1,0:T(8,128)(2,1)}, bf16[256,3072]{1,0:T(8,128)(2,1)}, u32[]{:S(2)}, u32[]{:S(2)}) collective-permute-start(bf16[256,3072]{1,0:T(8,128)(2,1)} %convolution_convert_fusion.2), channel_id=1, source_target_pairs={{0,8},{8,0},{16,24},{24,16},{1,9},{9,1},{17,25},{25,17},{2,10},{10... | collective-permute-start | bytes 4718600 | tf_op jit(solution)/shard_map/ppermute | solution.py:166
  197.4 36.8 %collective-permute-start.5 = (bf16[256,3072]{1,0:T(8,128)(2,1)}, bf16[256,3072]{1,0:T(8,128)(2,1)}, u32[]{:S(2)}, u32[]{:S(2)}) collective-permute-start(bf16[256,3072]{1,0:T(8,128)(2,1)} %convolution_convert_fusion.1), channel_id=1, source_target_pairs={{0,16},{8,24},{16,0},{24,8},{1,17},{9,25},{17,1},{25,9},{2,18},{10... | collective-permute-start | bytes 4718600 | tf_op jit(solution)/shard_map/ppermute | solution.py:166

commit v16 on v15

--- a/solution.py
+++ b/solution.py
@@ -28,7 +28,7 @@
     return first.astype(jnp.int32), second.astype(jnp.int32)
 
 
-def attention_kernel(pos_ref, count_ref, bias_ref, q_ref, own_ref, far_ref, out_ref, *, heads, head_size, scale):
+def attention_kernel(pos_ref, count_ref, bias_ref, q_ref, own_ref, far_ref, w_ref, out_ref, *, heads, head_size, scale):
     tile = pl.program_id(0)
     own_tiles = own_ref.shape[0]
     live_count = count_ref[tile]
@@ -48,6 +48,7 @@
 
     column = lax.broadcasted_iota(jnp.int32, (1, KMAX * TILE), 1) // TILE
     live = column < live_count
+    attended = []
     for head in range(heads):
         cols = pl.ds(head * head_size, head_size)
         q_head = queries[:, head * head_size:(head + 1) * head_size]
@@ -64,11 +65,14 @@
         w = jnp.exp(s - row_max)
         weight_sum = w.sum(axis=1, keepdims=True)
         total = jnp.dot(w.astype(jnp.bfloat16), values, preferred_element_type=jnp.float32)
-        out_ref[0, :, head * head_size:(head + 1) * head_size] = (total / weight_sum).astype(out_ref.dtype)
+        attended.append((total / weight_sum).astype(jnp.bfloat16))
+    merged = jnp.concatenate(attended, axis=1)
+    out_ref[0] = jnp.dot(merged, w_ref[...], preferred_element_type=jnp.float32).astype(out_ref.dtype)
 
 
-def attend(positions, live_counts, bias, queries, own_tiles, far_tiles, heads, head_size):
+def attend(positions, live_counts, bias, queries, own_tiles, far_tiles, weight, heads, head_size):
     _, token_count, width = queries.shape
+    out_width = weight.shape[1]
     tile_count = token_count // TILE
 
     def whole(array):
@@ -79,16 +83,16 @@
     )
     return pl.pallas_call(
         kernel,
-        out_shape=jax.ShapeDtypeStruct((1, token_count, width), jnp.bfloat16),
+        out_shape=jax.ShapeDtypeStruct((1, token_count, out_width), jnp.bfloat16),
         grid_spec=pltpu.PrefetchScalarGridSpec(
             num_scalar_prefetch=2,
             grid=(tile_count,),
             in_specs=[pl.BlockSpec(memory_space=pltpu.SMEM),
                       pl.BlockSpec((1, TILE, width), lambda t, pos, cnt: (0, t, 0)),
-                      whole(own_tiles), whole(far_tiles)],
-            out_specs=pl.BlockSpec((1, TILE, width), lambda t, pos, cnt: (0, t, 0)),
+                      whole(own_tiles), whole(far_tiles), whole(weight)],
+            out_specs=pl.BlockSpec((1, TILE, out_width), lambda t, pos, cnt: (0, t, 0)),
         ),
-    )(positions, live_counts, bias, queries, own_tiles, far_tiles)
+    )(positions, live_counts, bias, queries, own_tiles, far_tiles, weight)
 
 
 def partner_pairs(count, step):
@@ -157,10 +161,9 @@
         received.append(incoming)
         if index == len(order) - 1 and len(sent) >= 2:
             incoming, _ = lax.optimization_barrier((incoming, sent[-2]))
-        attended = attend(positions, live_counts, bias, projected, by_tile, incoming, heads_here, head_size)
-        partial_out = jnp.dot(
-            attended[0], out_weight, preferred_element_type=jnp.float32
-        ).astype(jnp.bfloat16)
+        partial_out = attend(
+            positions, live_counts, bias, projected, by_tile, incoming, out_weight, heads_here, head_size
+        )[0]
         partials.append(partial_out)
         if step > 0:
             partial_out = lax.ppermute(partial_out, "dp", partner_pairs(n_dp, step))

time: 240 us -> 243 us (1.012)
  matrix products: 36.2 us -> 21.9 us
  Pallas kernels: 29.1 us -> 40.3 us
  local copies, waits for them, and re-layouts: 11.1 us -> 18.8 us
  other arithmetic: 2.67 us -> 7.18 us
  waiting for transfers between devices: 115 us -> 111 us
    dot_general x4 -> x0, matrix products: 13.8 us -> none  [local(): jnp.dot(attended[0], out_weight, preferred_element_type=jnp.float32)]
    pallas_call x4, Pallas kernels: 29.1 us -> 40.3 us  [attend(): pl.pallas_call(kernel, out_shape=jax.ShapeDtypeStruct((1, token_count, ou...]
    unnamed x27 -> x33, local copies, waits for them, and re-layouts: 0.2 us -> 7.96 us
    broadcast_in_dim x0 -> x1, other arithmetic: none -> 4.51 us  [local(): return total.astype(jnp.bfloat16)[None]]
    ppermute x3, waiting for transfers between devices: 44.2 us -> 40.8 us  [local(): partial_out = lax.ppermute(partial_out, 'dp', partner_pairs(n_dp, step))]
  transfers between devices with their start and end apart: 10 -> 10, of which waited for: 7 -> 6; matrix products, arithmetic and copies ran while one was open for 16% -> 12% of each run, Pallas kernels for 12% -> 17%
where the time goes in v16:
time: 243 us
  waiting for transfers between devices  111 us (46%)
  Pallas kernels  40.3 us (17%)
  starting transfers between devices  30.6 us (13%)
  matrix products  21.9 us (9%)
  local copies, waits for them, and re-layouts  18.8 us (8%)
  blocking collectives  12.9 us (5%)
  other arithmetic  7.18 us (3%)
    ppermute x3, waiting for transfers between devices, local(): arrived[step] = lax.ppermute(own_tokens, 'dp', partner_pairs(n_dp, step))  53.4 us
    ppermute x3, waiting for transfers between devices, local(): partial_out = lax.ppermute(partial_out, 'dp', partner_pairs(n_dp, step))  40.8 us
    pallas_call x4, Pallas kernels, attend(): pl.pallas_call(kernel, out_shape=jax.ShapeDtypeStruct((1, token_count, ou...  40.3 us
    dot_general x4, matrix products, local(): jnp.einsum('td,sdh->sth', tokens, qkv_weight, preferred_element_type=jnp....  21.9 us
    all_to_all x4, starting transfers between devices, local(): incoming = lax.all_to_all(payload, 'ctx', 0, 0, tiled=True)  18.2 us
    all_to_all x4, waiting for transfers between devices, local(): incoming = lax.all_to_all(payload, 'ctx', 0, 0, tiled=True)  16.5 us
    all_gather x1, blocking collectives, local(): lax.all_gather(table, 'ctx', axis=0, tiled=True).astype(jnp.int32)  12.9 us
    unnamed x33, local copies, waits for them, and re-layouts  7.96 us
  transfers between devices with their start and end apart: 10, of which 6 were waited for; matrix products, arithmetic and copies ran while one was open for 12% of the time, Pallas kernels for 17%

profile of v16, /device:TPU:0, one launch (start us, length us, event | category | flops | bytes accessed | tf_op | source)
XLA Modules:
  0.0 242.7 jit_solution(1400067984951161939)
XLA Ops:
  0.0 3.9 %collective-permute-start = (bf16[256,3072]{1,0:T(8,128)(2,1)}, bf16[256,3072]{1,0:T(8,128)(2,1)S(1)}, u32[]{:S(2)}, u32[]{:S(2)}) collective-permute-start(bf16[256,3072]{1,0:T(8,128)(2,1)} %bitcast.1), channel_id=1, source_target_pairs={{0,24},{8,16},{16,8},{24,0},{1,25},{9,17},{17,9},{25,1},{2,26},{10... | collective-permute-start | bytes 4718600 | tf_op jit(solution)/shard_map/ppermute | solution.py:140
  5.4 12.9 %all-gather = f32[8,4,11]{2,1,0:T(4,128)S(1)} all-gather(f32[1,4,11]{2,1,0:T(4,128)S(1)} %fusion.36), channel_id=1, replica_groups=mesh['dp'=4,'ctx'=8] {'ctx'}, dimensions={0}, use_global_device_ids=true | all-gather | bytes 1584 | tf_op jit(solution)/shard_map/all_gather | solution.py:114
  19.1 19.4 %collective-permute-done = bf16[256,3072]{1,0:T(8,128)(2,1)S(1)} collective-permute-done((bf16[256,3072]{1,0:T(8,128)(2,1)}, bf16[256,3072]{1,0:T(8,128)(2,1)S(1)}, u32[]{:S(2)}, u32[]{:S(2)}) %collective-permute-start) | collective-permute-done | bytes 1572896 | tf_op jit(solution)/shard_map/ppermute | solution.py:140
  38.5 5.3 %fusion.31.q_ref = bf16[3,256,384]{2,1,0:T(8,128)(2,1)S(1)} fusion(bf16[3,3072,384]{2,1,0:T(8,128)(2,1)} %param.8, bf16[256,3072]{1,0:T(8,128)(2,1)S(1)} %collective-permute-done), kind=kOutput, calls=%fused_computation.24 | convolution fusion | flops 1812234240 | bytes 9240576 | tf_op jit(solution)/shard_map/td,sdh->sth/dot_general | solution.py:149
  46.6 5.1 %all-to-all-start = ((bf16[16,2,1,64,384]{4,3,2,1,0:T(8,128)(2,1)}), bf16[16,2,1,64,384]{4,3,2,1,0:T(8,128)(2,1)S(1)}, u32[]{:S(2)}, u32[]{:S(2)}) async-start(bf16[16,2,1,64,384]{4,3,2,1,0:T(8,128)(2,1)} %bitcast.106), calls=%async_computation | async-start | bytes 3145728 | tf_op jit(solution)/shard_map/all_to_all | solution.py:160
  54.6 34.0 %collective-permute-done.2 = bf16[256,3072]{1,0:T(8,128)(2,1)S(1)} collective-permute-done((bf16[256,3072]{1,0:T(8,128)(2,1)}, bf16[256,3072]{1,0:T(8,128)(2,1)S(1)}, u32[]{:S(2)}, u32[]{:S(2)}) %collective-permute-start.2) | collective-permute-done | bytes 1572896 | tf_op jit(solution)/shard_map/ppermute | solution.py:140
  88.7 5.3 %fusion.28.q_ref = bf16[3,256,384]{2,1,0:T(8,128)(2,1)S(1)} fusion(bf16[3,3072,384]{2,1,0:T(8,128)(2,1)} %param.8, bf16[256,3072]{1,0:T(8,128)(2,1)S(1)} %collective-permute-done.2), kind=kOutput, calls=%fused_computation.23 | convolution fusion | flops 1812234240 | bytes 9240576 | tf_op jit(solution)/shard_map/td,sdh->sth/dot_general | solution.py:149
  94.8 1.9 gather_fusion.3
  98.0 4.7 %all-to-all-start.1 = ((bf16[16,2,1,64,384]{4,3,2,1,0:T(8,128)(2,1)}), bf16[16,2,1,64,384]{4,3,2,1,0:T(8,128)(2,1)S(1)}, u32[]{:S(2)}, u32[]{:S(2)}) async-start(bf16[16,2,1,64,384]{4,3,2,1,0:T(8,128)(2,1)} %bitcast.104), calls=%async_computation.1 | async-start | bytes 3145728 | tf_op jit(solution)/shard_map/all_to_all | solution.py:160
  106.2 5.7 %fusion.25.q_ref = bf16[3,256,384]{2,1,0:T(8,128)(2,1)S(1)} fusion(bf16[3,3072,384]{2,1,0:T(8,128)(2,1)} %param.8, bf16[256,3072]{1,0:T(8,128)(2,1)} %collective-permute-done.4), kind=kOutput, calls=%fused_computation.22 | convolution fusion | flops 1812234240 | bytes 9240576 | tf_op jit(solution)/shard_map/td,sdh->sth/dot_general | solution.py:149
  112.9 1.9 gather_fusion.4
  114.8 10.1 %shard_map.73 = bf16[1,256,3072]{2,1,0:T(8,128)(2,1)} custom-call(s32[4,10]{1,0:T(4,128)} %add_select_fusion.2.pos_ref, s32[4]{0:T(128)} %count_ref.7, f32[4,3,10]{2,1,0:T(4,128)} %fusion.34.bias_ref, bf16[3,256,384]{2,1,0:T(8,128)(2,1)} %copy-done.9, bf16[4,2,1,64,384]{4,3,2,1,0:T(8,128)(2,1)} %bitcast.99, bf16[16,2,1,64,384]{4,3,2,1,0:T(8,128)(2,1)} %copy-done.4, ...), custom_call_target="tpu_custom_call" | custom-call | tf_op jit(solution)/shard_map/pallas_call | solution.py:84
  124.9 15.6 %all-to-all-done.1.far_ref = bf16[16,2,1,64,384]{4,3,2,1,0:T(8,128)(2,1)S(1)} async-done(((bf16[16,2,1,64,384]{4,3,2,1,0:T(8,128)(2,1)}), bf16[16,2,1,64,384]{4,3,2,1,0:T(8,128)(2,1)S(1)}, u32[]{:S(2)}, u32[]{:S(2)}) %all-to-all-start.1) | async-done | bytes 1572896 | tf_op jit(solution)/shard_map/all_to_all | solution.py:160
  141.7 3.6 %all-to-all-start.2 = ((bf16[16,2,1,64,384]{4,3,2,1,0:T(8,128)(2,1)}), bf16[16,2,1,64,384]{4,3,2,1,0:T(8,128)(2,1)S(1)}, u32[]{:S(2)}, u32[]{:S(2)}) async-start(bf16[16,2,1,64,384]{4,3,2,1,0:T(8,128)(2,1)} %bitcast.105), calls=%async_computation.2 | async-start | bytes 3145728 | tf_op jit(solution)/shard_map/all_to_all | solution.py:160
  145.3 2.5 %collective-permute-start.1 = (bf16[256,3072]{1,0:T(8,128)(2,1)}, bf16[256,3072]{1,0:T(8,128)(2,1)}, u32[]{:S(2)}, u32[]{:S(2)}) collective-permute-start(bf16[256,3072]{1,0:T(8,128)(2,1)} %bitcast.112), channel_id=1, source_target_pairs={{0,24},{8,16},{16,8},{24,0},{1,25},{9,17},{17,9},{25,1},{2,26},{10... | collective-permute-start | bytes 4718600 | tf_op jit(solution)/shard_map/ppermute | solution.py:169
  147.8 5.7 %fusion.22.q_ref = bf16[3,256,384]{2,1,0:T(8,128)(2,1)S(1)} fusion(bf16[3,3072,384]{2,1,0:T(8,128)(2,1)} %param.8, bf16[256,3072]{1,0:T(8,128)(2,1)} %bitcast.1), kind=kOutput, calls=%fused_computation.21 | convolution fusion | flops 1812234240 | bytes 9240576 | tf_op jit(solution)/shard_map/td,sdh->sth/dot_general | solution.py:149
  154.4 1.9 gather_fusion.5
  156.3 10.1 %shard_map.74 = bf16[1,256,3072]{2,1,0:T(8,128)(2,1)} custom-call(s32[4,10]{1,0:T(4,128)} %add_select_fusion.2.pos_ref, s32[4]{0:T(128)} %count_ref.7, f32[4,3,10]{2,1,0:T(4,128)} %fusion.34.bias_ref, bf16[3,256,384]{2,1,0:T(8,128)(2,1)} %copy-done.8, bf16[4,2,1,64,384]{4,3,2,1,0:T(8,128)(2,1)} %bitcast.97, bf16[16,2,1,64,384]{4,3,2,1,0:T(8,128)(2,1)} %copy-done.5, ...), custom_call_target="tpu_custom_call" | custom-call | tf_op jit(solution)/shard_map/pallas_call | solution.py:84
  166.4 16.8 %collective-permute-done.1 = bf16[256,3072]{1,0:T(8,128)(2,1)} collective-permute-done((bf16[256,3072]{1,0:T(8,128)(2,1)}, bf16[256,3072]{1,0:T(8,128)(2,1)}, u32[]{:S(2)}, u32[]{:S(2)}) %collective-permute-start.1) | collective-permute-done | bytes 1572896 | tf_op jit(solution)/shard_map/ppermute | solution.py:169
  184.4 4.8 %all-to-all-start.3 = ((bf16[16,2,1,64,384]{4,3,2,1,0:T(8,128)(2,1)}), bf16[16,2,1,64,384]{4,3,2,1,0:T(8,128)(2,1)S(1)}, u32[]{:S(2)}, u32[]{:S(2)}) async-start(bf16[16,2,1,64,384]{4,3,2,1,0:T(8,128)(2,1)} %bitcast.34), calls=%async_computation.3 | async-start | bytes 3145728 | tf_op jit(solution)/shard_map/all_to_all | solution.py:160
  190.6 10.1 %shard_map.75 = bf16[1,256,3072]{2,1,0:T(8,128)(2,1)} custom-call(s32[4,10]{1,0:T(4,128)} %add_select_fusion.2.pos_ref, s32[4]{0:T(128)} %count_ref.7, f32[4,3,10]{2,1,0:T(4,128)} %fusion.34.bias_ref, bf16[3,256,384]{2,1,0:T(8,128)(2,1)} %copy-done.10, bf16[4,2,1,64,384]{4,3,2,1,0:T(8,128)(2,1)} %bitcast.101, bf16[16,2,1,64,384]{4,3,2,1,0:T(8,128)(2,1)} %copy-done.6, ...), custom_call_target="tpu_custom_call" | custom-call | tf_op jit(solution)/shard_map/pallas_call | solution.py:84
  202.3 23.9 %collective-permute-done.3 = bf16[256,3072]{1,0:T(8,128)(2,1)S(1)} collective-permute-done((bf16[256,3072]{1,0:T(8,128)(2,1)}, bf16[256,3072]{1,0:T(8,128)(2,1)S(1)}, u32[]{:S(2)}, u32[]{:S(2)}) %collective-permute-start.3) | collective-permute-done | bytes 1572896 | tf_op jit(solution)/shard_map/ppermute | solution.py:169
  228.1 10.1 %shard_map.76 = bf16[1,256,3072]{2,1,0:T(8,128)(2,1)} custom-call(s32[4,10]{1,0:T(4,128)} %add_select_fusion.2.pos_ref, s32[4]{0:T(128)} %count_ref.7, f32[4,3,10]{2,1,0:T(4,128)} %fusion.34.bias_ref, bf16[3,256,384]{2,1,0:T(8,128)(2,1)} %copy-done.11, bf16[4,2,1,64,384]{4,3,2,1,0:T(8,128)(2,1)} %bitcast.103, bf16[16,2,1,64,384]{4,3,2,1,0:T(8,128)(2,1)} %copy-done.7, ...), custom_call_target="tpu_custom_call" | custom-call | tf_op jit(solution)/shard_map/pallas_call | solution.py:84
  238.2 4.5 %fusion.1 = bf16[1,256,3072]{2,1,0:T(8,128)(2,1)} fusion(bf16[256,3072]{1,0:T(8,128)(2,1)} %collective-permute-done.5, bf16[256,3072]{1,0:T(8,128)(2,1)S(1)} %collective-permute-done.3, bf16[256,3072]{1,0:T(8,128)(2,1)} %collective-permute-done.1, bf16[1,256,3072]{2,1,0:T(8,128)(2,1)} %shard_map.76), kind=kLoop, calls=%fused_computation.8 | loop fusion | flops 6291456 | bytes 7864320 | tf_op jit(solution)/shard_map/broadcast_in_dim | solution.py:173
  (88 shorter events, 22.6 us)
Async XLA Ops:
  0.0 38.5 %collective-permute-start = (bf16[256,3072]{1,0:T(8,128)(2,1)}, bf16[256,3072]{1,0:T(8,128)(2,1)S(1)}, u32[]{:S(2)}, u32[]{:S(2)}) collective-permute-start(bf16[256,3072]{1,0:T(8,128)(2,1)} %bitcast.1), channel_id=1, source_target_pairs={{0,24},{8,16},{16,8},{24,0},{1,25},{9,17},{17,9},{25,1},{2,26},{10... | collective-permute-start | bytes 4718600 | tf_op jit(solution)/shard_map/ppermute | solution.py:140
  44.6 1.9 copy-start.1
  46.6 50.2 %all-to-all-start = ((bf16[16,2,1,64,384]{4,3,2,1,0:T(8,128)(2,1)}), bf16[16,2,1,64,384]{4,3,2,1,0:T(8,128)(2,1)S(1)}, u32[]{:S(2)}, u32[]{:S(2)}) async-start(bf16[16,2,1,64,384]{4,3,2,1,0:T(8,128)(2,1)} %bitcast.106), calls=%async_computation | async-start | bytes 3145728 | tf_op jit(solution)/shard_map/all_to_all | solution.py:160
  51.6 37.0 %collective-permute-start.2 = (bf16[256,3072]{1,0:T(8,128)(2,1)}, bf16[256,3072]{1,0:T(8,128)(2,1)S(1)}, u32[]{:S(2)}, u32[]{:S(2)}) collective-permute-start(bf16[256,3072]{1,0:T(8,128)(2,1)} %bitcast.1), channel_id=1, source_target_pairs={{0,8},{8,0},{16,24},{24,16},{1,9},{9,1},{17,25},{25,17},{2,10},{10... | collective-permute-start | bytes 4718600 | tf_op jit(solution)/shard_map/ppermute | solution.py:140
  53.1 53.1 %collective-permute-start.4 = (bf16[256,3072]{1,0:T(8,128)(2,1)}, bf16[256,3072]{1,0:T(8,128)(2,1)}, u32[]{:S(2)}, u32[]{:S(2)}) collective-permute-start(bf16[256,3072]{1,0:T(8,128)(2,1)} %bitcast.1), channel_id=1, source_target_pairs={{0,16},{8,24},{16,0},{24,8},{1,17},{9,25},{17,1},{25,9},{2,18},{10... | collective-permute-start | bytes 4718600 | tf_op jit(solution)/shard_map/ppermute | solution.py:140
  93.9 0.9 copy-start.8
  94.8 2.0 copy-start
  96.8 1.2 copy-start.4
  96.8 5.9 %copy-start.12 = (s32[4,10]{1,0:T(4,128)S(1)}, s32[4,10]{1,0:T(4,128)}, u32[]{:S(2)}) copy-start(s32[4,10]{1,0:T(4,128)} %param.10) | copy-start | bytes 484
  96.8 5.9 %copy-start.13 = (s32[4]{0:T(128)S(1)}, s32[4]{0:T(128)}, u32[]{:S(2)}) copy-start(s32[4]{0:T(128)} %count_ref.7) | copy-start | bytes 52
  98.0 42.6 %all-to-all-start.1 = ((bf16[16,2,1,64,384]{4,3,2,1,0:T(8,128)(2,1)}), bf16[16,2,1,64,384]{4,3,2,1,0:T(8,128)(2,1)S(1)}, u32[]{:S(2)}, u32[]{:S(2)}) async-start(bf16[16,2,1,64,384]{4,3,2,1,0:T(8,128)(2,1)} %bitcast.104), calls=%async_computation.1 | async-start | bytes 3145728 | tf_op jit(solution)/shard_map/all_to_all | solution.py:160
  102.7 1.4 copy-start.15
  102.7 1.5 copy-start.14
  111.9 0.9 copy-start.10
  112.9 1.9 copy-start.2
  140.5 1.2 copy-start.5
  141.7 41.5 %all-to-all-start.2 = ((bf16[16,2,1,64,384]{4,3,2,1,0:T(8,128)(2,1)}), bf16[16,2,1,64,384]{4,3,2,1,0:T(8,128)(2,1)S(1)}, u32[]{:S(2)}, u32[]{:S(2)}) async-start(bf16[16,2,1,64,384]{4,3,2,1,0:T(8,128)(2,1)} %bitcast.105), calls=%async_computation.2 | async-start | bytes 3145728 | tf_op jit(solution)/shard_map/all_to_all | solution.py:160
  145.3 37.9 %collective-permute-start.1 = (bf16[256,3072]{1,0:T(8,128)(2,1)}, bf16[256,3072]{1,0:T(8,128)(2,1)}, u32[]{:S(2)}, u32[]{:S(2)}) collective-permute-start(bf16[256,3072]{1,0:T(8,128)(2,1)} %bitcast.112), channel_id=1, source_target_pairs={{0,24},{8,16},{16,8},{24,0},{1,25},{9,17},{17,9},{25,1},{2,26},{10... | collective-permute-start | bytes 4718600 | tf_op jit(solution)/shard_map/ppermute | solution.py:169
  154.4 1.9 copy-start.3
  183.2 1.1 copy-start.6
  184.4 42.6 %all-to-all-start.3 = ((bf16[16,2,1,64,384]{4,3,2,1,0:T(8,128)(2,1)}), bf16[16,2,1,64,384]{4,3,2,1,0:T(8,128)(2,1)S(1)}, u32[]{:S(2)}, u32[]{:S(2)}) async-start(bf16[16,2,1,64,384]{4,3,2,1,0:T(8,128)(2,1)} %bitcast.34), calls=%async_computation.3 | async-start | bytes 3145728 | tf_op jit(solution)/shard_map/all_to_all | solution.py:160
  189.1 37.0 %collective-permute-start.3 = (bf16[256,3072]{1,0:T(8,128)(2,1)}, bf16[256,3072]{1,0:T(8,128)(2,1)S(1)}, u32[]{:S(2)}, u32[]{:S(2)}) collective-permute-start(bf16[256,3072]{1,0:T(8,128)(2,1)} %bitcast.111), channel_id=1, source_target_pairs={{0,8},{8,0},{16,24},{24,16},{1,9},{9,1},{17,25},{25,17},{2,10},{10... | collective-permute-start | bytes 4718600 | tf_op jit(solution)/shard_map/ppermute | solution.py:169
  200.7 37.5 %collective-permute-start.5 = (bf16[256,3072]{1,0:T(8,128)(2,1)}, bf16[256,3072]{1,0:T(8,128)(2,1)}, u32[]{:S(2)}, u32[]{:S(2)}) collective-permute-start(bf16[256,3072]{1,0:T(8,128)(2,1)} %bitcast.113), channel_id=1, source_target_pairs={{0,16},{8,24},{16,0},{24,8},{1,17},{9,25},{17,1},{25,9},{2,18},{10... | collective-permute-start | bytes 4718600 | tf_op jit(solution)/shard_map/ppermute | solution.py:169
  227.0 1.1 copy-start.7
  (2 other events, 1.6 us)

commit v17 on v14

--- a/solution.py
+++ b/solution.py
@@ -140,8 +140,8 @@
     sent = []
     for index, step in enumerate(order):
         tokens = arrived[step]
-        if index >= 1:
-            tokens, _ = lax.optimization_barrier((tokens, received[max(index - 2, 0)]))
+        if index >= 2:
+            tokens, _ = lax.optimization_barrier((tokens, received[index - 2]))
         key_value = jnp.einsum(
             "td,sdh->sth", tokens, qkv_weight[1:3], preferred_element_type=jnp.float32
         ).astype(jnp.bfloat16)

time: 241 us -> 241 us (level)
  no operation moved by 1% of the time
where the time goes in v17:
time: 241 us; the launch traced here: 240 us
  waiting for transfers between devices  108 us (45%)
  matrix products  45.1 us (19%)
  starting transfers between devices  31.8 us (13%)
  Pallas kernels  29.1 us (12%)
  blocking collectives  12.9 us (5%)
  local copies, waits for them, and re-layouts  10.9 us (5%)
  other arithmetic  2.66 us (1%)
    ppermute x3, waiting for transfers between devices, local(): arrived[step] = lax.ppermute(own_tokens, 'dp', partner_pairs(n_dp, step))  53.4 us
    ppermute x3, waiting for transfers between devices, local(): partial_out = lax.ppermute(partial_out, 'dp', partner_pairs(n_dp, step))  39.2 us
    pallas_call x4, Pallas kernels, attend(): pl.pallas_call(kernel, out_shape=jax.ShapeDtypeStruct((1, token_count, wi...  29.1 us
    all_to_all x4, starting transfers between devices, local(): incoming = lax.all_to_all(payload, 'ctx', 0, 0, tiled=True)  19.3 us
    dot_general x4, matrix products, local(): jnp.einsum('td,sdh->sth', tokens, qkv_weight[1:3], preferred_element_type...  16.3 us
    all_to_all x4, waiting for transfers between devices, local(): incoming = lax.all_to_all(payload, 'ctx', 0, 0, tiled=True)  15.1 us
    dot_general x4, matrix products, local(): jnp.dot(tokens, qkv_weight[0], preferred_element_type=jnp.float32)  14.8 us
    dot_general x4, matrix products, local(): jnp.dot(attended[0], out_weight, preferred_element_type=jnp.float32)  14 us
  transfers between devices with their start and end apart: 10, of which 7 were waited for; matrix products, arithmetic and copies ran while one was open for 20% of the time, Pallas kernels for 12%

profile of v17, /device:TPU:0, one launch (start us, length us, event | category | flops | bytes accessed | tf_op | source)
XLA Modules:
  0.0 240.3 jit_solution(10457755967923280726)
XLA Ops:
  0.0 3.9 %collective-permute-start = (bf16[256,3072]{1,0:T(8,128)(2,1)}, bf16[256,3072]{1,0:T(8,128)(2,1)}, u32[]{:S(2)}, u32[]{:S(2)}) collective-permute-start(bf16[256,3072]{1,0:T(8,128)(2,1)} %bitcast.152), channel_id=1, source_target_pairs={{0,24},{8,16},{16,8},{24,0},{1,25},{9,17},{17,9},{25,1},{2,26},{10... | collective-permute-start | bytes 4718600 | tf_op jit(solution)/shard_map/ppermute | solution.py:136
  5.4 12.9 %all-gather = f32[8,4,11]{2,1,0:T(4,128)S(1)} all-gather(f32[1,4,11]{2,1,0:T(4,128)S(1)} %fusion.78), channel_id=1, replica_groups=mesh['dp'=4,'ctx'=8] {'ctx'}, dimensions={0}, use_global_device_ids=true | all-gather | bytes 1584 | tf_op jit(solution)/shard_map/all_gather | solution.py:110
  19.1 19.5 %collective-permute-done = bf16[256,3072]{1,0:T(8,128)(2,1)} collective-permute-done((bf16[256,3072]{1,0:T(8,128)(2,1)}, bf16[256,3072]{1,0:T(8,128)(2,1)}, u32[]{:S(2)}, u32[]{:S(2)}) %collective-permute-start) | collective-permute-done | bytes 1572896 | tf_op jit(solution)/shard_map/ppermute | solution.py:136
  38.6 4.2 %fusion.31 = bf16[2,384,256]{1,2,0:T(8,128)(2,1)S(1)} fusion(bf16[3,3072,384]{2,1,0:T(8,128)(2,1)} %param.8, bf16[256,3072]{1,0:T(8,128)(2,1)} %collective-permute-done), kind=kOutput, calls=%fused_computation.38 | convolution fusion | flops 1208156160 | bytes 6684672 | tf_op jit(solution)/shard_map/td,sdh->sth/dot_general | solution.py:145
  44.8 5.2 %all-to-all-start = ((bf16[16,2,1,64,384]{4,3,2,1,0:T(8,128)(2,1)}), bf16[16,2,1,64,384]{4,3,2,1,0:T(8,128)(2,1)}, u32[]{:S(2)}, u32[]{:S(2)}) async-start(bf16[16,2,1,64,384]{4,3,2,1,0:T(8,128)(2,1)} %bitcast.144), calls=%async_computation | async-start | bytes 3145728 | tf_op jit(solution)/shard_map/all_to_all | solution.py:156
  53.2 33.9 %collective-permute-done.2 = bf16[256,3072]{1,0:T(8,128)(2,1)} collective-permute-done((bf16[256,3072]{1,0:T(8,128)(2,1)}, bf16[256,3072]{1,0:T(8,128)(2,1)}, u32[]{:S(2)}, u32[]{:S(2)}) %collective-permute-start.2) | collective-permute-done | bytes 1572896 | tf_op jit(solution)/shard_map/ppermute | solution.py:136
  87.1 4.2 %fusion.26 = bf16[2,384,256]{1,2,0:T(8,128)(2,1)S(1)} fusion(bf16[3,3072,384]{2,1,0:T(8,128)(2,1)} %param.8, bf16[256,3072]{1,0:T(8,128)(2,1)} %collective-permute-done.2), kind=kOutput, calls=%fused_computation.37 | convolution fusion | flops 1208156160 | bytes 6684672 | tf_op jit(solution)/shard_map/td,sdh->sth/dot_general | solution.py:145
  93.3 4.9 %all-to-all-start.1 = ((bf16[16,2,1,64,384]{4,3,2,1,0:T(8,128)(2,1)}), bf16[16,2,1,64,384]{4,3,2,1,0:T(8,128)(2,1)}, u32[]{:S(2)}, u32[]{:S(2)}) async-start(bf16[16,2,1,64,384]{4,3,2,1,0:T(8,128)(2,1)} %bitcast.141), calls=%async_computation.1 | async-start | bytes 3145728 | tf_op jit(solution)/shard_map/all_to_all | solution.py:156
  101.5 3.8 %fusion.67.q_ref = bf16[1,256,384]{2,1,0:T(8,128)(2,1)} fusion(bf16[256,3072]{1,0:T(8,128)(2,1)} %collective-permute-done, bf16[3,3072,384]{2,1,0:T(8,128)(2,1)} %param.8), kind=kOutput, calls=%fused_computation.48 | convolution fusion | flops 604078080 | bytes 4128768 | tf_op jit(solution)/shard_map/dot_general | solution.py:160
  105.3 4.2 %fusion.36 = bf16[256,2,384]{2,0,1:T(8,128)(2,1)S(1)} fusion(bf16[3,3072,384]{2,1,0:T(8,128)(2,1)} %param.8, bf16[256,3072]{1,0:T(8,128)(2,1)} %collective-permute-done.4), kind=kOutput, calls=%fused_computation.39 | convolution fusion | flops 1208156160 | bytes 6684672 | tf_op jit(solution)/shard_map/td,sdh->sth/dot_general | solution.py:145
  111.5 7.3 %shard_map.73 = bf16[1,256,384]{2,1,0:T(8,128)(2,1)} custom-call(s32[4,10]{1,0:T(4,128)} %add_select_fusion.2.pos_ref, s32[4]{0:T(128)} %count_ref.7, f32[4,3,10]{2,1,0:T(4,128)} %fusion.76.bias_ref, bf16[1,256,384]{2,1,0:T(8,128)(2,1)} %fusion.67.q_ref, bf16[4,2,1,64,384]{4,3,2,1,0:T(8,128)(2,1)} %bitcast.134, bf16[16,2,1,64,384]{4,3,2,1,0:T(8,128)(2,1)} %all-to-all-done.far_ref), custom_call_target="tpu_custom_call" | custom-call | tf_op jit(solution)/shard_map/pallas_call | solution.py:80
  121.9 14.2 %all-to-all-done.1.far_ref = bf16[16,2,1,64,384]{4,3,2,1,0:T(8,128)(2,1)} async-done(((bf16[16,2,1,64,384]{4,3,2,1,0:T(8,128)(2,1)}), bf16[16,2,1,64,384]{4,3,2,1,0:T(8,128)(2,1)}, u32[]{:S(2)}, u32[]{:S(2)}) %all-to-all-start.1) | async-done | bytes 1572896 | tf_op jit(solution)/shard_map/all_to_all | solution.py:156
  136.1 4.5 %all-to-all-start.2 = ((bf16[16,2,1,64,384]{4,3,2,1,0:T(8,128)(2,1)}), bf16[16,2,1,64,384]{4,3,2,1,0:T(8,128)(2,1)}, u32[]{:S(2)}, u32[]{:S(2)}) async-start(bf16[16,2,1,64,384]{4,3,2,1,0:T(8,128)(2,1)} %bitcast.143), calls=%async_computation.2 | async-start | bytes 3145728 | tf_op jit(solution)/shard_map/all_to_all | solution.py:156
  143.1 3.8 %fusion.64.q_ref = bf16[1,256,384]{2,1,0:T(8,128)(2,1)} fusion(bf16[256,3072]{1,0:T(8,128)(2,1)} %collective-permute-done.2, bf16[3,3072,384]{2,1,0:T(8,128)(2,1)} %param.8), kind=kOutput, calls=%fused_computation.47 | convolution fusion | flops 604078080 | bytes 4128768 | tf_op jit(solution)/shard_map/dot_general | solution.py:160
  147.0 3.8 %fusion.41 = bf16[256,2,384]{2,0,1:T(8,128)(2,1)S(1)} fusion(bf16[3,3072,384]{2,1,0:T(8,128)(2,1)} %param.8, bf16[256,3072]{1,0:T(8,128)(2,1)S(1)} %bitcast.155), kind=kOutput, calls=%fused_computation.40 | convolution fusion | flops 1208156160 | bytes 6684672 | tf_op jit(solution)/shard_map/td,sdh->sth/dot_general | solution.py:145
  152.7 7.3 %shard_map.74 = bf16[1,256,384]{2,1,0:T(8,128)(2,1)} custom-call(s32[4,10]{1,0:T(4,128)} %add_select_fusion.2.pos_ref, s32[4]{0:T(128)} %count_ref.7, f32[4,3,10]{2,1,0:T(4,128)} %fusion.76.bias_ref, bf16[1,256,384]{2,1,0:T(8,128)(2,1)} %fusion.64.q_ref, bf16[4,2,1,64,384]{4,3,2,1,0:T(8,128)(2,1)} %bitcast.136, ...), custom_call_target="tpu_custom_call" | custom-call | tf_op jit(solution)/shard_map/pallas_call | solution.py:80
  163.1 15.3 %collective-permute-done.1 = bf16[256,3072]{1,0:T(8,128)(2,1)} collective-permute-done((bf16[256,3072]{1,0:T(8,128)(2,1)}, bf16[256,3072]{1,0:T(8,128)(2,1)}, u32[]{:S(2)}, u32[]{:S(2)}) %collective-permute-start.1) | collective-permute-done | bytes 1572896 | tf_op jit(solution)/shard_map/ppermute | solution.py:167
  178.3 4.8 %all-to-all-start.3 = ((bf16[16,2,1,64,384]{4,3,2,1,0:T(8,128)(2,1)}), bf16[16,2,1,64,384]{4,3,2,1,0:T(8,128)(2,1)}, u32[]{:S(2)}, u32[]{:S(2)}) async-start(bf16[16,2,1,64,384]{4,3,2,1,0:T(8,128)(2,1)} %bitcast.142), calls=%async_computation.3 | async-start | bytes 3145728 | tf_op jit(solution)/shard_map/all_to_all | solution.py:156
  184.6 3.8 %fusion.61.q_ref = bf16[1,256,384]{2,1,0:T(8,128)(2,1)} fusion(bf16[256,3072]{1,0:T(8,128)(2,1)} %collective-permute-done.4, bf16[3,3072,384]{2,1,0:T(8,128)(2,1)} %param.8), kind=kOutput, calls=%fused_computation.46 | convolution fusion | flops 604078080 | bytes 4128768 | tf_op jit(solution)/shard_map/dot_general | solution.py:160
  188.4 7.3 %shard_map.75 = bf16[1,256,384]{2,1,0:T(8,128)(2,1)} custom-call(s32[4,10]{1,0:T(4,128)} %add_select_fusion.2.pos_ref, s32[4]{0:T(128)} %count_ref.7, f32[4,3,10]{2,1,0:T(4,128)} %fusion.76.bias_ref, bf16[1,256,384]{2,1,0:T(8,128)(2,1)} %fusion.61.q_ref, bf16[4,2,1,64,384]{4,3,2,1,0:T(8,128)(2,1)} %bitcast.138, ...), custom_call_target="tpu_custom_call" | custom-call | tf_op jit(solution)/shard_map/pallas_call | solution.py:80
  203.7 16.5 %collective-permute-done.3 = bf16[256,3072]{1,0:T(8,128)(2,1)} collective-permute-done((bf16[256,3072]{1,0:T(8,128)(2,1)}, bf16[256,3072]{1,0:T(8,128)(2,1)}, u32[]{:S(2)}, u32[]{:S(2)}) %collective-permute-start.3) | collective-permute-done | bytes 1572896 | tf_op jit(solution)/shard_map/ppermute | solution.py:167
  221.1 7.3 %shard_map.76 = bf16[1,256,384]{2,1,0:T(8,128)(2,1)} custom-call(s32[4,10]{1,0:T(4,128)} %add_select_fusion.2.pos_ref, s32[4]{0:T(128)} %count_ref.7, f32[4,3,10]{2,1,0:T(4,128)} %fusion.76.bias_ref, bf16[1,256,384]{2,1,0:T(8,128)(2,1)} %fusion.58.q_ref, bf16[4,2,1,64,384]{4,3,2,1,0:T(8,128)(2,1)} %bitcast.140, ...), custom_call_target="tpu_custom_call" | custom-call | tf_op jit(solution)/shard_map/pallas_call | solution.py:80
  228.3 7.4 %collective-permute-done.5 = bf16[256,3072]{1,0:T(8,128)(2,1)} collective-permute-done((bf16[256,3072]{1,0:T(8,128)(2,1)}, bf16[256,3072]{1,0:T(8,128)(2,1)}, u32[]{:S(2)}, u32[]{:S(2)}) %collective-permute-start.5) | collective-permute-done | bytes 1572896 | tf_op jit(solution)/shard_map/ppermute | solution.py:167
  235.7 4.6 %fusion.17 = bf16[1,256,3072]{2,1,0:T(8,128)(2,1)} fusion(bf16[256,3072]{1,0:T(8,128)(2,1)} %collective-permute-done.5, bf16[256,3072]{1,0:T(8,128)(2,1)} %collective-permute-done.3, bf16[256,3072]{1,0:T(8,128)(2,1)} %collective-permute-done.1, bf16[384,3072]{1,0:T(8,128)(2,1)S(1)} %copy-done, bf16[1,256,384]{2,1,0:T(8,128)(2,1)} %shard_map.76), kind=kOutput, calls=%fused_computation.28 | convolution fusion | flops 611057664 | bytes 8847360 | tf_op jit(solution)/shard_map/dot_general | solution.py:162
  (81 shorter events, 35.6 us)
Async XLA Ops:
  0.0 118.8 %copy-start = (bf16[384,3072]{1,0:T(8,128)(2,1)S(1)}, bf16[384,3072]{1,0:T(8,128)(2,1)}, u32[]{:S(2)}) copy-start(bf16[384,3072]{1,0:T(8,128)(2,1)} %param.9) | copy-start | bytes 7077892
  0.0 38.6 %collective-permute-start = (bf16[256,3072]{1,0:T(8,128)(2,1)}, bf16[256,3072]{1,0:T(8,128)(2,1)}, u32[]{:S(2)}, u32[]{:S(2)}) collective-permute-start(bf16[256,3072]{1,0:T(8,128)(2,1)} %bitcast.152), channel_id=1, source_target_pairs={{0,24},{8,16},{16,8},{24,0},{1,25},{9,17},{17,9},{25,1},{2,26},{10... | collective-permute-start | bytes 4718600 | tf_op jit(solution)/shard_map/ppermute | solution.py:136
  42.9 1.9 copy-start.1
  44.8 8.2 %copy-start.7 = (s32[4,10]{1,0:T(4,128)S(1)}, s32[4,10]{1,0:T(4,128)}, u32[]{:S(2)}) copy-start(s32[4,10]{1,0:T(4,128)} %param.12) | copy-start | bytes 484
  44.8 8.3 %copy-start.5 = (s32[4,10]{1,0:T(4,128)S(1)}, s32[4,10]{1,0:T(4,128)}, u32[]{:S(2)}) copy-start(s32[4,10]{1,0:T(4,128)} %param.10) | copy-start | bytes 484
  44.8 48.5 %all-to-all-start = ((bf16[16,2,1,64,384]{4,3,2,1,0:T(8,128)(2,1)}), bf16[16,2,1,64,384]{4,3,2,1,0:T(8,128)(2,1)}, u32[]{:S(2)}, u32[]{:S(2)}) async-start(bf16[16,2,1,64,384]{4,3,2,1,0:T(8,128)(2,1)} %bitcast.144), calls=%async_computation | async-start | bytes 3145728 | tf_op jit(solution)/shard_map/all_to_all | solution.py:156
  50.0 37.1 %collective-permute-start.2 = (bf16[256,3072]{1,0:T(8,128)(2,1)}, bf16[256,3072]{1,0:T(8,128)(2,1)}, u32[]{:S(2)}, u32[]{:S(2)}) collective-permute-start(bf16[256,3072]{1,0:T(8,128)(2,1)} %bitcast.153), channel_id=1, source_target_pairs={{0,8},{8,0},{16,24},{24,16},{1,9},{9,1},{17,25},{25,17},{2,10},{10... | collective-permute-start | bytes 4718600 | tf_op jit(solution)/shard_map/ppermute | solution.py:136
  51.5 53.8 %collective-permute-start.4 = (bf16[256,3072]{1,0:T(8,128)(2,1)}, bf16[256,3072]{1,0:T(8,128)(2,1)}, u32[]{:S(2)}, u32[]{:S(2)}) collective-permute-start(bf16[256,3072]{1,0:T(8,128)(2,1)} %bitcast.154), channel_id=1, source_target_pairs={{0,16},{8,24},{16,0},{24,8},{1,17},{9,25},{17,1},{25,9},{2,18},{10... | collective-permute-start | bytes 4718600 | tf_op jit(solution)/shard_map/ppermute | solution.py:136
  91.4 1.9 copy-start.2
  93.3 4.9 %copy-start.6 = (s32[4]{0:T(128)S(1)}, s32[4]{0:T(128)}, u32[]{:S(2)}) copy-start(s32[4]{0:T(128)} %count_ref.7) | copy-start | bytes 52
  93.3 42.8 %all-to-all-start.1 = ((bf16[16,2,1,64,384]{4,3,2,1,0:T(8,128)(2,1)}), bf16[16,2,1,64,384]{4,3,2,1,0:T(8,128)(2,1)}, u32[]{:S(2)}, u32[]{:S(2)}) async-start(bf16[16,2,1,64,384]{4,3,2,1,0:T(8,128)(2,1)} %bitcast.141), calls=%async_computation.1 | async-start | bytes 3145728 | tf_op jit(solution)/shard_map/all_to_all | solution.py:156
  98.2 1.2 copy-start.8
  109.5 1.9 copy-start.3
  136.1 42.2 %all-to-all-start.2 = ((bf16[16,2,1,64,384]{4,3,2,1,0:T(8,128)(2,1)}), bf16[16,2,1,64,384]{4,3,2,1,0:T(8,128)(2,1)}, u32[]{:S(2)}, u32[]{:S(2)}) async-start(bf16[16,2,1,64,384]{4,3,2,1,0:T(8,128)(2,1)} %bitcast.143), calls=%async_computation.2 | async-start | bytes 3145728 | tf_op jit(solution)/shard_map/all_to_all | solution.py:156
  140.6 6.3 %copy-start.9 = (bf16[1,256,3072]{2,1,0:T(8,128)(2,1)S(1)}, bf16[1,256,3072]{2,1,0:T(8,128)(2,1)}, u32[]{:S(2)}) copy-start(bf16[1,256,3072]{2,1,0:T(8,128)(2,1)} %param.7) | copy-start | bytes 4718596
  140.6 37.7 %collective-permute-start.1 = (bf16[256,3072]{1,0:T(8,128)(2,1)}, bf16[256,3072]{1,0:T(8,128)(2,1)}, u32[]{:S(2)}, u32[]{:S(2)}) collective-permute-start(bf16[256,3072]{1,0:T(8,128)(2,1)} %convolution_convert_fusion.3), channel_id=1, source_target_pairs={{0,24},{8,16},{16,8},{24,0},{1,25},{9,17},{17,9},{25,1},{2,26},{10... | collective-permute-start | bytes 4718600 | tf_op jit(solution)/shard_map/ppermute | solution.py:167
  150.8 1.9 copy-start.4
  178.3 42.7 %all-to-all-start.3 = ((bf16[16,2,1,64,384]{4,3,2,1,0:T(8,128)(2,1)}), bf16[16,2,1,64,384]{4,3,2,1,0:T(8,128)(2,1)}, u32[]{:S(2)}, u32[]{:S(2)}) async-start(bf16[16,2,1,64,384]{4,3,2,1,0:T(8,128)(2,1)} %bitcast.142), calls=%async_computation.3 | async-start | bytes 3145728 | tf_op jit(solution)/shard_map/all_to_all | solution.py:156
  183.1 37.1 %collective-permute-start.3 = (bf16[256,3072]{1,0:T(8,128)(2,1)}, bf16[256,3072]{1,0:T(8,128)(2,1)}, u32[]{:S(2)}, u32[]{:S(2)}) collective-permute-start(bf16[256,3072]{1,0:T(8,128)(2,1)} %convolution_convert_fusion.2), channel_id=1, source_target_pairs={{0,8},{8,0},{16,24},{24,16},{1,9},{9,1},{17,25},{25,17},{2,10},{10... | collective-permute-start | bytes 4718600 | tf_op jit(solution)/shard_map/ppermute | solution.py:167
  195.7 4.7 %copy-start.10 = (bf16[1,256,3072]{2,1,0:T(8,128)(2,1)S(1)}, bf16[1,256,3072]{2,1,0:T(8,128)(2,1)}, u32[]{:S(2)}) copy-start(bf16[1,256,3072]{2,1,0:T(8,128)(2,1)} %param.7) | copy-start | bytes 4718596
  198.9 36.8 %collective-permute-start.5 = (bf16[256,3072]{1,0:T(8,128)(2,1)}, bf16[256,3072]{1,0:T(8,128)(2,1)}, u32[]{:S(2)}, u32[]{:S(2)}) collective-permute-start(bf16[256,3072]{1,0:T(8,128)(2,1)} %convolution_convert_fusion.1), channel_id=1, source_target_pairs={{0,16},{8,24},{16,0},{24,8},{1,17},{9,25},{17,1},{25,9},{2,18},{10... | collective-permute-start | bytes 4718600 | tf_op jit(solution)/shard_map/ppermute | solution.py:167

commit v18 on v17

--- a/solution.py
+++ b/solution.py
@@ -28,23 +28,19 @@
     return first.astype(jnp.int32), second.astype(jnp.int32)
 
 
-def attention_kernel(pos_ref, count_ref, bias_ref, q_ref, own_ref, far_ref, out_ref, *, heads, head_size, scale):
+def attention_kernel(pos_ref, count_ref, bias_ref, q_ref, own_ref, far_ref, out_ref, pool_ref, *, heads, head_size, scale):
     tile = pl.program_id(0)
     own_tiles = own_ref.shape[0]
     live_count = count_ref[tile]
     queries = q_ref[0]
-    picks = []
-    for slot in range(KMAX):
-        where = pos_ref[tile, slot]
-        picks.append((
-            where < own_tiles,
-            jnp.minimum(where, own_tiles - 1),
-            jnp.maximum(where - own_tiles, 0),
-        ))
+
+    @pl.when(tile == 0)
+    def _():
+        pool_ref[:own_tiles] = own_ref[...]
+        pool_ref[own_tiles:] = far_ref[...]
 
     def rows(part, slot, cols):
-        mine, near, far = picks[slot]
-        return jnp.where(mine, own_ref[near, part, 0, :, cols], far_ref[far, part, 0, :, cols])
+        return pool_ref[pos_ref[tile, slot], part, 0, :, cols]
 
     column = lax.broadcasted_iota(jnp.int32, (1, KMAX * TILE), 1) // TILE
     live = column < live_count
@@ -87,6 +83,9 @@
                       pl.BlockSpec((1, TILE, width), lambda t, pos, cnt: (0, t, 0)),
                       whole(own_tiles), whole(far_tiles)],
             out_specs=pl.BlockSpec((1, TILE, width), lambda t, pos, cnt: (0, t, 0)),
+            scratch_shapes=[pltpu.VMEM(
+                (own_tiles.shape[0] + far_tiles.shape[0],) + own_tiles.shape[1:], own_tiles.dtype
+            )],
         ),
     )(positions, live_counts, bias, queries, own_tiles, far_tiles)
 

time: 241 us -> 241 us (level)
  no operation moved by 1% of the time
where the time goes in v18:
time: 241 us; the launch traced here: 240 us
  waiting for transfers between devices  107 us (44%)
  matrix products  45.1 us (19%)
  starting transfers between devices  31.8 us (13%)
  Pallas kernels  29.8 us (12%)
  blocking collectives  12.9 us (5%)
  local copies, waits for them, and re-layouts  10.9 us (5%)
  other arithmetic  2.66 us (1%)
    ppermute x3, waiting for transfers between devices, local(): arrived[step] = lax.ppermute(own_tokens, 'dp', partner_pairs(n_dp, step))  53.4 us
    ppermute x3, waiting for transfers between devices, local(): partial_out = lax.ppermute(partial_out, 'dp', partner_pairs(n_dp, step))  38.8 us
    pallas_call x4, Pallas kernels, attend(): pl.pallas_call(kernel, out_shape=jax.ShapeDtypeStruct((1, token_count, wi...  29.8 us
    all_to_all x4, starting transfers between devices, local(): incoming = lax.all_to_all(payload, 'ctx', 0, 0, tiled=True)  19.3 us
    dot_general x4, matrix products, local(): jnp.einsum('td,sdh->sth', tokens, qkv_weight[1:3], preferred_element_type...  16.3 us
    all_to_all x4, waiting for transfers between devices, local(): incoming = lax.all_to_all(payload, 'ctx', 0, 0, tiled=True)  14.9 us
    dot_general x4, matrix products, local(): jnp.dot(tokens, qkv_weight[0], preferred_element_type=jnp.float32)  14.8 us
    dot_general x4, matrix products, local(): jnp.dot(attended[0], out_weight, preferred_element_type=jnp.float32)  14 us
  transfers between devices with their start and end apart: 10, of which 7 were waited for; matrix products, arithmetic and copies ran while one was open for 20% of the time, Pallas kernels for 12%

profile of v18, /device:TPU:0, one launch (start us, length us, event | category | flops | bytes accessed | tf_op | source)
XLA Modules:
  0.0 240.4 jit_solution(1446358103869508117)
XLA Ops:
  0.0 3.9 %collective-permute-start = (bf16[256,3072]{1,0:T(8,128)(2,1)}, bf16[256,3072]{1,0:T(8,128)(2,1)}, u32[]{:S(2)}, u32[]{:S(2)}) collective-permute-start(bf16[256,3072]{1,0:T(8,128)(2,1)} %bitcast.152), channel_id=1, source_target_pairs={{0,24},{8,16},{16,8},{24,0},{1,25},{9,17},{17,9},{25,1},{2,26},{10... | collective-permute-start | bytes 4718600 | tf_op jit(solution)/shard_map/ppermute | solution.py:135
  5.4 12.9 %all-gather = f32[8,4,11]{2,1,0:T(4,128)S(1)} all-gather(f32[1,4,11]{2,1,0:T(4,128)S(1)} %fusion.78), channel_id=1, replica_groups=mesh['dp'=4,'ctx'=8] {'ctx'}, dimensions={0}, use_global_device_ids=true | all-gather | bytes 1584 | tf_op jit(solution)/shard_map/all_gather | solution.py:109
  19.1 19.5 %collective-permute-done = bf16[256,3072]{1,0:T(8,128)(2,1)} collective-permute-done((bf16[256,3072]{1,0:T(8,128)(2,1)}, bf16[256,3072]{1,0:T(8,128)(2,1)}, u32[]{:S(2)}, u32[]{:S(2)}) %collective-permute-start) | collective-permute-done | bytes 1572896 | tf_op jit(solution)/shard_map/ppermute | solution.py:135
  38.6 4.2 %fusion.31 = bf16[2,384,256]{1,2,0:T(8,128)(2,1)S(1)} fusion(bf16[3,3072,384]{2,1,0:T(8,128)(2,1)} %param.8, bf16[256,3072]{1,0:T(8,128)(2,1)} %collective-permute-done), kind=kOutput, calls=%fused_computation.38 | convolution fusion | flops 1208156160 | bytes 6684672 | tf_op jit(solution)/shard_map/td,sdh->sth/dot_general | solution.py:144
  44.8 5.2 %all-to-all-start = ((bf16[16,2,1,64,384]{4,3,2,1,0:T(8,128)(2,1)}), bf16[16,2,1,64,384]{4,3,2,1,0:T(8,128)(2,1)}, u32[]{:S(2)}, u32[]{:S(2)}) async-start(bf16[16,2,1,64,384]{4,3,2,1,0:T(8,128)(2,1)} %bitcast.144), calls=%async_computation | async-start | bytes 3145728 | tf_op jit(solution)/shard_map/all_to_all | solution.py:155
  53.2 33.9 %collective-permute-done.2 = bf16[256,3072]{1,0:T(8,128)(2,1)} collective-permute-done((bf16[256,3072]{1,0:T(8,128)(2,1)}, bf16[256,3072]{1,0:T(8,128)(2,1)}, u32[]{:S(2)}, u32[]{:S(2)}) %collective-permute-start.2) | collective-permute-done | bytes 1572896 | tf_op jit(solution)/shard_map/ppermute | solution.py:135
  87.1 4.2 %fusion.26 = bf16[2,384,256]{1,2,0:T(8,128)(2,1)S(1)} fusion(bf16[3,3072,384]{2,1,0:T(8,128)(2,1)} %param.8, bf16[256,3072]{1,0:T(8,128)(2,1)} %collective-permute-done.2), kind=kOutput, calls=%fused_computation.37 | convolution fusion | flops 1208156160 | bytes 6684672 | tf_op jit(solution)/shard_map/td,sdh->sth/dot_general | solution.py:144
  93.3 4.9 %all-to-all-start.1 = ((bf16[16,2,1,64,384]{4,3,2,1,0:T(8,128)(2,1)}), bf16[16,2,1,64,384]{4,3,2,1,0:T(8,128)(2,1)}, u32[]{:S(2)}, u32[]{:S(2)}) async-start(bf16[16,2,1,64,384]{4,3,2,1,0:T(8,128)(2,1)} %bitcast.141), calls=%async_computation.1 | async-start | bytes 3145728 | tf_op jit(solution)/shard_map/all_to_all | solution.py:155
  101.5 3.8 %fusion.67.q_ref = bf16[1,256,384]{2,1,0:T(8,128)(2,1)} fusion(bf16[256,3072]{1,0:T(8,128)(2,1)} %collective-permute-done, bf16[3,3072,384]{2,1,0:T(8,128)(2,1)} %param.8), kind=kOutput, calls=%fused_computation.48 | convolution fusion | flops 604078080 | bytes 4128768 | tf_op jit(solution)/shard_map/dot_general | solution.py:159
  105.3 4.2 %fusion.36 = bf16[256,2,384]{2,0,1:T(8,128)(2,1)S(1)} fusion(bf16[3,3072,384]{2,1,0:T(8,128)(2,1)} %param.8, bf16[256,3072]{1,0:T(8,128)(2,1)} %collective-permute-done.4), kind=kOutput, calls=%fused_computation.39 | convolution fusion | flops 1208156160 | bytes 6684672 | tf_op jit(solution)/shard_map/td,sdh->sth/dot_general | solution.py:144
  111.5 7.5 %shard_map.73 = bf16[1,256,384]{2,1,0:T(8,128)(2,1)} custom-call(s32[4,10]{1,0:T(4,128)} %add_select_fusion.2.pos_ref, s32[4]{0:T(128)} %count_ref.7, f32[4,3,10]{2,1,0:T(4,128)} %fusion.76.bias_ref, bf16[1,256,384]{2,1,0:T(8,128)(2,1)} %fusion.67.q_ref, bf16[4,2,1,64,384]{4,3,2,1,0:T(8,128)(2,1)} %bitcast.134, bf16[16,2,1,64,384]{4,3,2,1,0:T(8,128)(2,1)} %all-to-all-done.far_ref), custom_call_target="tpu_custom_call" | custom-call | tf_op jit(solution)/shard_map/pallas_call | solution.py:76
  122.1 14.1 %all-to-all-done.1.far_ref = bf16[16,2,1,64,384]{4,3,2,1,0:T(8,128)(2,1)} async-done(((bf16[16,2,1,64,384]{4,3,2,1,0:T(8,128)(2,1)}), bf16[16,2,1,64,384]{4,3,2,1,0:T(8,128)(2,1)}, u32[]{:S(2)}, u32[]{:S(2)}) %all-to-all-start.1) | async-done | bytes 1572896 | tf_op jit(solution)/shard_map/all_to_all | solution.py:155
  136.1 4.5 %all-to-all-start.2 = ((bf16[16,2,1,64,384]{4,3,2,1,0:T(8,128)(2,1)}), bf16[16,2,1,64,384]{4,3,2,1,0:T(8,128)(2,1)}, u32[]{:S(2)}, u32[]{:S(2)}) async-start(bf16[16,2,1,64,384]{4,3,2,1,0:T(8,128)(2,1)} %bitcast.143), calls=%async_computation.2 | async-start | bytes 3145728 | tf_op jit(solution)/shard_map/all_to_all | solution.py:155
  143.1 3.8 %fusion.64.q_ref = bf16[1,256,384]{2,1,0:T(8,128)(2,1)} fusion(bf16[256,3072]{1,0:T(8,128)(2,1)} %collective-permute-done.2, bf16[3,3072,384]{2,1,0:T(8,128)(2,1)} %param.8), kind=kOutput, calls=%fused_computation.47 | convolution fusion | flops 604078080 | bytes 4128768 | tf_op jit(solution)/shard_map/dot_general | solution.py:159
  147.0 3.8 %fusion.41 = bf16[256,2,384]{2,0,1:T(8,128)(2,1)S(1)} fusion(bf16[3,3072,384]{2,1,0:T(8,128)(2,1)} %param.8, bf16[256,3072]{1,0:T(8,128)(2,1)S(1)} %bitcast.155), kind=kOutput, calls=%fused_computation.40 | convolution fusion | flops 1208156160 | bytes 6684672 | tf_op jit(solution)/shard_map/td,sdh->sth/dot_general | solution.py:144
  152.7 7.5 %shard_map.74 = bf16[1,256,384]{2,1,0:T(8,128)(2,1)} custom-call(s32[4,10]{1,0:T(4,128)} %add_select_fusion.2.pos_ref, s32[4]{0:T(128)} %count_ref.7, f32[4,3,10]{2,1,0:T(4,128)} %fusion.76.bias_ref, bf16[1,256,384]{2,1,0:T(8,128)(2,1)} %fusion.64.q_ref, bf16[4,2,1,64,384]{4,3,2,1,0:T(8,128)(2,1)} %bitcast.136, ...), custom_call_target="tpu_custom_call" | custom-call | tf_op jit(solution)/shard_map/pallas_call | solution.py:76
  163.2 15.1 %collective-permute-done.1 = bf16[256,3072]{1,0:T(8,128)(2,1)} collective-permute-done((bf16[256,3072]{1,0:T(8,128)(2,1)}, bf16[256,3072]{1,0:T(8,128)(2,1)}, u32[]{:S(2)}, u32[]{:S(2)}) %collective-permute-start.1) | collective-permute-done | bytes 1572896 | tf_op jit(solution)/shard_map/ppermute | solution.py:166
  178.3 4.8 %all-to-all-start.3 = ((bf16[16,2,1,64,384]{4,3,2,1,0:T(8,128)(2,1)}), bf16[16,2,1,64,384]{4,3,2,1,0:T(8,128)(2,1)}, u32[]{:S(2)}, u32[]{:S(2)}) async-start(bf16[16,2,1,64,384]{4,3,2,1,0:T(8,128)(2,1)} %bitcast.142), calls=%async_computation.3 | async-start | bytes 3145728 | tf_op jit(solution)/shard_map/all_to_all | solution.py:155
  184.6 3.8 %fusion.61.q_ref = bf16[1,256,384]{2,1,0:T(8,128)(2,1)} fusion(bf16[256,3072]{1,0:T(8,128)(2,1)} %collective-permute-done.4, bf16[3,3072,384]{2,1,0:T(8,128)(2,1)} %param.8), kind=kOutput, calls=%fused_computation.46 | convolution fusion | flops 604078080 | bytes 4128768 | tf_op jit(solution)/shard_map/dot_general | solution.py:159
  188.4 7.4 %shard_map.75 = bf16[1,256,384]{2,1,0:T(8,128)(2,1)} custom-call(s32[4,10]{1,0:T(4,128)} %add_select_fusion.2.pos_ref, s32[4]{0:T(128)} %count_ref.7, f32[4,3,10]{2,1,0:T(4,128)} %fusion.76.bias_ref, bf16[1,256,384]{2,1,0:T(8,128)(2,1)} %fusion.61.q_ref, bf16[4,2,1,64,384]{4,3,2,1,0:T(8,128)(2,1)} %bitcast.138, ...), custom_call_target="tpu_custom_call" | custom-call | tf_op jit(solution)/shard_map/pallas_call | solution.py:76
  203.9 16.3 %collective-permute-done.3 = bf16[256,3072]{1,0:T(8,128)(2,1)} collective-permute-done((bf16[256,3072]{1,0:T(8,128)(2,1)}, bf16[256,3072]{1,0:T(8,128)(2,1)}, u32[]{:S(2)}, u32[]{:S(2)}) %collective-permute-start.3) | collective-permute-done | bytes 1572896 | tf_op jit(solution)/shard_map/ppermute | solution.py:166
  221.1 7.4 %shard_map.76 = bf16[1,256,384]{2,1,0:T(8,128)(2,1)} custom-call(s32[4,10]{1,0:T(4,128)} %add_select_fusion.2.pos_ref, s32[4]{0:T(128)} %count_ref.7, f32[4,3,10]{2,1,0:T(4,128)} %fusion.76.bias_ref, bf16[1,256,384]{2,1,0:T(8,128)(2,1)} %fusion.58.q_ref, bf16[4,2,1,64,384]{4,3,2,1,0:T(8,128)(2,1)} %bitcast.140, ...), custom_call_target="tpu_custom_call" | custom-call | tf_op jit(solution)/shard_map/pallas_call | solution.py:76
  228.5 7.4 %collective-permute-done.5 = bf16[256,3072]{1,0:T(8,128)(2,1)} collective-permute-done((bf16[256,3072]{1,0:T(8,128)(2,1)}, bf16[256,3072]{1,0:T(8,128)(2,1)}, u32[]{:S(2)}, u32[]{:S(2)}) %collective-permute-start.5) | collective-permute-done | bytes 1572896 | tf_op jit(solution)/shard_map/ppermute | solution.py:166
  235.9 4.6 %fusion.17 = bf16[1,256,3072]{2,1,0:T(8,128)(2,1)} fusion(bf16[256,3072]{1,0:T(8,128)(2,1)} %collective-permute-done.5, bf16[256,3072]{1,0:T(8,128)(2,1)} %collective-permute-done.3, bf16[256,3072]{1,0:T(8,128)(2,1)} %collective-permute-done.1, bf16[384,3072]{1,0:T(8,128)(2,1)S(1)} %copy-done, bf16[1,256,384]{2,1,0:T(8,128)(2,1)} %shard_map.76), kind=kOutput, calls=%fused_computation.28 | convolution fusion | flops 611057664 | bytes 8847360 | tf_op jit(solution)/shard_map/dot_general | solution.py:161
  (81 shorter events, 35.6 us)
Async XLA Ops:
  0.0 118.9 %copy-start = (bf16[384,3072]{1,0:T(8,128)(2,1)S(1)}, bf16[384,3072]{1,0:T(8,128)(2,1)}, u32[]{:S(2)}) copy-start(bf16[384,3072]{1,0:T(8,128)(2,1)} %param.9) | copy-start | bytes 7077892
  0.0 38.6 %collective-permute-start = (bf16[256,3072]{1,0:T(8,128)(2,1)}, bf16[256,3072]{1,0:T(8,128)(2,1)}, u32[]{:S(2)}, u32[]{:S(2)}) collective-permute-start(bf16[256,3072]{1,0:T(8,128)(2,1)} %bitcast.152), channel_id=1, source_target_pairs={{0,24},{8,16},{16,8},{24,0},{1,25},{9,17},{17,9},{25,1},{2,26},{10... | collective-permute-start | bytes 4718600 | tf_op jit(solution)/shard_map/ppermute | solution.py:135
  42.9 1.9 copy-start.1
  44.8 8.2 %copy-start.7 = (s32[4,10]{1,0:T(4,128)S(1)}, s32[4,10]{1,0:T(4,128)}, u32[]{:S(2)}) copy-start(s32[4,10]{1,0:T(4,128)} %param.12) | copy-start | bytes 484
  44.8 8.3 %copy-start.5 = (s32[4,10]{1,0:T(4,128)S(1)}, s32[4,10]{1,0:T(4,128)}, u32[]{:S(2)}) copy-start(s32[4,10]{1,0:T(4,128)} %param.10) | copy-start | bytes 484
  44.8 48.5 %all-to-all-start = ((bf16[16,2,1,64,384]{4,3,2,1,0:T(8,128)(2,1)}), bf16[16,2,1,64,384]{4,3,2,1,0:T(8,128)(2,1)}, u32[]{:S(2)}, u32[]{:S(2)}) async-start(bf16[16,2,1,64,384]{4,3,2,1,0:T(8,128)(2,1)} %bitcast.144), calls=%async_computation | async-start | bytes 3145728 | tf_op jit(solution)/shard_map/all_to_all | solution.py:155
  50.0 37.1 %collective-permute-start.2 = (bf16[256,3072]{1,0:T(8,128)(2,1)}, bf16[256,3072]{1,0:T(8,128)(2,1)}, u32[]{:S(2)}, u32[]{:S(2)}) collective-permute-start(bf16[256,3072]{1,0:T(8,128)(2,1)} %bitcast.153), channel_id=1, source_target_pairs={{0,8},{8,0},{16,24},{24,16},{1,9},{9,1},{17,25},{25,17},{2,10},{10... | collective-permute-start | bytes 4718600 | tf_op jit(solution)/shard_map/ppermute | solution.py:135
  51.5 53.8 %collective-permute-start.4 = (bf16[256,3072]{1,0:T(8,128)(2,1)}, bf16[256,3072]{1,0:T(8,128)(2,1)}, u32[]{:S(2)}, u32[]{:S(2)}) collective-permute-start(bf16[256,3072]{1,0:T(8,128)(2,1)} %bitcast.154), channel_id=1, source_target_pairs={{0,16},{8,24},{16,0},{24,8},{1,17},{9,25},{17,1},{25,9},{2,18},{10... | collective-permute-start | bytes 4718600 | tf_op jit(solution)/shard_map/ppermute | solution.py:135
  91.4 1.9 copy-start.2
  93.3 4.9 %copy-start.6 = (s32[4]{0:T(128)S(1)}, s32[4]{0:T(128)}, u32[]{:S(2)}) copy-start(s32[4]{0:T(128)} %count_ref.7) | copy-start | bytes 52
  93.3 42.8 %all-to-all-start.1 = ((bf16[16,2,1,64,384]{4,3,2,1,0:T(8,128)(2,1)}), bf16[16,2,1,64,384]{4,3,2,1,0:T(8,128)(2,1)}, u32[]{:S(2)}, u32[]{:S(2)}) async-start(bf16[16,2,1,64,384]{4,3,2,1,0:T(8,128)(2,1)} %bitcast.141), calls=%async_computation.1 | async-start | bytes 3145728 | tf_op jit(solution)/shard_map/all_to_all | solution.py:155
  98.2 1.2 copy-start.8
  109.5 1.9 copy-start.3
  136.1 42.2 %all-to-all-start.2 = ((bf16[16,2,1,64,384]{4,3,2,1,0:T(8,128)(2,1)}), bf16[16,2,1,64,384]{4,3,2,1,0:T(8,128)(2,1)}, u32[]{:S(2)}, u32[]{:S(2)}) async-start(bf16[16,2,1,64,384]{4,3,2,1,0:T(8,128)(2,1)} %bitcast.143), calls=%async_computation.2 | async-start | bytes 3145728 | tf_op jit(solution)/shard_map/all_to_all | solution.py:155
  140.6 6.3 %copy-start.9 = (bf16[1,256,3072]{2,1,0:T(8,128)(2,1)S(1)}, bf16[1,256,3072]{2,1,0:T(8,128)(2,1)}, u32[]{:S(2)}) copy-start(bf16[1,256,3072]{2,1,0:T(8,128)(2,1)} %param.7) | copy-start | bytes 4718596
  140.6 37.7 %collective-permute-start.1 = (bf16[256,3072]{1,0:T(8,128)(2,1)}, bf16[256,3072]{1,0:T(8,128)(2,1)}, u32[]{:S(2)}, u32[]{:S(2)}) collective-permute-start(bf16[256,3072]{1,0:T(8,128)(2,1)} %convolution_convert_fusion.3), channel_id=1, source_target_pairs={{0,24},{8,16},{16,8},{24,0},{1,25},{9,17},{17,9},{25,1},{2,26},{10... | collective-permute-start | bytes 4718600 | tf_op jit(solution)/shard_map/ppermute | solution.py:166
  150.8 1.9 copy-start.4
  178.3 42.7 %all-to-all-start.3 = ((bf16[16,2,1,64,384]{4,3,2,1,0:T(8,128)(2,1)}), bf16[16,2,1,64,384]{4,3,2,1,0:T(8,128)(2,1)}, u32[]{:S(2)}, u32[]{:S(2)}) async-start(bf16[16,2,1,64,384]{4,3,2,1,0:T(8,128)(2,1)} %bitcast.142), calls=%async_computation.3 | async-start | bytes 3145728 | tf_op jit(solution)/shard_map/all_to_all | solution.py:155
  183.1 37.1 %collective-permute-start.3 = (bf16[256,3072]{1,0:T(8,128)(2,1)}, bf16[256,3072]{1,0:T(8,128)(2,1)}, u32[]{:S(2)}, u32[]{:S(2)}) collective-permute-start(bf16[256,3072]{1,0:T(8,128)(2,1)} %convolution_convert_fusion.2), channel_id=1, source_target_pairs={{0,8},{8,0},{16,24},{24,16},{1,9},{9,1},{17,25},{25,17},{2,10},{10... | collective-permute-start | bytes 4718600 | tf_op jit(solution)/shard_map/ppermute | solution.py:166
  195.9 4.7 %copy-start.10 = (bf16[1,256,3072]{2,1,0:T(8,128)(2,1)S(1)}, bf16[1,256,3072]{2,1,0:T(8,128)(2,1)}, u32[]{:S(2)}) copy-start(bf16[1,256,3072]{2,1,0:T(8,128)(2,1)} %param.7) | copy-start | bytes 4718596
  199.0 36.8 %collective-permute-start.5 = (bf16[256,3072]{1,0:T(8,128)(2,1)}, bf16[256,3072]{1,0:T(8,128)(2,1)}, u32[]{:S(2)}, u32[]{:S(2)}) collective-permute-start(bf16[256,3072]{1,0:T(8,128)(2,1)} %convolution_convert_fusion.1), channel_id=1, source_target_pairs={{0,16},{8,24},{16,0},{24,8},{1,17},{9,25},{17,1},{25,9},{2,18},{10... | collective-permute-start | bytes 4718600 | tf_op jit(solution)/shard_map/ppermute | solution.py:166

commit v19 on v17

--- a/solution.py
+++ b/solution.py
@@ -28,8 +28,8 @@
     return first.astype(jnp.int32), second.astype(jnp.int32)
 
 
-def attention_kernel(pos_ref, count_ref, bias_ref, q_ref, own_ref, far_ref, out_ref, *, heads, head_size, scale):
-    tile = pl.program_id(0)
+def attention_kernel(pos_ref, count_ref, bias_ref, q_ref, own_ref, far_ref, out_ref, *, heads, head_size, scale, first):
+    tile = pl.program_id(0) + first
     own_tiles = own_ref.shape[0]
     live_count = count_ref[tile]
     queries = q_ref[0]
@@ -67,24 +67,24 @@
         out_ref[0, :, head * head_size:(head + 1) * head_size] = (total / weight_sum).astype(out_ref.dtype)
 
 
-def attend(positions, live_counts, bias, queries, own_tiles, far_tiles, heads, head_size):
+def attend(positions, live_counts, bias, queries, own_tiles, far_tiles, heads, head_size, first=0, count=None):
     _, token_count, width = queries.shape
-    tile_count = token_count // TILE
+    tile_count = token_count // TILE if count is None else count
 
     def whole(array):
         return pl.BlockSpec(array.shape, lambda t, pos, cnt: (0,) * array.ndim)
 
     kernel = functools.partial(
-        attention_kernel, heads=heads, head_size=head_size, scale=1.0 / math.sqrt(head_size)
+        attention_kernel, heads=heads, head_size=head_size, scale=1.0 / math.sqrt(head_size), first=first
     )
     return pl.pallas_call(
         kernel,
-        out_shape=jax.ShapeDtypeStruct((1, token_count, width), jnp.bfloat16),
+        out_shape=jax.ShapeDtypeStruct((1, tile_count * TILE, width), jnp.bfloat16),
         grid_spec=pltpu.PrefetchScalarGridSpec(
             num_scalar_prefetch=2,
             grid=(tile_count,),
             in_specs=[pl.BlockSpec(memory_space=pltpu.SMEM),
-                      pl.BlockSpec((1, TILE, width), lambda t, pos, cnt: (0, t, 0)),
+                      pl.BlockSpec((1, TILE, width), lambda t, pos, cnt: (0, t + first, 0)),
                       whole(own_tiles), whole(far_tiles)],
             out_specs=pl.BlockSpec((1, TILE, width), lambda t, pos, cnt: (0, t, 0)),
         ),
@@ -158,14 +158,29 @@
         if index == len(order) - 1 and len(sent) >= 2:
             incoming, _ = lax.optimization_barrier((incoming, sent[-2]))
         queries = jnp.dot(tokens, qkv_weight[0], preferred_element_type=jnp.float32).astype(jnp.bfloat16)
-        attended = attend(positions, live_counts, bias, queries[None], by_tile, incoming, heads_here, head_size)
-        partial_out = jnp.dot(
-            attended[0], out_weight, preferred_element_type=jnp.float32
-        ).astype(jnp.bfloat16)
-        partials.append(partial_out)
-        if step > 0:
-            partial_out = lax.ppermute(partial_out, "dp", partner_pairs(n_dp, step))
+        if index == len(order) - 2 and step > 0 and tile_count % 2 == 0:
+            halves = []
+            for first in (0, tile_count // 2):
+                part = attend(
+                    positions, live_counts, bias, queries[None], by_tile, incoming, heads_here, head_size,
+                    first, tile_count // 2,
+                )
+                part = jnp.dot(part[0], out_weight, preferred_element_type=jnp.float32).astype(jnp.bfloat16)
+                halves.append(lax.ppermute(part, "dp", partner_pairs(n_dp, step)))
+            partial_out = jnp.concatenate(halves, axis=0)
+            partials.append(partial_out)
             sent.append(partial_out)
+        else:
+            attended = attend(
+                positions, live_counts, bias, queries[None], by_tile, incoming, heads_here, head_size
+            )
+            partial_out = jnp.dot(
+                attended[0], out_weight, preferred_element_type=jnp.float32
+            ).astype(jnp.bfloat16)
+            partials.append(partial_out)
+            if step > 0:
+                partial_out = lax.ppermute(partial_out, "dp", partner_pairs(n_dp, step))
+                sent.append(partial_out)
         contribution = partial_out.astype(jnp.float32)
         total = contribution if total is None else total + contribution
     return total.astype(jnp.bfloat16)[None]

time: 241 us -> 245 us (1.017)
  Pallas kernels: 29.1 us -> 32 us
    ppermute x3 -> x2, waiting for transfers between devices: 39.2 us -> 27.6 us  [local(): partial_out = lax.ppermute(partial_out, 'dp', partner_pairs(n_dp, step))]
    ppermute x0 -> x2, waiting for transfers between devices: none -> 11 us  [local(): halves.append(lax.ppermute(part, 'dp', partner_pairs(n_dp, step)))]
    dot_general x0 -> x2, matrix products: none -> 3.94 us  [local(): jnp.dot(part[0], out_weight, preferred_element_type=jnp.float32)]
    dot_general x4 -> x3, matrix products: 14 us -> 10.4 us  [local(): jnp.dot(attended[0], out_weight, preferred_element_type=jnp.float32)]
    pallas_call x4 -> x5, Pallas kernels: 29.1 us -> 32 us  [attend(): pl.pallas_call(kernel, out_shape=jax.ShapeDtypeStruct((1, tile_count * TI...]
    ppermute x3 -> x2, starting transfers between devices: 5.51 us -> 4 us  [local(): partial_out = lax.ppermute(partial_out, 'dp', partner_pairs(n_dp, step))]
  transfers between devices with their start and end apart: 10 -> 11, of which waited for: 7 -> 7; matrix products, arithmetic and copies ran while one was open for 20% -> 20% of each run, Pallas kernels for 12% -> 13%
where the time goes in v19:
time: 245 us; the launch traced here: 244 us
  waiting for transfers between devices  107 us (44%)
  matrix products  45.5 us (19%)
  starting transfers between devices  32.3 us (13%)
  Pallas kernels  32 us (13%)
  blocking collectives  12.9 us (5%)
  local copies, waits for them, and re-layouts  10.9 us (4%)
  other arithmetic  2.71 us (1%)
    ppermute x3, waiting for transfers between devices, local(): arrived[step] = lax.ppermute(own_tokens, 'dp', partner_pairs(n_dp, step))  53.4 us
    pallas_call x5, Pallas kernels, attend(): pl.pallas_call(kernel, out_shape=jax.ShapeDtypeStruct((1, tile_count * TI...  32 us
    ppermute x2, waiting for transfers between devices, local(): partial_out = lax.ppermute(partial_out, 'dp', partner_pairs(n_dp, step))  27.6 us
    all_to_all x4, starting transfers between devices, local(): incoming = lax.all_to_all(payload, 'ctx', 0, 0, tiled=True)  19.3 us
    dot_general x4, matrix products, local(): jnp.einsum('td,sdh->sth', tokens, qkv_weight[1:3], preferred_element_type...  16.3 us
    all_to_all x4, waiting for transfers between devices, local(): incoming = lax.all_to_all(payload, 'ctx', 0, 0, tiled=True)  15.1 us
    dot_general x4, matrix products, local(): jnp.dot(tokens, qkv_weight[0], preferred_element_type=jnp.float32)  14.8 us
    all_gather x1, blocking collectives, local(): lax.all_gather(table, 'ctx', axis=0, tiled=True).astype(jnp.int32)  12.9 us
  transfers between devices with their start and end apart: 11, of which 7 were waited for; matrix products, arithmetic and copies ran while one was open for 20% of the time, Pallas kernels for 13%

profile of v19, /device:TPU:0, one launch (start us, length us, event | category | flops | bytes accessed | tf_op | source)
XLA Modules:
  0.0 243.7 jit_solution(9911549848698630230)
XLA Ops:
  0.0 3.9 %collective-permute-start = (bf16[256,3072]{1,0:T(8,128)(2,1)}, bf16[256,3072]{1,0:T(8,128)(2,1)}, u32[]{:S(2)}, u32[]{:S(2)}) collective-permute-start(bf16[256,3072]{1,0:T(8,128)(2,1)} %bitcast.157), channel_id=1, source_target_pairs={{0,24},{8,16},{16,8},{24,0},{1,25},{9,17},{17,9},{25,1},{2,26},{10... | collective-permute-start | bytes 4718600 | tf_op jit(solution)/shard_map/ppermute | solution.py:136
  5.4 12.9 %all-gather = f32[8,4,11]{2,1,0:T(4,128)S(1)} all-gather(f32[1,4,11]{2,1,0:T(4,128)S(1)} %fusion.79), channel_id=1, replica_groups=mesh['dp'=4,'ctx'=8] {'ctx'}, dimensions={0}, use_global_device_ids=true | all-gather | bytes 1584 | tf_op jit(solution)/shard_map/all_gather | solution.py:110
  19.1 19.5 %collective-permute-done = bf16[256,3072]{1,0:T(8,128)(2,1)} collective-permute-done((bf16[256,3072]{1,0:T(8,128)(2,1)}, bf16[256,3072]{1,0:T(8,128)(2,1)}, u32[]{:S(2)}, u32[]{:S(2)}) %collective-permute-start) | collective-permute-done | bytes 1572896 | tf_op jit(solution)/shard_map/ppermute | solution.py:136
  38.6 4.2 %fusion.31 = bf16[2,384,256]{1,2,0:T(8,128)(2,1)S(1)} fusion(bf16[3,3072,384]{2,1,0:T(8,128)(2,1)} %param.8, bf16[256,3072]{1,0:T(8,128)(2,1)} %collective-permute-done), kind=kOutput, calls=%fused_computation.39 | convolution fusion | flops 1208156160 | bytes 6684672 | tf_op jit(solution)/shard_map/td,sdh->sth/dot_general | solution.py:145
  44.8 5.2 %all-to-all-start = ((bf16[16,2,1,64,384]{4,3,2,1,0:T(8,128)(2,1)}), bf16[16,2,1,64,384]{4,3,2,1,0:T(8,128)(2,1)}, u32[]{:S(2)}, u32[]{:S(2)}) async-start(bf16[16,2,1,64,384]{4,3,2,1,0:T(8,128)(2,1)} %bitcast.149), calls=%async_computation | async-start | bytes 3145728 | tf_op jit(solution)/shard_map/all_to_all | solution.py:156
  53.2 33.9 %collective-permute-done.2 = bf16[256,3072]{1,0:T(8,128)(2,1)} collective-permute-done((bf16[256,3072]{1,0:T(8,128)(2,1)}, bf16[256,3072]{1,0:T(8,128)(2,1)}, u32[]{:S(2)}, u32[]{:S(2)}) %collective-permute-start.2) | collective-permute-done | bytes 1572896 | tf_op jit(solution)/shard_map/ppermute | solution.py:136
  87.1 4.2 %fusion.26 = bf16[2,384,256]{1,2,0:T(8,128)(2,1)S(1)} fusion(bf16[3,3072,384]{2,1,0:T(8,128)(2,1)} %param.8, bf16[256,3072]{1,0:T(8,128)(2,1)} %collective-permute-done.2), kind=kOutput, calls=%fused_computation.38 | convolution fusion | flops 1208156160 | bytes 6684672 | tf_op jit(solution)/shard_map/td,sdh->sth/dot_general | solution.py:145
  93.3 4.9 %all-to-all-start.1 = ((bf16[16,2,1,64,384]{4,3,2,1,0:T(8,128)(2,1)}), bf16[16,2,1,64,384]{4,3,2,1,0:T(8,128)(2,1)}, u32[]{:S(2)}, u32[]{:S(2)}) async-start(bf16[16,2,1,64,384]{4,3,2,1,0:T(8,128)(2,1)} %bitcast.146), calls=%async_computation.1 | async-start | bytes 3145728 | tf_op jit(solution)/shard_map/all_to_all | solution.py:156
  101.5 3.8 %fusion.67.q_ref = bf16[1,256,384]{2,1,0:T(8,128)(2,1)} fusion(bf16[256,3072]{1,0:T(8,128)(2,1)} %collective-permute-done, bf16[3,3072,384]{2,1,0:T(8,128)(2,1)} %param.8), kind=kOutput, calls=%fused_computation.49 | convolution fusion | flops 604078080 | bytes 4128768 | tf_op jit(solution)/shard_map/dot_general | solution.py:160
  105.4 4.2 %fusion.36 = bf16[256,2,384]{2,0,1:T(8,128)(2,1)S(1)} fusion(bf16[3,3072,384]{2,1,0:T(8,128)(2,1)} %param.8, bf16[256,3072]{1,0:T(8,128)(2,1)} %collective-permute-done.4), kind=kOutput, calls=%fused_computation.40 | convolution fusion | flops 1208156160 | bytes 6684672 | tf_op jit(solution)/shard_map/td,sdh->sth/dot_general | solution.py:145
  111.5 7.3 %shard_map.73 = bf16[1,256,384]{2,1,0:T(8,128)(2,1)} custom-call(s32[4,10]{1,0:T(4,128)} %add_select_fusion.2.pos_ref, s32[4]{0:T(128)} %count_ref.9, f32[4,3,10]{2,1,0:T(4,128)} %fusion.77.bias_ref, bf16[1,256,384]{2,1,0:T(8,128)(2,1)} %fusion.67.q_ref, bf16[4,2,1,64,384]{4,3,2,1,0:T(8,128)(2,1)} %bitcast.141, bf16[16,2,1,64,384]{4,3,2,1,0:T(8,128)(2,1)} %all-to-all-done.far_ref), custom_call_target="tpu_custom_call" | custom-call | tf_op jit(solution)/shard_map/pallas_call | solution.py:80
  121.9 14.2 %all-to-all-done.1.far_ref = bf16[16,2,1,64,384]{4,3,2,1,0:T(8,128)(2,1)} async-done(((bf16[16,2,1,64,384]{4,3,2,1,0:T(8,128)(2,1)}), bf16[16,2,1,64,384]{4,3,2,1,0:T(8,128)(2,1)}, u32[]{:S(2)}, u32[]{:S(2)}) %all-to-all-start.1) | async-done | bytes 1572896 | tf_op jit(solution)/shard_map/all_to_all | solution.py:156
  136.1 4.5 %all-to-all-start.2 = ((bf16[16,2,1,64,384]{4,3,2,1,0:T(8,128)(2,1)}), bf16[16,2,1,64,384]{4,3,2,1,0:T(8,128)(2,1)}, u32[]{:S(2)}, u32[]{:S(2)}) async-start(bf16[16,2,1,64,384]{4,3,2,1,0:T(8,128)(2,1)} %bitcast.148), calls=%async_computation.2 | async-start | bytes 3145728 | tf_op jit(solution)/shard_map/all_to_all | solution.py:156
  143.1 3.8 %fusion.64.q_ref = bf16[1,256,384]{2,1,0:T(8,128)(2,1)} fusion(bf16[256,3072]{1,0:T(8,128)(2,1)} %collective-permute-done.2, bf16[3,3072,384]{2,1,0:T(8,128)(2,1)} %param.8), kind=kOutput, calls=%fused_computation.48 | convolution fusion | flops 604078080 | bytes 4128768 | tf_op jit(solution)/shard_map/dot_general | solution.py:160
  152.7 7.3 %shard_map.74 = bf16[1,256,384]{2,1,0:T(8,128)(2,1)} custom-call(s32[4,10]{1,0:T(4,128)} %add_select_fusion.2.pos_ref, s32[4]{0:T(128)} %count_ref.9, f32[4,3,10]{2,1,0:T(4,128)} %fusion.77.bias_ref, bf16[1,256,384]{2,1,0:T(8,128)(2,1)} %fusion.64.q_ref, bf16[4,2,1,64,384]{4,3,2,1,0:T(8,128)(2,1)} %bitcast.143, ...), custom_call_target="tpu_custom_call" | custom-call | tf_op jit(solution)/shard_map/pallas_call | solution.py:80
  163.0 15.3 %collective-permute-done.1 = bf16[256,3072]{1,0:T(8,128)(2,1)} collective-permute-done((bf16[256,3072]{1,0:T(8,128)(2,1)}, bf16[256,3072]{1,0:T(8,128)(2,1)}, u32[]{:S(2)}, u32[]{:S(2)}) %collective-permute-start.1) | collective-permute-done | bytes 1572896 | tf_op jit(solution)/shard_map/ppermute | solution.py:182
  178.3 4.8 %all-to-all-start.3 = ((bf16[16,2,1,64,384]{4,3,2,1,0:T(8,128)(2,1)}), bf16[16,2,1,64,384]{4,3,2,1,0:T(8,128)(2,1)}, u32[]{:S(2)}, u32[]{:S(2)}) async-start(bf16[16,2,1,64,384]{4,3,2,1,0:T(8,128)(2,1)} %bitcast.147), calls=%async_computation.3 | async-start | bytes 3145728 | tf_op jit(solution)/shard_map/all_to_all | solution.py:156
  184.6 3.8 %fusion.61.q_ref = bf16[1,256,384]{2,1,0:T(8,128)(2,1)} fusion(bf16[256,3072]{1,0:T(8,128)(2,1)} %collective-permute-done.4, bf16[3,3072,384]{2,1,0:T(8,128)(2,1)} %param.8), kind=kOutput, calls=%fused_computation.47 | convolution fusion | flops 604078080 | bytes 4128768 | tf_op jit(solution)/shard_map/dot_general | solution.py:160
  188.4 5.1 %shard_map.76 = bf16[1,128,384]{2,1,0:T(8,128)(2,1)} custom-call(s32[4,10]{1,0:T(4,128)} %add_select_fusion.2.pos_ref, s32[4]{0:T(128)} %count_ref.9, f32[4,3,10]{2,1,0:T(4,128)} %fusion.77.bias_ref, bf16[1,256,384]{2,1,0:T(8,128)(2,1)} %fusion.61.q_ref, bf16[4,2,1,64,384]{4,3,2,1,0:T(8,128)(2,1)} %bitcast.138, ...), custom_call_target="tpu_custom_call" | custom-call | tf_op jit(solution)/shard_map/pallas_call | solution.py:80
  193.5 5.1 %shard_map.75 = bf16[1,128,384]{2,1,0:T(8,128)(2,1)} custom-call(s32[4,10]{1,0:T(4,128)} %add_select_fusion.2.pos_ref, s32[4]{0:T(128)} %count_ref.9, f32[4,3,10]{2,1,0:T(4,128)} %fusion.77.bias_ref, bf16[1,256,384]{2,1,0:T(8,128)(2,1)} %fusion.61.q_ref, bf16[4,2,1,64,384]{4,3,2,1,0:T(8,128)(2,1)} %bitcast.139, ...), custom_call_target="tpu_custom_call" | custom-call | tf_op jit(solution)/shard_map/pallas_call | solution.py:80
  207.9 12.3 %collective-permute-done.3 = bf16[256,3072]{1,0:T(8,128)(2,1)} collective-permute-done((bf16[256,3072]{1,0:T(8,128)(2,1)}, bf16[256,3072]{1,0:T(8,128)(2,1)}, u32[]{:S(2)}, u32[]{:S(2)}) %collective-permute-start.3) | collective-permute-done | bytes 1572896 | tf_op jit(solution)/shard_map/ppermute | solution.py:182
  221.0 7.3 %shard_map.77 = bf16[1,256,384]{2,1,0:T(8,128)(2,1)} custom-call(s32[4,10]{1,0:T(4,128)} %add_select_fusion.2.pos_ref, s32[4]{0:T(128)} %count_ref.9, f32[4,3,10]{2,1,0:T(4,128)} %fusion.77.bias_ref, bf16[1,256,384]{2,1,0:T(8,128)(2,1)} %fusion.58.q_ref, bf16[4,2,1,64,384]{4,3,2,1,0:T(8,128)(2,1)} %bitcast.145, ...), custom_call_target="tpu_custom_call" | custom-call | tf_op jit(solution)/shard_map/pallas_call | solution.py:80
  228.3 11.0 %collective-permute-done.5 = bf16[128,3072]{1,0:T(8,128)(2,1)} collective-permute-done((bf16[128,3072]{1,0:T(8,128)(2,1)}, bf16[128,3072]{1,0:T(8,128)(2,1)}, u32[]{:S(2)}, u32[]{:S(2)}) %collective-permute-start.5) | collective-permute-done | bytes 786464 | tf_op jit(solution)/shard_map/ppermute | solution.py:169
  239.4 4.3 %fusion.17 = bf16[1,256,3072]{2,1,0:T(8,128)(2,1)} fusion(bf16[256,3072]{1,0:T(8,128)(2,1)} %collective-permute-done.3, bf16[256,3072]{1,0:T(8,128)(2,1)} %collective-permute-done.1, bf16[128,3072]{1,0:T(8,128)(2,1)S(1)} %collective-permute-done.6, bf16[128,3072]{1,0:T(8,128)(2,1)} %collective-permute-done.5, bf16[384,3072]{1,0:T(8,128)(2,1)S(1)} %copy-done, ...), kind=kOutput, calls=%fused_computation.29 | convolution fusion | flops 613416960 | bytes 8847360 | tf_op jit(solution)/shard_map/dot_general | solution.py:177
  (87 shorter events, 40.6 us)
Async XLA Ops:
  0.0 118.8 %copy-start = (bf16[384,3072]{1,0:T(8,128)(2,1)S(1)}, bf16[384,3072]{1,0:T(8,128)(2,1)}, u32[]{:S(2)}) copy-start(bf16[384,3072]{1,0:T(8,128)(2,1)} %param.9) | copy-start | bytes 7077892
  0.0 38.6 %collective-permute-start = (bf16[256,3072]{1,0:T(8,128)(2,1)}, bf16[256,3072]{1,0:T(8,128)(2,1)}, u32[]{:S(2)}, u32[]{:S(2)}) collective-permute-start(bf16[256,3072]{1,0:T(8,128)(2,1)} %bitcast.157), channel_id=1, source_target_pairs={{0,24},{8,16},{16,8},{24,0},{1,25},{9,17},{17,9},{25,1},{2,26},{10... | collective-permute-start | bytes 4718600 | tf_op jit(solution)/shard_map/ppermute | solution.py:136
  42.9 1.9 copy-start.2
  44.8 8.2 %copy-start.8 = (s32[4,10]{1,0:T(4,128)S(1)}, s32[4,10]{1,0:T(4,128)}, u32[]{:S(2)}) copy-start(s32[4,10]{1,0:T(4,128)} %param.12) | copy-start | bytes 484
  44.8 8.3 %copy-start.6 = (s32[4,10]{1,0:T(4,128)S(1)}, s32[4,10]{1,0:T(4,128)}, u32[]{:S(2)}) copy-start(s32[4,10]{1,0:T(4,128)} %param.10) | copy-start | bytes 484
  44.8 48.5 %all-to-all-start = ((bf16[16,2,1,64,384]{4,3,2,1,0:T(8,128)(2,1)}), bf16[16,2,1,64,384]{4,3,2,1,0:T(8,128)(2,1)}, u32[]{:S(2)}, u32[]{:S(2)}) async-start(bf16[16,2,1,64,384]{4,3,2,1,0:T(8,128)(2,1)} %bitcast.149), calls=%async_computation | async-start | bytes 3145728 | tf_op jit(solution)/shard_map/all_to_all | solution.py:156
  50.0 37.1 %collective-permute-start.2 = (bf16[256,3072]{1,0:T(8,128)(2,1)}, bf16[256,3072]{1,0:T(8,128)(2,1)}, u32[]{:S(2)}, u32[]{:S(2)}) collective-permute-start(bf16[256,3072]{1,0:T(8,128)(2,1)} %bitcast.158), channel_id=1, source_target_pairs={{0,8},{8,0},{16,24},{24,16},{1,9},{9,1},{17,25},{25,17},{2,10},{10... | collective-permute-start | bytes 4718600 | tf_op jit(solution)/shard_map/ppermute | solution.py:136
  51.5 53.9 %collective-permute-start.4 = (bf16[256,3072]{1,0:T(8,128)(2,1)}, bf16[256,3072]{1,0:T(8,128)(2,1)}, u32[]{:S(2)}, u32[]{:S(2)}) collective-permute-start(bf16[256,3072]{1,0:T(8,128)(2,1)} %bitcast.159), channel_id=1, source_target_pairs={{0,16},{8,24},{16,0},{24,8},{1,17},{9,25},{17,1},{25,9},{2,18},{10... | collective-permute-start | bytes 4718600 | tf_op jit(solution)/shard_map/ppermute | solution.py:136
  91.4 1.9 copy-start.3
  93.3 4.9 %copy-start.7 = (s32[4]{0:T(128)S(1)}, s32[4]{0:T(128)}, u32[]{:S(2)}) copy-start(s32[4]{0:T(128)} %count_ref.9) | copy-start | bytes 52
  93.3 42.8 %all-to-all-start.1 = ((bf16[16,2,1,64,384]{4,3,2,1,0:T(8,128)(2,1)}), bf16[16,2,1,64,384]{4,3,2,1,0:T(8,128)(2,1)}, u32[]{:S(2)}, u32[]{:S(2)}) async-start(bf16[16,2,1,64,384]{4,3,2,1,0:T(8,128)(2,1)} %bitcast.146), calls=%async_computation.1 | async-start | bytes 3145728 | tf_op jit(solution)/shard_map/all_to_all | solution.py:156
  98.2 1.2 copy-start.9
  109.6 1.9 copy-start.1
  136.1 42.2 %all-to-all-start.2 = ((bf16[16,2,1,64,384]{4,3,2,1,0:T(8,128)(2,1)}), bf16[16,2,1,64,384]{4,3,2,1,0:T(8,128)(2,1)}, u32[]{:S(2)}, u32[]{:S(2)}) async-start(bf16[16,2,1,64,384]{4,3,2,1,0:T(8,128)(2,1)} %bitcast.148), calls=%async_computation.2 | async-start | bytes 3145728 | tf_op jit(solution)/shard_map/all_to_all | solution.py:156
  140.6 6.3 %copy-start.10 = (bf16[1,256,3072]{2,1,0:T(8,128)(2,1)S(1)}, bf16[1,256,3072]{2,1,0:T(8,128)(2,1)}, u32[]{:S(2)}) copy-start(bf16[1,256,3072]{2,1,0:T(8,128)(2,1)} %param.7) | copy-start | bytes 4718596
  140.6 37.7 %collective-permute-start.1 = (bf16[256,3072]{1,0:T(8,128)(2,1)}, bf16[256,3072]{1,0:T(8,128)(2,1)}, u32[]{:S(2)}, u32[]{:S(2)}) collective-permute-start(bf16[256,3072]{1,0:T(8,128)(2,1)} %convolution_convert_fusion.2), channel_id=1, source_target_pairs={{0,24},{8,16},{16,8},{24,0},{1,25},{9,17},{17,9},{25,1},{2,26},{10... | collective-permute-start | bytes 4718600 | tf_op jit(solution)/shard_map/ppermute | solution.py:182
  150.8 2.0 copy-start.4
  178.3 42.7 %all-to-all-start.3 = ((bf16[16,2,1,64,384]{4,3,2,1,0:T(8,128)(2,1)}), bf16[16,2,1,64,384]{4,3,2,1,0:T(8,128)(2,1)}, u32[]{:S(2)}, u32[]{:S(2)}) async-start(bf16[16,2,1,64,384]{4,3,2,1,0:T(8,128)(2,1)} %bitcast.147), calls=%async_computation.3 | async-start | bytes 3145728 | tf_op jit(solution)/shard_map/all_to_all | solution.py:156
  183.1 37.1 %collective-permute-start.3 = (bf16[256,3072]{1,0:T(8,128)(2,1)}, bf16[256,3072]{1,0:T(8,128)(2,1)}, u32[]{:S(2)}, u32[]{:S(2)}) collective-permute-start(bf16[256,3072]{1,0:T(8,128)(2,1)} %convolution_convert_fusion.1), channel_id=1, source_target_pairs={{0,8},{8,0},{16,24},{24,16},{1,9},{9,1},{17,25},{25,17},{2,10},{10... | collective-permute-start | bytes 4718600 | tf_op jit(solution)/shard_map/ppermute | solution.py:182
  198.6 2.4 copy-start.5
  200.9 3.6 %copy-start.11 = (bf16[1,256,3072]{2,1,0:T(8,128)(2,1)S(1)}, bf16[1,256,3072]{2,1,0:T(8,128)(2,1)}, u32[]{:S(2)}) copy-start(bf16[1,256,3072]{2,1,0:T(8,128)(2,1)} %param.7) | copy-start | bytes 4718596
  202.5 25.8 %collective-permute-start.6 = (bf16[128,3072]{1,0:T(8,128)(2,1)}, bf16[128,3072]{1,0:T(8,128)(2,1)S(1)}, u32[]{:S(2)}, u32[]{:S(2)}) collective-permute-start(bf16[128,3072]{1,0:T(8,128)(2,1)} %convolution_convert_fusion.3), channel_id=1, source_target_pairs={{0,16},{8,24},{16,0},{24,8},{1,17},{9,25},{17,1},{25,9},{2,18},{10... | collective-permute-start | bytes 2359304 | tf_op jit(solution)/shard_map/ppermute | solution.py:169
  204.0 35.3 %collective-permute-start.5 = (bf16[128,3072]{1,0:T(8,128)(2,1)}, bf16[128,3072]{1,0:T(8,128)(2,1)}, u32[]{:S(2)}, u32[]{:S(2)}) collective-permute-start(bf16[128,3072]{1,0:T(8,128)(2,1)} %convolution_convert_fusion.4), channel_id=1, source_target_pairs={{0,16},{8,24},{16,0},{24,8},{1,17},{9,25},{17,1},{25,9},{2,18},{10... | collective-permute-start | bytes 2359304 | tf_op jit(solution)/shard_map/ppermute | solution.py:169

commit v20 on v15

--- a/solution.py
+++ b/solution.py
@@ -166,7 +166,12 @@
             partial_out = lax.ppermute(partial_out, "dp", partner_pairs(n_dp, step))
             sent.append(partial_out)
         contribution = partial_out.astype(jnp.float32)
+        if index == len(order) - 2 and len(order) > 1:
+            late = contribution
+            continue
         total = contribution if total is None else total + contribution
+    if len(order) > 1:
+        total = lax.optimization_barrier(total) + late
     return total.astype(jnp.bfloat16)[None]
 
 

time: 240 us -> 238 us (level)
  other arithmetic: 2.67 us -> 5.7 us
  waiting for transfers between devices: 115 us -> 112 us
    broadcast_in_dim x0 -> x1, other arithmetic: none -> 3.02 us  [local(): return total.astype(jnp.bfloat16)[None]]
    ppermute x3, waiting for transfers between devices: 44.2 us -> 41.4 us  [local(): partial_out = lax.ppermute(partial_out, 'dp', partner_pairs(n_dp, step))]
  transfers between devices with their start and end apart: 10 -> 10, of which waited for: 7 -> 7; matrix products, arithmetic and copies ran while one was open for 16% -> 17% of each run, Pallas kernels for 12% -> 12%
where the time goes in v20:
time: 238 us; the launch traced here: 237 us
  waiting for transfers between devices  112 us (47%)
  matrix products  34.5 us (14%)
  starting transfers between devices  31.7 us (13%)
  Pallas kernels  29.1 us (12%)
  blocking collectives  12.9 us (5%)
  local copies, waits for them, and re-layouts  11 us (5%)
  other arithmetic  5.7 us (2%)
    ppermute x3, waiting for transfers between devices, local(): arrived[step] = lax.ppermute(own_tokens, 'dp', partner_pairs(n_dp, step))  53.5 us
    ppermute x3, waiting for transfers between devices, local(): partial_out = lax.ppermute(partial_out, 'dp', partner_pairs(n_dp, step))  41.4 us
    pallas_call x4, Pallas kernels, attend(): pl.pallas_call(kernel, out_shape=jax.ShapeDtypeStruct((1, token_count, wi...  29.1 us
    dot_general x4, matrix products, local(): jnp.einsum('td,sdh->sth', tokens, qkv_weight, preferred_element_type=jnp....  22.3 us
    all_to_all x4, starting transfers between devices, local(): incoming = lax.all_to_all(payload, 'ctx', 0, 0, tiled=True)  19.2 us
    all_to_all x4, waiting for transfers between devices, local(): incoming = lax.all_to_all(payload, 'ctx', 0, 0, tiled=True)  17.1 us
    all_gather x1, blocking collectives, local(): lax.all_gather(table, 'ctx', axis=0, tiled=True).astype(jnp.int32)  12.9 us
    dot_general x4, matrix products, local(): jnp.dot(attended[0], out_weight, preferred_element_type=jnp.float32)  12.2 us
  transfers between devices with their start and end apart: 10, of which 7 were waited for; matrix products, arithmetic and copies ran while one was open for 17% of the time, Pallas kernels for 12%

profile of v20, /device:TPU:0, one launch (start us, length us, event | category | flops | bytes accessed | tf_op | source)
XLA Modules:
  0.0 237.3 jit_solution(4689875595065516794)
XLA Ops:
  0.0 3.9 %collective-permute-start = (bf16[256,3072]{1,0:T(8,128)(2,1)}, bf16[256,3072]{1,0:T(8,128)(2,1)}, u32[]{:S(2)}, u32[]{:S(2)}) collective-permute-start(bf16[256,3072]{1,0:T(8,128)(2,1)} %bitcast.127), channel_id=1, source_target_pairs={{0,24},{8,16},{16,8},{24,0},{1,25},{9,17},{17,9},{25,1},{2,26},{10... | collective-permute-start | bytes 4718600 | tf_op jit(solution)/shard_map/ppermute | solution.py:136
  5.4 12.9 %all-gather = f32[8,4,11]{2,1,0:T(4,128)S(1)} all-gather(f32[1,4,11]{2,1,0:T(4,128)S(1)} %fusion.42), channel_id=1, replica_groups=mesh['dp'=4,'ctx'=8] {'ctx'}, dimensions={0}, use_global_device_ids=true | all-gather | bytes 1584 | tf_op jit(solution)/shard_map/all_gather | solution.py:110
  19.1 19.5 %collective-permute-done = bf16[256,3072]{1,0:T(8,128)(2,1)} collective-permute-done((bf16[256,3072]{1,0:T(8,128)(2,1)}, bf16[256,3072]{1,0:T(8,128)(2,1)}, u32[]{:S(2)}, u32[]{:S(2)}) %collective-permute-start) | collective-permute-done | bytes 1572896 | tf_op jit(solution)/shard_map/ppermute | solution.py:136
  38.6 5.7 %fusion.31.q_ref = bf16[3,256,384]{2,1,0:T(8,128)(2,1)S(1)} fusion(bf16[3,3072,384]{2,1,0:T(8,128)(2,1)} %param.8, bf16[256,3072]{1,0:T(8,128)(2,1)} %collective-permute-done), kind=kOutput, calls=%fused_computation.29 | convolution fusion | flops 1812234240 | bytes 9240576 | tf_op jit(solution)/shard_map/td,sdh->sth/dot_general | solution.py:145
  46.3 5.2 %all-to-all-start = ((bf16[16,2,1,64,384]{4,3,2,1,0:T(8,128)(2,1)}), bf16[16,2,1,64,384]{4,3,2,1,0:T(8,128)(2,1)}, u32[]{:S(2)}, u32[]{:S(2)}) async-start(bf16[16,2,1,64,384]{4,3,2,1,0:T(8,128)(2,1)} %bitcast.119), calls=%async_computation | async-start | bytes 3145728 | tf_op jit(solution)/shard_map/all_to_all | solution.py:156
  54.6 34.0 %collective-permute-done.2 = bf16[256,3072]{1,0:T(8,128)(2,1)S(1)} collective-permute-done((bf16[256,3072]{1,0:T(8,128)(2,1)}, bf16[256,3072]{1,0:T(8,128)(2,1)S(1)}, u32[]{:S(2)}, u32[]{:S(2)}) %collective-permute-start.2) | collective-permute-done | bytes 1572896 | tf_op jit(solution)/shard_map/ppermute | solution.py:136
  88.6 5.2 %fusion.28.q_ref = bf16[3,256,384]{2,1,0:T(8,128)(2,1)S(1)} fusion(bf16[3,3072,384]{2,1,0:T(8,128)(2,1)} %param.8, bf16[256,3072]{1,0:T(8,128)(2,1)S(1)} %collective-permute-done.2), kind=kOutput, calls=%fused_computation.28 | convolution fusion | flops 1812234240 | bytes 9240576 | tf_op jit(solution)/shard_map/td,sdh->sth/dot_general | solution.py:145
  95.9 4.7 %all-to-all-start.1 = ((bf16[16,2,1,64,384]{4,3,2,1,0:T(8,128)(2,1)}), bf16[16,2,1,64,384]{4,3,2,1,0:T(8,128)(2,1)}, u32[]{:S(2)}, u32[]{:S(2)}) async-start(bf16[16,2,1,64,384]{4,3,2,1,0:T(8,128)(2,1)} %bitcast.116), calls=%async_computation.1 | async-start | bytes 3145728 | tf_op jit(solution)/shard_map/all_to_all | solution.py:156
  104.1 5.7 %fusion.22.q_ref = bf16[3,256,384]{2,1,0:T(8,128)(2,1)S(1)} fusion(bf16[3,3072,384]{2,1,0:T(8,128)(2,1)} %param.8, bf16[256,3072]{1,0:T(8,128)(2,1)} %collective-permute-done.4), kind=kOutput, calls=%fused_computation.26 | convolution fusion | flops 1812234240 | bytes 9240576 | tf_op jit(solution)/shard_map/td,sdh->sth/dot_general | solution.py:145
  111.9 7.3 %shard_map.73 = bf16[1,256,384]{2,1,0:T(8,128)(2,1)} custom-call(s32[4,10]{1,0:T(4,128)} %add_select_fusion.2.pos_ref, s32[4]{0:T(128)} %count_ref.7, f32[4,3,10]{2,1,0:T(4,128)} %fusion.40.bias_ref, bf16[3,256,384]{2,1,0:T(8,128)(2,1)} %copy-done.5, bf16[4,2,1,64,384]{4,3,2,1,0:T(8,128)(2,1)} %bitcast.109, bf16[16,2,1,64,384]{4,3,2,1,0:T(8,128)(2,1)} %all-to-all-done.far_ref), custom_call_target="tpu_custom_call" | custom-call | tf_op jit(solution)/shard_map/pallas_call | solution.py:80
  119.1 3.2 %convolution_convert_fusion.3 = bf16[256,3072]{1,0:T(8,128)(2,1)} fusion(bf16[384,3072]{1,0:T(8,128)(2,1)S(1)} %copy-done, bf16[1,256,384]{2,1,0:T(8,128)(2,1)} %shard_map.73), kind=kOutput, calls=%fused_computation.10 | convolution fusion | flops 604766208 | bytes 4128768 | tf_op jit(solution)/shard_map/dot_general | solution.py:161
  122.3 16.2 %all-to-all-done.1.far_ref = bf16[16,2,1,64,384]{4,3,2,1,0:T(8,128)(2,1)} async-done(((bf16[16,2,1,64,384]{4,3,2,1,0:T(8,128)(2,1)}), bf16[16,2,1,64,384]{4,3,2,1,0:T(8,128)(2,1)}, u32[]{:S(2)}, u32[]{:S(2)}) %all-to-all-start.1) | async-done | bytes 1572896 | tf_op jit(solution)/shard_map/all_to_all | solution.py:156
  138.5 4.5 %all-to-all-start.3 = ((bf16[16,2,1,64,384]{4,3,2,1,0:T(8,128)(2,1)}), bf16[16,2,1,64,384]{4,3,2,1,0:T(8,128)(2,1)}, u32[]{:S(2)}, u32[]{:S(2)}) async-start(bf16[16,2,1,64,384]{4,3,2,1,0:T(8,128)(2,1)} %bitcast.118), calls=%async_computation.3 | async-start | bytes 3145728 | tf_op jit(solution)/shard_map/all_to_all | solution.py:156
  145.5 5.7 %fusion.25.q_ref = bf16[3,256,384]{2,1,0:T(8,128)(2,1)S(1)} fusion(bf16[3,3072,384]{2,1,0:T(8,128)(2,1)} %param.8, bf16[256,3072]{1,0:T(8,128)(2,1)} %bitcast.130), kind=kOutput, calls=%fused_computation.27 | convolution fusion | flops 1812234240 | bytes 9240576 | tf_op jit(solution)/shard_map/td,sdh->sth/dot_general | solution.py:145
  153.3 7.3 %shard_map.74 = bf16[1,256,384]{2,1,0:T(8,128)(2,1)} custom-call(s32[4,10]{1,0:T(4,128)} %add_select_fusion.2.pos_ref, s32[4]{0:T(128)} %count_ref.7, f32[4,3,10]{2,1,0:T(4,128)} %fusion.40.bias_ref, bf16[3,256,384]{2,1,0:T(8,128)(2,1)} %copy-done.6, bf16[4,2,1,64,384]{4,3,2,1,0:T(8,128)(2,1)} %bitcast.111, bf16[16,2,1,64,384]{4,3,2,1,0:T(8,128)(2,1)} %all-to-all-done.1.far_ref), custom_call_target="tpu_custom_call" | custom-call | tf_op jit(solution)/shard_map/pallas_call | solution.py:80
  160.6 3.1 %convolution_convert_fusion.2 = bf16[256,3072]{1,0:T(8,128)(2,1)} fusion(bf16[384,3072]{1,0:T(8,128)(2,1)S(1)} %copy-done, bf16[1,256,384]{2,1,0:T(8,128)(2,1)} %shard_map.74), kind=kOutput, calls=%fused_computation.9 | convolution fusion | flops 604766208 | bytes 4128768 | tf_op jit(solution)/shard_map/dot_general | solution.py:161
  163.6 17.1 %collective-permute-done.1 = bf16[256,3072]{1,0:T(8,128)(2,1)} collective-permute-done((bf16[256,3072]{1,0:T(8,128)(2,1)}, bf16[256,3072]{1,0:T(8,128)(2,1)}, u32[]{:S(2)}, u32[]{:S(2)}) %collective-permute-start.1) | collective-permute-done | bytes 1572896 | tf_op jit(solution)/shard_map/ppermute | solution.py:166
  180.7 4.8 %all-to-all-start.2 = ((bf16[16,2,1,64,384]{4,3,2,1,0:T(8,128)(2,1)}), bf16[16,2,1,64,384]{4,3,2,1,0:T(8,128)(2,1)}, u32[]{:S(2)}, u32[]{:S(2)}) async-start(bf16[16,2,1,64,384]{4,3,2,1,0:T(8,128)(2,1)} %bitcast.117), calls=%async_computation.2 | async-start | bytes 3145728 | tf_op jit(solution)/shard_map/all_to_all | solution.py:156
  187.0 7.3 %shard_map.76 = bf16[1,256,384]{2,1,0:T(8,128)(2,1)} custom-call(s32[4,10]{1,0:T(4,128)} %add_select_fusion.2.pos_ref, s32[4]{0:T(128)} %count_ref.7, f32[4,3,10]{2,1,0:T(4,128)} %fusion.40.bias_ref, bf16[3,256,384]{2,1,0:T(8,128)(2,1)} %copy-done.7, bf16[4,2,1,64,384]{4,3,2,1,0:T(8,128)(2,1)} %bitcast.113, bf16[16,2,1,64,384]{4,3,2,1,0:T(8,128)(2,1)} %all-to-all-done.3.far_ref), custom_call_target="tpu_custom_call" | custom-call | tf_op jit(solution)/shard_map/pallas_call | solution.py:80
  194.3 3.1 %convolution_convert_fusion = bf16[256,3072]{1,0:T(8,128)(2,1)} fusion(bf16[384,3072]{1,0:T(8,128)(2,1)S(1)} %copy-done, bf16[1,256,384]{2,1,0:T(8,128)(2,1)} %shard_map.76), kind=kOutput, calls=%fused_computation.6 | convolution fusion | flops 604766208 | bytes 4128768 | tf_op jit(solution)/shard_map/dot_general | solution.py:161
  198.9 23.7 %collective-permute-done.3 = bf16[256,3072]{1,0:T(8,128)(2,1)} collective-permute-done((bf16[256,3072]{1,0:T(8,128)(2,1)}, bf16[256,3072]{1,0:T(8,128)(2,1)}, u32[]{:S(2)}, u32[]{:S(2)}) %collective-permute-start.3) | collective-permute-done | bytes 1572896 | tf_op jit(solution)/shard_map/ppermute | solution.py:166
  223.5 7.3 %shard_map.75 = bf16[1,256,384]{2,1,0:T(8,128)(2,1)} custom-call(s32[4,10]{1,0:T(4,128)} %add_select_fusion.2.pos_ref, s32[4]{0:T(128)} %count_ref.7, f32[4,3,10]{2,1,0:T(4,128)} %fusion.40.bias_ref, bf16[3,256,384]{2,1,0:T(8,128)(2,1)} %copy-done.8, bf16[4,2,1,64,384]{4,3,2,1,0:T(8,128)(2,1)} %bitcast.115, bf16[16,2,1,64,384]{4,3,2,1,0:T(8,128)(2,1)} %all-to-all-done.2.far_ref), custom_call_target="tpu_custom_call" | custom-call | tf_op jit(solution)/shard_map/pallas_call | solution.py:80
  230.7 2.9 %add_add_fusion = f32[256,3072]{1,0:T(8,128)S(1)} fusion(bf16[256,3072]{1,0:T(8,128)(2,1)} %collective-permute-done.3, bf16[256,3072]{1,0:T(8,128)(2,1)} %collective-permute-done.1, bf16[384,3072]{1,0:T(8,128)(2,1)S(1)} %copy-done, bf16[1,256,384]{2,1,0:T(8,128)(2,1)} %shard_map.75), kind=kOutput, calls=%fused_computation.12 | convolution fusion | flops 608698368 | bytes 8847360 | tf_op jit(solution)/shard_map/dot_general | solution.py:161
  234.2 3.0 %fusion.1 = bf16[1,256,3072]{2,1,0:T(8,128)(2,1)} fusion(f32[256,3072]{1,0:T(8,128)S(1)} %add_add_fusion, bf16[256,3072]{1,0:T(8,128)(2,1)} %collective-permute-done.5), kind=kLoop, calls=%fused_computation.13 | loop fusion | flops 2359296 | bytes 6291456 | tf_op jit(solution)/shard_map/broadcast_in_dim | solution.py:175
  (86 shorter events, 23.6 us)
Async XLA Ops:
  0.0 119.1 %copy-start = (bf16[384,3072]{1,0:T(8,128)(2,1)S(1)}, bf16[384,3072]{1,0:T(8,128)(2,1)}, u32[]{:S(2)}) copy-start(bf16[384,3072]{1,0:T(8,128)(2,1)} %param.9) | copy-start | bytes 7077892
  0.0 38.6 %collective-permute-start = (bf16[256,3072]{1,0:T(8,128)(2,1)}, bf16[256,3072]{1,0:T(8,128)(2,1)}, u32[]{:S(2)}, u32[]{:S(2)}) collective-permute-start(bf16[256,3072]{1,0:T(8,128)(2,1)} %bitcast.127), channel_id=1, source_target_pairs={{0,24},{8,16},{16,8},{24,0},{1,25},{9,17},{17,9},{25,1},{2,26},{10... | collective-permute-start | bytes 4718600 | tf_op jit(solution)/shard_map/ppermute | solution.py:136
  44.3 2.0 copy-start.5
  44.4 1.9 copy-start.1
  46.3 8.2 %copy-start.9 = (s32[4,10]{1,0:T(4,128)S(1)}, s32[4,10]{1,0:T(4,128)}, u32[]{:S(2)}) copy-start(s32[4,10]{1,0:T(4,128)} %param.10) | copy-start | bytes 484
  46.3 49.5 %all-to-all-start = ((bf16[16,2,1,64,384]{4,3,2,1,0:T(8,128)(2,1)}), bf16[16,2,1,64,384]{4,3,2,1,0:T(8,128)(2,1)}, u32[]{:S(2)}, u32[]{:S(2)}) async-start(bf16[16,2,1,64,384]{4,3,2,1,0:T(8,128)(2,1)} %bitcast.119), calls=%async_computation | async-start | bytes 3145728 | tf_op jit(solution)/shard_map/all_to_all | solution.py:156
  51.6 37.0 %collective-permute-start.2 = (bf16[256,3072]{1,0:T(8,128)(2,1)}, bf16[256,3072]{1,0:T(8,128)(2,1)S(1)}, u32[]{:S(2)}, u32[]{:S(2)}) collective-permute-start(bf16[256,3072]{1,0:T(8,128)(2,1)} %bitcast.128), channel_id=1, source_target_pairs={{0,8},{8,0},{16,24},{24,16},{1,9},{9,1},{17,25},{25,17},{2,10},{10... | collective-permute-start | bytes 4718600 | tf_op jit(solution)/shard_map/ppermute | solution.py:136
  53.0 51.1 %collective-permute-start.4 = (bf16[256,3072]{1,0:T(8,128)(2,1)}, bf16[256,3072]{1,0:T(8,128)(2,1)}, u32[]{:S(2)}, u32[]{:S(2)}) collective-permute-start(bf16[256,3072]{1,0:T(8,128)(2,1)} %bitcast.129), channel_id=1, source_target_pairs={{0,16},{8,24},{16,0},{24,8},{1,17},{9,25},{17,1},{25,9},{2,18},{10... | collective-permute-start | bytes 4718600 | tf_op jit(solution)/shard_map/ppermute | solution.py:136
  93.8 2.0 copy-start.6
  93.9 1.9 copy-start.2
  95.8 4.8 %copy-start.10 = (s32[4]{0:T(128)S(1)}, s32[4]{0:T(128)}, u32[]{:S(2)}) copy-start(s32[4]{0:T(128)} %count_ref.7) | copy-start | bytes 52
  95.9 42.7 %all-to-all-start.1 = ((bf16[16,2,1,64,384]{4,3,2,1,0:T(8,128)(2,1)}), bf16[16,2,1,64,384]{4,3,2,1,0:T(8,128)(2,1)}, u32[]{:S(2)}, u32[]{:S(2)}) async-start(bf16[16,2,1,64,384]{4,3,2,1,0:T(8,128)(2,1)} %bitcast.116), calls=%async_computation.1 | async-start | bytes 3145728 | tf_op jit(solution)/shard_map/all_to_all | solution.py:156
  100.6 1.3 copy-start.12
  100.6 1.5 copy-start.11
  109.8 2.0 copy-start.7
  109.9 1.9 copy-start.3
  138.5 42.2 %all-to-all-start.3 = ((bf16[16,2,1,64,384]{4,3,2,1,0:T(8,128)(2,1)}), bf16[16,2,1,64,384]{4,3,2,1,0:T(8,128)(2,1)}, u32[]{:S(2)}, u32[]{:S(2)}) async-start(bf16[16,2,1,64,384]{4,3,2,1,0:T(8,128)(2,1)} %bitcast.118), calls=%async_computation.3 | async-start | bytes 3145728 | tf_op jit(solution)/shard_map/all_to_all | solution.py:156
  143.0 37.7 %collective-permute-start.1 = (bf16[256,3072]{1,0:T(8,128)(2,1)}, bf16[256,3072]{1,0:T(8,128)(2,1)}, u32[]{:S(2)}, u32[]{:S(2)}) collective-permute-start(bf16[256,3072]{1,0:T(8,128)(2,1)} %convolution_convert_fusion.3), channel_id=1, source_target_pairs={{0,24},{8,16},{16,8},{24,0},{1,25},{9,17},{17,9},{25,1},{2,26},{10... | collective-permute-start | bytes 4718600 | tf_op jit(solution)/shard_map/ppermute | solution.py:166
  151.2 2.0 copy-start.8
  151.4 1.9 copy-start.4
  180.7 42.7 %all-to-all-start.2 = ((bf16[16,2,1,64,384]{4,3,2,1,0:T(8,128)(2,1)}), bf16[16,2,1,64,384]{4,3,2,1,0:T(8,128)(2,1)}, u32[]{:S(2)}, u32[]{:S(2)}) async-start(bf16[16,2,1,64,384]{4,3,2,1,0:T(8,128)(2,1)} %bitcast.117), calls=%async_computation.2 | async-start | bytes 3145728 | tf_op jit(solution)/shard_map/all_to_all | solution.py:156
  185.5 37.1 %collective-permute-start.3 = (bf16[256,3072]{1,0:T(8,128)(2,1)}, bf16[256,3072]{1,0:T(8,128)(2,1)}, u32[]{:S(2)}, u32[]{:S(2)}) collective-permute-start(bf16[256,3072]{1,0:T(8,128)(2,1)} %convolution_convert_fusion.2), channel_id=1, source_target_pairs={{0,8},{8,0},{16,24},{24,16},{1,9},{9,1},{17,25},{25,17},{2,10},{10... | collective-permute-start | bytes 4718600 | tf_op jit(solution)/shard_map/ppermute | solution.py:166
  197.4 36.8 %collective-permute-start.5 = (bf16[256,3072]{1,0:T(8,128)(2,1)}, bf16[256,3072]{1,0:T(8,128)(2,1)}, u32[]{:S(2)}, u32[]{:S(2)}) collective-permute-start(bf16[256,3072]{1,0:T(8,128)(2,1)} %convolution_convert_fusion), channel_id=1, source_target_pairs={{0,16},{8,24},{16,0},{24,8},{1,17},{9,25},{17,1},{25,9},{2,18},{10... | collective-permute-start | bytes 4718600 | tf_op jit(solution)/shard_map/ppermute | solution.py:166

commit v21 on v17

--- a/solution.py
+++ b/solution.py
@@ -167,7 +167,12 @@
             partial_out = lax.ppermute(partial_out, "dp", partner_pairs(n_dp, step))
             sent.append(partial_out)
         contribution = partial_out.astype(jnp.float32)
+        if index == len(order) - 2 and len(order) > 1:
+            late = contribution
+            continue
         total = contribution if total is None else total + contribution
+    if len(order) > 1:
+        total = lax.optimization_barrier(total) + late
     return total.astype(jnp.bfloat16)[None]
 
 

time: 241 us -> 239 us (level)
  other arithmetic: 2.66 us -> 5.75 us
  waiting for transfers between devices: 108 us -> 105 us
    broadcast_in_dim x0 -> x1, other arithmetic: none -> 3.02 us  [local(): return total.astype(jnp.bfloat16)[None]]
    ppermute x3, waiting for transfers between devices: 39.2 us -> 36.2 us  [local(): partial_out = lax.ppermute(partial_out, 'dp', partner_pairs(n_dp, step))]
  transfers between devices with their start and end apart: 10 -> 10, of which waited for: 7 -> 7; matrix products, arithmetic and copies ran while one was open for 20% -> 21% of each run, Pallas kernels for 12% -> 12%
where the time goes in v21:
time: 239 us
  waiting for transfers between devices  105 us (44%)
  matrix products  43.3 us (18%)
  starting transfers between devices  31.6 us (13%)
  Pallas kernels  29.1 us (12%)
  blocking collectives  12.9 us (5%)
  local copies, waits for them, and re-layouts  11 us (5%)
  other arithmetic  5.75 us (2%)
    ppermute x3, waiting for transfers between devices, local(): arrived[step] = lax.ppermute(own_tokens, 'dp', partner_pairs(n_dp, step))  53.5 us
    ppermute x3, waiting for transfers between devices, local(): partial_out = lax.ppermute(partial_out, 'dp', partner_pairs(n_dp, step))  36.2 us
    pallas_call x4, Pallas kernels, attend(): pl.pallas_call(kernel, out_shape=jax.ShapeDtypeStruct((1, token_count, wi...  29.1 us
    all_to_all x4, starting transfers between devices, local(): incoming = lax.all_to_all(payload, 'ctx', 0, 0, tiled=True)  19.2 us
    dot_general x4, matrix products, local(): jnp.einsum('td,sdh->sth', tokens, qkv_weight[1:3], preferred_element_type...  16.3 us
    all_to_all x4, waiting for transfers between devices, local(): incoming = lax.all_to_all(payload, 'ctx', 0, 0, tiled=True)  15 us
    dot_general x4, matrix products, local(): jnp.dot(tokens, qkv_weight[0], preferred_element_type=jnp.float32)  14.7 us
    all_gather x1, blocking collectives, local(): lax.all_gather(table, 'ctx', axis=0, tiled=True).astype(jnp.int32)  12.9 us
  transfers between devices with their start and end apart: 10, of which 7 were waited for; matrix products, arithmetic and copies ran while one was open for 21% of the time, Pallas kernels for 12%

profile of v21, /device:TPU:0, one launch (start us, length us, event | category | flops | bytes accessed | tf_op | source)
XLA Modules:
  0.0 238.6 jit_solution(577006382730649341)
XLA Ops:
  0.0 3.9 %collective-permute-start = (bf16[256,3072]{1,0:T(8,128)(2,1)}, bf16[256,3072]{1,0:T(8,128)(2,1)}, u32[]{:S(2)}, u32[]{:S(2)}) collective-permute-start(bf16[256,3072]{1,0:T(8,128)(2,1)} %bitcast.152), channel_id=1, source_target_pairs={{0,24},{8,16},{16,8},{24,0},{1,25},{9,17},{17,9},{25,1},{2,26},{10... | collective-permute-start | bytes 4718600 | tf_op jit(solution)/shard_map/ppermute | solution.py:136
  5.4 12.9 %all-gather = f32[8,4,11]{2,1,0:T(4,128)S(1)} all-gather(f32[1,4,11]{2,1,0:T(4,128)S(1)} %fusion.78), channel_id=1, replica_groups=mesh['dp'=4,'ctx'=8] {'ctx'}, dimensions={0}, use_global_device_ids=true | all-gather | bytes 1584 | tf_op jit(solution)/shard_map/all_gather | solution.py:110
  19.1 19.5 %collective-permute-done = bf16[256,3072]{1,0:T(8,128)(2,1)} collective-permute-done((bf16[256,3072]{1,0:T(8,128)(2,1)}, bf16[256,3072]{1,0:T(8,128)(2,1)}, u32[]{:S(2)}, u32[]{:S(2)}) %collective-permute-start) | collective-permute-done | bytes 1572896 | tf_op jit(solution)/shard_map/ppermute | solution.py:136
  38.6 4.2 %fusion.31 = bf16[2,384,256]{1,2,0:T(8,128)(2,1)S(1)} fusion(bf16[3,3072,384]{2,1,0:T(8,128)(2,1)} %param.8, bf16[256,3072]{1,0:T(8,128)(2,1)} %collective-permute-done), kind=kOutput, calls=%fused_computation.39 | convolution fusion | flops 1208156160 | bytes 6684672 | tf_op jit(solution)/shard_map/td,sdh->sth/dot_general | solution.py:145
  44.8 5.2 %all-to-all-start = ((bf16[16,2,1,64,384]{4,3,2,1,0:T(8,128)(2,1)}), bf16[16,2,1,64,384]{4,3,2,1,0:T(8,128)(2,1)}, u32[]{:S(2)}, u32[]{:S(2)}) async-start(bf16[16,2,1,64,384]{4,3,2,1,0:T(8,128)(2,1)} %bitcast.144), calls=%async_computation | async-start | bytes 3145728 | tf_op jit(solution)/shard_map/all_to_all | solution.py:156
  53.2 33.9 %collective-permute-done.2 = bf16[256,3072]{1,0:T(8,128)(2,1)} collective-permute-done((bf16[256,3072]{1,0:T(8,128)(2,1)}, bf16[256,3072]{1,0:T(8,128)(2,1)}, u32[]{:S(2)}, u32[]{:S(2)}) %collective-permute-start.2) | collective-permute-done | bytes 1572896 | tf_op jit(solution)/shard_map/ppermute | solution.py:136
  87.1 4.2 %fusion.26 = bf16[2,384,256]{1,2,0:T(8,128)(2,1)S(1)} fusion(bf16[3,3072,384]{2,1,0:T(8,128)(2,1)} %param.8, bf16[256,3072]{1,0:T(8,128)(2,1)} %collective-permute-done.2), kind=kOutput, calls=%fused_computation.38 | convolution fusion | flops 1208156160 | bytes 6684672 | tf_op jit(solution)/shard_map/td,sdh->sth/dot_general | solution.py:145
  93.3 4.7 %all-to-all-start.1 = ((bf16[16,2,1,64,384]{4,3,2,1,0:T(8,128)(2,1)}), bf16[16,2,1,64,384]{4,3,2,1,0:T(8,128)(2,1)}, u32[]{:S(2)}, u32[]{:S(2)}) async-start(bf16[16,2,1,64,384]{4,3,2,1,0:T(8,128)(2,1)} %bitcast.141), calls=%async_computation.1 | async-start | bytes 3145728 | tf_op jit(solution)/shard_map/all_to_all | solution.py:156
  101.4 3.8 %fusion.67.q_ref = bf16[1,256,384]{2,1,0:T(8,128)(2,1)} fusion(bf16[256,3072]{1,0:T(8,128)(2,1)} %collective-permute-done, bf16[3,3072,384]{2,1,0:T(8,128)(2,1)} %param.8), kind=kOutput, calls=%fused_computation.49 | convolution fusion | flops 604078080 | bytes 4128768 | tf_op jit(solution)/shard_map/dot_general | solution.py:160
  105.2 4.2 %fusion.41 = bf16[256,2,384]{2,0,1:T(8,128)(2,1)S(1)} fusion(bf16[3,3072,384]{2,1,0:T(8,128)(2,1)} %param.8, bf16[256,3072]{1,0:T(8,128)(2,1)} %collective-permute-done.4), kind=kOutput, calls=%fused_computation.41 | convolution fusion | flops 1208156160 | bytes 6684672 | tf_op jit(solution)/shard_map/td,sdh->sth/dot_general | solution.py:145
  111.5 7.3 %shard_map.73 = bf16[1,256,384]{2,1,0:T(8,128)(2,1)} custom-call(s32[4,10]{1,0:T(4,128)} %add_select_fusion.2.pos_ref, s32[4]{0:T(128)} %count_ref.7, f32[4,3,10]{2,1,0:T(4,128)} %fusion.76.bias_ref, bf16[1,256,384]{2,1,0:T(8,128)(2,1)} %fusion.67.q_ref, bf16[4,2,1,64,384]{4,3,2,1,0:T(8,128)(2,1)} %bitcast.134, bf16[16,2,1,64,384]{4,3,2,1,0:T(8,128)(2,1)} %all-to-all-done.far_ref), custom_call_target="tpu_custom_call" | custom-call | tf_op jit(solution)/shard_map/pallas_call | solution.py:80
  121.8 14.1 %all-to-all-done.1.far_ref = bf16[16,2,1,64,384]{4,3,2,1,0:T(8,128)(2,1)} async-done(((bf16[16,2,1,64,384]{4,3,2,1,0:T(8,128)(2,1)}), bf16[16,2,1,64,384]{4,3,2,1,0:T(8,128)(2,1)}, u32[]{:S(2)}, u32[]{:S(2)}) %all-to-all-start.1) | async-done | bytes 1572896 | tf_op jit(solution)/shard_map/all_to_all | solution.py:156
  136.0 4.5 %all-to-all-start.3 = ((bf16[16,2,1,64,384]{4,3,2,1,0:T(8,128)(2,1)}), bf16[16,2,1,64,384]{4,3,2,1,0:T(8,128)(2,1)}, u32[]{:S(2)}, u32[]{:S(2)}) async-start(bf16[16,2,1,64,384]{4,3,2,1,0:T(8,128)(2,1)} %bitcast.143), calls=%async_computation.3 | async-start | bytes 3145728 | tf_op jit(solution)/shard_map/all_to_all | solution.py:156
  143.0 3.8 %fusion.64.q_ref = bf16[1,256,384]{2,1,0:T(8,128)(2,1)} fusion(bf16[256,3072]{1,0:T(8,128)(2,1)} %collective-permute-done.2, bf16[3,3072,384]{2,1,0:T(8,128)(2,1)} %param.8), kind=kOutput, calls=%fused_computation.48 | convolution fusion | flops 604078080 | bytes 4128768 | tf_op jit(solution)/shard_map/dot_general | solution.py:160
  146.8 3.8 %fusion.36 = bf16[256,2,384]{2,0,1:T(8,128)(2,1)S(1)} fusion(bf16[3,3072,384]{2,1,0:T(8,128)(2,1)} %param.8, bf16[256,3072]{1,0:T(8,128)(2,1)S(1)} %bitcast.155), kind=kOutput, calls=%fused_computation.40 | convolution fusion | flops 1208156160 | bytes 6684672 | tf_op jit(solution)/shard_map/td,sdh->sth/dot_general | solution.py:145
  152.5 7.3 %shard_map.74 = bf16[1,256,384]{2,1,0:T(8,128)(2,1)} custom-call(s32[4,10]{1,0:T(4,128)} %add_select_fusion.2.pos_ref, s32[4]{0:T(128)} %count_ref.7, f32[4,3,10]{2,1,0:T(4,128)} %fusion.76.bias_ref, bf16[1,256,384]{2,1,0:T(8,128)(2,1)} %fusion.64.q_ref, bf16[4,2,1,64,384]{4,3,2,1,0:T(8,128)(2,1)} %bitcast.136, ...), custom_call_target="tpu_custom_call" | custom-call | tf_op jit(solution)/shard_map/pallas_call | solution.py:80
  162.9 15.3 %collective-permute-done.1 = bf16[256,3072]{1,0:T(8,128)(2,1)} collective-permute-done((bf16[256,3072]{1,0:T(8,128)(2,1)}, bf16[256,3072]{1,0:T(8,128)(2,1)}, u32[]{:S(2)}, u32[]{:S(2)}) %collective-permute-start.1) | collective-permute-done | bytes 1572896 | tf_op jit(solution)/shard_map/ppermute | solution.py:167
  178.2 4.8 %all-to-all-start.2 = ((bf16[16,2,1,64,384]{4,3,2,1,0:T(8,128)(2,1)}), bf16[16,2,1,64,384]{4,3,2,1,0:T(8,128)(2,1)}, u32[]{:S(2)}, u32[]{:S(2)}) async-start(bf16[16,2,1,64,384]{4,3,2,1,0:T(8,128)(2,1)} %bitcast.142), calls=%async_computation.2 | async-start | bytes 3145728 | tf_op jit(solution)/shard_map/all_to_all | solution.py:156
  184.4 3.8 %fusion.58.q_ref = bf16[1,256,384]{2,1,0:T(8,128)(2,1)} fusion(bf16[256,3072]{1,0:T(8,128)(2,1)} %collective-permute-done.4, bf16[3,3072,384]{2,1,0:T(8,128)(2,1)} %param.8), kind=kOutput, calls=%fused_computation.46 | convolution fusion | flops 604078080 | bytes 4128768 | tf_op jit(solution)/shard_map/dot_general | solution.py:160
  188.2 7.3 %shard_map.76 = bf16[1,256,384]{2,1,0:T(8,128)(2,1)} custom-call(s32[4,10]{1,0:T(4,128)} %add_select_fusion.2.pos_ref, s32[4]{0:T(128)} %count_ref.7, f32[4,3,10]{2,1,0:T(4,128)} %fusion.76.bias_ref, bf16[1,256,384]{2,1,0:T(8,128)(2,1)} %fusion.58.q_ref, bf16[4,2,1,64,384]{4,3,2,1,0:T(8,128)(2,1)} %bitcast.138, ...), custom_call_target="tpu_custom_call" | custom-call | tf_op jit(solution)/shard_map/pallas_call | solution.py:80
  200.2 3.3 %fusion.61.q_ref = bf16[1,256,384]{2,1,0:T(8,128)(2,1)} fusion(bf16[256,3072]{1,0:T(8,128)(2,1)S(1)} %bitcast.156, bf16[3,3072,384]{2,1,0:T(8,128)(2,1)} %param.8), kind=kOutput, calls=%fused_computation.47 | convolution fusion | flops 604078080 | bytes 4128768 | tf_op jit(solution)/shard_map/dot_general | solution.py:160
  203.6 16.5 %collective-permute-done.3 = bf16[256,3072]{1,0:T(8,128)(2,1)} collective-permute-done((bf16[256,3072]{1,0:T(8,128)(2,1)}, bf16[256,3072]{1,0:T(8,128)(2,1)}, u32[]{:S(2)}, u32[]{:S(2)}) %collective-permute-start.3) | collective-permute-done | bytes 1572896 | tf_op jit(solution)/shard_map/ppermute | solution.py:167
  220.9 7.3 %shard_map.75 = bf16[1,256,384]{2,1,0:T(8,128)(2,1)} custom-call(s32[4,10]{1,0:T(4,128)} %add_select_fusion.2.pos_ref, s32[4]{0:T(128)} %count_ref.7, f32[4,3,10]{2,1,0:T(4,128)} %fusion.76.bias_ref, bf16[1,256,384]{2,1,0:T(8,128)(2,1)} %fusion.61.q_ref, bf16[4,2,1,64,384]{4,3,2,1,0:T(8,128)(2,1)} %bitcast.140, ...), custom_call_target="tpu_custom_call" | custom-call | tf_op jit(solution)/shard_map/pallas_call | solution.py:80
  231.1 4.4 %collective-permute-done.5 = bf16[256,3072]{1,0:T(8,128)(2,1)} collective-permute-done((bf16[256,3072]{1,0:T(8,128)(2,1)}, bf16[256,3072]{1,0:T(8,128)(2,1)}, u32[]{:S(2)}, u32[]{:S(2)}) %collective-permute-start.5) | collective-permute-done | bytes 1572896 | tf_op jit(solution)/shard_map/ppermute | solution.py:167
  (82 shorter events, 38.3 us)
Async XLA Ops:
  0.0 118.8 %copy-start = (bf16[384,3072]{1,0:T(8,128)(2,1)S(1)}, bf16[384,3072]{1,0:T(8,128)(2,1)}, u32[]{:S(2)}) copy-start(bf16[384,3072]{1,0:T(8,128)(2,1)} %param.9) | copy-start | bytes 7077892
  0.0 38.6 %collective-permute-start = (bf16[256,3072]{1,0:T(8,128)(2,1)}, bf16[256,3072]{1,0:T(8,128)(2,1)}, u32[]{:S(2)}, u32[]{:S(2)}) collective-permute-start(bf16[256,3072]{1,0:T(8,128)(2,1)} %bitcast.152), channel_id=1, source_target_pairs={{0,24},{8,16},{16,8},{24,0},{1,25},{9,17},{17,9},{25,1},{2,26},{10... | collective-permute-start | bytes 4718600 | tf_op jit(solution)/shard_map/ppermute | solution.py:136
  42.9 1.9 copy-start.1
  44.8 8.2 %copy-start.5 = (s32[4,10]{1,0:T(4,128)S(1)}, s32[4,10]{1,0:T(4,128)}, u32[]{:S(2)}) copy-start(s32[4,10]{1,0:T(4,128)} %param.10) | copy-start | bytes 484
  44.8 8.3 %copy-start.6 = (s32[4]{0:T(128)S(1)}, s32[4]{0:T(128)}, u32[]{:S(2)}) copy-start(s32[4]{0:T(128)} %count_ref.7) | copy-start | bytes 52
  44.8 48.5 %all-to-all-start = ((bf16[16,2,1,64,384]{4,3,2,1,0:T(8,128)(2,1)}), bf16[16,2,1,64,384]{4,3,2,1,0:T(8,128)(2,1)}, u32[]{:S(2)}, u32[]{:S(2)}) async-start(bf16[16,2,1,64,384]{4,3,2,1,0:T(8,128)(2,1)} %bitcast.144), calls=%async_computation | async-start | bytes 3145728 | tf_op jit(solution)/shard_map/all_to_all | solution.py:156
  50.0 37.1 %collective-permute-start.2 = (bf16[256,3072]{1,0:T(8,128)(2,1)}, bf16[256,3072]{1,0:T(8,128)(2,1)}, u32[]{:S(2)}, u32[]{:S(2)}) collective-permute-start(bf16[256,3072]{1,0:T(8,128)(2,1)} %bitcast.153), channel_id=1, source_target_pairs={{0,8},{8,0},{16,24},{24,16},{1,9},{9,1},{17,25},{25,17},{2,10},{10... | collective-permute-start | bytes 4718600 | tf_op jit(solution)/shard_map/ppermute | solution.py:136
  51.5 53.7 %collective-permute-start.4 = (bf16[256,3072]{1,0:T(8,128)(2,1)}, bf16[256,3072]{1,0:T(8,128)(2,1)}, u32[]{:S(2)}, u32[]{:S(2)}) collective-permute-start(bf16[256,3072]{1,0:T(8,128)(2,1)} %bitcast.154), channel_id=1, source_target_pairs={{0,16},{8,24},{16,0},{24,8},{1,17},{9,25},{17,1},{25,9},{2,18},{10... | collective-permute-start | bytes 4718600 | tf_op jit(solution)/shard_map/ppermute | solution.py:136
  91.4 1.9 copy-start.2
  93.3 42.7 %all-to-all-start.1 = ((bf16[16,2,1,64,384]{4,3,2,1,0:T(8,128)(2,1)}), bf16[16,2,1,64,384]{4,3,2,1,0:T(8,128)(2,1)}, u32[]{:S(2)}, u32[]{:S(2)}) async-start(bf16[16,2,1,64,384]{4,3,2,1,0:T(8,128)(2,1)} %bitcast.141), calls=%async_computation.1 | async-start | bytes 3145728 | tf_op jit(solution)/shard_map/all_to_all | solution.py:156
  98.0 1.2 copy-start.8
  98.0 1.3 copy-start.7
  109.5 2.0 copy-start.3
  136.0 42.2 %all-to-all-start.3 = ((bf16[16,2,1,64,384]{4,3,2,1,0:T(8,128)(2,1)}), bf16[16,2,1,64,384]{4,3,2,1,0:T(8,128)(2,1)}, u32[]{:S(2)}, u32[]{:S(2)}) async-start(bf16[16,2,1,64,384]{4,3,2,1,0:T(8,128)(2,1)} %bitcast.143), calls=%async_computation.3 | async-start | bytes 3145728 | tf_op jit(solution)/shard_map/all_to_all | solution.py:156
  140.5 6.3 %copy-start.9 = (bf16[1,256,3072]{2,1,0:T(8,128)(2,1)S(1)}, bf16[1,256,3072]{2,1,0:T(8,128)(2,1)}, u32[]{:S(2)}) copy-start(bf16[1,256,3072]{2,1,0:T(8,128)(2,1)} %param.7) | copy-start | bytes 4718596
  140.5 37.7 %collective-permute-start.1 = (bf16[256,3072]{1,0:T(8,128)(2,1)}, bf16[256,3072]{1,0:T(8,128)(2,1)}, u32[]{:S(2)}, u32[]{:S(2)}) collective-permute-start(bf16[256,3072]{1,0:T(8,128)(2,1)} %convolution_convert_fusion.3), channel_id=1, source_target_pairs={{0,24},{8,16},{16,8},{24,0},{1,25},{9,17},{17,9},{25,1},{2,26},{10... | collective-permute-start | bytes 4718600 | tf_op jit(solution)/shard_map/ppermute | solution.py:167
  150.6 1.9 copy-start.4
  178.2 42.7 %all-to-all-start.2 = ((bf16[16,2,1,64,384]{4,3,2,1,0:T(8,128)(2,1)}), bf16[16,2,1,64,384]{4,3,2,1,0:T(8,128)(2,1)}, u32[]{:S(2)}, u32[]{:S(2)}) async-start(bf16[16,2,1,64,384]{4,3,2,1,0:T(8,128)(2,1)} %bitcast.142), calls=%async_computation.2 | async-start | bytes 3145728 | tf_op jit(solution)/shard_map/all_to_all | solution.py:156
  182.9 37.1 %collective-permute-start.3 = (bf16[256,3072]{1,0:T(8,128)(2,1)}, bf16[256,3072]{1,0:T(8,128)(2,1)}, u32[]{:S(2)}, u32[]{:S(2)}) collective-permute-start(bf16[256,3072]{1,0:T(8,128)(2,1)} %convolution_convert_fusion.2), channel_id=1, source_target_pairs={{0,8},{8,0},{16,24},{24,16},{1,9},{9,1},{17,25},{25,17},{2,10},{10... | collective-permute-start | bytes 4718600 | tf_op jit(solution)/shard_map/ppermute | solution.py:167
  195.5 4.7 %copy-start.10 = (bf16[1,256,3072]{2,1,0:T(8,128)(2,1)S(1)}, bf16[1,256,3072]{2,1,0:T(8,128)(2,1)}, u32[]{:S(2)}) copy-start(bf16[1,256,3072]{2,1,0:T(8,128)(2,1)} %param.7) | copy-start | bytes 4718596
  198.7 36.8 %collective-permute-start.5 = (bf16[256,3072]{1,0:T(8,128)(2,1)}, bf16[256,3072]{1,0:T(8,128)(2,1)}, u32[]{:S(2)}, u32[]{:S(2)}) collective-permute-start(bf16[256,3072]{1,0:T(8,128)(2,1)} %convolution_convert_fusion), channel_id=1, source_target_pairs={{0,16},{8,24},{16,0},{24,8},{1,17},{9,25},{17,1},{25,9},{2,18},{10... | collective-permute-start | bytes 4718600 | tf_op jit(solution)/shard_map/ppermute | solution.py:167
